TPU v7x, 32 devices: a whole 2x2x4 slice. The times are simulated.
32 devices in a mesh: clips: 2 (over y), tm: 4 (over x, core), rows: 4 (over z).
Axes of the slice: x: 2, y: 2, z: 4, core: 2. Of those that a mesh axis runs over, the one named last changes fastest.
Arguments:
- segment_input: bfloat16 [4, 8, 4, 32, 384], P('clips', 'tm', 'rows'), parts along dimension 0, may hold values from -6 to 6
- inner_input: bfloat16 [4, 8, 4, 32, 384], P('clips', 'tm', 'rows'), parts along dimension 0, may hold values from -6 to 6
- lengths: int32 [4, 4], P('clips', 'tm'), parts along dimension 0, may hold values from 1 to 2
- inner_gain: float32 [384], replicated, may hold values from 0.25 to 1.75
- causal_weight: bfloat16 [3, 3, 3, 384, 384], replicated, may hold values from -0.0625 to 0.0625
- causal_bias: float32 [384], replicated, may hold values from -3 to 3
- attention_gain: float32 [384], replicated, may hold values from 0.25 to 1.75
- triple_weight: bfloat16 [384, 1152], replicated, may hold values from -0.4375 to 0.4375
- triple_bias: float32 [1152], replicated, may hold values from -150 to 150
- output_weight: bfloat16 [384, 384], replicated, may hold values from -0.3125 to 0.3125
- output_bias: float32 [384], replicated, may hold values from -3 to 3
Outputs:
- encoded: bfloat16 [4, 8, 4, 32, 384], P('clips', 'tm', 'rows'), parts along dimension 0
There are 2 independent parts, one for each index of `clips`. A program takes and returns all parts, laid end to end along the dimension named above; an argument that names none is the same for every part. Nothing has to cross between parts.
Inputs may be any that keep to these rules, and one draw needn't show every extreme that they name: The valid frames of a clip in a section are that section's first lengths[b, s] frame slots.
All inputs are finite; a program needn't handle non-finite values.
Results may differ from a plain program's by a relative error of at most 0.0062.
Values may be sent and summed in bfloat16 or wider, within the bound.
No kernel may reach another device: no remote copies, remote signals or barrier semaphores. Data moves between devices by JAX's collectives and lax.ppermute only.
A program may use at most 128 MiB of HBM per device.

v0:
```python
import math

import jax
import jax.numpy as jnp
from jax import lax
from jax.sharding import PartitionSpec as P

EPSILON = 1e-06


def prefix(part, axis, combine, identity):
    place = lax.axis_index(axis)
    gathered = jax.tree.map(lambda a: lax.all_gather(a, axis), part)
    state = jax.tree.map(lambda a, e: jnp.zeros_like(a) + jnp.asarray(e, a.dtype), part, identity)

    def one(step, state):
        return combine(
            state, jax.tree.map(lambda a: lax.dynamic_index_in_dim(a, step, 0, False), gathered)
        )

    return lax.fori_loop(0, place, one, state)


def as_sent(x):

    def short(part):
        return part.astype(jnp.bfloat16) if part.dtype == jnp.float32 else part

    return jax.tree.map(short, x)


def with_halo(cells, sides, width):
    for axis, dim in sides:
        count = lax.axis_size(axis)
        ends = count - 1
        head = lax.slice_in_dim(cells, 0, width, axis=dim)
        tail = lax.slice_in_dim(cells, cells.shape[dim] - width, cells.shape[dim], axis=dim)
        cells = jnp.concatenate(
            [
                lax.ppermute(tail, axis, [(i, (i + 1) % count) for i in range(ends)]),
                cells,
                lax.ppermute(head, axis, [((i + 1) % count, i) for i in range(ends)]),
            ],
            axis=dim,
        )
    return cells


def normalize(field, gain):
    widened = field.astype(jnp.float32)
    return widened * lax.rsqrt(jnp.mean(widened * widened, axis=-1, keepdims=True) + EPSILON) * gain


def last_two(extended, counts):
    slot_total = extended.shape[1]
    chosen = []
    for position in range(2):
        target = counts + position
        picked = jnp.zeros_like(extended[:, 0])
        for slot_index in range(slot_total):
            matches = (target == slot_index)[:, None, None, None]
            picked = jnp.where(matches, extended[:, slot_index], picked)
        chosen.append(picked)
    return jnp.stack(chosen, axis=1)


def summarize(activated, counts):
    blanks = jnp.zeros((activated.shape[0], 2) + activated.shape[2:], activated.dtype)
    summary = last_two(jnp.concatenate([blanks, activated], axis=1), counts)
    return (summary, jnp.minimum(counts, 2).astype(jnp.bfloat16))


def join_later(earlier, later):
    early_frames, early_count = earlier
    late_frames, late_count = later
    complete = (late_count > 1.5)[:, None, None, None, None]
    single = (late_count > 0.5)[:, None, None, None, None]
    shifted = jnp.concatenate([early_frames[:, 1:], late_frames[:, 1:]], axis=1)
    frames = jnp.where(complete, late_frames, jnp.where(single, shifted, early_frames))
    total_count = jnp.minimum(early_count + late_count, 2.0).astype(early_count.dtype)
    return (frames, total_count)


def incoming_cache(summary, counts):
    starting = (jnp.zeros_like(summary), jnp.zeros_like(counts))
    combined = prefix((summary, counts), "tm", join_later, starting)
    return combined[0]


def convolve(padded, causal_weight, causal_bias):
    clip_count, slot_total, rows_padded, column_count, channels = padded.shape
    frame_count = slot_total - 2
    row_count = rows_padded - 2
    widened = jnp.pad(padded, ((0, 0), (0, 0), (0, 0), (1, 1), (0, 0)))
    summed = jnp.zeros((clip_count * frame_count * row_count * column_count, channels), jnp.float32)
    for delta_time in range(3):
        for delta_row in range(3):
            window = widened[
                :, delta_time : delta_time + frame_count, delta_row : delta_row + row_count
            ]
            columns = jnp.concatenate(
                [window[:, :, :, delta_col : delta_col + column_count] for delta_col in range(3)],
                axis=-1,
            )
            kernel = causal_weight[delta_time, delta_row].reshape(3 * channels, channels)
            summed = summed + jnp.dot(
                columns.reshape(-1, 3 * channels), kernel, preferred_element_type=jnp.float32
            )
    return summed.reshape(clip_count, frame_count, row_count, column_count, channels) + causal_bias


def attend(normed, triple_weight, triple_bias, output_weight, output_bias):
    frame_count, places, channels = normed.shape
    packed = (
        jnp.dot(normed.reshape(-1, channels), triple_weight, preferred_element_type=jnp.float32)
        + triple_bias
    )
    packed = packed.reshape(frame_count, places, 3 * channels)
    queries = packed[:, :, :channels]
    key_vectors = packed[:, :, channels : 2 * channels]
    values = packed[:, :, 2 * channels :].astype(jnp.bfloat16)
    scores = jnp.einsum(
        "nqc,nkc->nqk", queries, key_vectors, precision=lax.Precision.HIGHEST
    ) / math.sqrt(channels)
    row_max = jnp.max(scores, axis=-1, keepdims=True)
    exponent = jnp.exp(scores - row_max)
    weights = (exponent / jnp.sum(exponent, axis=-1, keepdims=True)).astype(jnp.bfloat16)
    attended = jnp.einsum(
        "nqk,nkc->nqc", weights, values, preferred_element_type=jnp.float32
    ).astype(jnp.bfloat16)
    projected = (
        jnp.dot(attended.reshape(-1, channels), output_weight, preferred_element_type=jnp.float32)
        + output_bias
    )
    return projected.reshape(frame_count, places, channels).astype(jnp.bfloat16)


def body(
    segment_input,
    inner_input,
    lengths,
    inner_gain,
    causal_weight,
    causal_bias,
    attention_gain,
    triple_weight,
    triple_bias,
    output_weight,
    output_bias,
):
    clip_count, frame_count, row_count, column_count, channels = segment_input.shape
    activated = jax.nn.silu(normalize(inner_input, inner_gain)).astype(jnp.bfloat16)
    counts = lengths[:, 0]
    live_mask = (jnp.arange(frame_count, dtype=jnp.int32)[None, :] < counts[:, None]).astype(
        jnp.float32
    )
    carried = incoming_cache(*summarize(activated, counts))
    extended = jnp.concatenate([carried, activated], axis=1)
    padded = with_halo(as_sent(extended), (("rows", 2),), 1).astype(extended.dtype)
    convolved = convolve(padded, causal_weight, causal_bias)
    residual = (segment_input.astype(jnp.float32) + convolved).astype(jnp.bfloat16)
    residual = lax.optimization_barrier(residual)
    normed = normalize(residual, attention_gain).astype(jnp.bfloat16)
    row_devices = lax.axis_size("rows")
    per_device = clip_count * frame_count // row_devices
    grouped = normed.reshape(row_devices, per_device, row_count, column_count, channels)
    portion = lax.all_to_all(grouped, "rows", split_axis=0, concat_axis=2, tiled=True)
    owned = portion.shape[1]
    height = portion.shape[2]
    flat = portion.reshape(owned, height * column_count, channels)
    result = attend(flat, triple_weight, triple_bias, output_weight, output_bias)
    result = result.reshape(1, owned, height, column_count, channels)
    projected = lax.all_to_all(result, "rows", split_axis=2, concat_axis=0, tiled=True)
    projected = projected.reshape(clip_count, frame_count, row_count, column_count, channels)
    projected = lax.optimization_barrier(projected)
    summed = residual.astype(jnp.float32) + projected.astype(jnp.float32)
    return (summed * live_mask[:, :, None, None, None]).astype(jnp.bfloat16)


def solution(mesh):
    placed = (
        P("clips", "tm", "rows", None, None),
        P("clips", "tm", "rows", None, None),
        P("clips", "tm"),
        P(),
        P(),
        P(),
        P(),
        P(),
        P(),
        P(),
        P(),
    )
    return jax.shard_map(
        body,
        mesh=mesh,
        in_specs=placed,
        out_specs=P("clips", "tm", "rows", None, None),
        check_vma=False,
    )
```

profile of v0, /device:TPU:0, one launch (start us, length us, event | category | flops | bytes accessed | tf_op | source)
XLA Modules:
  0.0 58.6 jit_solution(12638604743484779682)
XLA Ops:
  0.0 0.0 copy-start
  0.0 0.7 %convert_bitcast_fusion = bf16[2]{0:T(256)(128)(2,1)S(1)} fusion(s32[2,1]{0,1:T(1,128)} %param.15), kind=kLoop, calls=%fused_computation.75 | loop fusion | flops 4 | bytes 12
  0.7 0.7 %broadcast_compare_fusion.1 = (pred[2]{0:T(512)(128)(4,1)S(1)}, pred[2]{0:T(512)(128)(4,1)S(1)}, pred[2]{0:T(512)(128)(4,1)S(1)}, pred[2]{0:T(512)(128)(4,1)S(1)}) fusion(s32[2,1]{0,1:T(1,128)} %param.15), kind=kLoop, calls=%fused_computation.79 | loop fusion | flops 10 | bytes 16 | tf_op jit(solution)/shard_map/eq | solution.py:61
  1.4 1.0 %fusion.7 = f32[2,2,32]{2,1,0:T(2,128)S(1)} fusion(bf16[2,2,1,32,384]{4,3,2,1,0:T(8,128)(2,1)} %param.14), kind=kLoop, calls=%fused_computation.45 | loop fusion | flops 147328 | bytes 98816 | tf_op jit(solution)/shard_map/reduce_sum | solution.py:51
  2.4 1.3 %dynamic-slice = u32[1]{0:T(128)} dynamic-slice(u32[32]{0:T(128)} %constant.64, u32[]{:T(128)S(6)} %add.130), dynamic_slice_sizes={1} | dynamic-slice | bytes 12
  4.3 0.2 dynamic-update-slice
  4.6 8.3 %all-reduce.1 = bf16[8]{0:T(256)(128)(2,1)S(1)} all-reduce(bf16[8]{0:T(256)(128)(2,1)S(1)} %dynamic-update-slice), channel_id=2, replica_groups=mesh['clips'=2,'tm'=4,'rows'=4] {'tm'}, use_global_device_ids=true, to_apply=%add.1 | all-reduce | flops 8 | bytes 32
  12.9 0.1 reshape.278
  13.0 1.0 %fusion.14 = bf16[2,2,1,32,384]{4,3,2,1,0:T(8,128)(2,1)S(1)} fusion(bf16[2,2,1,32,384]{4,3,2,1,0:T(8,128)(2,1)} %param.14, f32[384]{0:T(512)} %param.16, f32[2,2,32]{2,1,0:T(2,128)S(1)} %add_rsqrt_fusion.1), kind=kLoop, calls=%fused_computation.52 | loop fusion | flops 393216 | bytes 198656 | tf_op jit(solution)/shard_map/convert_element_type | solution.py:152
  14.0 0.1 select_select_fusion.1
  14.1 6.1 %all-gather.1 = bf16[8,2,1,32,384]{4,3,2,1,0:T(8,128)(2,1)S(1)} all-gather(bf16[2,2,1,32,384]{4,3,2,1,0:T(8,128)(2,1)S(1)} %pad_maximum_fusion.10), channel_id=3, replica_groups=mesh['clips'=2,'tm'=4,'rows'=4] {'tm'}, dimensions={0}, use_global_device_ids=true | all-gather | bytes 491520 | tf_op jit(solution)/shard_map/all_gather | solution.py:13
  20.4 1.3 %collective-permute-start.1 = (bf16[2,4,1,32,384]{4,3,2,1,0:T(8,128)(2,1)S(1)}, bf16[2,4,1,32,384]{4,3,2,1,0:T(8,128)(2,1)S(1)}, u32[]{:S(2)}, u32[]{:S(2)}) collective-permute-start(bf16[2,4,1,32,384]{4,3,2,1,0:T(8,128)(2,1)S(1)} %pad_maximum_fusion.9), channel_id=1, source_target_pairs={{1,0},{2,1},{3,2},{5,4},{6,5},{7,6},{9,8},{10,9},{11,10},{13,12},{... | collective-permute-start | bytes 589832 | tf_op jit(solution)/shard_map/ppermute | solution.py:42
  21.7 4.6 %collective-permute-start = (bf16[2,4,1,32,384]{4,3,2,1,0:T(8,128)(2,1)S(1)}, bf16[2,4,1,32,384]{4,3,2,1,0:T(8,128)(2,1)S(1)}, u32[]{:S(2)}, u32[]{:S(2)}) collective-permute-start(bf16[2,4,1,32,384]{4,3,2,1,0:T(8,128)(2,1)S(1)} %pad_maximum_fusion.9), channel_id=1, source_target_pairs={{0,1},{1,2},{2,3},{4,5},{5,6},{6,7},{8,9},{9,10},{10,11},{12,13},{... | collective-permute-start | bytes 589832 | tf_op jit(solution)/shard_map/ppermute | solution.py:40
  26.2 3.9 %fusion.29 = (bf16[1,1,3,384,384]{4,3,2,1,0:T(8,128)(2,1)S(1)}, bf16[1,1,3,384,384]{4,3,2,1,0:T(8,128)(2,1)S(1)}, bf16[1,1,3,384,384]{4,3,2,1,0:T(8,128)(2,1)S(1...) fusion(bf16[3,3,3,384,384]{4,3,2,1,0:T(8,128)(2,1)} %param.17), kind=kLoop, calls=%fused_computation.80 | loop fusion | bytes 15925248 | tf_op jit(solution)/shard_map/slice | solution.py:105
  30.2 0.0 collective-permute-done.1
  30.2 0.6 collective-permute-done
  30.8 0.3 select_maximum_fusion
  31.1 0.3 fusion.30
  31.5 0.1 pad_maximum_fusion
  31.5 0.3 fusion.34
  31.9 0.3 convolution_add_fusion.9
  32.2 0.1 pad_maximum_fusion.2
  32.3 0.3 convolution_add_fusion.8
  32.6 0.3 convolution_add_fusion.7
  32.9 0.1 pad_maximum_fusion.4
  33.0 0.3 convolution_add_fusion.6
  33.3 0.3 convolution_add_fusion.5
  33.6 0.1 pad_maximum_fusion.6
  33.7 0.3 convolution_add_fusion.4
  34.0 0.3 convolution_add_fusion.3
  34.4 0.0 copy-start.2
  34.4 0.0 copy-start.4
  34.4 0.0 copy-start.5
  34.4 0.0 copy-start.3
  34.4 0.3 convolution_add_fusion.2
  34.8 0.5 copy-done.2
  35.2 0.0 copy-done.4
  35.2 0.0 copy-start.1
  35.3 0.0 copy-start.6
  35.3 0.1 fusion.15
  35.4 0.0 copy-done.5
  35.4 0.1 fusion.17
  35.5 11.4 %all_to_all.8 = bf16[4,1,1,32,384]{4,3,2,1,0:T(8,128)(2,1)S(1)} all-to-all(bf16[4,1,1,32,384]{4,3,2,1,0:T(8,128)(2,1)S(1)} %bitcast.111), channel_id=1, replica_groups=mesh['clips'=2,'tm'=4,'rows'=4] {'rows'}, dimensions={0} | all-to-all | bytes 196608 | tf_op jit(solution)/shard_map/all_to_all | solution.py:167
  46.9 0.0 copy-done
  46.9 0.0 copy-done.3
  46.9 0.0 copy-start.7
  46.9 0.3 fusion.1
  47.3 0.4 fusion.33
  47.7 0.0 copy-done.1
  47.7 0.0 copy-done.6
  47.7 1.0 %fusion.3 = bf16[128,384]{1,0:T(8,128)(2,1)} fusion(bf16[384,384]{1,0:T(8,128)(2,1)S(1)} %copy-done.1, f32[1,128,1152]{2,1,0:T(8,128)S(1)} %fusion.1, f32[384]{0:T(512)S(1)} %copy-done.6, f32[128,128]{0,1:T(8,128)S(1)} %get-tuple-element.117, f32[128]{0:T(128)S(1)} %fusion.24, f32[128]{0:T(128)S(1)} %get-tuple-element.116), kind=kOutput, calls=%fused_computation.20 | convolution fusion | flops 50528256 | bytes 560128 | tf_op jit(solution)/shard_map/dot_general | solution.py:132
  48.8 3.3 %all-to-all-start.1 = ((bf16[1,1,4,32,384]{4,3,1,0,2:T(8,128)(2,1)}), bf16[1,1,4,32,384]{4,3,1,0,2:T(8,128)(2,1)S(1)}, u32[]{:S(2)}, u32[]{:S(2)}) async-start(bf16[1,1,4,32,384]{4,3,1,0,2:T(8,128)(2,1)} %bitcast.35), calls=%async_computation.1 | async-start | bytes 196608 | tf_op jit(solution)/shard_map/all_to_all | solution.py:173
  52.1 0.0 copy-done.7
  52.1 0.1 compare_convert_fusion
  52.2 5.7 %all-to-all-done.1 = bf16[1,1,4,32,384]{4,3,1,0,2:T(8,128)(2,1)S(1)} async-done(((bf16[1,1,4,32,384]{4,3,1,0,2:T(8,128)(2,1)}), bf16[1,1,4,32,384]{4,3,1,0,2:T(8,128)(2,1)S(1)}, u32[]{:S(2)}, u32[]{:S(2)}) %all-to-all-start.1) | async-done | bytes 98336 | tf_op jit(solution)/shard_map/all_to_all | solution.py:173
  57.9 0.7 %fusion.19 = bf16[2,2,1,32,384]{4,3,2,1,0:T(8,128)(2,1)} fusion(bf16[2,2,1,32,384]{4,3,2,1,0:T(8,128)(2,1)S(1)} %add_convert_fusion, bf16[2,2,1,32,384]{4,3,1,0,2:T(8,128)(2,1)S(1)} %bitcast.113, f32[2,2]{1,0:T(2,128)S(1)} %compare_convert_fusion), kind=kLoop, calls=%fused_computation.57 | loop fusion | flops 245760 | bytes 294928 | tf_op jit(solution)/shard_map/convert_element_type | solution.py:177
  (13 shorter events, 0.3 us)
Async XLA Ops:
  0.0 46.9 %copy-start = (bf16[384,1152]{1,0:T(8,128)(2,1)S(1)}, bf16[384,1152]{1,0:T(8,128)(2,1)}, u32[]{:S(2)}) copy-start(bf16[384,1152]{1,0:T(8,128)(2,1)} %param.20) | copy-start | bytes 2654212
  20.4 9.8 %collective-permute-start.1 = (bf16[2,4,1,32,384]{4,3,2,1,0:T(8,128)(2,1)S(1)}, bf16[2,4,1,32,384]{4,3,2,1,0:T(8,128)(2,1)S(1)}, u32[]{:S(2)}, u32[]{:S(2)}) collective-permute-start(bf16[2,4,1,32,384]{4,3,2,1,0:T(8,128)(2,1)S(1)} %pad_maximum_fusion.9), channel_id=1, source_target_pairs={{1,0},{2,1},{3,2},{5,4},{6,5},{7,6},{9,8},{10,9},{11,10},{13,12},{... | collective-permute-start | bytes 589832 | tf_op jit(solution)/shard_map/ppermute | solution.py:42
  21.7 9.1 %collective-permute-start = (bf16[2,4,1,32,384]{4,3,2,1,0:T(8,128)(2,1)S(1)}, bf16[2,4,1,32,384]{4,3,2,1,0:T(8,128)(2,1)S(1)}, u32[]{:S(2)}, u32[]{:S(2)}) collective-permute-start(bf16[2,4,1,32,384]{4,3,2,1,0:T(8,128)(2,1)S(1)} %pad_maximum_fusion.9), channel_id=1, source_target_pairs={{0,1},{1,2},{2,3},{4,5},{5,6},{6,7},{8,9},{9,10},{10,11},{12,13},{... | collective-permute-start | bytes 589832 | tf_op jit(solution)/shard_map/ppermute | solution.py:40
  34.4 0.9 %copy-start.2 = (bf16[2,2,1,32,384]{4,3,2,1,0:T(8,128)(2,1)S(1)}, bf16[2,2,1,32,384]{4,3,2,1,0:T(8,128)(2,1)}, u32[]{:S(2)}) copy-start(bf16[2,2,1,32,384]{4,3,2,1,0:T(8,128)(2,1)} %param.13) | copy-start | bytes 294916
  34.4 0.9 %copy-start.4 = (f32[384]{0:T(512)S(1)}, f32[384]{0:T(512)}, u32[]{:S(2)}) copy-start(f32[384]{0:T(512)} %param.18) | copy-start | bytes 4612
  34.4 1.0 %copy-start.5 = (f32[384]{0:T(512)S(1)}, f32[384]{0:T(512)}, u32[]{:S(2)}) copy-start(f32[384]{0:T(512)} %param.19) | copy-start | bytes 4612
  34.4 12.5 %copy-start.3 = (f32[1152]{0:T(1024)S(1)}, f32[1152]{0:T(1024)}, u32[]{:S(2)}) copy-start(f32[1152]{0:T(1024)} %param.21) | copy-start | bytes 13828
  35.2 12.5 %copy-start.1 = (bf16[384,384]{1,0:T(8,128)(2,1)S(1)}, bf16[384,384]{1,0:T(8,128)(2,1)}, u32[]{:S(2)}) copy-start(bf16[384,384]{1,0:T(8,128)(2,1)} %param.22) | copy-start | bytes 884740
  35.3 12.5 %copy-start.6 = (f32[384]{0:T(512)S(1)}, f32[384]{0:T(512)}, u32[]{:S(2)}) copy-start(f32[384]{0:T(512)} %param.23) | copy-start | bytes 4612
  46.9 5.2 %copy-start.7 = (s32[2,1]{0,1:T(1,128)S(1)}, s32[2,1]{0,1:T(1,128)}, u32[]{:S(2)}) copy-start(s32[2,1]{0,1:T(1,128)} %param.15) | copy-start | bytes 28
  48.8 9.1 %all-to-all-start.1 = ((bf16[1,1,4,32,384]{4,3,1,0,2:T(8,128)(2,1)}), bf16[1,1,4,32,384]{4,3,1,0,2:T(8,128)(2,1)S(1)}, u32[]{:S(2)}, u32[]{:S(2)}) async-start(bf16[1,1,4,32,384]{4,3,1,0,2:T(8,128)(2,1)} %bitcast.35), calls=%async_computation.1 | async-start | bytes 196608 | tf_op jit(solution)/shard_map/all_to_all | solution.py:173
where the time goes:
time: 59.1 us; the launch traced here: 58.6 us
  blocking collectives  25.9 us (44%)
  starting transfers between devices  9.15 us (15%)
  local copies, waits for them, and re-layouts  6.47 us (11%)
  waiting for transfers between devices  6.3 us (11%)
  other arithmetic  5.2 us (9%)
  matrix products  4.62 us (8%)
  between operations  0.98 us (2%)
    all_to_all x1, blocking collectives, body(): lax.all_to_all(grouped, 'rows', split_axis=0, concat_axis=2, tiled=True)  11.4 us
    unnamed x1, blocking collectives  8.31 us
    all_gather x1, blocking collectives, prefix(): gathered = jax.tree.map(lambda a: lax.all_gather(a, axis), part)  6.15 us
    all_to_all x1, waiting for transfers between devices, body(): lax.all_to_all(result, 'rows', split_axis=2, concat_axis=0, tiled=True)  5.72 us
    ppermute x1, starting transfers between devices, with_halo(): lax.ppermute(tail, axis, [(i, (i + 1) % count) for i in range(ends)])  4.56 us
    slice x1, local copies, waits for them, and re-layouts, convolve(): causal_weight[delta_time, delta_row].reshape(3 * channels, channels)  3.94 us
    all_to_all x1, starting transfers between devices, body(): lax.all_to_all(result, 'rows', split_axis=2, concat_axis=0, tiled=True)  3.3 us
    dot_general x9, matrix products, convolve(): jnp.dot(columns.reshape(-1, 3 * channels), kernel, preferred_element_type...  2.83 us
  transfers between devices with their start and end apart: 3, of which 2 were waited for; matrix products, arithmetic and copies ran while one was open for 7% of the time, Pallas kernels for 0%

commit v1 on v0

--- a/solution.py
+++ b/solution.py
@@ -177,6 +177,100 @@
     return (summed * live_mask[:, :, None, None, None]).astype(jnp.bfloat16)
 
 
+def activate(field, gain):
+    return jax.nn.silu(normalize(field, gain)).astype(jnp.bfloat16)
+
+
+def gathered_body(
+    segment_input,
+    inner_input,
+    lengths,
+    inner_gain,
+    causal_weight,
+    causal_bias,
+    attention_gain,
+    triple_weight,
+    triple_bias,
+    output_weight,
+    output_bias,
+):
+    clip_count, frame_count, row_count, column_count, channels = segment_input.shape
+    sections = lax.axis_size("tm")
+    inner_all = lax.all_gather(inner_input, "rows", axis=2, tiled=True)
+    segment_all = lax.all_gather(segment_input, "rows", axis=2, tiled=True)
+    counts = lengths[:, 0]
+    wide = (counts > 1)[:, None, None, None]
+    last_raw = jnp.where(wide, inner_all[:, frame_count - 1], inner_all[:, 0])
+    prev_raw = lax.ppermute(inner_all, "tm", [(i, i + 1) for i in range(sections - 1)])
+    prev_counts = lax.ppermute(counts, "tm", [(i, i + 1) for i in range(sections - 1)])
+    before_raw = lax.ppermute(last_raw, "tm", [(i, i + 2) for i in range(sections - 2)])
+    own = activate(inner_all, inner_gain)
+    prev = activate(prev_raw, inner_gain)
+    before = activate(before_raw, inner_gain)
+    prev_wide = (prev_counts > 1)[:, None, None, None]
+    carried = jnp.stack(
+        [
+            jnp.where(prev_wide, prev[:, frame_count - 2], before),
+            jnp.where(prev_wide, prev[:, frame_count - 1], prev[:, 0]),
+        ],
+        axis=1,
+    )
+    extended = jnp.concatenate([carried, own], axis=1)
+    padded = jnp.pad(extended, ((0, 0), (0, 0), (1, 1), (0, 0), (0, 0)))
+    convolved = convolve(padded, causal_weight, causal_bias)
+    residual = (segment_all.astype(jnp.float32) + convolved).astype(jnp.bfloat16)
+    normed = normalize(residual, attention_gain).astype(jnp.bfloat16)
+    height = normed.shape[2]
+    frames = clip_count * frame_count
+    places = height * column_count
+    flat = normed.reshape(frames * places, channels)
+    packed = (
+        jnp.dot(flat, triple_weight[:, channels:], preferred_element_type=jnp.float32)
+        + triple_bias[channels:]
+    ).reshape(frames, places, 2 * channels)
+    key_vectors = packed[:, :, :channels]
+    values = packed[:, :, channels:].astype(jnp.bfloat16)
+    start = lax.axis_index("rows") * row_count
+    mine = lax.dynamic_slice_in_dim(normed, start, row_count, axis=2)
+    queries = (
+        jnp.dot(
+            mine.reshape(-1, channels), triple_weight[:, :channels],
+            preferred_element_type=jnp.float32,
+        )
+        + triple_bias[:channels]
+    ).reshape(frames, row_count * column_count, channels)
+    scores = jnp.einsum(
+        "nqc,nkc->nqk", queries, key_vectors, precision=lax.Precision.HIGHEST
+    ) / math.sqrt(channels)
+    row_max = jnp.max(scores, axis=-1, keepdims=True)
+    exponent = jnp.exp(scores - row_max)
+    weights = (exponent / jnp.sum(exponent, axis=-1, keepdims=True)).astype(jnp.bfloat16)
+    attended = jnp.einsum(
+        "nqk,nkc->nqc", weights, values, preferred_element_type=jnp.float32
+    ).astype(jnp.bfloat16)
+    projected = (
+        jnp.dot(attended.reshape(-1, channels), output_weight, preferred_element_type=jnp.float32)
+        + output_bias
+    ).astype(jnp.bfloat16)
+    projected = projected.reshape(clip_count, frame_count, row_count, column_count, channels)
+    residual_mine = lax.dynamic_slice_in_dim(residual, start, row_count, axis=2)
+    live_mask = (jnp.arange(frame_count, dtype=jnp.int32)[None, :] < counts[:, None]).astype(
+        jnp.float32
+    )
+    summed = residual_mine.astype(jnp.float32) + projected.astype(jnp.float32)
+    return (summed * live_mask[:, :, None, None, None]).astype(jnp.bfloat16)
+
+
+GATHER_LIMIT = 1 << 22
+
+
+def chosen_body(segment_input, inner_input, *rest):
+    gathered = inner_input.size * inner_input.dtype.itemsize * lax.axis_size("rows")
+    if gathered <= GATHER_LIMIT:
+        return gathered_body(segment_input, inner_input, *rest)
+    return body(segment_input, inner_input, *rest)
+
+
 def solution(mesh):
     placed = (
         P("clips", "tm", "rows", None, None),
@@ -192,7 +286,7 @@
         P(),
     )
     return jax.shard_map(
-        body,
+        chosen_body,
         mesh=mesh,
         in_specs=placed,
         out_specs=P("clips", "tm", "rows", None, None),

time: 59.1 us -> 70.7 us (1.20)
  local copies, waits for them, and re-layouts: 6.47 us -> 15.4 us
  blocking collectives: 25.9 us -> 32.6 us
  waiting for transfers between devices: 6.3 us -> 0.01 us
  matrix products: 4.62 us -> 9.39 us
  starting transfers between devices: 9.15 us -> 6.7 us
    all_gather x1 -> x2, blocking collectives: 6.15 us -> 32.6 us  [the longest x1 16.6 us: gathered_body(): inner_all = lax.all_gather(inner_input, 'rows', axis=2, tiled=True)]
    all_to_all x1 -> x0, blocking collectives: 11.4 us -> none  [body(): lax.all_to_all(grouped, 'rows', split_axis=0, concat_axis=2, tiled=True)]
    unnamed x1 -> x0, blocking collectives: 8.31 us -> none
    all_to_all x1 -> x0, waiting for transfers between devices: 5.72 us -> none  [body(): lax.all_to_all(result, 'rows', split_axis=2, concat_axis=0, tiled=True)]
    dot_general x9, matrix products: 2.83 us -> 7.15 us  [convolve(): jnp.dot(columns.reshape(-1, 3 * channels), kernel, preferred_element_type...]
    slice x3 -> x2, local copies, waits for them, and re-layouts: 0.39 us -> 3.81 us  [convolve(): window[:, :, :, delta_col:delta_col + column_count]]
    all_to_all x1 -> x0, starting transfers between devices: 3.3 us -> none  [body(): lax.all_to_all(result, 'rows', split_axis=2, concat_axis=0, tiled=True)]
    unnamed x19 -> x34, local copies, waits for them, and re-layouts: 2.04 us -> 5.33 us
  transfers between devices with their start and end apart: 3 -> 3, of which waited for: 2 -> 0; matrix products, arithmetic and copies ran while one was open for 7% -> 11% of each run, Pallas kernels for 0% -> 0%
where the time goes in v1:
time: 70.7 us; the launch traced here: 70.2 us
  blocking collectives  32.6 us (46%)
  local copies, waits for them, and re-layouts  15.4 us (22%)
  matrix products  9.39 us (13%)
  starting transfers between devices  6.7 us (9%)
  other arithmetic  5.64 us (8%)
    all_gather x1, blocking collectives, gathered_body(): inner_all = lax.all_gather(inner_input, 'rows', axis=2, tiled=True)  16.6 us
    all_gather x1, blocking collectives, gathered_body(): segment_all = lax.all_gather(segment_input, 'rows', axis=2, tiled=True)  16 us
    dot_general x9, matrix products, convolve(): jnp.dot(columns.reshape(-1, 3 * channels), kernel, preferred_element_type...  7.15 us
    slice x1, local copies, waits for them, and re-layouts, convolve(): causal_weight[delta_time, delta_row].reshape(3 * channels, channels)  5.45 us
    unnamed x34, local copies, waits for them, and re-layouts  5.33 us
    ppermute x1, starting transfers between devices, gathered_body(): lax.ppermute(last_raw, 'tm', [(i, i + 2) for i in range(sections - 2)])  4 us
    slice x2, local copies, waits for them, and re-layouts, convolve(): window[:, :, :, delta_col:delta_col + column_count]  3.81 us
  transfers between devices with their start and end apart: 3, of which 0 were waited for; matrix products, arithmetic and copies ran while one was open for 11% of the time, Pallas kernels for 0%

profile of v1, /device:TPU:0, one launch (start us, length us, event | category | flops | bytes accessed | tf_op | source)
XLA Modules:
  0.0 70.2 jit_solution(4416258537205051209)
XLA Ops:
  0.0 16.6 %all_gather.7 = bf16[2,2,4,32,384]{4,3,2,1,0:T(8,128)(2,1)S(1)} all-gather(bf16[2,2,1,32,384]{4,3,2,1,0:T(8,128)(2,1)} %param.12), channel_id=1, replica_groups=mesh['clips'=2,'tm'=4,'rows'=4] {'rows'}, dimensions={2}, use_global_device_ids=true | all-gather | bytes 491520 | tf_op jit(solution)/shard_map/all_gather | solution.py:199
  16.6 0.8 %copy.33 = bf16[2,2,4,32,384]{4,3,2,0,1:T(8,128)(2,1)} copy(bf16[2,2,4,32,384]{4,3,2,1,0:T(8,128)(2,1)S(1)} %all_gather.7) | data formatting | bytes 786432 | tf_op jit(solution)/shard_map/all_gather | solution.py:199
  17.4 1.3 %collective-permute-start.1 = (bf16[2,2,4,32,384]{4,3,2,0,1:T(8,128)(2,1)}, bf16[2,2,4,32,384]{4,3,2,0,1:T(8,128)(2,1)S(1)}, u32[]{:S(2)}, u32[]{:S(2)}) collective-permute-start(bf16[2,2,4,32,384]{4,3,2,0,1:T(8,128)(2,1)} %copy.33), channel_id=1, source_target_pairs={{0,4},{4,8},{8,12},{1,5},{5,9},{9,13},{2,6},{6,10},{10,14},{3,7},{... | collective-permute-start | bytes 1179656 | tf_op jit(solution)/shard_map/ppermute | solution.py:204
  18.7 0.7 broadcast_compare_fusion
  19.4 0.8 %fusion.42 = bf16[2,4,32,384]{3,2,1,0:T(8,128)(2,1)} fusion(pred[2]{0:T(512)(128)(4,1)S(1)} %broadcast_compare_fusion, bf16[2,2,4,32,384]{4,3,2,1,0:T(8,128)(2,1)S(1)} %all_gather.7), kind=kLoop, calls=%fused_computation.98 | loop fusion | flops 98304 | bytes 589826 | tf_op jit(solution)/shard_map/jit(_where)/select_n | solution.py:203
  20.2 4.0 %collective-permute-start.2 = (bf16[2,4,32,384]{3,2,1,0:T(8,128)(2,1)}, bf16[2,4,32,384]{3,2,1,0:T(8,128)(2,1)S(1)}, u32[]{:S(2)}, u32[]{:S(2)}) collective-permute-start(bf16[2,4,32,384]{3,2,1,0:T(8,128)(2,1)} %fusion.42), channel_id=1, source_target_pairs={{0,8},{4,12},{1,9},{5,13},{2,10},{6,14},{3,11},{7,15},{16,24},{20,... | collective-permute-start | bytes 589832 | tf_op jit(solution)/shard_map/ppermute | solution.py:206
  24.2 1.4 %collective-permute-start = (s32[2]{0:T(128)S(1)}, s32[2]{0:T(128)S(1)}, u32[]{:S(2)}, u32[]{:S(2)}) collective-permute-start(s32[2]{0:T(128)S(1)} %bitcast.102), channel_id=1, source_target_pairs={{0,4},{4,8},{8,12},{1,5},{5,9},{9,13},{2,6},{6,10},{10,14},{3,7},{... | collective-permute-start | bytes 32 | tf_op jit(solution)/shard_map/ppermute | solution.py:205
  25.6 0.2 fusion.20
  25.8 0.1 compare_convert_fusion
  25.9 0.0 copy-start.10
  25.9 0.0 copy-start.11
  25.9 5.4 %fusion.52 = (bf16[1,1,3,384,384]{4,3,2,1,0:T(8,128)(2,1)S(1)}, bf16[1,1,3,384,384]{4,3,2,1,0:T(8,128)(2,1)}, bf16[1,1,3,384,384]{4,3,2,1,0:T(8,128)(2,1)}, bf16...) fusion(bf16[3,3,3,384,384]{4,3,2,1,0:T(8,128)(2,1)} %param.15), kind=kLoop, calls=%fused_computation.119 | loop fusion | bytes 15925248 | tf_op jit(solution)/shard_map/slice | solution.py:105
  31.3 16.0 %all_gather.6 = bf16[2,2,4,32,384]{4,3,2,1,0:T(8,128)(2,1)} all-gather(bf16[2,2,1,32,384]{4,3,2,1,0:T(8,128)(2,1)S(1)} %copy-done.10), channel_id=1, replica_groups=mesh['clips'=2,'tm'=4,'rows'=4] {'rows'}, dimensions={2}, use_global_device_ids=true | all-gather | bytes 491520 | tf_op jit(solution)/shard_map/all_gather | solution.py:200
  47.3 0.4 fusion.26
  47.7 0.0 collective-permute-done
  47.7 0.0 collective-permute-done.2
  47.7 0.1 fusion.31
  47.9 0.0 collective-permute-done.1
  47.9 0.2 fusion.12
  48.1 0.3 fusion.19
  48.4 0.1 fusion.41
  48.5 0.2 fusion.45
  48.7 0.1 fusion.6
  48.9 3.5 %pad_slice_fusion.1 = (bf16[2,2,4,32,384]{4,3,2,1,0:T(8,128)(2,1)S(1)}, bf16[2,2,4,32,384]{4,3,2,1,0:T(8,128)(2,1)S(1)}, bf16[2,2,4,32,384]{4,3,2,1,0:T(8,128)(2...) fusion(bf16[2,4,6,32,384]{4,3,2,1,0:T(8,128)(2,1)S(1)} %fusion.6), kind=kLoop, calls=%fused_computation.37 | loop fusion | bytes 9437184 | tf_op jit(solution)/shard_map/slice | solution.py:102
  52.4 0.3 fusion.53
  52.7 0.3 pad_maximum_fusion.1
  53.0 0.9 %copy-done.9 = bf16[1,1,3,384,384]{4,3,2,1,0:T(8,128)(2,1)S(1)} copy-done((bf16[1,1,3,384,384]{4,3,2,1,0:T(8,128)(2,1)S(1)}, bf16[1,1,3,384,384]{4,3,2,1,0:T(8,128)(2,1)}, u32[]{:S(2)}) %copy-start.9) | copy-done | bytes 884760
  53.9 0.8 %fusion.55 = f32[512,384]{1,0:T(8,128)S(1)} fusion(bf16[512,1152]{1,0:T(8,128)(2,1)S(1)} %bitcast.96, bf16[1152,384]{1,0:T(8,128)(2,1)S(1)} %bitcast.97), kind=kOutput, calls=%fused_computation.122 | convolution fusion | flops 452984832 | bytes 2850816 | tf_op jit(solution)/shard_map/dot_general | solution.py:106
  54.7 0.4 pad_maximum_fusion.7
  55.1 0.7 %copy-done.6 = bf16[1,1,3,384,384]{4,3,2,1,0:T(8,128)(2,1)S(1)} copy-done((bf16[1,1,3,384,384]{4,3,2,1,0:T(8,128)(2,1)S(1)}, bf16[1,1,3,384,384]{4,3,2,1,0:T(8,128)(2,1)}, u32[]{:S(2)}) %copy-start.6) | copy-done | bytes 884760
  55.8 0.8 %convolution_add_fusion.8 = f32[512,384]{1,0:T(8,128)S(1)} fusion(f32[512,384]{1,0:T(8,128)S(1)} %fusion.55, bf16[512,1152]{1,0:T(8,128)(2,1)S(1)} %bitcast.80, bf16[1152,384]{1,0:T(8,128)(2,1)S(1)} %bitcast.93), kind=kOutput, calls=%fused_computation.15 | convolution fusion | flops 453181440 | bytes 3637248 | tf_op jit(solution)/shard_map/dot_general | solution.py:106
  56.6 0.4 copy-done.5
  57.0 0.8 %convolution_add_fusion.7 = f32[512,384]{1,0:T(8,128)S(1)} fusion(f32[512,384]{1,0:T(8,128)S(1)} %convolution_add_fusion.8, bf16[512,1152]{1,0:T(8,128)(2,1)S(1)} %bitcast.81, bf16[1152,384]{1,0:T(8,128)(2,1)S(1)} %bitcast.92), kind=kOutput, calls=%fused_computation.14 | convolution fusion | flops 453181440 | bytes 3637248 | tf_op jit(solution)/shard_map/dot_general | solution.py:106
  57.8 0.3 pad_maximum_fusion.4
  58.1 0.9 %copy-done.4 = bf16[1,1,3,384,384]{4,3,2,1,0:T(8,128)(2,1)S(1)} copy-done((bf16[1,1,3,384,384]{4,3,2,1,0:T(8,128)(2,1)S(1)}, bf16[1,1,3,384,384]{4,3,2,1,0:T(8,128)(2,1)}, u32[]{:S(2)}) %copy-start.4) | copy-done | bytes 884760
  59.0 0.8 %convolution_add_fusion.6 = f32[512,384]{1,0:T(8,128)S(1)} fusion(f32[512,384]{1,0:T(8,128)S(1)} %convolution_add_fusion.7, bf16[512,1152]{1,0:T(8,128)(2,1)S(1)} %bitcast.84, bf16[1152,384]{1,0:T(8,128)(2,1)S(1)} %bitcast.91), kind=kOutput, calls=%fused_computation.13 | convolution fusion | flops 453181440 | bytes 3637248 | tf_op jit(solution)/shard_map/dot_general | solution.py:106
  59.8 0.4 copy-done.3
  60.1 0.8 %convolution_add_fusion.5 = f32[512,384]{1,0:T(8,128)S(1)} fusion(f32[512,384]{1,0:T(8,128)S(1)} %convolution_add_fusion.6, bf16[512,1152]{1,0:T(8,128)(2,1)S(1)} %bitcast.79, bf16[1152,384]{1,0:T(8,128)(2,1)S(1)} %bitcast.90), kind=kOutput, calls=%fused_computation.12 | convolution fusion | flops 453181440 | bytes 3637248 | tf_op jit(solution)/shard_map/dot_general | solution.py:106
  60.9 0.4 copy-done.2
  61.3 0.8 %convolution_add_fusion.4 = f32[512,384]{1,0:T(8,128)S(1)} fusion(f32[512,384]{1,0:T(8,128)S(1)} %convolution_add_fusion.5, bf16[512,1152]{1,0:T(8,128)(2,1)S(1)} %bitcast.83, bf16[1152,384]{1,0:T(8,128)(2,1)S(1)} %bitcast.89), kind=kOutput, calls=%fused_computation.11 | convolution fusion | flops 453181440 | bytes 3637248 | tf_op jit(solution)/shard_map/dot_general | solution.py:106
  62.1 0.0 copy-start.1
  62.1 0.3 pad_maximum_fusion.6
  62.4 0.9 %copy-done.1 = bf16[1,1,3,384,384]{4,3,2,1,0:T(8,128)(2,1)S(1)} copy-done((bf16[1,1,3,384,384]{4,3,2,1,0:T(8,128)(2,1)S(1)}, bf16[1,1,3,384,384]{4,3,2,1,0:T(8,128)(2,1)}, u32[]{:S(2)}) %copy-start.1) | copy-done | bytes 884760
  63.3 0.8 %convolution_add_fusion.3 = f32[512,384]{1,0:T(8,128)S(1)} fusion(f32[512,384]{1,0:T(8,128)S(1)} %convolution_add_fusion.4, bf16[512,1152]{1,0:T(8,128)(2,1)S(1)} %bitcast.85, bf16[1152,384]{1,0:T(8,128)(2,1)S(1)} %bitcast.88), kind=kOutput, calls=%fused_computation.10 | convolution fusion | flops 453181440 | bytes 3637248 | tf_op jit(solution)/shard_map/dot_general | solution.py:106
  64.1 0.8 %convolution_add_fusion.2 = f32[512,384]{1,0:T(8,128)S(1)} fusion(f32[512,384]{1,0:T(8,128)S(1)} %convolution_add_fusion.3, bf16[512,1152]{1,0:T(8,128)(2,1)S(1)} %bitcast.78, bf16[1152,384]{1,0:T(8,128)(2,1)S(1)} %bitcast.87), kind=kOutput, calls=%fused_computation.9 | convolution fusion | flops 453181440 | bytes 3637248 | tf_op jit(solution)/shard_map/dot_general | solution.py:106
  64.9 0.0 copy-start.13
  64.9 0.8 %convolution_add_fusion.1 = f32[512,384]{1,0:T(8,128)S(1)} fusion(f32[512,384]{1,0:T(8,128)S(1)} %convolution_add_fusion.2, bf16[512,1152]{1,0:T(8,128)(2,1)S(1)} %bitcast.82, bf16[1152,384]{1,0:T(8,128)(2,1)S(1)} %bitcast.86), kind=kOutput, calls=%fused_computation.8 | convolution fusion | flops 453181440 | bytes 3637248 | tf_op jit(solution)/shard_map/dot_general | solution.py:106
  65.7 0.0 copy-start.14
  65.7 0.0 copy-start.8
  65.7 0.1 copy-done.7
  65.9 0.2 fusion.22
  66.1 0.3 copy-done.14
  66.4 0.2 fusion.24
  66.6 0.0 slice-start
  66.7 0.3 copy-done.8
  66.9 0.6 convolution_add_fusion
  67.5 0.0 copy-start.15
  67.5 0.2 convolution_add_fusion.10
  67.7 1.0 %convolution_multiply_fusion = f32[4,32,128]{2,1,0:T(8,128)S(1)} fusion(f32[4,32,384]{2,1,0:T(8,128)S(1)} %bitcast.98, f32[4,128,768]{2,1,0:T(8,128)S(1)} %bitcast.76), kind=kOutput, calls=%fused_computation.35 | convolution fusion | flops 75513856 | bytes 1048576 | tf_op jit(solution)/shard_map/nqc,nkc->nqk/dot_general | solution.py:242
  68.7 0.2 fusion.54
  68.9 0.3 convolution_convert_fusion
  69.2 0.0 copy-done
  69.2 0.2 fusion.9
  69.4 0.7 %fusion.44 = bf16[2,2,1,32,384]{4,3,2,1,0:T(8,128)(2,1)} fusion(bf16[2,2,1,32,384]{4,3,2,1,0:T(8,128)(2,1)S(1)} %bitcast.101, f32[2,2]{1,0:T(2,128)S(1)} %compare_convert_fusion, bf16[2,2,4,32,384]{4,3,2,1,0:T(8,128)(2,1)S(1)} %get-tuple-element.6, s32[]{:T(128)S(6)} %select_n.18), kind=kLoop, calls=%fused_computation.102 | loop fusion | flops 245760 | bytes 294932 | tf_op jit(solution)/shard_map/convert_element_type | solution.py:261
  (23 shorter events, 0.1 us)
Async XLA Ops:
  0.0 69.2 %copy-start = (bf16[384,384]{1,0:T(8,128)(2,1)S(1)}, bf16[384,384]{1,0:T(8,128)(2,1)}, u32[]{:S(2)}) copy-start(bf16[384,384]{1,0:T(8,128)(2,1)} %param.20) | copy-start | bytes 884740
  0.0 24.2 %copy-start.16 = (s32[2,1]{0,1:T(1,128)S(1)}, s32[2,1]{0,1:T(1,128)}, u32[]{:S(2)}) copy-start(s32[2,1]{0,1:T(1,128)} %param.13) | copy-start | bytes 28
  0.0 25.7 %copy-start.12 = (f32[1152]{0:T(1024)S(1)}, f32[1152]{0:T(1024)}, u32[]{:S(2)}) copy-start(f32[1152]{0:T(1024)} %param.19) | copy-start | bytes 13828
  17.4 30.5 %collective-permute-start.1 = (bf16[2,2,4,32,384]{4,3,2,0,1:T(8,128)(2,1)}, bf16[2,2,4,32,384]{4,3,2,0,1:T(8,128)(2,1)S(1)}, u32[]{:S(2)}, u32[]{:S(2)}) collective-permute-start(bf16[2,2,4,32,384]{4,3,2,0,1:T(8,128)(2,1)} %copy.33), channel_id=1, source_target_pairs={{0,4},{4,8},{8,12},{1,5},{5,9},{9,13},{2,6},{6,10},{10,14},{3,7},{... | collective-permute-start | bytes 1179656 | tf_op jit(solution)/shard_map/ppermute | solution.py:204
  20.2 27.6 %collective-permute-start.2 = (bf16[2,4,32,384]{3,2,1,0:T(8,128)(2,1)}, bf16[2,4,32,384]{3,2,1,0:T(8,128)(2,1)S(1)}, u32[]{:S(2)}, u32[]{:S(2)}) collective-permute-start(bf16[2,4,32,384]{3,2,1,0:T(8,128)(2,1)} %fusion.42), channel_id=1, source_target_pairs={{0,8},{4,12},{1,9},{5,13},{2,10},{6,14},{3,11},{7,15},{16,24},{20,... | collective-permute-start | bytes 589832 | tf_op jit(solution)/shard_map/ppermute | solution.py:206
  24.2 23.5 %collective-permute-start = (s32[2]{0:T(128)S(1)}, s32[2]{0:T(128)S(1)}, u32[]{:S(2)}, u32[]{:S(2)}) collective-permute-start(s32[2]{0:T(128)S(1)} %bitcast.102), channel_id=1, source_target_pairs={{0,4},{4,8},{8,12},{1,5},{5,9},{9,13},{2,6},{6,10},{10,14},{3,7},{... | collective-permute-start | bytes 32 | tf_op jit(solution)/shard_map/ppermute | solution.py:205
  25.9 5.5 %copy-start.10 = (bf16[2,2,1,32,384]{4,3,2,1,0:T(8,128)(2,1)S(1)}, bf16[2,2,1,32,384]{4,3,2,1,0:T(8,128)(2,1)}, u32[]{:S(2)}) copy-start(bf16[2,2,1,32,384]{4,3,2,1,0:T(8,128)(2,1)} %param.11) | copy-start | bytes 294916
  25.9 21.5 %copy-start.11 = (f32[384]{0:T(512)S(1)}, f32[384]{0:T(512)}, u32[]{:S(2)}) copy-start(f32[384]{0:T(512)} %param.14) | copy-start | bytes 4612
  52.7 1.2 %copy-start.9 = (bf16[1,1,3,384,384]{4,3,2,1,0:T(8,128)(2,1)S(1)}, bf16[1,1,3,384,384]{4,3,2,1,0:T(8,128)(2,1)}, u32[]{:S(2)}) copy-start(bf16[1,1,3,384,384]{4,3,2,1,0:T(8,128)(2,1)} %get-tuple-element.14) | copy-start | bytes 2654212
  54.7 1.2 %copy-start.6 = (bf16[1,1,3,384,384]{4,3,2,1,0:T(8,128)(2,1)S(1)}, bf16[1,1,3,384,384]{4,3,2,1,0:T(8,128)(2,1)}, u32[]{:S(2)}) copy-start(bf16[1,1,3,384,384]{4,3,2,1,0:T(8,128)(2,1)} %get-tuple-element.13) | copy-start | bytes 2654212
  55.8 1.2 %copy-start.5 = (bf16[1,1,3,384,384]{4,3,2,1,0:T(8,128)(2,1)S(1)}, bf16[1,1,3,384,384]{4,3,2,1,0:T(8,128)(2,1)}, u32[]{:S(2)}) copy-start(bf16[1,1,3,384,384]{4,3,2,1,0:T(8,128)(2,1)} %get-tuple-element.12) | copy-start | bytes 2654212
  57.8 1.2 %copy-start.4 = (bf16[1,1,3,384,384]{4,3,2,1,0:T(8,128)(2,1)S(1)}, bf16[1,1,3,384,384]{4,3,2,1,0:T(8,128)(2,1)}, u32[]{:S(2)}) copy-start(bf16[1,1,3,384,384]{4,3,2,1,0:T(8,128)(2,1)} %get-tuple-element.11) | copy-start | bytes 2654212
  59.0 1.2 %copy-start.3 = (bf16[1,1,3,384,384]{4,3,2,1,0:T(8,128)(2,1)S(1)}, bf16[1,1,3,384,384]{4,3,2,1,0:T(8,128)(2,1)}, u32[]{:S(2)}) copy-start(bf16[1,1,3,384,384]{4,3,2,1,0:T(8,128)(2,1)} %get-tuple-element.10) | copy-start | bytes 2654212
  60.1 1.2 %copy-start.2 = (bf16[1,1,3,384,384]{4,3,2,1,0:T(8,128)(2,1)S(1)}, bf16[1,1,3,384,384]{4,3,2,1,0:T(8,128)(2,1)}, u32[]{:S(2)}) copy-start(bf16[1,1,3,384,384]{4,3,2,1,0:T(8,128)(2,1)} %get-tuple-element.9) | copy-start | bytes 2654212
  62.1 1.2 %copy-start.1 = (bf16[1,1,3,384,384]{4,3,2,1,0:T(8,128)(2,1)S(1)}, bf16[1,1,3,384,384]{4,3,2,1,0:T(8,128)(2,1)}, u32[]{:S(2)}) copy-start(bf16[1,1,3,384,384]{4,3,2,1,0:T(8,128)(2,1)} %get-tuple-element.8) | copy-start | bytes 2654212
  64.9 1.0 %copy-start.7 = (bf16[2,2,4,32,384]{4,3,2,1,0:T(8,128)(2,1)S(1)}, bf16[2,2,4,32,384]{4,3,2,1,0:T(8,128)(2,1)}, u32[]{:S(2)}) copy-start(bf16[2,2,4,32,384]{4,3,2,1,0:T(8,128)(2,1)} %all_gather.6) | copy-start | bytes 1179652
  64.9 1.0 %copy-start.13 = (f32[384]{0:T(512)S(1)}, f32[384]{0:T(512)}, u32[]{:S(2)}) copy-start(f32[384]{0:T(512)} %param.16) | copy-start | bytes 4612
  65.7 0.7 %copy-start.14 = (f32[384]{0:T(512)S(1)}, f32[384]{0:T(512)}, u32[]{:S(2)}) copy-start(f32[384]{0:T(512)} %param.17) | copy-start | bytes 4612
  65.7 1.2 %copy-start.8 = (bf16[384,1152]{1,0:T(8,128)(2,1)S(1)}, bf16[384,1152]{1,0:T(8,128)(2,1)}, u32[]{:S(2)}) copy-start(bf16[384,1152]{1,0:T(8,128)(2,1)} %param.18) | copy-start | bytes 2654212
  66.6 0.9 %slice-start = ((f32[1152]{0:T(1024)}), f32[384]{0:T(512)S(1)}, s32[]{:S(2)}) async-start(f32[1152]{0:T(1024)} %param.19), calls=%async_computation | async-start | bytes 4096 | tf_op jit(solution)/shard_map/slice | solution.py:240
  67.5 1.7 %copy-start.15 = (f32[384]{0:T(512)S(1)}, f32[384]{0:T(512)}, u32[]{:S(2)}) copy-start(f32[384]{0:T(512)} %param.21) | copy-start | bytes 4612

commit v2 on v1

--- a/solution.py
+++ b/solution.py
@@ -181,6 +181,17 @@
     return jax.nn.silu(normalize(field, gain)).astype(jnp.bfloat16)
 
 
+def conv3d(frames, causal_weight, time_padding):
+    return lax.conv_general_dilated(
+        frames,
+        causal_weight,
+        window_strides=(1, 1, 1),
+        padding=(time_padding, (1, 1), (1, 1)),
+        dimension_numbers=("NDHWC", "DHWIO", "NDHWC"),
+        preferred_element_type=jnp.float32,
+    )
+
+
 def gathered_body(
     segment_input,
     inner_input,
@@ -196,15 +207,19 @@
 ):
     clip_count, frame_count, row_count, column_count, channels = segment_input.shape
     sections = lax.axis_size("tm")
-    inner_all = lax.all_gather(inner_input, "rows", axis=2, tiled=True)
-    segment_all = lax.all_gather(segment_input, "rows", axis=2, tiled=True)
     counts = lengths[:, 0]
+    ahead = [(i, i + 1) for i in range(sections - 1)]
+    prev_counts = lax.ppermute(counts, "tm", ahead)
+    both = jnp.concatenate([inner_input, segment_input], axis=0)
+    both_all = lax.all_gather(both, "rows", axis=2, tiled=True)
+    inner_all = both_all[:clip_count]
+    segment_all = both_all[clip_count:]
     wide = (counts > 1)[:, None, None, None]
     last_raw = jnp.where(wide, inner_all[:, frame_count - 1], inner_all[:, 0])
-    prev_raw = lax.ppermute(inner_all, "tm", [(i, i + 1) for i in range(sections - 1)])
-    prev_counts = lax.ppermute(counts, "tm", [(i, i + 1) for i in range(sections - 1)])
+    prev_raw = lax.ppermute(inner_all, "tm", ahead)
     before_raw = lax.ppermute(last_raw, "tm", [(i, i + 2) for i in range(sections - 2)])
     own = activate(inner_all, inner_gain)
+    own_part = conv3d(own, causal_weight, (2, 0))
     prev = activate(prev_raw, inner_gain)
     before = activate(before_raw, inner_gain)
     prev_wide = (prev_counts > 1)[:, None, None, None]
@@ -215,9 +230,8 @@
         ],
         axis=1,
     )
-    extended = jnp.concatenate([carried, own], axis=1)
-    padded = jnp.pad(extended, ((0, 0), (0, 0), (1, 1), (0, 0), (0, 0)))
-    convolved = convolve(padded, causal_weight, causal_bias)
+    carried_part = conv3d(carried, causal_weight, (0, frame_count))
+    convolved = own_part + carried_part + causal_bias
     residual = (segment_all.astype(jnp.float32) + convolved).astype(jnp.bfloat16)
     normed = normalize(residual, attention_gain).astype(jnp.bfloat16)
     height = normed.shape[2]

time: 70.7 us -> 65 us (0.919)
  the two profiles are of different devices: /device:TPU:0 before, /device:TPU:1 now
where the time goes in v2:
time: 65 us; the launch traced here: 64.8 us
  matrix products  22.4 us (34%)
  blocking collectives  17.9 us (28%)
  starting transfers between devices  9.81 us (15%)
  other arithmetic  5.62 us (9%)
  waiting for transfers between devices  5.46 us (8%)
  local copies, waits for them, and re-layouts  3.06 us (5%)
    conv_general_dilated x2, matrix products, conv3d(): lax.conv_general_dilated(frames, causal_weight, window_strides=(1, 1, 1),...  20.2 us
    all_gather x1, blocking collectives, gathered_body(): both_all = lax.all_gather(both, 'rows', axis=2, tiled=True)  17.9 us
    ppermute x1, waiting for transfers between devices, gathered_body(): prev_raw = lax.ppermute(inner_all, 'tm', ahead)  5.46 us
    ppermute x1, starting transfers between devices, gathered_body(): prev_counts = lax.ppermute(counts, 'tm', ahead)  4.63 us
    ppermute x1, starting transfers between devices, gathered_body(): prev_raw = lax.ppermute(inner_all, 'tm', ahead)  3.88 us
    unnamed x25, local copies, waits for them, and re-layouts  1.5 us
    ppermute x1, starting transfers between devices, gathered_body(): lax.ppermute(last_raw, 'tm', [(i, i + 2) for i in range(sections - 2)])  1.3 us
  transfers between devices with their start and end apart: 3, of which 1 were waited for; matrix products, arithmetic and copies ran while one was open for 3% of the time, Pallas kernels for 0%

profile of v2, /device:TPU:1, one launch (start us, length us, event | category | flops | bytes accessed | tf_op | source)
XLA Modules:
  0.0 64.8 jit_solution(6598093223761162605)
XLA Ops:
  0.0 0.0 copy-start
  0.0 4.6 %collective-permute-start = (s32[2]{0:T(128)}, s32[2]{0:T(128)S(1)}, u32[]{:S(2)}, u32[]{:S(2)}) collective-permute-start(s32[2]{0:T(128)} %bitcast.72), channel_id=1, source_target_pairs={{0,4},{4,8},{8,12},{1,5},{5,9},{9,13},{2,6},{6,10},{10,14},{3,7},{... | collective-permute-start | bytes 32 | tf_op jit(solution)/shard_map/ppermute | solution.py:212
  4.6 0.7 %broadcast_compare_fusion = pred[2]{0:T(512)(128)(4,1)S(1)} fusion(s32[2,1]{0,1:T(1,128)} %param.13), kind=kLoop, calls=%fused_computation.89 | loop fusion | flops 2 | bytes 10 | tf_op jit(solution)/shard_map/gt | solution.py:217
  5.3 1.0 %pad_maximum_fusion = bf16[4,2,1,32,384]{4,3,1,0,2:T(8,128)(2,1)S(1)} fusion(bf16[2,2,1,32,384]{4,3,1,0,2:T(8,128)(2,1)} %bitcast.70, bf16[2,2,1,32,384]{4,3,1,0,2:T(8,128)(2,1)} %bitcast.71), kind=kLoop, calls=%fused_computation.71 | loop fusion | flops 98304 | bytes 393216 | tf_op jit(solution)/shard_map/concatenate | solution.py:213
  6.3 17.9 %all_gather.3 = bf16[4,2,4,32,384]{4,3,1,0,2:T(8,128)(2,1)S(1)} all-gather(bf16[4,2,1,32,384]{4,3,1,0,2:T(8,128)(2,1)S(1)} %pad_maximum_fusion), channel_id=1, replica_groups=mesh['clips'=2,'tm'=4,'rows'=4] {'rows'}, dimensions={2}, use_global_device_ids=true | all-gather | bytes 983040 | tf_op jit(solution)/shard_map/all_gather | solution.py:214
  24.2 0.0 copy-start.8
  24.2 0.0 copy-start.3
  24.2 0.1 fusion.48
  24.3 0.0 copy-start.2
  24.3 1.3 %collective-permute-start.2 = (bf16[2,4,32,384]{3,2,0,1:T(8,128)(2,1)S(1)}, bf16[2,4,32,384]{3,2,0,1:T(8,128)(2,1)S(1)}, u32[]{:S(2)}, u32[]{:S(2)}) collective-permute-start(bf16[2,4,32,384]{3,2,0,1:T(8,128)(2,1)S(1)} %fusion.48), channel_id=1, source_target_pairs={{0,8},{4,12},{1,9},{5,13},{2,10},{6,14},{3,11},{7,15},{16,24},{20,... | collective-permute-start | bytes 589832 | tf_op jit(solution)/shard_map/ppermute | solution.py:220
  25.6 0.1 fusion.59
  25.8 3.9 %collective-permute-start.1 = (bf16[2,2,4,32,384]{4,3,0,2,1:T(8,128)(2,1)S(1)}, bf16[2,2,4,32,384]{4,3,0,2,1:T(8,128)(2,1)S(1)}, u32[]{:S(2)}, u32[]{:S(2)}) collective-permute-start(bf16[2,2,4,32,384]{4,3,0,2,1:T(8,128)(2,1)S(1)} %copy.107), channel_id=1, source_target_pairs={{0,4},{4,8},{8,12},{1,5},{5,9},{9,13},{2,6},{6,10},{10,14},{3,7},{... | collective-permute-start | bytes 1179656 | tf_op jit(solution)/shard_map/ppermute | solution.py:219
  29.7 0.0 copy-done.8
  29.7 0.1 compare_convert_fusion
  29.8 0.0 copy-done.3
  29.8 0.2 fusion.8
  30.0 0.0 collective-permute-done
  30.0 0.0 collective-permute-done.2
  30.0 0.1 fusion.37
  30.1 5.5 %collective-permute-done.1 = bf16[2,2,4,32,384]{4,3,0,2,1:T(8,128)(2,1)S(1)} collective-permute-done((bf16[2,2,4,32,384]{4,3,0,2,1:T(8,128)(2,1)S(1)}, bf16[2,2,4,32,384]{4,3,0,2,1:T(8,128)(2,1)S(1)}, u32[]{:S(2)}, u32[]{:S(2)}) %collective-permute-start.1) | collective-permute-done | bytes 393248 | tf_op jit(solution)/shard_map/ppermute | solution.py:219
  35.6 0.2 fusion.16
  35.8 0.0 copy-done.2
  35.8 0.5 fusion.45
  36.3 0.3 copy.110
  36.7 0.4 pad.clone
  37.0 0.1 slice.57
  37.1 0.6 fusion.30
  37.7 0.1 slice_select_fusion
  37.8 0.2 fusion.51
  38.1 0.0 copy-start.4
  38.1 0.3 copy.111
  38.5 0.4 pad.2.clone
  38.8 0.1 slice.62
  39.0 0.0 slice-start
  39.0 0.6 fusion.31
  39.6 0.0 copy-done.4
  39.6 0.0 slice-start.1
  39.6 0.0 copy-start.5
  39.6 13.2 %convolution_select_fusion = f32[2,4,16,5,384]{4,2,3,1,0:T(8,128)S(1)} fusion(bf16[3,3,3,384,384]{4,3,2,1,0:T(8,128)(2,1)} %param.15, bf16[2,4,2,8,7,384]{5,2,4,3,1,0:T(2,128)(2,1)S(1)} %fusion.31, pred[16,5]{0,1:T(8,128)(4,1)S(1)} %copy-done.4), kind=kOutput, calls=%fused_computation.5 | convolution fusion | flops 2123612160 | bytes 9633872 | tf_op jit(solution)/shard_map/conv_general_dilated | solution.py:185
  52.8 0.0 slice-done
  52.8 0.0 slice-done.1
  52.8 0.0 copy-done.5
  52.8 7.0 %fusion.4 = f32[2,4,16,5,384]{4,2,3,1,0:T(8,128)S(1)} fusion(f32[2,4,16,5,384]{4,2,3,1,0:T(8,128)S(1)} %convolution_select_fusion, bf16[3,3,3,384,384]{4,3,2,1,0:T(8,128)(2,1)S(1)} %bitcast.57, bf16[2,4,2,8,7,384]{5,2,4,3,1,0:T(2,128)(2,1)S(1)} %fusion.30, f32[384]{0:T(512)S(1)} %copy-done.5, pred[16,5]{0,1:T(8,128)(4,1)S(1)} %copy-done.4), kind=kOutput, calls=%fused_computation.8 | convolution fusion | flops 2124103680 | bytes 10618448 | tf_op jit(solution)/shard_map/conv_general_dilated | solution.py:185
  59.9 0.4 copy.101
  60.2 0.0 copy-start.6
  60.3 0.1 slice.63
  60.3 0.0 copy-start.1
  60.4 0.0 slice-start.2
  60.4 0.2 fusion.24
  60.6 0.3 copy-done.6
  60.9 0.2 fusion.26
  61.1 0.4 copy-done.1
  61.5 0.0 slice-done.2
  61.5 0.2 convolution_add_fusion.2
  61.7 0.6 convolution_add_fusion
  62.3 0.0 copy-start.7
  62.3 0.9 %convolution_multiply_fusion = f32[4,32,128]{2,1,0:T(8,128)S(1)} fusion(f32[4,32,384]{2,1,0:T(8,128)S(1)} %bitcast.66, f32[4,128,768]{2,1,0:T(8,128)S(1)} %bitcast.58), kind=kOutput, calls=%fused_computation.15 | convolution fusion | flops 75513856 | bytes 1048576 | tf_op jit(solution)/shard_map/nqc,nkc->nqk/dot_general | solution.py:256
  63.3 0.2 fusion.60
  63.5 0.3 convolution_convert_fusion
  63.8 0.0 copy-done
  63.8 0.0 copy-done.7
  63.8 0.2 fusion.5
  64.0 0.7 %fusion.50 = bf16[2,2,1,32,384]{4,3,2,1,0:T(8,128)(2,1)} fusion(bf16[2,2,1,32,384]{4,3,2,1,0:T(8,128)(2,1)S(1)} %bitcast.69, f32[2,2]{1,0:T(2,128)S(1)} %compare_convert_fusion, bf16[2,2,4,32,384]{4,3,2,1,0:T(8,128)(2,1)S(1)} %get-tuple-element.6, s32[]{:T(128)S(6)} %select_n.18), kind=kLoop, calls=%fused_computation.74 | loop fusion | flops 245760 | bytes 294932 | tf_op jit(solution)/shard_map/convert_element_type | solution.py:275
  (12 shorter events, 0.2 us)
Async XLA Ops:
  0.0 63.8 %copy-start = (bf16[384,384]{1,0:T(8,128)(2,1)S(1)}, bf16[384,384]{1,0:T(8,128)(2,1)}, u32[]{:S(2)}) copy-start(bf16[384,384]{1,0:T(8,128)(2,1)} %param.20) | copy-start | bytes 884740
  0.0 30.0 %collective-permute-start = (s32[2]{0:T(128)}, s32[2]{0:T(128)S(1)}, u32[]{:S(2)}, u32[]{:S(2)}) collective-permute-start(s32[2]{0:T(128)} %bitcast.72), channel_id=1, source_target_pairs={{0,4},{4,8},{8,12},{1,5},{5,9},{9,13},{2,6},{6,10},{10,14},{3,7},{... | collective-permute-start | bytes 32 | tf_op jit(solution)/shard_map/ppermute | solution.py:212
  24.2 5.5 %copy-start.8 = (s32[2,1]{0,1:T(1,128)S(1)}, s32[2,1]{0,1:T(1,128)}, u32[]{:S(2)}) copy-start(s32[2,1]{0,1:T(1,128)} %param.13) | copy-start | bytes 28
  24.2 5.6 %copy-start.3 = (f32[1152]{0:T(1024)S(1)}, f32[1152]{0:T(1024)}, u32[]{:S(2)}) copy-start(f32[1152]{0:T(1024)} %param.19) | copy-start | bytes 13828
  24.3 11.5 %copy-start.2 = (f32[384]{0:T(512)S(1)}, f32[384]{0:T(512)}, u32[]{:S(2)}) copy-start(f32[384]{0:T(512)} %param.14) | copy-start | bytes 4612
  24.3 5.7 %collective-permute-start.2 = (bf16[2,4,32,384]{3,2,0,1:T(8,128)(2,1)S(1)}, bf16[2,4,32,384]{3,2,0,1:T(8,128)(2,1)S(1)}, u32[]{:S(2)}, u32[]{:S(2)}) collective-permute-start(bf16[2,4,32,384]{3,2,0,1:T(8,128)(2,1)S(1)} %fusion.48), channel_id=1, source_target_pairs={{0,8},{4,12},{1,9},{5,13},{2,10},{6,14},{3,11},{7,15},{16,24},{20,... | collective-permute-start | bytes 589832 | tf_op jit(solution)/shard_map/ppermute | solution.py:220
  25.8 9.8 %collective-permute-start.1 = (bf16[2,2,4,32,384]{4,3,0,2,1:T(8,128)(2,1)S(1)}, bf16[2,2,4,32,384]{4,3,0,2,1:T(8,128)(2,1)S(1)}, u32[]{:S(2)}, u32[]{:S(2)}) collective-permute-start(bf16[2,2,4,32,384]{4,3,0,2,1:T(8,128)(2,1)S(1)} %copy.107), channel_id=1, source_target_pairs={{0,4},{4,8},{8,12},{1,5},{5,9},{9,13},{2,6},{6,10},{10,14},{3,7},{... | collective-permute-start | bytes 1179656 | tf_op jit(solution)/shard_map/ppermute | solution.py:219
  38.1 1.4 %copy-start.4 = (pred[16,5]{0,1:T(8,128)(4,1)S(1)}, pred[16,5]{0,1:T(8,128)(4,1)}, u32[]{:S(2)}) copy-start(pred[16,5]{0,1:T(8,128)(4,1)} %constant.44) | copy-start | bytes 244
  39.0 13.8 %slice-start = ((s8[7962624]{0:T(1024)(128)(4,1)}), s8[4194304]{0:T(1024)(128)(4,1)S(1)}, s32[]{:S(2)}) async-start(s8[7962624]{0:T(1024)(128)(4,1)} %bitcast.56), calls=%async_computation | async-start | bytes 8388608
  39.6 13.2 %slice-start.1 = ((s8[7962624]{0:T(1024)(128)(4,1)}), s8[3768320]{0:T(1024)(128)(4,1)S(1)}, s32[]{:S(2)}) async-start(s8[7962624]{0:T(1024)(128)(4,1)} %bitcast.56), calls=%async_computation.1 | async-start | bytes 7536640
  39.6 13.2 %copy-start.5 = (f32[384]{0:T(512)S(1)}, f32[384]{0:T(512)}, u32[]{:S(2)}) copy-start(f32[384]{0:T(512)} %param.16) | copy-start | bytes 4612
  60.2 0.7 %copy-start.6 = (f32[384]{0:T(512)S(1)}, f32[384]{0:T(512)}, u32[]{:S(2)}) copy-start(f32[384]{0:T(512)} %param.17) | copy-start | bytes 4612
  60.3 1.2 %copy-start.1 = (bf16[384,1152]{1,0:T(8,128)(2,1)S(1)}, bf16[384,1152]{1,0:T(8,128)(2,1)}, u32[]{:S(2)}) copy-start(bf16[384,1152]{1,0:T(8,128)(2,1)} %param.18) | copy-start | bytes 2654212
  60.4 1.2 %slice-start.2 = ((f32[1152]{0:T(1024)}), f32[384]{0:T(512)S(1)}, s32[]{:S(2)}) async-start(f32[1152]{0:T(1024)} %param.19), calls=%async_computation.2 | async-start | bytes 4096 | tf_op jit(solution)/shard_map/slice | solution.py:254
  62.3 1.5 %copy-start.7 = (f32[384]{0:T(512)S(1)}, f32[384]{0:T(512)}, u32[]{:S(2)}) copy-start(f32[384]{0:T(512)} %param.21) | copy-start | bytes 4612

commit v3 on v2

--- a/solution.py
+++ b/solution.py
@@ -4,6 +4,8 @@
 import jax.numpy as jnp
 from jax import lax
 from jax.sharding import PartitionSpec as P
+from jax.experimental import pallas as pl
+from jax.experimental.pallas import tpu as pltpu
 
 EPSILON = 1e-06
 
@@ -181,15 +183,57 @@
     return jax.nn.silu(normalize(field, gain)).astype(jnp.bfloat16)
 
 
-def conv3d(frames, causal_weight, time_padding):
-    return lax.conv_general_dilated(
-        frames,
-        causal_weight,
-        window_strides=(1, 1, 1),
-        padding=(time_padding, (1, 1), (1, 1)),
-        dimension_numbers=("NDHWC", "DHWIO", "NDHWC"),
-        preferred_element_type=jnp.float32,
-    )
+def conv_kernel(x_ref, w_ref, b_ref, o_ref, acc_ref):
+    kt = pl.program_id(0)
+    kh = pl.program_id(1)
+    clips, slots, rows, columns, width = x_ref.shape
+    frames = slots - 2
+    height = rows - 2
+
+    @pl.when((kt == 0) & (kh == 0))
+    def _():
+        acc_ref[...] = jnp.zeros_like(acc_ref)
+
+    window = x_ref[:, pl.ds(kt, frames), pl.ds(kh, height), :, :]
+    lhs = window.reshape(clips * frames * height * columns, width)
+    weight = w_ref[...].reshape(width, w_ref.shape[-1])
+    acc_ref[...] += jnp.dot(lhs, weight, preferred_element_type=jnp.float32)
+
+    @pl.when((kt == 2) & (kh == 2))
+    def _():
+        o_ref[...] = acc_ref[...] + b_ref[...]
+
+
+def conv_all_rows(extended, causal_weight, causal_bias):
+    clips, slots, height, columns, channels = extended.shape
+    frames = slots - 2
+    padded = jnp.pad(extended, ((0, 0), (0, 0), (1, 1), (1, 1), (0, 0)))
+    taps = jnp.concatenate(
+        [padded[:, :, :, kw : kw + columns] for kw in range(3)], axis=-1
+    )
+    places = clips * frames * height * columns
+    out = pl.pallas_call(
+        conv_kernel,
+        grid=(3, 3),
+        in_specs=[
+            pl.BlockSpec(taps.shape, lambda kt, kh: (0, 0, 0, 0, 0)),
+            pl.BlockSpec((None, None, 3, channels, channels), lambda kt, kh: (kt, kh, 0, 0, 0)),
+            pl.BlockSpec((1, channels), lambda kt, kh: (0, 0)),
+        ],
+        out_specs=pl.BlockSpec((places, channels), lambda kt, kh: (0, 0)),
+        out_shape=jax.ShapeDtypeStruct((places, channels), jnp.float32),
+        scratch_shapes=[pltpu.VMEM((places, channels), jnp.float32)],
+        compiler_params=pltpu.CompilerParams(
+            dimension_semantics=("arbitrary", "arbitrary"),
+            vmem_limit_bytes=48 * 1024 * 1024,
+        ),
+        cost_estimate=pl.CostEstimate(
+            flops=2 * places * 27 * channels * channels,
+            transcendentals=0,
+            bytes_accessed=causal_weight.size * 2 + taps.size * 2 + places * channels * 4,
+        ),
+    )(taps, causal_weight, causal_bias.reshape(1, channels))
+    return out.reshape(clips, frames, height, columns, channels)
 
 
 def gathered_body(
@@ -219,7 +263,6 @@
     prev_raw = lax.ppermute(inner_all, "tm", ahead)
     before_raw = lax.ppermute(last_raw, "tm", [(i, i + 2) for i in range(sections - 2)])
     own = activate(inner_all, inner_gain)
-    own_part = conv3d(own, causal_weight, (2, 0))
     prev = activate(prev_raw, inner_gain)
     before = activate(before_raw, inner_gain)
     prev_wide = (prev_counts > 1)[:, None, None, None]
@@ -230,8 +273,8 @@
         ],
         axis=1,
     )
-    carried_part = conv3d(carried, causal_weight, (0, frame_count))
-    convolved = own_part + carried_part + causal_bias
+    extended = jnp.concatenate([carried, own], axis=1)
+    convolved = conv_all_rows(extended, causal_weight, causal_bias)
     residual = (segment_all.astype(jnp.float32) + convolved).astype(jnp.bfloat16)
     normed = normalize(residual, attention_gain).astype(jnp.bfloat16)
     height = normed.shape[2]

time: 65 us -> 52.5 us (0.81)
  matrix products: 22.4 us -> 2.25 us
  Pallas kernels: 0 us -> 10.1 us
  other arithmetic: 5.62 us -> 4.1 us
  local copies, waits for them, and re-layouts: 3.06 us -> 2.32 us
    conv_general_dilated x2 -> x0, matrix products: 20.2 us -> none  [conv3d(): lax.conv_general_dilated(frames, causal_weight, window_strides=(1, 1, 1),...]
    pallas_call x0 -> x1, Pallas kernels: none -> 10.1 us  [conv_all_rows(): pl.pallas_call(conv_kernel, grid=(3, 3), in_specs=[pl.BlockSpec(taps.shap...]
    ppermute x1, waiting for transfers between devices: 5.46 us -> 0.01 us  [gathered_body(): prev_raw = lax.ppermute(inner_all, 'tm', ahead)]
    ppermute x1, waiting for transfers between devices: 0.01 us -> 5.36 us  [gathered_body(): prev_counts = lax.ppermute(counts, 'tm', ahead)]
    ppermute x1, starting transfers between devices: 4.63 us -> 1.92 us  [gathered_body(): prev_counts = lax.ppermute(counts, 'tm', ahead)]
    ppermute x1, starting transfers between devices: 3.88 us -> 6.32 us  [gathered_body(): prev_raw = lax.ppermute(inner_all, 'tm', ahead)]
    conv_general_dilated x2 -> x0, other arithmetic: 1.16 us -> none  [conv3d(): lax.conv_general_dilated(frames, causal_weight, window_strides=(1, 1, 1),...]
    concatenate x0 -> x2, other arithmetic: none -> 0.87 us  [the longest x1 0.48 us: gathered_body(): extended = jnp.concatenate([carried, own], axis=1)]
  transfers between devices with their start and end apart: 3 -> 3, of which waited for: 1 -> 1; matrix products, arithmetic and copies ran while one was open for 3% -> 1% of each run, Pallas kernels for 0% -> 0%
where the time goes in v3:
time: 52.5 us; the launch traced here: 52.1 us
  blocking collectives  18 us (34%)
  Pallas kernels  10.1 us (19%)
  starting transfers between devices  9.55 us (18%)
  waiting for transfers between devices  5.37 us (10%)
  other arithmetic  4.1 us (8%)
  local copies, waits for them, and re-layouts  2.32 us (4%)
  matrix products  2.25 us (4%)
    all_gather x1, blocking collectives, gathered_body(): both_all = lax.all_gather(both, 'rows', axis=2, tiled=True)  18 us
    pallas_call x1, Pallas kernels, conv_all_rows(): pl.pallas_call(conv_kernel, grid=(3, 3), in_specs=[pl.BlockSpec(taps.shap...  10.1 us
    ppermute x1, starting transfers between devices, gathered_body(): prev_raw = lax.ppermute(inner_all, 'tm', ahead)  6.32 us
    ppermute x1, waiting for transfers between devices, gathered_body(): prev_counts = lax.ppermute(counts, 'tm', ahead)  5.36 us
    ppermute x1, starting transfers between devices, gathered_body(): prev_counts = lax.ppermute(counts, 'tm', ahead)  1.92 us
    ppermute x1, starting transfers between devices, gathered_body(): lax.ppermute(last_raw, 'tm', [(i, i + 2) for i in range(sections - 2)])  1.3 us
  transfers between devices with their start and end apart: 3, of which 1 were waited for; matrix products, arithmetic and copies ran while one was open for 1% of the time, Pallas kernels for 0%

profile of v3, /device:TPU:1, one launch (start us, length us, event | category | flops | bytes accessed | tf_op | source)
XLA Modules:
  0.0 52.1 jit_solution(11772380265845201113)
XLA Ops:
  0.0 0.0 copy-start
  0.0 0.0 copy-start.7
  0.0 1.0 %pad_maximum_fusion.1 = bf16[4,2,1,32,384]{4,3,2,1,0:T(8,128)(2,1)S(1)} fusion(bf16[2,2,1,32,384]{4,3,2,1,0:T(8,128)(2,1)} %param.11, bf16[2,2,1,32,384]{4,3,2,1,0:T(8,128)(2,1)} %param.12), kind=kLoop, calls=%fused_computation.65 | loop fusion | flops 98304 | bytes 393216 | tf_op jit(solution)/shard_map/concatenate | solution.py:257
  1.0 0.0 copy-start.3
  1.0 0.0 copy-start.6
  1.1 0.0 copy-start.2
  1.1 18.0 %all_gather.3 = bf16[4,2,4,32,384]{4,3,2,0,1:T(8,128)(2,1)S(1)} all-gather(bf16[4,2,1,32,384]{4,3,2,0,1:T(8,128)(2,1)S(1)} %copy.34), channel_id=1, replica_groups=mesh['clips'=2,'tm'=4,'rows'=4] {'rows'}, dimensions={2}, use_global_device_ids=true | all-gather | bytes 983040 | tf_op jit(solution)/shard_map/all_gather | solution.py:258
  19.2 6.3 %collective-permute-start.1 = (bf16[2,2,4,32,384]{4,3,2,0,1:T(8,128)(2,1)S(1)}, bf16[2,2,4,32,384]{4,3,2,0,1:T(8,128)(2,1)S(1)}, u32[]{:S(2)}, u32[]{:S(2)}) collective-permute-start(bf16[2,2,4,32,384]{4,3,2,0,1:T(8,128)(2,1)S(1)} %slice.65), channel_id=1, source_target_pairs={{0,4},{4,8},{8,12},{1,5},{5,9},{9,13},{2,6},{6,10},{10,14},{3,7},{... | collective-permute-start | bytes 1179656 | tf_op jit(solution)/shard_map/ppermute | solution.py:263
  25.5 0.0 copy-done.7
  25.5 0.1 fusion.33
  25.6 1.3 %collective-permute-start.2 = (bf16[2,4,32,384]{3,2,1,0:T(8,128)(2,1)S(1)}, bf16[2,4,32,384]{3,2,1,0:T(8,128)(2,1)S(1)}, u32[]{:S(2)}, u32[]{:S(2)}) collective-permute-start(bf16[2,4,32,384]{3,2,1,0:T(8,128)(2,1)S(1)} %fusion.33), channel_id=1, source_target_pairs={{0,8},{4,12},{1,9},{5,13},{2,10},{6,14},{3,11},{7,15},{16,24},{20,... | collective-permute-start | bytes 589832 | tf_op jit(solution)/shard_map/ppermute | solution.py:264
  26.9 1.9 %collective-permute-start = (s32[2]{0:T(128)S(1)}, s32[2]{0:T(128)S(1)}, u32[]{:S(2)}, u32[]{:S(2)}) collective-permute-start(s32[2]{0:T(128)S(1)} %bitcast.41), channel_id=1, source_target_pairs={{0,4},{4,8},{8,12},{1,5},{5,9},{9,13},{2,6},{6,10},{10,14},{3,7},{... | collective-permute-start | bytes 32 | tf_op jit(solution)/shard_map/ppermute | solution.py:256
  28.9 0.2 fusion.12
  29.0 0.0 copy-done.3
  29.1 0.0 copy-done.6
  29.1 5.4 %collective-permute-done = s32[2]{0:T(128)S(1)} collective-permute-done((s32[2]{0:T(128)S(1)}, s32[2]{0:T(128)S(1)}, u32[]{:S(2)}, u32[]{:S(2)}) %collective-permute-start) | collective-permute-done | bytes 40 | tf_op jit(solution)/shard_map/ppermute | solution.py:256
  34.5 0.0 collective-permute-done.2
  34.5 0.1 fusion.23
  34.6 0.0 collective-permute-done.1
  34.6 0.2 fusion.10
  34.8 0.0 copy-done.2
  34.8 0.4 exponential_add_fusion
  35.2 0.3 fusion.19
  35.5 0.1 slice_select_fusion
  35.6 0.2 fusion.36
  35.8 0.5 select_maximum_fusion
  36.3 0.8 %fusion.40 = (bf16[2,4,6,32,384]{4,3,2,1,0:T(8,128)(2,1)S(1)}, bf16[2,4,6,32,384]{4,3,2,1,0:T(8,128)(2,1)S(1)}, bf16[2,4,6,32,384]{4,3,2,1,0:T(8,128)(2,1)S(1)}) fusion(bf16[2,4,6,34,384]{4,3,2,1,0:T(8,128)(2,1)S(1)} %select_maximum_fusion), kind=kLoop, calls=%fused_computation.81 | loop fusion | bytes 7077888 | tf_op jit(solution)/shard_map/slice | solution.py:212
  37.1 0.4 pad_maximum_fusion.x_ref
  37.5 10.1 %shard_map.109 = f32[512,384]{1,0:T(8,128)S(1)} custom-call(bf16[2,4,6,32,1152]{4,3,2,1,0:T(8,128)(2,1)S(1)} %pad_maximum_fusion.x_ref, bf16[3,3,3,384,384]{4,3,2,1,0:T(8,128)(2,1)} %w_ref.1, f32[1,384]{1,0:T(1,128)S(1)} %reshape.107.b_ref), custom_call_target="tpu_custom_call" | custom-call | flops 4076863488 | bytes 12288000 | tf_op jit(solution)/shard_map/pallas_call | solution.py:215
  47.6 0.0 copy-start.4
  47.6 0.0 copy-start.1
  47.7 0.2 fusion.14
  47.9 0.4 copy-done.4
  48.3 0.2 fusion.16
  48.5 0.0 slice-start
  48.6 0.2 copy-done.1
  48.8 0.6 %convolution_add_fusion = f32[512,768]{1,0:T(8,128)S(1)} fusion(bf16[512,384]{1,0:T(8,128)(2,1)S(1)} %bitcast.36, f32[768]{0:T(1024)S(1)} %slice.61, bf16[384,1152]{1,0:T(8,128)(2,1)S(1)} %copy-done.1), kind=kOutput, calls=%fused_computation.9 | convolution fusion | flops 302383104 | bytes 2560000 | tf_op jit(solution)/shard_map/dot_general | solution.py:285
  49.4 0.0 copy-start.5
  49.4 0.0 slice-done
  49.4 0.2 convolution_add_fusion.2
  49.6 1.0 %convolution_multiply_fusion = f32[4,32,128]{2,1,0:T(8,128)S(1)} fusion(f32[4,32,384]{2,1,0:T(8,128)S(1)} %bitcast.37, f32[4,128,768]{2,1,0:T(8,128)S(1)} %bitcast.34), kind=kOutput, calls=%fused_computation.21 | convolution fusion | flops 75513856 | bytes 1048576 | tf_op jit(solution)/shard_map/nqc,nkc->nqk/dot_general | solution.py:299
  50.6 0.2 fusion.41
  50.8 0.3 convolution_convert_fusion
  51.1 0.0 copy-done
  51.1 0.0 copy-done.5
  51.1 0.2 fusion.7
  51.3 0.1 fusion.35
  51.4 0.7 %copy.33 = bf16[2,2,1,32,384]{4,3,2,1,0:T(8,128)(2,1)} copy(bf16[2,2,1,32,384]{4,3,2,0,1:T(8,128)(2,1)S(1)} %fusion.35) | data formatting | bytes 196608 | tf_op jit(solution)/shard_map/convert_element_type | solution.py:318
  (14 shorter events, 0.2 us)
Async XLA Ops:
  0.0 51.1 %copy-start = (bf16[384,384]{1,0:T(8,128)(2,1)S(1)}, bf16[384,384]{1,0:T(8,128)(2,1)}, u32[]{:S(2)}) copy-start(bf16[384,384]{1,0:T(8,128)(2,1)} %param.20) | copy-start | bytes 884740
  0.0 25.5 %copy-start.7 = (s32[2,1]{0,1:T(1,128)S(1)}, s32[2,1]{0,1:T(1,128)}, u32[]{:S(2)}) copy-start(s32[2,1]{0,1:T(1,128)} %param.13) | copy-start | bytes 28
  1.0 28.0 %copy-start.3 = (f32[1152]{0:T(1024)S(1)}, f32[1152]{0:T(1024)}, u32[]{:S(2)}) copy-start(f32[1152]{0:T(1024)} %param.19) | copy-start | bytes 13828
  1.0 28.0 %copy-start.6 = (f32[384]{0:T(512)S(1)}, f32[384]{0:T(512)}, u32[]{:S(2)}) copy-start(f32[384]{0:T(512)} %param.16) | copy-start | bytes 4612
  1.1 33.7 %copy-start.2 = (f32[384]{0:T(512)S(1)}, f32[384]{0:T(512)}, u32[]{:S(2)}) copy-start(f32[384]{0:T(512)} %param.14) | copy-start | bytes 4612
  19.2 15.4 %collective-permute-start.1 = (bf16[2,2,4,32,384]{4,3,2,0,1:T(8,128)(2,1)S(1)}, bf16[2,2,4,32,384]{4,3,2,0,1:T(8,128)(2,1)S(1)}, u32[]{:S(2)}, u32[]{:S(2)}) collective-permute-start(bf16[2,2,4,32,384]{4,3,2,0,1:T(8,128)(2,1)S(1)} %slice.65), channel_id=1, source_target_pairs={{0,4},{4,8},{8,12},{1,5},{5,9},{9,13},{2,6},{6,10},{10,14},{3,7},{... | collective-permute-start | bytes 1179656 | tf_op jit(solution)/shard_map/ppermute | solution.py:263
  25.6 8.8 %collective-permute-start.2 = (bf16[2,4,32,384]{3,2,1,0:T(8,128)(2,1)S(1)}, bf16[2,4,32,384]{3,2,1,0:T(8,128)(2,1)S(1)}, u32[]{:S(2)}, u32[]{:S(2)}) collective-permute-start(bf16[2,4,32,384]{3,2,1,0:T(8,128)(2,1)S(1)} %fusion.33), channel_id=1, source_target_pairs={{0,8},{4,12},{1,9},{5,13},{2,10},{6,14},{3,11},{7,15},{16,24},{20,... | collective-permute-start | bytes 589832 | tf_op jit(solution)/shard_map/ppermute | solution.py:264
  26.9 7.5 %collective-permute-start = (s32[2]{0:T(128)S(1)}, s32[2]{0:T(128)S(1)}, u32[]{:S(2)}, u32[]{:S(2)}) collective-permute-start(s32[2]{0:T(128)S(1)} %bitcast.41), channel_id=1, source_target_pairs={{0,4},{4,8},{8,12},{1,5},{5,9},{9,13},{2,6},{6,10},{10,14},{3,7},{... | collective-permute-start | bytes 32 | tf_op jit(solution)/shard_map/ppermute | solution.py:256
  47.6 0.7 %copy-start.4 = (f32[384]{0:T(512)S(1)}, f32[384]{0:T(512)}, u32[]{:S(2)}) copy-start(f32[384]{0:T(512)} %param.17) | copy-start | bytes 4612
  47.6 1.2 %copy-start.1 = (bf16[384,1152]{1,0:T(8,128)(2,1)S(1)}, bf16[384,1152]{1,0:T(8,128)(2,1)}, u32[]{:S(2)}) copy-start(bf16[384,1152]{1,0:T(8,128)(2,1)} %param.18) | copy-start | bytes 2654212
  48.5 0.9 %slice-start = ((f32[1152]{0:T(1024)}), f32[384]{0:T(512)S(1)}, s32[]{:S(2)}) async-start(f32[1152]{0:T(1024)} %param.19), calls=%async_computation | async-start | bytes 4096 | tf_op jit(solution)/shard_map/slice | solution.py:297
  49.4 1.7 %copy-start.5 = (f32[384]{0:T(512)S(1)}, f32[384]{0:T(512)}, u32[]{:S(2)}) copy-start(f32[384]{0:T(512)} %param.21) | copy-start | bytes 4612

commit v4 on v2

--- a/solution.py
+++ b/solution.py
@@ -1,9 +1,12 @@
+import functools
 import math
 
 import jax
 import jax.numpy as jnp
 from jax import lax
 from jax.sharding import PartitionSpec as P
+from jax.experimental import pallas as pl
+from jax.experimental.pallas import tpu as pltpu
 
 EPSILON = 1e-06
 
@@ -181,15 +184,99 @@
     return jax.nn.silu(normalize(field, gain)).astype(jnp.bfloat16)
 
 
-def conv3d(frames, causal_weight, time_padding):
-    return lax.conv_general_dilated(
-        frames,
-        causal_weight,
-        window_strides=(1, 1, 1),
-        padding=(time_padding, (1, 1), (1, 1)),
-        dimension_numbers=("NDHWC", "DHWIO", "NDHWC"),
-        preferred_element_type=jnp.float32,
-    )
+def conv_part_kernel(plan, x_ref, w_ref, o_ref, acc_ref):
+    step = pl.program_id(0)
+    clips, held, rows, columns, width = x_ref.shape
+    height = rows - 2
+    places = clips * height * columns
+
+    @pl.when(step == 0)
+    def _():
+        acc_ref[...] = jnp.zeros_like(acc_ref)
+
+    for index, pairs in enumerate(plan):
+
+        @pl.when(step == index)
+        def _():
+            for frame, slot in pairs:
+                for kh in range(3):
+                    lhs = x_ref[:, frame, kh : kh + height, :, :].reshape(places, width)
+                    weight = w_ref[kh].reshape(width, w_ref.shape[-1])
+                    acc_ref[slot] += jnp.dot(lhs, weight, preferred_element_type=jnp.float32)
+
+    @pl.when(step == len(plan) - 1)
+    def _():
+        o_ref[...] = acc_ref[...]
+
+
+def conv_part(frames, causal_weight, plan, first_tap, slots):
+    clips, held, height, columns, channels = frames.shape
+    padded = jnp.pad(frames, ((0, 0), (0, 0), (1, 1), (1, 1), (0, 0)))
+    taps = jnp.concatenate(
+        [padded[:, :, :, kw : kw + columns] for kw in range(3)], axis=-1
+    )
+    places = clips * height * columns
+    dots = sum(len(pairs) for pairs in plan) * 3
+    return pl.pallas_call(
+        functools.partial(conv_part_kernel, plan),
+        grid=(len(plan),),
+        in_specs=[
+            pl.BlockSpec(taps.shape, lambda i: (0, 0, 0, 0, 0)),
+            pl.BlockSpec(
+                (None, 3, 3, channels, channels), lambda i: (first_tap + i, 0, 0, 0, 0)
+            ),
+        ],
+        out_specs=pl.BlockSpec((slots, places, channels), lambda i: (0, 0, 0)),
+        out_shape=jax.ShapeDtypeStruct((slots, places, channels), jnp.float32),
+        scratch_shapes=[pltpu.VMEM((slots, places, channels), jnp.float32)],
+        compiler_params=pltpu.CompilerParams(
+            dimension_semantics=("arbitrary",),
+            vmem_limit_bytes=48 * 1024 * 1024,
+        ),
+        cost_estimate=pl.CostEstimate(
+            flops=2 * places * dots * 3 * channels * channels,
+            transcendentals=0,
+            bytes_accessed=len(plan) * 9 * channels * channels * 2
+            + taps.size * 2
+            + slots * places * channels * 4,
+        ),
+    )(taps, causal_weight)
+
+
+def conv_plans(slots):
+    own, carried = {}, {}
+    for kt in range(3):
+        for slot in range(slots):
+            source = slot + kt
+            if source >= 2:
+                own.setdefault(kt, []).append((source - 2, slot))
+            else:
+                carried.setdefault(kt, []).append((source, slot))
+    return own, carried
+
+
+def plan_of(table):
+    taps = sorted(table)
+    assert taps == list(range(taps[0], taps[-1] + 1))
+    return tuple(tuple(table[kt]) for kt in taps), taps[0]
+
+
+def own_conv(own_frames, causal_weight):
+    own_table, _ = conv_plans(own_frames.shape[1])
+    own_plan, own_first = plan_of(own_table)
+    return conv_part(own_frames, causal_weight, own_plan, own_first, own_frames.shape[1])
+
+
+def carried_conv(carried_frames, causal_weight, slots):
+    _, carried_table = conv_plans(slots)
+    carried_plan, carried_first = plan_of(carried_table)
+    return conv_part(carried_frames, causal_weight, carried_plan, carried_first, slots)
+
+
+def frame_major(total, clips, height, columns):
+    slots, places, channels = total.shape
+    total = total.reshape(slots, clips, height, columns, channels)
+    return jnp.transpose(total, (1, 0, 2, 3, 4))
 
 
 def gathered_body(
@@ -219,7 +306,10 @@
     prev_raw = lax.ppermute(inner_all, "tm", ahead)
     before_raw = lax.ppermute(last_raw, "tm", [(i, i + 2) for i in range(sections - 2)])
     own = activate(inner_all, inner_gain)
-    own_part = conv3d(own, causal_weight, (2, 0))
+    own_sum = own_conv(own, causal_weight)
+    own_sum, prev_raw, before_raw, prev_counts = lax.optimization_barrier(
+        (own_sum, prev_raw, before_raw, prev_counts)
+    )
     prev = activate(prev_raw, inner_gain)
     before = activate(before_raw, inner_gain)
     prev_wide = (prev_counts > 1)[:, None, None, None]
@@ -230,8 +320,9 @@
         ],
         axis=1,
     )
-    carried_part = conv3d(carried, causal_weight, (0, frame_count))
-    convolved = own_part + carried_part + causal_bias
+    carried_sum = carried_conv(carried, causal_weight, frame_count)
+    height = inner_all.shape[2]
+    convolved = frame_major(own_sum + carried_sum, clip_count, height, column_count) + causal_bias
     residual = (segment_all.astype(jnp.float32) + convolved).astype(jnp.bfloat16)
     normed = normalize(residual, attention_gain).astype(jnp.bfloat16)
     height = normed.shape[2]

time: 65 us -> 49.5 us (0.76)
  the two profiles are of different devices: /device:TPU:1 before, /device:TPU:0 now
where the time goes in v4:
time: 49.5 us; the launch traced here: 49.2 us
  blocking collectives  21.3 us (43%)
  Pallas kernels  10.1 us (20%)
  starting transfers between devices  6.7 us (14%)
  other arithmetic  4.45 us (9%)
  local copies, waits for them, and re-layouts  4.12 us (8%)
  matrix products  2.24 us (5%)
    all_gather x1, blocking collectives, gathered_body(): both_all = lax.all_gather(both, 'rows', axis=2, tiled=True)  21.3 us
    pallas_call x2, Pallas kernels, conv_part(): pl.pallas_call(functools.partial(conv_part_kernel, plan), grid=(len(plan)...  10.1 us
    ppermute x1, starting transfers between devices, gathered_body(): lax.ppermute(last_raw, 'tm', [(i, i + 2) for i in range(sections - 2)])  4 us
    unnamed x16, local copies, waits for them, and re-layouts  1.74 us
    ppermute x1, starting transfers between devices, gathered_body(): prev_counts = lax.ppermute(counts, 'tm', ahead)  1.39 us
    ppermute x1, starting transfers between devices, gathered_body(): prev_raw = lax.ppermute(inner_all, 'tm', ahead)  1.3 us
    concatenate x1, other arithmetic, gathered_body(): both = jnp.concatenate([inner_input, segment_input], axis=0)  1.01 us
  transfers between devices with their start and end apart: 3, of which 0 were waited for; matrix products, arithmetic and copies ran while one was open for 4% of the time, Pallas kernels for 10%

profile of v4, /device:TPU:0, one launch (start us, length us, event | category | flops | bytes accessed | tf_op | source)
XLA Modules:
  0.0 49.2 jit_solution(15078424733346022252)
XLA Ops:
  0.0 0.0 copy-start
  0.0 0.0 copy-start.7
  0.0 0.0 copy-start.2
  0.0 1.0 %pad_maximum_fusion.2 = bf16[4,2,1,32,384]{4,3,2,1,0:T(8,128)(2,1)S(1)} fusion(bf16[2,2,1,32,384]{4,3,2,1,0:T(8,128)(2,1)} %param.11, bf16[2,2,1,32,384]{4,3,2,1,0:T(8,128)(2,1)} %param.12), kind=kLoop, calls=%fused_computation.73 | loop fusion | flops 98304 | bytes 393216 | tf_op jit(solution)/shard_map/concatenate | solution.py:300
  1.0 21.3 %all_gather.3 = bf16[4,2,4,32,384]{4,3,2,0,1:T(8,128)(2,1)S(1)} all-gather(bf16[4,2,1,32,384]{4,3,2,0,1:T(8,128)(2,1)S(1)} %copy.29), channel_id=1, replica_groups=mesh['clips'=2,'tm'=4,'rows'=4] {'rows'}, dimensions={2}, use_global_device_ids=true | all-gather | bytes 983040 | tf_op jit(solution)/shard_map/all_gather | solution.py:301
  22.3 0.8 %slice.77 = bf16[2,2,4,32,384]{4,3,2,0,1:T(8,128)(2,1)} slice(bf16[4,2,4,32,384]{4,3,2,0,1:T(8,128)(2,1)S(1)} %all_gather.3), slice={[0:2], [0:2], [0:4], [0:32], [0:384]} | slice | bytes 786432 | tf_op jit(solution)/shard_map/slice | solution.py:302
  23.1 1.3 %collective-permute-start = (bf16[2,2,4,32,384]{4,3,2,0,1:T(8,128)(2,1)}, bf16[2,2,4,32,384]{4,3,2,0,1:T(8,128)(2,1)S(1)}, u32[]{:S(2)}, u32[]{:S(2)}) collective-permute-start(bf16[2,2,4,32,384]{4,3,2,0,1:T(8,128)(2,1)} %slice.77), channel_id=1, source_target_pairs={{0,4},{4,8},{8,12},{1,5},{5,9},{9,13},{2,6},{6,10},{10,14},{3,7},{... | collective-permute-start | bytes 1179656 | tf_op jit(solution)/shard_map/ppermute | solution.py:306
  24.4 0.0 copy-done.7
  24.5 0.8 %fusion.45 = bf16[2,4,32,384]{3,2,1,0:T(8,128)(2,1)} fusion(bf16[4,2,4,32,384]{4,3,2,0,1:T(8,128)(2,1)S(1)} %all_gather.3, pred[2]{0:T(512)(128)(4,1)S(1)} %broadcast_compare_fusion.1), kind=kLoop, calls=%fused_computation.71 | loop fusion | flops 98304 | bytes 589826 | tf_op jit(solution)/shard_map/jit(_where)/select_n | solution.py:305
  25.2 4.0 %collective-permute-start.1 = (bf16[2,4,32,384]{3,2,1,0:T(8,128)(2,1)}, bf16[2,4,32,384]{3,2,1,0:T(8,128)(2,1)S(1)}, u32[]{:S(2)}, u32[]{:S(2)}) collective-permute-start(bf16[2,4,32,384]{3,2,1,0:T(8,128)(2,1)} %fusion.45), channel_id=1, source_target_pairs={{0,8},{4,12},{1,9},{5,13},{2,10},{6,14},{3,11},{7,15},{16,24},{20,... | collective-permute-start | bytes 589832 | tf_op jit(solution)/shard_map/ppermute | solution.py:307
  29.2 1.4 %collective-permute-start.2 = (s32[2]{0:T(128)S(1)}, s32[2]{0:T(128)S(1)}, u32[]{:S(2)}, u32[]{:S(2)}) collective-permute-start(s32[2]{0:T(128)S(1)} %bitcast.53), channel_id=1, source_target_pairs={{0,4},{4,8},{8,12},{1,5},{5,9},{9,13},{2,6},{6,10},{10,14},{3,7},{... | collective-permute-start | bytes 32 | tf_op jit(solution)/shard_map/ppermute | solution.py:299
  30.6 0.2 fusion.9
  30.8 0.0 copy-done.2
  30.8 0.3 fusion.16
  31.1 0.3 pad_slice_fusion.2
  31.5 0.0 copy-start.3
  31.5 0.2 pad_maximum_fusion
  31.7 0.5 %copy-done.3 = f32[1152]{0:T(1024)S(1)} copy-done((f32[1152]{0:T(1024)S(1)}, f32[1152]{0:T(1024)}, u32[]{:S(2)}) %copy-start.3) | copy-done | bytes 4632
  32.2 0.1 copy.21.x_ref
  32.3 5.0 %shard_map.109 = f32[2,256,384]{2,1,0:T(8,128)S(1)} custom-call(bf16[2,2,6,32,1152]{4,3,2,1,0:T(8,128)(2,1)S(1)} %copy.21.x_ref, bf16[3,3,3,384,384]{4,3,2,1,0:T(8,128)(2,1)} %w_ref.3), custom_call_target="tpu_custom_call" | custom-call | flops 2038431744 | bytes 7864320 | tf_op jit(solution)/shard_map/pallas_call | solution.py:220
  37.4 0.0 collective-permute-done.2
  37.4 0.0 collective-permute-done.1
  37.4 0.0 collective-permute-done
  37.4 0.2 fusion.17
  37.6 0.3 fusion.24
  37.9 0.1 fusion.34
  38.0 0.1 fusion.44
  38.1 0.2 fusion.48
  38.4 0.2 fusion.31
  38.6 0.4 fusion.52
  38.9 0.2 pad_maximum_fusion.1.x_ref
  39.1 5.0 %shard_map.110 = f32[2,256,384]{2,1,0:T(8,128)S(1)} custom-call(bf16[2,2,6,32,1152]{4,3,2,1,0:T(8,128)(2,1)S(1)} %pad_maximum_fusion.1.x_ref, bf16[3,3,3,384,384]{4,3,2,1,0:T(8,128)(2,1)} %w_ref.3), custom_call_target="tpu_custom_call" | custom-call | flops 2038431744 | bytes 7864320 | tf_op jit(solution)/shard_map/pallas_call | solution.py:220
  44.1 0.0 copy-start.4
  44.2 0.0 copy-start.5
  44.2 0.1 add.105
  44.3 0.6 %copy-done.4 = f32[384]{0:T(512)S(1)} copy-done((f32[384]{0:T(512)S(1)}, f32[384]{0:T(512)}, u32[]{:S(2)}) %copy-start.4) | copy-done | bytes 1560
  44.8 0.0 copy-start.1
  44.8 0.2 fusion.25
  45.1 0.0 copy-done.5
  45.1 0.2 fusion.27
  45.3 0.0 slice-start
  45.4 0.6 %copy-done.1 = bf16[384,1152]{1,0:T(8,128)(2,1)S(1)} copy-done((bf16[384,1152]{1,0:T(8,128)(2,1)S(1)}, bf16[384,1152]{1,0:T(8,128)(2,1)}, u32[]{:S(2)}) %copy-start.1) | copy-done | bytes 884760
  46.0 0.6 %convolution_add_fusion = f32[512,768]{1,0:T(8,128)S(1)} fusion(bf16[512,384]{1,0:T(8,128)(2,1)S(1)} %bitcast.48, f32[768]{0:T(1024)S(1)} %slice.73, bf16[384,1152]{1,0:T(8,128)(2,1)S(1)} %copy-done.1), kind=kOutput, calls=%fused_computation.7 | convolution fusion | flops 302383104 | bytes 2560000 | tf_op jit(solution)/shard_map/dot_general | solution.py:333
  46.6 0.0 copy-start.6
  46.6 0.0 slice-done
  46.6 0.2 convolution_add_fusion.2
  46.8 0.9 %convolution_multiply_fusion = f32[4,32,128]{2,1,0:T(8,128)S(1)} fusion(f32[4,32,384]{2,1,0:T(8,128)S(1)} %bitcast.49, f32[4,128,768]{2,1,0:T(8,128)S(1)} %bitcast.45), kind=kOutput, calls=%fused_computation.17 | convolution fusion | flops 75513856 | bytes 1048576 | tf_op jit(solution)/shard_map/nqc,nkc->nqk/dot_general | solution.py:347
  47.8 0.2 fusion.53
  48.0 0.3 convolution_convert_fusion
  48.3 0.0 copy-done
  48.3 0.0 copy-done.6
  48.3 0.2 fusion.4
  48.5 0.1 fusion.47
  48.6 0.7 %copy.28 = bf16[2,2,1,32,384]{4,3,2,1,0:T(8,128)(2,1)} copy(bf16[2,2,1,32,384]{4,3,2,0,1:T(8,128)(2,1)S(1)} %fusion.47) | data formatting | bytes 196608 | tf_op jit(solution)/shard_map/convert_element_type | solution.py:366
  (12 shorter events, 0.2 us)
Async XLA Ops:
  0.0 48.3 %copy-start = (bf16[384,384]{1,0:T(8,128)(2,1)S(1)}, bf16[384,384]{1,0:T(8,128)(2,1)}, u32[]{:S(2)}) copy-start(bf16[384,384]{1,0:T(8,128)(2,1)} %param.20) | copy-start | bytes 884740
  0.0 24.4 %copy-start.7 = (s32[2,1]{0,1:T(1,128)S(1)}, s32[2,1]{0,1:T(1,128)}, u32[]{:S(2)}) copy-start(s32[2,1]{0,1:T(1,128)} %param.13) | copy-start | bytes 28
  0.0 30.8 %copy-start.2 = (f32[384]{0:T(512)S(1)}, f32[384]{0:T(512)}, u32[]{:S(2)}) copy-start(f32[384]{0:T(512)} %param.14) | copy-start | bytes 4612
  23.1 14.3 %collective-permute-start = (bf16[2,2,4,32,384]{4,3,2,0,1:T(8,128)(2,1)}, bf16[2,2,4,32,384]{4,3,2,0,1:T(8,128)(2,1)S(1)}, u32[]{:S(2)}, u32[]{:S(2)}) collective-permute-start(bf16[2,2,4,32,384]{4,3,2,0,1:T(8,128)(2,1)} %slice.77), channel_id=1, source_target_pairs={{0,4},{4,8},{8,12},{1,5},{5,9},{9,13},{2,6},{6,10},{10,14},{3,7},{... | collective-permute-start | bytes 1179656 | tf_op jit(solution)/shard_map/ppermute | solution.py:306
  25.2 12.1 %collective-permute-start.1 = (bf16[2,4,32,384]{3,2,1,0:T(8,128)(2,1)}, bf16[2,4,32,384]{3,2,1,0:T(8,128)(2,1)S(1)}, u32[]{:S(2)}, u32[]{:S(2)}) collective-permute-start(bf16[2,4,32,384]{3,2,1,0:T(8,128)(2,1)} %fusion.45), channel_id=1, source_target_pairs={{0,8},{4,12},{1,9},{5,13},{2,10},{6,14},{3,11},{7,15},{16,24},{20,... | collective-permute-start | bytes 589832 | tf_op jit(solution)/shard_map/ppermute | solution.py:307
  29.2 8.1 %collective-permute-start.2 = (s32[2]{0:T(128)S(1)}, s32[2]{0:T(128)S(1)}, u32[]{:S(2)}, u32[]{:S(2)}) collective-permute-start(s32[2]{0:T(128)S(1)} %bitcast.53), channel_id=1, source_target_pairs={{0,4},{4,8},{8,12},{1,5},{5,9},{9,13},{2,6},{6,10},{10,14},{3,7},{... | collective-permute-start | bytes 32 | tf_op jit(solution)/shard_map/ppermute | solution.py:299
  31.5 0.7 %copy-start.3 = (f32[1152]{0:T(1024)S(1)}, f32[1152]{0:T(1024)}, u32[]{:S(2)}) copy-start(f32[1152]{0:T(1024)} %param.19) | copy-start | bytes 13828
  44.1 0.7 %copy-start.4 = (f32[384]{0:T(512)S(1)}, f32[384]{0:T(512)}, u32[]{:S(2)}) copy-start(f32[384]{0:T(512)} %param.16) | copy-start | bytes 4612
  44.2 0.9 %copy-start.5 = (f32[384]{0:T(512)S(1)}, f32[384]{0:T(512)}, u32[]{:S(2)}) copy-start(f32[384]{0:T(512)} %param.17) | copy-start | bytes 4612
  44.8 1.2 %copy-start.1 = (bf16[384,1152]{1,0:T(8,128)(2,1)S(1)}, bf16[384,1152]{1,0:T(8,128)(2,1)}, u32[]{:S(2)}) copy-start(bf16[384,1152]{1,0:T(8,128)(2,1)} %param.18) | copy-start | bytes 2654212
  45.3 1.3 %slice-start = ((f32[1152]{0:T(1024)}), f32[384]{0:T(512)S(1)}, s32[]{:S(2)}) async-start(f32[1152]{0:T(1024)} %param.19), calls=%async_computation | async-start | bytes 4096 | tf_op jit(solution)/shard_map/slice | solution.py:345
  46.6 1.7 %copy-start.6 = (f32[384]{0:T(512)S(1)}, f32[384]{0:T(512)}, u32[]{:S(2)}) copy-start(f32[384]{0:T(512)} %param.21) | copy-start | bytes 4612

commit v5 on v4

--- a/solution.py
+++ b/solution.py
@@ -184,29 +184,32 @@
     return jax.nn.silu(normalize(field, gain)).astype(jnp.bfloat16)
 
 
-def conv_part_kernel(plan, x_ref, w_ref, o_ref, acc_ref):
-    step = pl.program_id(0)
+def conv_part_kernel(plan, first_tap, x_ref, w_hbm, o_ref, w_vmem, sems):
     clips, held, rows, columns, width = x_ref.shape
     height = rows - 2
     places = clips * height * columns
-
-    @pl.when(step == 0)
-    def _():
-        acc_ref[...] = jnp.zeros_like(acc_ref)
-
+    channels = w_vmem.shape[-1]
+    copies = []
+    for index in range(len(plan)):
+        for kh in range(3):
+            slot_index = index * 3 + kh
+            copy = pltpu.make_async_copy(
+                w_hbm.at[first_tap + index, kh], w_vmem.at[slot_index], sems.at[slot_index]
+            )
+            copy.start()
+            copies.append(copy)
+    totals = [None] * o_ref.shape[0]
     for index, pairs in enumerate(plan):
-
-        @pl.when(step == index)
-        def _():
+        for kh in range(3):
+            slot_index = index * 3 + kh
+            copies[slot_index].wait()
+            weight = w_vmem[slot_index].reshape(width, channels)
             for frame, slot in pairs:
-                for kh in range(3):
-                    lhs = x_ref[:, frame, kh : kh + height, :, :].reshape(places, width)
-                    weight = w_ref[kh].reshape(width, w_ref.shape[-1])
-                    acc_ref[slot] += jnp.dot(lhs, weight, preferred_element_type=jnp.float32)
-
-    @pl.when(step == len(plan) - 1)
-    def _():
-        o_ref[...] = acc_ref[...]
+                lhs = x_ref[:, frame, kh : kh + height, :, :].reshape(places, width)
+                term = jnp.dot(lhs, weight, preferred_element_type=jnp.float32)
+                totals[slot] = term if totals[slot] is None else totals[slot] + term
+    for slot, total in enumerate(totals):
+        o_ref[slot] = total
 
 
 def conv_part(frames, causal_weight, plan, first_tap, slots):
@@ -217,26 +220,24 @@
     )
     places = clips * height * columns
     dots = sum(len(pairs) for pairs in plan) * 3
+    blocks = len(plan) * 3
     return pl.pallas_call(
-        functools.partial(conv_part_kernel, plan),
-        grid=(len(plan),),
+        functools.partial(conv_part_kernel, plan, first_tap),
         in_specs=[
-            pl.BlockSpec(taps.shape, lambda i: (0, 0, 0, 0, 0)),
-            pl.BlockSpec(
-                (None, 3, 3, channels, channels), lambda i: (first_tap + i, 0, 0, 0, 0)
-            ),
+            pl.BlockSpec(memory_space=pltpu.VMEM),
+            pl.BlockSpec(memory_space=pl.ANY),
         ],
-        out_specs=pl.BlockSpec((slots, places, channels), lambda i: (0, 0, 0)),
+        out_specs=pl.BlockSpec(memory_space=pltpu.VMEM),
         out_shape=jax.ShapeDtypeStruct((slots, places, channels), jnp.float32),
-        scratch_shapes=[pltpu.VMEM((slots, places, channels), jnp.float32)],
-        compiler_params=pltpu.CompilerParams(
-            dimension_semantics=("arbitrary",),
-            vmem_limit_bytes=48 * 1024 * 1024,
-        ),
+        scratch_shapes=[
+            pltpu.VMEM((blocks, 3, channels, channels), causal_weight.dtype),
+            pltpu.SemaphoreType.DMA((blocks,)),
+        ],
+        compiler_params=pltpu.CompilerParams(vmem_limit_bytes=48 * 1024 * 1024),
         cost_estimate=pl.CostEstimate(
             flops=2 * places * dots * 3 * channels * channels,
             transcendentals=0,
-            bytes_accessed=len(plan) * 9 * channels * channels * 2
+            bytes_accessed=blocks * 3 * channels * channels * 2
             + taps.size * 2
             + slots * places * channels * 4,
         ),

time: 49.5 us -> 49.8 us (level)
  no operation moved by 1% of the time
where the time goes in v5:
time: 49.8 us; the launch traced here: 49.5 us
  blocking collectives  21.3 us (43%)
  Pallas kernels  10.3 us (21%)
  starting transfers between devices  6.7 us (13%)
  other arithmetic  4.45 us (9%)
  local copies, waits for them, and re-layouts  4.12 us (8%)
  matrix products  2.24 us (4%)
    all_gather x1, blocking collectives, gathered_body(): both_all = lax.all_gather(both, 'rows', axis=2, tiled=True)  21.3 us
    pallas_call x2, Pallas kernels, conv_part(): pl.pallas_call(functools.partial(conv_part_kernel, plan, first_tap), in_s...  10.3 us
    ppermute x1, starting transfers between devices, gathered_body(): lax.ppermute(last_raw, 'tm', [(i, i + 2) for i in range(sections - 2)])  4 us
    unnamed x16, local copies, waits for them, and re-layouts  1.74 us
    ppermute x1, starting transfers between devices, gathered_body(): prev_counts = lax.ppermute(counts, 'tm', ahead)  1.39 us
    ppermute x1, starting transfers between devices, gathered_body(): prev_raw = lax.ppermute(inner_all, 'tm', ahead)  1.3 us
    concatenate x1, other arithmetic, gathered_body(): both = jnp.concatenate([inner_input, segment_input], axis=0)  1.01 us
  transfers between devices with their start and end apart: 3, of which 0 were waited for; matrix products, arithmetic and copies ran while one was open for 4% of the time, Pallas kernels for 10%

profile of v5, /device:TPU:0, one launch (start us, length us, event | category | flops | bytes accessed | tf_op | source)
XLA Modules:
  0.0 49.5 jit_solution(12233094343809488799)
XLA Ops:
  0.0 0.0 copy-start
  0.0 0.0 copy-start.7
  0.0 0.0 copy-start.2
  0.0 1.0 %pad_maximum_fusion.2 = bf16[4,2,1,32,384]{4,3,2,1,0:T(8,128)(2,1)S(1)} fusion(bf16[2,2,1,32,384]{4,3,2,1,0:T(8,128)(2,1)} %param.11, bf16[2,2,1,32,384]{4,3,2,1,0:T(8,128)(2,1)} %param.12), kind=kLoop, calls=%fused_computation.73 | loop fusion | flops 98304 | bytes 393216 | tf_op jit(solution)/shard_map/concatenate | solution.py:301
  1.0 21.3 %all_gather.3 = bf16[4,2,4,32,384]{4,3,2,0,1:T(8,128)(2,1)S(1)} all-gather(bf16[4,2,1,32,384]{4,3,2,0,1:T(8,128)(2,1)S(1)} %copy.29), channel_id=1, replica_groups=mesh['clips'=2,'tm'=4,'rows'=4] {'rows'}, dimensions={2}, use_global_device_ids=true | all-gather | bytes 983040 | tf_op jit(solution)/shard_map/all_gather | solution.py:302
  22.3 0.8 %slice.77 = bf16[2,2,4,32,384]{4,3,2,0,1:T(8,128)(2,1)} slice(bf16[4,2,4,32,384]{4,3,2,0,1:T(8,128)(2,1)S(1)} %all_gather.3), slice={[0:2], [0:2], [0:4], [0:32], [0:384]} | slice | bytes 786432 | tf_op jit(solution)/shard_map/slice | solution.py:303
  23.1 1.3 %collective-permute-start = (bf16[2,2,4,32,384]{4,3,2,0,1:T(8,128)(2,1)}, bf16[2,2,4,32,384]{4,3,2,0,1:T(8,128)(2,1)S(1)}, u32[]{:S(2)}, u32[]{:S(2)}) collective-permute-start(bf16[2,2,4,32,384]{4,3,2,0,1:T(8,128)(2,1)} %slice.77), channel_id=1, source_target_pairs={{0,4},{4,8},{8,12},{1,5},{5,9},{9,13},{2,6},{6,10},{10,14},{3,7},{... | collective-permute-start | bytes 1179656 | tf_op jit(solution)/shard_map/ppermute | solution.py:307
  24.4 0.0 copy-done.7
  24.5 0.8 %fusion.45 = bf16[2,4,32,384]{3,2,1,0:T(8,128)(2,1)} fusion(bf16[4,2,4,32,384]{4,3,2,0,1:T(8,128)(2,1)S(1)} %all_gather.3, pred[2]{0:T(512)(128)(4,1)S(1)} %broadcast_compare_fusion.1), kind=kLoop, calls=%fused_computation.71 | loop fusion | flops 98304 | bytes 589826 | tf_op jit(solution)/shard_map/jit(_where)/select_n | solution.py:306
  25.2 4.0 %collective-permute-start.1 = (bf16[2,4,32,384]{3,2,1,0:T(8,128)(2,1)}, bf16[2,4,32,384]{3,2,1,0:T(8,128)(2,1)S(1)}, u32[]{:S(2)}, u32[]{:S(2)}) collective-permute-start(bf16[2,4,32,384]{3,2,1,0:T(8,128)(2,1)} %fusion.45), channel_id=1, source_target_pairs={{0,8},{4,12},{1,9},{5,13},{2,10},{6,14},{3,11},{7,15},{16,24},{20,... | collective-permute-start | bytes 589832 | tf_op jit(solution)/shard_map/ppermute | solution.py:308
  29.2 1.4 %collective-permute-start.2 = (s32[2]{0:T(128)S(1)}, s32[2]{0:T(128)S(1)}, u32[]{:S(2)}, u32[]{:S(2)}) collective-permute-start(s32[2]{0:T(128)S(1)} %bitcast.53), channel_id=1, source_target_pairs={{0,4},{4,8},{8,12},{1,5},{5,9},{9,13},{2,6},{6,10},{10,14},{3,7},{... | collective-permute-start | bytes 32 | tf_op jit(solution)/shard_map/ppermute | solution.py:300
  30.6 0.2 fusion.9
  30.8 0.0 copy-done.2
  30.8 0.3 fusion.16
  31.1 0.3 pad_slice_fusion.2
  31.5 0.0 copy-start.3
  31.5 0.2 pad_maximum_fusion
  31.7 0.5 copy-done.3
  32.2 0.1 copy.21.x_ref
  32.3 5.1 %shard_map.109 = f32[2,256,384]{2,1,0:T(8,128)S(1)} custom-call(bf16[2,2,6,32,1152]{4,3,2,1,0:T(8,128)(2,1)S(1)} %copy.21.x_ref, bf16[3,3,3,384,384]{4,3,2,1,0:T(8,128)(2,1)} %w_hbm.3), custom_call_target="tpu_custom_call" | custom-call | flops 2038431744 | bytes 7864320 | tf_op jit(solution)/shard_map/pallas_call | solution.py:224
  37.4 0.0 collective-permute-done.2
  37.4 0.0 collective-permute-done.1
  37.4 0.0 collective-permute-done
  37.4 0.2 fusion.17
  37.6 0.3 fusion.24
  37.9 0.1 fusion.34
  38.1 0.1 fusion.44
  38.2 0.2 fusion.48
  38.4 0.2 fusion.31
  38.6 0.4 fusion.52
  39.0 0.2 pad_maximum_fusion.1.x_ref
  39.1 5.3 %shard_map.110 = f32[2,256,384]{2,1,0:T(8,128)S(1)} custom-call(bf16[2,2,6,32,1152]{4,3,2,1,0:T(8,128)(2,1)S(1)} %pad_maximum_fusion.1.x_ref, bf16[3,3,3,384,384]{4,3,2,1,0:T(8,128)(2,1)} %w_hbm.3), custom_call_target="tpu_custom_call" | custom-call | flops 2038431744 | bytes 7864320 | tf_op jit(solution)/shard_map/pallas_call | solution.py:224
  44.4 0.0 copy-start.4
  44.4 0.0 copy-start.5
  44.4 0.1 add.105
  44.5 0.6 %copy-done.4 = f32[384]{0:T(512)S(1)} copy-done((f32[384]{0:T(512)S(1)}, f32[384]{0:T(512)}, u32[]{:S(2)}) %copy-start.4) | copy-done | bytes 1560
  45.1 0.0 copy-start.1
  45.1 0.2 fusion.25
  45.3 0.0 copy-done.5
  45.4 0.2 fusion.27
  45.5 0.0 slice-start
  45.6 0.6 %copy-done.1 = bf16[384,1152]{1,0:T(8,128)(2,1)S(1)} copy-done((bf16[384,1152]{1,0:T(8,128)(2,1)S(1)}, bf16[384,1152]{1,0:T(8,128)(2,1)}, u32[]{:S(2)}) %copy-start.1) | copy-done | bytes 884760
  46.3 0.6 %convolution_add_fusion = f32[512,768]{1,0:T(8,128)S(1)} fusion(bf16[512,384]{1,0:T(8,128)(2,1)S(1)} %bitcast.48, f32[768]{0:T(1024)S(1)} %slice.73, bf16[384,1152]{1,0:T(8,128)(2,1)S(1)} %copy-done.1), kind=kOutput, calls=%fused_computation.7 | convolution fusion | flops 302383104 | bytes 2560000 | tf_op jit(solution)/shard_map/dot_general | solution.py:334
  46.8 0.0 copy-start.6
  46.9 0.0 slice-done
  46.9 0.2 convolution_add_fusion.2
  47.1 0.9 %convolution_multiply_fusion = f32[4,32,128]{2,1,0:T(8,128)S(1)} fusion(f32[4,32,384]{2,1,0:T(8,128)S(1)} %bitcast.49, f32[4,128,768]{2,1,0:T(8,128)S(1)} %bitcast.45), kind=kOutput, calls=%fused_computation.17 | convolution fusion | flops 75513856 | bytes 1048576 | tf_op jit(solution)/shard_map/nqc,nkc->nqk/dot_general | solution.py:348
  48.0 0.2 fusion.53
  48.2 0.3 convolution_convert_fusion
  48.5 0.0 copy-done
  48.5 0.0 copy-done.6
  48.6 0.2 fusion.4
  48.8 0.1 fusion.47
  48.9 0.7 %copy.28 = bf16[2,2,1,32,384]{4,3,2,1,0:T(8,128)(2,1)} copy(bf16[2,2,1,32,384]{4,3,2,0,1:T(8,128)(2,1)S(1)} %fusion.47) | data formatting | bytes 196608 | tf_op jit(solution)/shard_map/convert_element_type | solution.py:367
  (12 shorter events, 0.2 us)
Async XLA Ops:
  0.0 48.5 %copy-start = (bf16[384,384]{1,0:T(8,128)(2,1)S(1)}, bf16[384,384]{1,0:T(8,128)(2,1)}, u32[]{:S(2)}) copy-start(bf16[384,384]{1,0:T(8,128)(2,1)} %param.20) | copy-start | bytes 884740
  0.0 24.4 %copy-start.7 = (s32[2,1]{0,1:T(1,128)S(1)}, s32[2,1]{0,1:T(1,128)}, u32[]{:S(2)}) copy-start(s32[2,1]{0,1:T(1,128)} %param.13) | copy-start | bytes 28
  0.0 30.8 %copy-start.2 = (f32[384]{0:T(512)S(1)}, f32[384]{0:T(512)}, u32[]{:S(2)}) copy-start(f32[384]{0:T(512)} %param.14) | copy-start | bytes 4612
  23.1 14.3 %collective-permute-start = (bf16[2,2,4,32,384]{4,3,2,0,1:T(8,128)(2,1)}, bf16[2,2,4,32,384]{4,3,2,0,1:T(8,128)(2,1)S(1)}, u32[]{:S(2)}, u32[]{:S(2)}) collective-permute-start(bf16[2,2,4,32,384]{4,3,2,0,1:T(8,128)(2,1)} %slice.77), channel_id=1, source_target_pairs={{0,4},{4,8},{8,12},{1,5},{5,9},{9,13},{2,6},{6,10},{10,14},{3,7},{... | collective-permute-start | bytes 1179656 | tf_op jit(solution)/shard_map/ppermute | solution.py:307
  25.2 12.2 %collective-permute-start.1 = (bf16[2,4,32,384]{3,2,1,0:T(8,128)(2,1)}, bf16[2,4,32,384]{3,2,1,0:T(8,128)(2,1)S(1)}, u32[]{:S(2)}, u32[]{:S(2)}) collective-permute-start(bf16[2,4,32,384]{3,2,1,0:T(8,128)(2,1)} %fusion.45), channel_id=1, source_target_pairs={{0,8},{4,12},{1,9},{5,13},{2,10},{6,14},{3,11},{7,15},{16,24},{20,... | collective-permute-start | bytes 589832 | tf_op jit(solution)/shard_map/ppermute | solution.py:308
  29.2 8.2 %collective-permute-start.2 = (s32[2]{0:T(128)S(1)}, s32[2]{0:T(128)S(1)}, u32[]{:S(2)}, u32[]{:S(2)}) collective-permute-start(s32[2]{0:T(128)S(1)} %bitcast.53), channel_id=1, source_target_pairs={{0,4},{4,8},{8,12},{1,5},{5,9},{9,13},{2,6},{6,10},{10,14},{3,7},{... | collective-permute-start | bytes 32 | tf_op jit(solution)/shard_map/ppermute | solution.py:300
  31.5 0.7 %copy-start.3 = (f32[1152]{0:T(1024)S(1)}, f32[1152]{0:T(1024)}, u32[]{:S(2)}) copy-start(f32[1152]{0:T(1024)} %param.19) | copy-start | bytes 13828
  44.4 0.7 %copy-start.4 = (f32[384]{0:T(512)S(1)}, f32[384]{0:T(512)}, u32[]{:S(2)}) copy-start(f32[384]{0:T(512)} %param.16) | copy-start | bytes 4612
  44.4 0.9 %copy-start.5 = (f32[384]{0:T(512)S(1)}, f32[384]{0:T(512)}, u32[]{:S(2)}) copy-start(f32[384]{0:T(512)} %param.17) | copy-start | bytes 4612
  45.1 1.2 %copy-start.1 = (bf16[384,1152]{1,0:T(8,128)(2,1)S(1)}, bf16[384,1152]{1,0:T(8,128)(2,1)}, u32[]{:S(2)}) copy-start(bf16[384,1152]{1,0:T(8,128)(2,1)} %param.18) | copy-start | bytes 2654212
  45.5 1.3 %slice-start = ((f32[1152]{0:T(1024)}), f32[384]{0:T(512)S(1)}, s32[]{:S(2)}) async-start(f32[1152]{0:T(1024)} %param.19), calls=%async_computation | async-start | bytes 4096 | tf_op jit(solution)/shard_map/slice | solution.py:346
  46.8 1.7 %copy-start.6 = (f32[384]{0:T(512)S(1)}, f32[384]{0:T(512)}, u32[]{:S(2)}) copy-start(f32[384]{0:T(512)} %param.21) | copy-start | bytes 4612

commit v6 on v5

--- a/solution.py
+++ b/solution.py
@@ -187,7 +187,7 @@
 def conv_part_kernel(plan, first_tap, x_ref, w_hbm, o_ref, w_vmem, sems):
     clips, held, rows, columns, width = x_ref.shape
     height = rows - 2
-    places = clips * height * columns
+    places = height * columns
     channels = w_vmem.shape[-1]
     copies = []
     for index in range(len(plan)):
@@ -198,18 +198,23 @@
             )
             copy.start()
             copies.append(copy)
-    totals = [None] * o_ref.shape[0]
-    for index, pairs in enumerate(plan):
+    written = set()
+    for index, (frame, slot, count) in enumerate(plan):
         for kh in range(3):
             slot_index = index * 3 + kh
             copies[slot_index].wait()
             weight = w_vmem[slot_index].reshape(width, channels)
-            for frame, slot in pairs:
-                lhs = x_ref[:, frame, kh : kh + height, :, :].reshape(places, width)
-                term = jnp.dot(lhs, weight, preferred_element_type=jnp.float32)
-                totals[slot] = term if totals[slot] is None else totals[slot] + term
-    for slot, total in enumerate(totals):
-        o_ref[slot] = total
+            lhs = x_ref[:, frame : frame + count, kh : kh + height, :, :]
+            lhs = lhs.reshape(clips * count * places, width)
+            term = jnp.dot(lhs, weight, preferred_element_type=jnp.float32)
+            term = term.reshape(clips, count, places, channels)
+            for part in range(count):
+                target = slot + part
+                if target in written:
+                    o_ref[:, target] += term[:, part]
+                else:
+                    o_ref[:, target] = term[:, part]
+                    written.add(target)
 
 
 def conv_part(frames, causal_weight, plan, first_tap, slots):
@@ -218,8 +223,8 @@
     taps = jnp.concatenate(
         [padded[:, :, :, kw : kw + columns] for kw in range(3)], axis=-1
     )
-    places = clips * height * columns
-    dots = sum(len(pairs) for pairs in plan) * 3
+    places = height * columns
+    dots = sum(count for _, _, count in plan) * 3
     blocks = len(plan) * 3
     return pl.pallas_call(
         functools.partial(conv_part_kernel, plan, first_tap),
@@ -228,18 +233,18 @@
             pl.BlockSpec(memory_space=pl.ANY),
         ],
         out_specs=pl.BlockSpec(memory_space=pltpu.VMEM),
-        out_shape=jax.ShapeDtypeStruct((slots, places, channels), jnp.float32),
+        out_shape=jax.ShapeDtypeStruct((clips, slots, places, channels), jnp.float32),
         scratch_shapes=[
             pltpu.VMEM((blocks, 3, channels, channels), causal_weight.dtype),
             pltpu.SemaphoreType.DMA((blocks,)),
         ],
         compiler_params=pltpu.CompilerParams(vmem_limit_bytes=48 * 1024 * 1024),
         cost_estimate=pl.CostEstimate(
-            flops=2 * places * dots * 3 * channels * channels,
+            flops=2 * clips * places * dots * 3 * channels * channels,
             transcendentals=0,
             bytes_accessed=blocks * 3 * channels * channels * 2
             + taps.size * 2
-            + slots * places * channels * 4,
+            + clips * slots * places * channels * 4,
         ),
     )(taps, causal_weight)
 
@@ -259,7 +264,13 @@
 def plan_of(table):
     taps = sorted(table)
     assert taps == list(range(taps[0], taps[-1] + 1))
-    return tuple(tuple(table[kt]) for kt in taps), taps[0]
+    runs = []
+    for kt in taps:
+        pairs = sorted(table[kt], key=lambda pair: pair[1])
+        frame, slot = pairs[0]
+        assert pairs == [(frame + k, slot + k) for k in range(len(pairs))]
+        runs.append((frame, slot, len(pairs)))
+    return tuple(runs), taps[0]
 
 
 def own_conv(own_frames, causal_weight):
@@ -275,9 +286,8 @@
 
 
 def frame_major(total, clips, height, columns):
-    slots, places, channels = total.shape
-    total = total.reshape(slots, clips, height, columns, channels)
-    return jnp.transpose(total, (1, 0, 2, 3, 4))
+    clips, slots, places, channels = total.shape
+    return total.reshape(clips, slots, height, columns, channels)
 
 
 def gathered_body(

time: 49.8 us -> 49.8 us (level)
  no operation moved by 1% of the time
where the time goes in v6:
time: 49.8 us; the launch traced here: 49.5 us
  blocking collectives  21.3 us (43%)
  Pallas kernels  10.3 us (21%)
  starting transfers between devices  6.7 us (13%)
  other arithmetic  4.45 us (9%)
  local copies, waits for them, and re-layouts  4.11 us (8%)
  matrix products  2.24 us (4%)
    all_gather x1, blocking collectives, gathered_body(): both_all = lax.all_gather(both, 'rows', axis=2, tiled=True)  21.3 us
    pallas_call x2, Pallas kernels, conv_part(): pl.pallas_call(functools.partial(conv_part_kernel, plan, first_tap), in_s...  10.3 us
    ppermute x1, starting transfers between devices, gathered_body(): lax.ppermute(last_raw, 'tm', [(i, i + 2) for i in range(sections - 2)])  4 us
    unnamed x16, local copies, waits for them, and re-layouts  1.68 us
    ppermute x1, starting transfers between devices, gathered_body(): prev_counts = lax.ppermute(counts, 'tm', ahead)  1.39 us
    ppermute x1, starting transfers between devices, gathered_body(): prev_raw = lax.ppermute(inner_all, 'tm', ahead)  1.3 us
    concatenate x1, other arithmetic, gathered_body(): both = jnp.concatenate([inner_input, segment_input], axis=0)  1.01 us
  transfers between devices with their start and end apart: 3, of which 0 were waited for; matrix products, arithmetic and copies ran while one was open for 4% of the time, Pallas kernels for 10%

profile of v6, /device:TPU:0, one launch (start us, length us, event | category | flops | bytes accessed | tf_op | source)
XLA Modules:
  0.0 49.5 jit_solution(1793361843877037126)
XLA Ops:
  0.0 0.0 copy-start
  0.0 0.0 copy-start.7
  0.0 0.0 copy-start.2
  0.0 1.0 %pad_maximum_fusion.2 = bf16[4,2,1,32,384]{4,3,2,1,0:T(8,128)(2,1)S(1)} fusion(bf16[2,2,1,32,384]{4,3,2,1,0:T(8,128)(2,1)} %param.11, bf16[2,2,1,32,384]{4,3,2,1,0:T(8,128)(2,1)} %param.12), kind=kLoop, calls=%fused_computation.72 | loop fusion | flops 98304 | bytes 393216 | tf_op jit(solution)/shard_map/concatenate | solution.py:311
  1.0 21.3 %all_gather.3 = bf16[4,2,4,32,384]{4,3,2,0,1:T(8,128)(2,1)S(1)} all-gather(bf16[4,2,1,32,384]{4,3,2,0,1:T(8,128)(2,1)S(1)} %copy.31), channel_id=1, replica_groups=mesh['clips'=2,'tm'=4,'rows'=4] {'rows'}, dimensions={2}, use_global_device_ids=true | all-gather | bytes 983040 | tf_op jit(solution)/shard_map/all_gather | solution.py:312
  22.3 0.8 %slice.77 = bf16[2,2,4,32,384]{4,3,2,0,1:T(8,128)(2,1)} slice(bf16[4,2,4,32,384]{4,3,2,0,1:T(8,128)(2,1)S(1)} %all_gather.3), slice={[0:2], [0:2], [0:4], [0:32], [0:384]} | slice | bytes 786432 | tf_op jit(solution)/shard_map/slice | solution.py:313
  23.1 1.3 %collective-permute-start = (bf16[2,2,4,32,384]{4,3,2,0,1:T(8,128)(2,1)}, bf16[2,2,4,32,384]{4,3,2,0,1:T(8,128)(2,1)S(1)}, u32[]{:S(2)}, u32[]{:S(2)}) collective-permute-start(bf16[2,2,4,32,384]{4,3,2,0,1:T(8,128)(2,1)} %slice.77), channel_id=1, source_target_pairs={{0,4},{4,8},{8,12},{1,5},{5,9},{9,13},{2,6},{6,10},{10,14},{3,7},{... | collective-permute-start | bytes 1179656 | tf_op jit(solution)/shard_map/ppermute | solution.py:317
  24.4 0.0 copy-done.7
  24.5 0.8 %fusion.44 = bf16[2,4,32,384]{3,2,1,0:T(8,128)(2,1)} fusion(bf16[4,2,4,32,384]{4,3,2,0,1:T(8,128)(2,1)S(1)} %all_gather.3, pred[2]{0:T(512)(128)(4,1)S(1)} %broadcast_compare_fusion.1), kind=kLoop, calls=%fused_computation.70 | loop fusion | flops 98304 | bytes 589826 | tf_op jit(solution)/shard_map/jit(_where)/select_n | solution.py:316
  25.2 4.0 %collective-permute-start.1 = (bf16[2,4,32,384]{3,2,1,0:T(8,128)(2,1)}, bf16[2,4,32,384]{3,2,1,0:T(8,128)(2,1)S(1)}, u32[]{:S(2)}, u32[]{:S(2)}) collective-permute-start(bf16[2,4,32,384]{3,2,1,0:T(8,128)(2,1)} %fusion.44), channel_id=1, source_target_pairs={{0,8},{4,12},{1,9},{5,13},{2,10},{6,14},{3,11},{7,15},{16,24},{20,... | collective-permute-start | bytes 589832 | tf_op jit(solution)/shard_map/ppermute | solution.py:318
  29.2 1.4 %collective-permute-start.2 = (s32[2]{0:T(128)S(1)}, s32[2]{0:T(128)S(1)}, u32[]{:S(2)}, u32[]{:S(2)}) collective-permute-start(s32[2]{0:T(128)S(1)} %bitcast.48), channel_id=1, source_target_pairs={{0,4},{4,8},{8,12},{1,5},{5,9},{9,13},{2,6},{6,10},{10,14},{3,7},{... | collective-permute-start | bytes 32 | tf_op jit(solution)/shard_map/ppermute | solution.py:310
  30.6 0.2 fusion.9
  30.8 0.0 copy-done.2
  30.8 0.3 fusion.16
  31.1 0.3 pad_slice_fusion.2
  31.5 0.0 copy-start.3
  31.5 0.2 pad_maximum_fusion
  31.7 0.5 copy-done.3
  32.2 0.1 copy.22.x_ref
  32.3 5.1 %shard_map.109 = f32[2,2,128,384]{3,2,1,0:T(8,128)S(1)} custom-call(bf16[2,2,6,32,1152]{4,3,2,1,0:T(8,128)(2,1)S(1)} %copy.22.x_ref, bf16[3,3,3,384,384]{4,3,2,1,0:T(8,128)(2,1)} %w_hbm.3), custom_call_target="tpu_custom_call" | custom-call | flops 2038431744 | bytes 7864320 | tf_op jit(solution)/shard_map/pallas_call | solution.py:229
  37.4 0.0 collective-permute-done.2
  37.5 0.0 collective-permute-done.1
  37.5 0.0 collective-permute-done
  37.5 0.2 fusion.17
  37.7 0.3 fusion.24
  38.0 0.1 fusion.33
  38.1 0.1 fusion.43
  38.2 0.2 fusion.47
  38.5 0.2 fusion.30
  38.6 0.4 fusion.50
  39.0 0.2 pad_maximum_fusion.1.x_ref
  39.2 5.2 %shard_map.110 = f32[2,2,128,384]{3,2,1,0:T(8,128)S(1)} custom-call(bf16[2,2,6,32,1152]{4,3,2,1,0:T(8,128)(2,1)S(1)} %pad_maximum_fusion.1.x_ref, bf16[3,3,3,384,384]{4,3,2,1,0:T(8,128)(2,1)} %w_hbm.3), custom_call_target="tpu_custom_call" | custom-call | flops 2038431744 | bytes 7864320 | tf_op jit(solution)/shard_map/pallas_call | solution.py:229
  44.4 0.0 copy-start.4
  44.4 0.1 add.102
  44.5 0.0 copy-start.5
  44.5 0.1 copy.26
  44.6 0.5 %copy-done.4 = f32[384]{0:T(512)S(1)} copy-done((f32[384]{0:T(512)S(1)}, f32[384]{0:T(512)}, u32[]{:S(2)}) %copy-start.4) | copy-done | bytes 1560
  45.1 0.0 copy-start.1
  45.1 0.2 fusion.25
  45.3 0.0 copy-done.5
  45.3 0.2 fusion.27
  45.5 0.0 slice-start
  45.6 0.6 %copy-done.1 = bf16[384,1152]{1,0:T(8,128)(2,1)S(1)} copy-done((bf16[384,1152]{1,0:T(8,128)(2,1)S(1)}, bf16[384,1152]{1,0:T(8,128)(2,1)}, u32[]{:S(2)}) %copy-start.1) | copy-done | bytes 884760
  46.3 0.6 %convolution_add_fusion = f32[512,768]{1,0:T(8,128)S(1)} fusion(bf16[512,384]{1,0:T(8,128)(2,1)S(1)} %bitcast.43, f32[768]{0:T(1024)S(1)} %slice.73, bf16[384,1152]{1,0:T(8,128)(2,1)S(1)} %copy-done.1), kind=kOutput, calls=%fused_computation.7 | convolution fusion | flops 302383104 | bytes 2560000 | tf_op jit(solution)/shard_map/dot_general | solution.py:344
  46.8 0.0 copy-start.6
  46.8 0.0 slice-done
  46.9 0.2 convolution_add_fusion.2
  47.1 0.9 %convolution_multiply_fusion = f32[4,32,128]{2,1,0:T(8,128)S(1)} fusion(f32[4,32,384]{2,1,0:T(8,128)S(1)} %bitcast.44, f32[4,128,768]{2,1,0:T(8,128)S(1)} %bitcast.40), kind=kOutput, calls=%fused_computation.17 | convolution fusion | flops 75513856 | bytes 1048576 | tf_op jit(solution)/shard_map/nqc,nkc->nqk/dot_general | solution.py:358
  48.0 0.2 fusion.51
  48.2 0.3 convolution_convert_fusion
  48.5 0.0 copy-done
  48.5 0.0 copy-done.6
  48.5 0.2 fusion.4
  48.8 0.1 fusion.46
  48.8 0.7 %copy.30 = bf16[2,2,1,32,384]{4,3,2,1,0:T(8,128)(2,1)} copy(bf16[2,2,1,32,384]{4,3,2,0,1:T(8,128)(2,1)S(1)} %fusion.46) | data formatting | bytes 196608 | tf_op jit(solution)/shard_map/convert_element_type | solution.py:377
  (12 shorter events, 0.2 us)
Async XLA Ops:
  0.0 48.5 %copy-start = (bf16[384,384]{1,0:T(8,128)(2,1)S(1)}, bf16[384,384]{1,0:T(8,128)(2,1)}, u32[]{:S(2)}) copy-start(bf16[384,384]{1,0:T(8,128)(2,1)} %param.20) | copy-start | bytes 884740
  0.0 24.4 %copy-start.7 = (s32[2,1]{0,1:T(1,128)S(1)}, s32[2,1]{0,1:T(1,128)}, u32[]{:S(2)}) copy-start(s32[2,1]{0,1:T(1,128)} %param.13) | copy-start | bytes 28
  0.0 30.8 %copy-start.2 = (f32[384]{0:T(512)S(1)}, f32[384]{0:T(512)}, u32[]{:S(2)}) copy-start(f32[384]{0:T(512)} %param.14) | copy-start | bytes 4612
  23.1 14.3 %collective-permute-start = (bf16[2,2,4,32,384]{4,3,2,0,1:T(8,128)(2,1)}, bf16[2,2,4,32,384]{4,3,2,0,1:T(8,128)(2,1)S(1)}, u32[]{:S(2)}, u32[]{:S(2)}) collective-permute-start(bf16[2,2,4,32,384]{4,3,2,0,1:T(8,128)(2,1)} %slice.77), channel_id=1, source_target_pairs={{0,4},{4,8},{8,12},{1,5},{5,9},{9,13},{2,6},{6,10},{10,14},{3,7},{... | collective-permute-start | bytes 1179656 | tf_op jit(solution)/shard_map/ppermute | solution.py:317
  25.2 12.2 %collective-permute-start.1 = (bf16[2,4,32,384]{3,2,1,0:T(8,128)(2,1)}, bf16[2,4,32,384]{3,2,1,0:T(8,128)(2,1)S(1)}, u32[]{:S(2)}, u32[]{:S(2)}) collective-permute-start(bf16[2,4,32,384]{3,2,1,0:T(8,128)(2,1)} %fusion.44), channel_id=1, source_target_pairs={{0,8},{4,12},{1,9},{5,13},{2,10},{6,14},{3,11},{7,15},{16,24},{20,... | collective-permute-start | bytes 589832 | tf_op jit(solution)/shard_map/ppermute | solution.py:318
  29.2 8.2 %collective-permute-start.2 = (s32[2]{0:T(128)S(1)}, s32[2]{0:T(128)S(1)}, u32[]{:S(2)}, u32[]{:S(2)}) collective-permute-start(s32[2]{0:T(128)S(1)} %bitcast.48), channel_id=1, source_target_pairs={{0,4},{4,8},{8,12},{1,5},{5,9},{9,13},{2,6},{6,10},{10,14},{3,7},{... | collective-permute-start | bytes 32 | tf_op jit(solution)/shard_map/ppermute | solution.py:310
  31.5 0.7 %copy-start.3 = (f32[1152]{0:T(1024)S(1)}, f32[1152]{0:T(1024)}, u32[]{:S(2)}) copy-start(f32[1152]{0:T(1024)} %param.19) | copy-start | bytes 13828
  44.4 0.7 %copy-start.4 = (f32[384]{0:T(512)S(1)}, f32[384]{0:T(512)}, u32[]{:S(2)}) copy-start(f32[384]{0:T(512)} %param.16) | copy-start | bytes 4612
  44.5 0.8 %copy-start.5 = (f32[384]{0:T(512)S(1)}, f32[384]{0:T(512)}, u32[]{:S(2)}) copy-start(f32[384]{0:T(512)} %param.17) | copy-start | bytes 4612
  45.1 1.2 %copy-start.1 = (bf16[384,1152]{1,0:T(8,128)(2,1)S(1)}, bf16[384,1152]{1,0:T(8,128)(2,1)}, u32[]{:S(2)}) copy-start(bf16[384,1152]{1,0:T(8,128)(2,1)} %param.18) | copy-start | bytes 2654212
  45.5 1.3 %slice-start = ((f32[1152]{0:T(1024)}), f32[384]{0:T(512)S(1)}, s32[]{:S(2)}) async-start(f32[1152]{0:T(1024)} %param.19), calls=%async_computation | async-start | bytes 4096 | tf_op jit(solution)/shard_map/slice | solution.py:356
  46.8 1.7 %copy-start.6 = (f32[384]{0:T(512)S(1)}, f32[384]{0:T(512)}, u32[]{:S(2)}) copy-start(f32[384]{0:T(512)} %param.21) | copy-start | bytes 4612

commit v7 on v6

--- a/solution.py
+++ b/solution.py
@@ -249,40 +249,14 @@
     )(taps, causal_weight)
 
 
-def conv_plans(slots):
-    own, carried = {}, {}
-    for kt in range(3):
-        for slot in range(slots):
-            source = slot + kt
-            if source >= 2:
-                own.setdefault(kt, []).append((source - 2, slot))
-            else:
-                carried.setdefault(kt, []).append((source, slot))
-    return own, carried
-
-
-def plan_of(table):
-    taps = sorted(table)
-    assert taps == list(range(taps[0], taps[-1] + 1))
-    runs = []
-    for kt in taps:
-        pairs = sorted(table[kt], key=lambda pair: pair[1])
-        frame, slot = pairs[0]
-        assert pairs == [(frame + k, slot + k) for k in range(len(pairs))]
-        runs.append((frame, slot, len(pairs)))
-    return tuple(runs), taps[0]
-
-
 def own_conv(own_frames, causal_weight):
-    own_table, _ = conv_plans(own_frames.shape[1])
-    own_plan, own_first = plan_of(own_table)
-    return conv_part(own_frames, causal_weight, own_plan, own_first, own_frames.shape[1])
+    slots = own_frames.shape[1]
+    return conv_part(own_frames, causal_weight, ((0, 0, slots),), 2, slots)
 
 
 def carried_conv(carried_frames, causal_weight, slots):
-    _, carried_table = conv_plans(slots)
-    carried_plan, carried_first = plan_of(carried_table)
-    return conv_part(carried_frames, causal_weight, carried_plan, carried_first, slots)
+    plan = ((0, 0, slots), (1, 0, slots))
+    return conv_part(carried_frames, causal_weight, plan, 0, slots)
 
 
 def frame_major(total, clips, height, columns):
@@ -331,6 +305,7 @@
         ],
         axis=1,
     )
+    carried = jnp.concatenate([carried, own[:, : frame_count - 1]], axis=1)
     carried_sum = carried_conv(carried, causal_weight, frame_count)
     height = inner_all.shape[2]
     convolved = frame_major(own_sum + carried_sum, clip_count, height, column_count) + causal_bias

time: 49.8 us -> 51.2 us (1.028)
  other arithmetic: 4.45 us -> 6.77 us
    add x0 -> x1, other arithmetic: none -> 1.26 us  [activate(): return jax.nn.silu(normalize(field, gain)).astype(jnp.bfloat16)]
    reduce_sum x4, other arithmetic: 0.65 us -> 1.64 us  [normalize(): jnp.mean(widened * widened, axis=-1, keepdims=True) + EPSILON]
    ppermute x1, starting transfers between devices: 1.3 us -> 2.04 us  [gathered_body(): prev_raw = lax.ppermute(inner_all, 'tm', ahead)]
    ppermute x1, starting transfers between devices: 4 us -> 3.29 us  [gathered_body(): lax.ppermute(last_raw, 'tm', [(i, i + 2) for i in range(sections - 2)])]
    unnamed x16 -> x18, local copies, waits for them, and re-layouts: 1.68 us -> 1.12 us
  transfers between devices with their start and end apart: 3 -> 3, of which waited for: 0 -> 0; matrix products, arithmetic and copies ran while one was open for 4% -> 3% of each run, Pallas kernels for 10% -> 7%
where the time goes in v7:
time: 51.2 us; the launch traced here: 50.9 us
  blocking collectives  21.3 us (42%)
  Pallas kernels  9.86 us (19%)
  other arithmetic  6.77 us (13%)
  starting transfers between devices  6.72 us (13%)
  local copies, waits for them, and re-layouts  3.6 us (7%)
  matrix products  2.24 us (4%)
    all_gather x1, blocking collectives, gathered_body(): both_all = lax.all_gather(both, 'rows', axis=2, tiled=True)  21.3 us
    pallas_call x2, Pallas kernels, conv_part(): pl.pallas_call(functools.partial(conv_part_kernel, plan, first_tap), in_s...  9.86 us
    ppermute x1, starting transfers between devices, gathered_body(): lax.ppermute(last_raw, 'tm', [(i, i + 2) for i in range(sections - 2)])  3.29 us
    ppermute x1, starting transfers between devices, gathered_body(): prev_raw = lax.ppermute(inner_all, 'tm', ahead)  2.04 us
    reduce_sum x4, other arithmetic, normalize(): jnp.mean(widened * widened, axis=-1, keepdims=True) + EPSILON  1.64 us
    ppermute x1, starting transfers between devices, gathered_body(): prev_counts = lax.ppermute(counts, 'tm', ahead)  1.39 us
    add x1, other arithmetic, activate(): return jax.nn.silu(normalize(field, gain)).astype(jnp.bfloat16)  1.26 us
    unnamed x18, local copies, waits for them, and re-layouts  1.12 us
  transfers between devices with their start and end apart: 3, of which 0 were waited for; matrix products, arithmetic and copies ran while one was open for 3% of the time, Pallas kernels for 7%

profile of v7, /device:TPU:0, one launch (start us, length us, event | category | flops | bytes accessed | tf_op | source)
XLA Modules:
  0.0 50.9 jit_solution(6552632862513029979)
XLA Ops:
  0.0 0.0 copy-start
  0.0 0.0 copy-start.8
  0.0 0.0 copy-start.3
  0.0 1.0 %pad_maximum_fusion.2 = bf16[4,2,1,32,384]{4,3,2,1,0:T(8,128)(2,1)S(1)} fusion(bf16[2,2,1,32,384]{4,3,2,1,0:T(8,128)(2,1)} %param.11, bf16[2,2,1,32,384]{4,3,2,1,0:T(8,128)(2,1)} %param.12), kind=kLoop, calls=%fused_computation.68 | loop fusion | flops 98304 | bytes 393216 | tf_op jit(solution)/shard_map/concatenate | solution.py:285
  1.0 21.3 %all_gather.3 = bf16[4,2,4,32,384]{4,3,2,0,1:T(8,128)(2,1)S(1)} all-gather(bf16[4,2,1,32,384]{4,3,2,0,1:T(8,128)(2,1)S(1)} %copy.35), channel_id=1, replica_groups=mesh['clips'=2,'tm'=4,'rows'=4] {'rows'}, dimensions={2}, use_global_device_ids=true | all-gather | bytes 983040 | tf_op jit(solution)/shard_map/all_gather | solution.py:286
  22.3 0.8 %slice.81 = bf16[2,2,4,32,384]{4,3,2,0,1:T(8,128)(2,1)} slice(bf16[4,2,4,32,384]{4,3,2,0,1:T(8,128)(2,1)S(1)} %all_gather.3), slice={[0:2], [0:2], [0:4], [0:32], [0:384]} | slice | bytes 786432 | tf_op jit(solution)/shard_map/slice | solution.py:287
  23.1 2.0 %collective-permute-start = (bf16[2,2,4,32,384]{4,3,2,0,1:T(8,128)(2,1)}, bf16[2,2,4,32,384]{4,3,2,0,1:T(8,128)(2,1)}, u32[]{:S(2)}, u32[]{:S(2)}) collective-permute-start(bf16[2,2,4,32,384]{4,3,2,0,1:T(8,128)(2,1)} %slice.81), channel_id=1, source_target_pairs={{0,4},{4,8},{8,12},{1,5},{5,9},{9,13},{2,6},{6,10},{10,14},{3,7},{... | collective-permute-start | bytes 1179656 | tf_op jit(solution)/shard_map/ppermute | solution.py:291
  25.2 0.0 copy-done.8
  25.2 0.8 %fusion.32 = bf16[2,4,32,384]{3,2,1,0:T(8,128)(2,1)} fusion(bf16[4,2,4,32,384]{4,3,2,0,1:T(8,128)(2,1)S(1)} %all_gather.3, pred[2]{0:T(512)(128)(4,1)S(1)} %broadcast_compare_fusion.1), kind=kLoop, calls=%fused_computation.66 | loop fusion | flops 98304 | bytes 589826 | tf_op jit(solution)/shard_map/jit(_where)/select_n | solution.py:290
  25.9 3.3 %collective-permute-start.1 = (bf16[2,4,32,384]{3,2,1,0:T(8,128)(2,1)}, bf16[2,4,32,384]{3,2,1,0:T(8,128)(2,1)S(1)}, u32[]{:S(2)}, u32[]{:S(2)}) collective-permute-start(bf16[2,4,32,384]{3,2,1,0:T(8,128)(2,1)} %fusion.32), channel_id=1, source_target_pairs={{0,8},{4,12},{1,9},{5,13},{2,10},{6,14},{3,11},{7,15},{16,24},{20,... | collective-permute-start | bytes 589832 | tf_op jit(solution)/shard_map/ppermute | solution.py:292
  29.2 1.4 %collective-permute-start.2 = (s32[2]{0:T(128)S(1)}, s32[2]{0:T(128)S(1)}, u32[]{:S(2)}, u32[]{:S(2)}) collective-permute-start(s32[2]{0:T(128)S(1)} %bitcast.41), channel_id=1, source_target_pairs={{0,4},{4,8},{8,12},{1,5},{5,9},{9,13},{2,6},{6,10},{10,14},{3,7},{... | collective-permute-start | bytes 32 | tf_op jit(solution)/shard_map/ppermute | solution.py:284
  30.6 0.2 fusion.10
  30.8 0.0 copy-done.3
  30.8 0.2 negate_exponential_fusion
  31.0 0.1 fusion.19
  31.2 0.0 copy-start.1
  31.2 0.3 pad_slice_fusion.2
  31.5 0.0 copy-start.4
  31.5 0.2 pad_maximum_fusion.1.x_ref
  31.7 0.2 copy-done.1
  31.9 0.3 copy-done.4
  32.2 3.7 %shard_map.109 = f32[2,2,128,384]{3,2,1,0:T(8,128)S(1)} custom-call(bf16[2,2,6,32,1152]{4,3,2,1,0:T(8,128)(2,1)S(1)} %pad_maximum_fusion.1.x_ref, bf16[3,3,3,384,384]{4,3,2,1,0:T(8,128)(2,1)} %w_hbm.3), custom_call_target="tpu_custom_call" | custom-call | flops 1358954496 | bytes 5210112 | tf_op jit(solution)/shard_map/pallas_call | solution.py:229
  35.9 0.0 collective-permute-done.2
  35.9 0.0 collective-permute-done.1
  35.9 0.0 collective-permute-done
  36.0 1.1 %fusion.12 = f32[2,2,4,32]{3,2,0,1:T(4,128)S(1)} fusion(bf16[2,2,4,32,384]{4,3,2,0,1:T(8,128)(2,1)} %collective-permute-done), kind=kLoop, calls=%fused_computation.34 | loop fusion | flops 589312 | bytes 395264 | tf_op jit(solution)/shard_map/reduce_sum | solution.py:54
  37.1 0.0 slice-start
  37.1 1.3 %exponential_add_fusion = (f32[2,2,4,32,384]{4,3,2,0,1:T(8,128)S(1)}, f32[2,2,4,32,384]{4,3,2,0,1:T(8,128)S(1)}) fusion(f32[384]{0:T(512)S(1)} %copy-done.3, f32[2,2,4,32]{3,2,0,1:T(4,128)S(1)} %add_rsqrt_fusion.1, bf16[2,2,4,32,384]{4,3,2,0,1:T(8,128)(2,1)} %collective-permute-done), kind=kLoop, calls=%fused_computation.49 | loop fusion | flops 983040 | bytes 1969664 | tf_op jit(solution)/shard_map/jit(silu)/add | solution.py:184
  38.4 0.1 fusion.22
  38.6 0.1 fusion.18
  38.7 0.1 slice_select_fusion
  38.8 0.2 fusion.35
  39.0 0.0 slice-done
  39.1 0.3 select_maximum_fusion
  39.4 0.6 %fusion.38 = (bf16[2,3,6,32,384]{4,3,2,1,0:T(8,128)(2,1)S(1)}, bf16[2,3,6,32,384]{4,3,2,1,0:T(8,128)(2,1)S(1)}, bf16[2,3,6,32,384]{4,3,2,1,0:T(8,128)(2,1)S(1)}) fusion(bf16[2,3,6,34,384]{4,3,2,1,0:T(8,128)(2,1)S(1)} %select_maximum_fusion), kind=kLoop, calls=%fused_computation.84 | loop fusion | bytes 5308416 | tf_op jit(solution)/shard_map/slice | solution.py:224
  39.9 0.3 pad_maximum_fusion.x_ref
  40.2 6.2 %shard_map.110 = f32[2,2,128,384]{3,2,1,0:T(8,128)S(1)} custom-call(bf16[2,3,6,32,1152]{4,3,2,1,0:T(8,128)(2,1)S(1)} %pad_maximum_fusion.x_ref, bf16[3,3,3,384,384]{4,3,2,1,0:T(8,128)(2,1)} %w_hbm.3), custom_call_target="tpu_custom_call" | custom-call | flops 2717908992 | bytes 8749056 | tf_op jit(solution)/shard_map/pallas_call | solution.py:229
  46.4 0.0 copy-start.5
  46.4 0.0 copy-start.6
  46.4 0.1 add.102
  46.5 0.0 copy-start.2
  46.5 0.1 copy.30
  46.5 0.5 copy-done.5
  47.0 0.2 fusion.14
  47.3 0.0 copy-done.6
  47.3 0.0 slice-start.1
  47.3 0.2 fusion.16
  47.6 0.1 copy-done.2
  47.6 0.0 copy-start.7
  47.6 0.6 %convolution_add_fusion = f32[512,768]{1,0:T(8,128)S(1)} fusion(bf16[512,384]{1,0:T(8,128)(2,1)S(1)} %bitcast.36, f32[768]{0:T(1024)S(1)} %slice.77, bf16[384,1152]{1,0:T(8,128)(2,1)S(1)} %copy-done.2), kind=kOutput, calls=%fused_computation.10 | convolution fusion | flops 302383104 | bytes 2560000 | tf_op jit(solution)/shard_map/dot_general | solution.py:319
  48.2 0.0 slice-done.1
  48.2 0.2 convolution_add_fusion.2
  48.4 0.9 %convolution_multiply_fusion = f32[4,32,128]{2,1,0:T(8,128)S(1)} fusion(f32[4,32,384]{2,1,0:T(8,128)S(1)} %bitcast.37, f32[4,128,768]{2,1,0:T(8,128)S(1)} %bitcast.33), kind=kOutput, calls=%fused_computation.17 | convolution fusion | flops 75513856 | bytes 1048576 | tf_op jit(solution)/shard_map/nqc,nkc->nqk/dot_general | solution.py:333
  49.4 0.2 fusion.39
  49.6 0.3 convolution_convert_fusion
  49.9 0.0 copy-done
  49.9 0.0 copy-done.7
  49.9 0.2 fusion.4
  50.1 0.1 fusion.34
  50.2 0.7 %copy.34 = bf16[2,2,1,32,384]{4,3,2,1,0:T(8,128)(2,1)} copy(bf16[2,2,1,32,384]{4,3,2,0,1:T(8,128)(2,1)S(1)} %fusion.34) | data formatting | bytes 196608 | tf_op jit(solution)/shard_map/convert_element_type | solution.py:352
  (12 shorter events, 0.2 us)
Async XLA Ops:
  0.0 49.9 %copy-start = (bf16[384,384]{1,0:T(8,128)(2,1)S(1)}, bf16[384,384]{1,0:T(8,128)(2,1)}, u32[]{:S(2)}) copy-start(bf16[384,384]{1,0:T(8,128)(2,1)} %param.20) | copy-start | bytes 884740
  0.0 25.2 %copy-start.8 = (s32[2,1]{0,1:T(1,128)S(1)}, s32[2,1]{0,1:T(1,128)}, u32[]{:S(2)}) copy-start(s32[2,1]{0,1:T(1,128)} %param.13) | copy-start | bytes 28
  0.0 30.8 %copy-start.3 = (f32[384]{0:T(512)S(1)}, f32[384]{0:T(512)}, u32[]{:S(2)}) copy-start(f32[384]{0:T(512)} %param.14) | copy-start | bytes 4612
  23.1 12.8 %collective-permute-start = (bf16[2,2,4,32,384]{4,3,2,0,1:T(8,128)(2,1)}, bf16[2,2,4,32,384]{4,3,2,0,1:T(8,128)(2,1)}, u32[]{:S(2)}, u32[]{:S(2)}) collective-permute-start(bf16[2,2,4,32,384]{4,3,2,0,1:T(8,128)(2,1)} %slice.81), channel_id=1, source_target_pairs={{0,4},{4,8},{8,12},{1,5},{5,9},{9,13},{2,6},{6,10},{10,14},{3,7},{... | collective-permute-start | bytes 1179656 | tf_op jit(solution)/shard_map/ppermute | solution.py:291
  25.9 10.0 %collective-permute-start.1 = (bf16[2,4,32,384]{3,2,1,0:T(8,128)(2,1)}, bf16[2,4,32,384]{3,2,1,0:T(8,128)(2,1)S(1)}, u32[]{:S(2)}, u32[]{:S(2)}) collective-permute-start(bf16[2,4,32,384]{3,2,1,0:T(8,128)(2,1)} %fusion.32), channel_id=1, source_target_pairs={{0,8},{4,12},{1,9},{5,13},{2,10},{6,14},{3,11},{7,15},{16,24},{20,... | collective-permute-start | bytes 589832 | tf_op jit(solution)/shard_map/ppermute | solution.py:292
  29.2 6.7 %collective-permute-start.2 = (s32[2]{0:T(128)S(1)}, s32[2]{0:T(128)S(1)}, u32[]{:S(2)}, u32[]{:S(2)}) collective-permute-start(s32[2]{0:T(128)S(1)} %bitcast.41), channel_id=1, source_target_pairs={{0,4},{4,8},{8,12},{1,5},{5,9},{9,13},{2,6},{6,10},{10,14},{3,7},{... | collective-permute-start | bytes 32 | tf_op jit(solution)/shard_map/ppermute | solution.py:284
  31.2 0.7 %copy-start.1 = (bf16[2,2,4,32,384]{4,3,2,1,0:T(8,128)(2,1)}, bf16[2,2,4,32,384]{4,3,2,1,0:T(8,128)(2,1)S(1)}, u32[]{:S(2)}) copy-start(bf16[2,2,4,32,384]{4,3,2,1,0:T(8,128)(2,1)S(1)} %fusion.19) | copy-start | bytes 1179652
  31.5 0.7 %copy-start.4 = (f32[1152]{0:T(1024)S(1)}, f32[1152]{0:T(1024)}, u32[]{:S(2)}) copy-start(f32[1152]{0:T(1024)} %param.19) | copy-start | bytes 13828
  37.1 1.9 %slice-start = ((bf16[2,2,4,32,384]{4,3,2,1,0:T(8,128)(2,1)}), bf16[2,1,4,32,384]{4,3,2,1,0:T(8,128)(2,1)S(1)}, s32[]{:S(2)}) async-start(bf16[2,2,4,32,384]{4,3,2,1,0:T(8,128)(2,1)} %copy-done.1), calls=%async_computation | async-start | bytes 393216 | tf_op jit(solution)/shard_map/slice | solution.py:308
  46.4 0.7 %copy-start.5 = (f32[384]{0:T(512)S(1)}, f32[384]{0:T(512)}, u32[]{:S(2)}) copy-start(f32[384]{0:T(512)} %param.16) | copy-start | bytes 4612
  46.4 0.9 %copy-start.6 = (f32[384]{0:T(512)S(1)}, f32[384]{0:T(512)}, u32[]{:S(2)}) copy-start(f32[384]{0:T(512)} %param.17) | copy-start | bytes 4612
  46.5 1.2 %copy-start.2 = (bf16[384,1152]{1,0:T(8,128)(2,1)S(1)}, bf16[384,1152]{1,0:T(8,128)(2,1)}, u32[]{:S(2)}) copy-start(bf16[384,1152]{1,0:T(8,128)(2,1)} %param.18) | copy-start | bytes 2654212
  47.3 0.9 %slice-start.1 = ((f32[1152]{0:T(1024)}), f32[384]{0:T(512)S(1)}, s32[]{:S(2)}) async-start(f32[1152]{0:T(1024)} %param.19), calls=%async_computation.1 | async-start | bytes 4096 | tf_op jit(solution)/shard_map/slice | solution.py:331
  47.6 2.3 %copy-start.7 = (f32[384]{0:T(512)S(1)}, f32[384]{0:T(512)}, u32[]{:S(2)}) copy-start(f32[384]{0:T(512)} %param.21) | copy-start | bytes 4612

commit v8 on v6

--- a/solution.py
+++ b/solution.py
@@ -307,14 +307,32 @@
     sections = lax.axis_size("tm")
     counts = lengths[:, 0]
     ahead = [(i, i + 1) for i in range(sections - 1)]
-    prev_counts = lax.ppermute(counts, "tm", ahead)
-    both = jnp.concatenate([inner_input, segment_input], axis=0)
-    both_all = lax.all_gather(both, "rows", axis=2, tiled=True)
-    inner_all = both_all[:clip_count]
-    segment_all = both_all[clip_count:]
+    row_devices = lax.axis_size("rows")
+    row_place = lax.axis_index("rows")
+    segment_own = segment_input.reshape(clip_count, frame_count, row_count * column_count, channels)
+    received = [segment_own] + [
+        lax.ppermute(
+            segment_own, "rows", [(i, (i + shift) % row_devices) for i in range(row_devices)]
+        )
+        for shift in range(1, row_devices)
+    ]
+    inner_all = lax.all_gather(inner_input, "rows", axis=2, tiled=True)
+    by_shift = jnp.stack(received)
+    order = (row_place - jnp.arange(row_devices)) % row_devices
+    segment_all = jnp.take(by_shift, order, axis=0)
+    segment_all = jnp.moveaxis(segment_all, 0, 2).reshape(
+        clip_count, frame_count, row_devices * row_count, column_count, channels
+    )
     wide = (counts > 1)[:, None, None, None]
     last_raw = jnp.where(wide, inner_all[:, frame_count - 1], inner_all[:, 0])
-    prev_raw = lax.ppermute(inner_all, "tm", ahead)
+    height = inner_all.shape[2]
+    marks = jnp.broadcast_to(
+        counts.astype(inner_all.dtype)[:, None, None, None, None],
+        (clip_count, frame_count, height, column_count, 128),
+    )
+    sent = lax.ppermute(jnp.concatenate([inner_all, marks], axis=-1), "tm", ahead)
+    prev_raw = sent[..., :channels]
+    prev_counts = sent[:, 0, 0, 0, channels]
     before_raw = lax.ppermute(last_raw, "tm", [(i, i + 2) for i in range(sections - 2)])
     own = activate(inner_all, inner_gain)
     own_sum = own_conv(own, causal_weight)
@@ -332,7 +350,6 @@
         axis=1,
     )
     carried_sum = carried_conv(carried, causal_weight, frame_count)
-    height = inner_all.shape[2]
     convolved = frame_major(own_sum + carried_sum, clip_count, height, column_count) + causal_bias
     residual = (segment_all.astype(jnp.float32) + convolved).astype(jnp.bfloat16)
     normed = normalize(residual, attention_gain).astype(jnp.bfloat16)

time: 49.8 us -> 53.3 us (1.070)
  starting transfers between devices: 6.7 us -> 11.4 us
  blocking collectives: 21.3 us -> 17.7 us
  other arithmetic: 4.45 us -> 5.88 us
  local copies, waits for them, and re-layouts: 4.11 us -> 4.96 us
    ppermute x2 -> x4, starting transfers between devices: 2.69 us -> 8.22 us  [the longest x3 6.13 us: gathered_body(): lax.ppermute(segment_own, 'rows', [(i, (i + shift) % row_devices) for i i...]
    all_gather x1, blocking collectives: 21.3 us -> 17.7 us  [gathered_body(): inner_all = lax.all_gather(inner_input, 'rows', axis=2, tiled=True)]
    slice x1 -> x2, local copies, waits for them, and re-layouts: 0.78 us -> 1.81 us  [the longest x1 1.04 us: gathered_body(): prev_raw = sent[..., :channels]]
    ppermute x1, starting transfers between devices: 4 us -> 3.23 us  [gathered_body(): lax.ppermute(last_raw, 'tm', [(i, i + 2) for i in range(sections - 2)])]
    convert_element_type x0 -> x1, other arithmetic: none -> 0.66 us  [gathered_body(): counts.astype(inner_all.dtype)[:, None, None, None, None]]
    convert_element_type x1 -> x0, local copies, waits for them, and re-layouts: 0.65 us -> none  [gathered_body(): return (summed * live_mask[:, :, None, None, None]).astype(jnp.bfloat16)]
    convert_element_type x1, other arithmetic: 0.09 us -> 0.73 us  [gathered_body(): return (summed * live_mask[:, :, None, None, None]).astype(jnp.bfloat16)]
    gather x0 -> x1, local copies, waits for them, and re-layouts: none -> 0.63 us  [gathered_body(): segment_all = jnp.take(by_shift, order, axis=0)]
  transfers between devices with their start and end apart: 3 -> 5, of which waited for: 0 -> 0; matrix products, arithmetic and copies ran while one was open for 4% -> 13% of each run, Pallas kernels for 10% -> 10%
where the time goes in v8:
time: 53.3 us; the launch traced here: 53 us
  blocking collectives  17.7 us (33%)
  starting transfers between devices  11.4 us (21%)
  Pallas kernels  10.4 us (20%)
  other arithmetic  5.88 us (11%)
  local copies, waits for them, and re-layouts  4.96 us (9%)
  matrix products  2.24 us (4%)
    all_gather x1, blocking collectives, gathered_body(): inner_all = lax.all_gather(inner_input, 'rows', axis=2, tiled=True)  17.7 us
    pallas_call x2, Pallas kernels, conv_part(): pl.pallas_call(functools.partial(conv_part_kernel, plan, first_tap), in_s...  10.4 us
    ppermute x3, starting transfers between devices, gathered_body(): lax.ppermute(segment_own, 'rows', [(i, (i + shift) % row_devices) for i i...  6.13 us
    ppermute x1, starting transfers between devices, gathered_body(): lax.ppermute(last_raw, 'tm', [(i, i + 2) for i in range(sections - 2)])  3.23 us
    ppermute x1, starting transfers between devices, gathered_body(): lax.ppermute(jnp.concatenate([inner_all, marks], axis=-1), 'tm', ahead)  2.1 us
    unnamed x19, local copies, waits for them, and re-layouts  1.51 us
  transfers between devices with their start and end apart: 5, of which 0 were waited for; matrix products, arithmetic and copies ran while one was open for 13% of the time, Pallas kernels for 10%

profile of v8, /device:TPU:0, one launch (start us, length us, event | category | flops | bytes accessed | tf_op | source)
XLA Modules:
  0.0 53.0 jit_solution(3895010687129630550)
XLA Ops:
  0.0 0.0 copy-start
  0.0 0.0 copy-start.8
  0.0 5.1 %collective-permute-start.2 = (bf16[2,2,32,384]{3,2,1,0:T(8,128)(2,1)}, bf16[2,2,32,384]{3,2,1,0:T(8,128)(2,1)S(1)}, u32[]{:S(2)}, u32[]{:S(2)}) collective-permute-start(bf16[2,2,32,384]{3,2,1,0:T(8,128)(2,1)} %bitcast.63), channel_id=1, source_target_pairs={{0,3},{1,0},{2,1},{3,2},{4,7},{5,4},{6,5},{7,6},{8,11},{9,8},{10,9... | collective-permute-start | bytes 294920 | tf_op jit(solution)/shard_map/ppermute | solution.py:314
  5.1 0.0 collective-permute-start.1
  5.1 1.0 %collective-permute-start = (bf16[2,2,32,384]{3,2,1,0:T(8,128)(2,1)}, bf16[2,2,32,384]{3,2,1,0:T(8,128)(2,1)S(1)}, u32[]{:S(2)}, u32[]{:S(2)}) collective-permute-start(bf16[2,2,32,384]{3,2,1,0:T(8,128)(2,1)} %bitcast.65), channel_id=1, source_target_pairs={{0,1},{1,2},{2,3},{3,0},{4,5},{5,6},{6,7},{7,4},{8,9},{9,10},{10,1... | collective-permute-start | bytes 294920 | tf_op jit(solution)/shard_map/ppermute | solution.py:314
  6.1 0.9 %copy.46 = bf16[2,2,1,32,384]{4,3,2,0,1:T(8,128)(2,1)S(1)} copy(bf16[2,2,1,32,384]{4,3,2,1,0:T(8,128)(2,1)} %param.12) | data formatting | bytes 196608 | tf_op args[1]
  7.0 17.7 %all_gather.3 = bf16[2,2,4,32,384]{4,3,2,0,1:T(8,128)(2,1)S(1)} all-gather(bf16[2,2,1,32,384]{4,3,2,0,1:T(8,128)(2,1)S(1)} %copy.46), channel_id=1, replica_groups=mesh['clips'=2,'tm'=4,'rows'=4] {'rows'}, dimensions={2}, use_global_device_ids=true | all-gather | bytes 491520 | tf_op jit(solution)/shard_map/all_gather | solution.py:319
  24.7 0.7 %bitcast_convert_fusion = bf16[2]{0:T(256)(128)(2,1)S(1)} fusion(s32[2,1]{0,1:T(1,128)} %param.13), kind=kLoop, calls=%fused_computation.109 | loop fusion | flops 2 | bytes 12 | tf_op jit(solution)/shard_map/convert_element_type | solution.py:330
  25.4 0.1 broadcast_in_dim.32
  25.5 0.9 %pad_maximum_fusion.2 = bf16[2,2,4,32,512]{4,3,2,0,1:T(8,128)(2,1)} fusion(bf16[2,2,4,32,128]{4,3,2,0,1:T(8,128)(2,1)S(1)} %broadcast_in_dim.32, bf16[2,2,4,32,384]{4,3,2,0,1:T(8,128)(2,1)S(1)} %all_gather.3), kind=kLoop, calls=%fused_computation.58 | loop fusion | flops 1048576 | bytes 1048576 | tf_op jit(solution)/shard_map/concatenate | solution.py:333
  26.3 2.1 %collective-permute-start.3 = (bf16[2,2,4,32,512]{4,3,2,0,1:T(8,128)(2,1)}, bf16[2,2,4,32,512]{4,3,2,0,1:T(8,128)(2,1)}, u32[]{:S(2)}, u32[]{:S(2)}) collective-permute-start(bf16[2,2,4,32,512]{4,3,2,0,1:T(8,128)(2,1)} %pad_maximum_fusion.2), channel_id=1, source_target_pairs={{0,4},{4,8},{8,12},{1,5},{5,9},{9,13},{2,6},{6,10},{10,14},{3,7},{... | collective-permute-start | bytes 1572872 | tf_op jit(solution)/shard_map/ppermute | solution.py:333
  28.4 0.0 copy-done.8
  28.4 0.8 %fusion.45 = bf16[2,4,32,384]{3,2,1,0:T(8,128)(2,1)} fusion(bf16[2,2,4,32,384]{4,3,2,0,1:T(8,128)(2,1)S(1)} %all_gather.3, pred[2]{0:T(512)(128)(4,1)S(1)} %broadcast_compare_fusion.1), kind=kLoop, calls=%fused_computation.75 | loop fusion | flops 98304 | bytes 589826 | tf_op jit(solution)/shard_map/jit(_where)/select_n | solution.py:327
  29.2 3.2 %collective-permute-start.4 = (bf16[2,4,32,384]{3,2,1,0:T(8,128)(2,1)}, bf16[2,4,32,384]{3,2,1,0:T(8,128)(2,1)S(1)}, u32[]{:S(2)}, u32[]{:S(2)}) collective-permute-start(bf16[2,4,32,384]{3,2,1,0:T(8,128)(2,1)} %fusion.45), channel_id=1, source_target_pairs={{0,8},{4,12},{1,9},{5,13},{2,10},{6,14},{3,11},{7,15},{16,24},{20,... | collective-permute-start | bytes 589832 | tf_op jit(solution)/shard_map/ppermute | solution.py:336
  32.4 0.2 fusion.9
  32.6 0.0 copy-done.4
  32.6 0.0 copy-done.3
  32.7 0.3 fusion.16
  33.0 0.3 pad_slice_fusion.2
  33.3 0.2 pad_maximum_fusion
  33.5 0.1 copy.47.x_ref
  33.7 0.0 copy-start.2
  33.7 5.2 %shard_map.109 = f32[2,2,128,384]{3,2,1,0:T(8,128)S(1)} custom-call(bf16[2,2,6,32,1152]{4,3,2,1,0:T(8,128)(2,1)S(1)} %copy.47.x_ref, bf16[3,3,3,384,384]{4,3,2,1,0:T(8,128)(2,1)} %w_hbm.3), custom_call_target="tpu_custom_call" | custom-call | flops 2038431744 | bytes 7864320 | tf_op jit(solution)/shard_map/pallas_call | solution.py:229
  38.9 0.1 compare_convert_fusion
  38.9 0.0 collective-permute-done.2
  38.9 0.0 collective-permute-done.1
  39.0 0.0 collective-permute-done
  39.0 0.0 copy-done.2
  39.0 0.1 pad_maximum_fusion.3
  39.0 0.6 %gather_fusion = bf16[4,2,2,32,384]{4,3,2,1,0:T(8,128)(2,1)S(1)} fusion(bf16[4,2,2,32,384]{4,3,2,1,0:T(8,128)(2,1)S(1)} %pad_maximum_fusion.3, s32[1024]{0:T(1024)S(1)} %pad_clamp_fusion), kind=kCustom, calls=%fused_computation | custom fusion | bytes 786448 | tf_op jit(solution)/shard_map/jit(_take)/gather | solution.py:322
  39.7 0.0 collective-permute-done.3
  39.7 1.0 %slice.76 = bf16[2,2,4,32,384]{4,3,2,0,1:T(8,128)(2,1)S(1)} slice(bf16[2,2,4,32,512]{4,3,2,0,1:T(8,128)(2,1)} %collective-permute-done.3), slice={[0:2], [0:2], [0:4], [0:32], [0:384]} | slice | bytes 786432 | tf_op jit(solution)/shard_map/slice | solution.py:334
  40.7 0.8 %slice_reduce_fusion = bf16[2]{0:T(256)(128)(2,1)S(1)} fusion(bf16[2,2,4,32,512]{4,3,2,0,1:T(8,128)(2,1)} %collective-permute-done.3), kind=kLoop, calls=%fused_computation.101 | loop fusion | bytes 8 | tf_op jit(solution)/shard_map/slice | solution.py:335
  41.5 0.0 collective-permute-done.4
  41.5 0.2 fusion.17
  41.7 0.3 fusion.24
  42.0 0.1 fusion.34
  42.2 0.1 fusion.44
  42.3 0.2 fusion.48
  42.5 0.2 fusion.31
  42.7 0.4 fusion.58
  43.1 0.2 pad_maximum_fusion.1.x_ref
  43.2 5.2 %shard_map.110 = f32[2,2,128,384]{3,2,1,0:T(8,128)S(1)} custom-call(bf16[2,2,6,32,1152]{4,3,2,1,0:T(8,128)(2,1)S(1)} %pad_maximum_fusion.1.x_ref, bf16[3,3,3,384,384]{4,3,2,1,0:T(8,128)(2,1)} %w_hbm.3), custom_call_target="tpu_custom_call" | custom-call | flops 2038431744 | bytes 7864320 | tf_op jit(solution)/shard_map/pallas_call | solution.py:229
  48.4 0.0 copy-start.5
  48.5 0.0 copy-start.6
  48.5 0.1 add.138
  48.6 0.0 copy-start.1
  48.6 0.6 %copy-done.5 = f32[384]{0:T(512)S(1)} copy-done((f32[384]{0:T(512)S(1)}, f32[384]{0:T(512)}, u32[]{:S(2)}) %copy-start.5) | copy-done | bytes 1560
  49.1 0.3 fusion.25
  49.5 0.0 copy-done.6
  49.5 0.2 fusion.27
  49.6 0.0 slice-start
  49.7 0.0 copy-done.1
  49.7 0.6 %convolution_add_fusion = f32[512,768]{1,0:T(8,128)S(1)} fusion(bf16[512,384]{1,0:T(8,128)(2,1)S(1)} %bitcast.58, f32[768]{0:T(1024)S(1)} %slice.71, bf16[384,1152]{1,0:T(8,128)(2,1)S(1)} %copy-done.1), kind=kOutput, calls=%fused_computation.8 | convolution fusion | flops 302383104 | bytes 2560000 | tf_op jit(solution)/shard_map/dot_general | solution.py:361
  50.3 0.0 copy-start.7
  50.3 0.0 slice-done
  50.3 0.2 convolution_add_fusion.2
  50.6 1.0 %convolution_multiply_fusion = f32[4,32,128]{2,1,0:T(8,128)S(1)} fusion(f32[4,32,384]{2,1,0:T(8,128)S(1)} %bitcast.59, f32[4,128,768]{2,1,0:T(8,128)S(1)} %bitcast.55), kind=kOutput, calls=%fused_computation.18 | convolution fusion | flops 75513856 | bytes 1048576 | tf_op jit(solution)/shard_map/nqc,nkc->nqk/dot_general | solution.py:375
  51.5 0.2 fusion.59
  51.7 0.3 convolution_convert_fusion
  52.0 0.0 copy-done
  52.0 0.0 copy-done.7
  52.0 0.2 fusion.4
  52.2 0.7 %fusion.49 = bf16[2,2,1,32,384]{4,3,2,1,0:T(8,128)(2,1)} fusion(bf16[2,2,1,32,384]{4,3,1,0,2:T(8,128)(2,1)S(1)} %bitcast.62, f32[2,2]{1,0:T(2,128)S(1)} %compare_convert_fusion, bf16[2,2,4,32,384]{4,3,1,0,2:T(8,128)(2,1)S(1)} %get-tuple-element.14, s32[]{:T(128)S(6)} %select_n.63), kind=kLoop, calls=%fused_computation.81 | loop fusion | flops 245760 | bytes 294932 | tf_op jit(solution)/shard_map/convert_element_type | solution.py:394
  (15 shorter events, 0.2 us)
Async XLA Ops:
  0.0 52.0 %copy-start = (bf16[384,384]{1,0:T(8,128)(2,1)S(1)}, bf16[384,384]{1,0:T(8,128)(2,1)}, u32[]{:S(2)}) copy-start(bf16[384,384]{1,0:T(8,128)(2,1)} %param.20) | copy-start | bytes 884740
  0.0 28.4 %copy-start.8 = (s32[2,1]{0,1:T(1,128)S(1)}, s32[2,1]{0,1:T(1,128)}, u32[]{:S(2)}) copy-start(s32[2,1]{0,1:T(1,128)} %param.13) | copy-start | bytes 28
  0.0 32.6 %copy-start.4 = (f32[1152]{0:T(1024)S(1)}, f32[1152]{0:T(1024)}, u32[]{:S(2)}) copy-start(f32[1152]{0:T(1024)} %param.19) | copy-start | bytes 13828
  0.0 32.6 %copy-start.3 = (f32[384]{0:T(512)S(1)}, f32[384]{0:T(512)}, u32[]{:S(2)}) copy-start(f32[384]{0:T(512)} %param.14) | copy-start | bytes 4612
  0.0 38.9 %collective-permute-start.2 = (bf16[2,2,32,384]{3,2,1,0:T(8,128)(2,1)}, bf16[2,2,32,384]{3,2,1,0:T(8,128)(2,1)S(1)}, u32[]{:S(2)}, u32[]{:S(2)}) collective-permute-start(bf16[2,2,32,384]{3,2,1,0:T(8,128)(2,1)} %bitcast.63), channel_id=1, source_target_pairs={{0,3},{1,0},{2,1},{3,2},{4,7},{5,4},{6,5},{7,6},{8,11},{9,8},{10,9... | collective-permute-start | bytes 294920 | tf_op jit(solution)/shard_map/ppermute | solution.py:314
  5.1 33.8 %collective-permute-start.1 = (bf16[2,2,32,384]{3,2,1,0:T(8,128)(2,1)}, bf16[2,2,32,384]{3,2,1,0:T(8,128)(2,1)S(1)}, u32[]{:S(2)}, u32[]{:S(2)}) collective-permute-start(bf16[2,2,32,384]{3,2,1,0:T(8,128)(2,1)} %bitcast.64), channel_id=1, source_target_pairs={{0,2},{1,3},{2,0},{3,1},{4,6},{5,7},{6,4},{7,5},{8,10},{9,11},{10,... | collective-permute-start | bytes 294920 | tf_op jit(solution)/shard_map/ppermute | solution.py:314
  5.1 33.8 %collective-permute-start = (bf16[2,2,32,384]{3,2,1,0:T(8,128)(2,1)}, bf16[2,2,32,384]{3,2,1,0:T(8,128)(2,1)S(1)}, u32[]{:S(2)}, u32[]{:S(2)}) collective-permute-start(bf16[2,2,32,384]{3,2,1,0:T(8,128)(2,1)} %bitcast.65), channel_id=1, source_target_pairs={{0,1},{1,2},{2,3},{3,0},{4,5},{5,6},{6,7},{7,4},{8,9},{9,10},{10,1... | collective-permute-start | bytes 294920 | tf_op jit(solution)/shard_map/ppermute | solution.py:314
  26.3 13.4 %collective-permute-start.3 = (bf16[2,2,4,32,512]{4,3,2,0,1:T(8,128)(2,1)}, bf16[2,2,4,32,512]{4,3,2,0,1:T(8,128)(2,1)}, u32[]{:S(2)}, u32[]{:S(2)}) collective-permute-start(bf16[2,2,4,32,512]{4,3,2,0,1:T(8,128)(2,1)} %pad_maximum_fusion.2), channel_id=1, source_target_pairs={{0,4},{4,8},{8,12},{1,5},{5,9},{9,13},{2,6},{6,10},{10,14},{3,7},{... | collective-permute-start | bytes 1572872 | tf_op jit(solution)/shard_map/ppermute | solution.py:333
  29.2 12.3 %collective-permute-start.4 = (bf16[2,4,32,384]{3,2,1,0:T(8,128)(2,1)}, bf16[2,4,32,384]{3,2,1,0:T(8,128)(2,1)S(1)}, u32[]{:S(2)}, u32[]{:S(2)}) collective-permute-start(bf16[2,4,32,384]{3,2,1,0:T(8,128)(2,1)} %fusion.45), channel_id=1, source_target_pairs={{0,8},{4,12},{1,9},{5,13},{2,10},{6,14},{3,11},{7,15},{16,24},{20,... | collective-permute-start | bytes 589832 | tf_op jit(solution)/shard_map/ppermute | solution.py:336
  33.7 5.3 %copy-start.2 = (bf16[2,2,1,32,384]{4,3,2,1,0:T(8,128)(2,1)S(1)}, bf16[2,2,1,32,384]{4,3,2,1,0:T(8,128)(2,1)}, u32[]{:S(2)}) copy-start(bf16[2,2,1,32,384]{4,3,2,1,0:T(8,128)(2,1)} %param.11) | copy-start | bytes 294916
  48.4 0.7 %copy-start.5 = (f32[384]{0:T(512)S(1)}, f32[384]{0:T(512)}, u32[]{:S(2)}) copy-start(f32[384]{0:T(512)} %param.16) | copy-start | bytes 4612
  48.5 1.0 %copy-start.6 = (f32[384]{0:T(512)S(1)}, f32[384]{0:T(512)}, u32[]{:S(2)}) copy-start(f32[384]{0:T(512)} %param.17) | copy-start | bytes 4612
  48.6 1.2 %copy-start.1 = (bf16[384,1152]{1,0:T(8,128)(2,1)S(1)}, bf16[384,1152]{1,0:T(8,128)(2,1)}, u32[]{:S(2)}) copy-start(bf16[384,1152]{1,0:T(8,128)(2,1)} %param.18) | copy-start | bytes 2654212
  49.6 0.7 %slice-start = ((f32[1152]{0:T(1024)}), f32[384]{0:T(512)S(1)}, s32[]{:S(2)}) async-start(f32[1152]{0:T(1024)} %param.19), calls=%async_computation | async-start | bytes 4096 | tf_op jit(solution)/shard_map/slice | solution.py:373
  50.3 1.7 %copy-start.7 = (f32[384]{0:T(512)S(1)}, f32[384]{0:T(512)}, u32[]{:S(2)}) copy-start(f32[384]{0:T(512)} %param.21) | copy-start | bytes 4612

commit v9 on v6

--- a/solution.py
+++ b/solution.py
@@ -313,16 +313,14 @@
     inner_all = both_all[:clip_count]
     segment_all = both_all[clip_count:]
     wide = (counts > 1)[:, None, None, None]
-    last_raw = jnp.where(wide, inner_all[:, frame_count - 1], inner_all[:, 0])
-    prev_raw = lax.ppermute(inner_all, "tm", ahead)
-    before_raw = lax.ppermute(last_raw, "tm", [(i, i + 2) for i in range(sections - 2)])
     own = activate(inner_all, inner_gain)
+    last = jnp.where(wide, own[:, frame_count - 1], own[:, 0])
+    prev = lax.ppermute(own, "tm", ahead)
+    before = lax.ppermute(last, "tm", [(i, i + 2) for i in range(sections - 2)])
     own_sum = own_conv(own, causal_weight)
-    own_sum, prev_raw, before_raw, prev_counts = lax.optimization_barrier(
-        (own_sum, prev_raw, before_raw, prev_counts)
-    )
-    prev = activate(prev_raw, inner_gain)
-    before = activate(before_raw, inner_gain)
+    own_sum, prev, before, prev_counts = lax.optimization_barrier(
+        (own_sum, prev, before, prev_counts)
+    )
     prev_wide = (prev_counts > 1)[:, None, None, None]
     carried = jnp.stack(
         [

time: 49.8 us -> 50.3 us (1.010)
  other arithmetic: 4.45 us -> 5.74 us
  local copies, waits for them, and re-layouts: 4.11 us -> 3.32 us
    select_n x1, other arithmetic: 0.09 us -> 1.15 us  [gathered_body(): jnp.where(prev_wide, prev[:, frame_count - 1], prev[:, 0])]
    another operation x2, other arithmetic: 0.41 us -> 1.23 us  [gathered_body(): jnp.stack([jnp.where(prev_wide, prev[:, frame_count - 2], before), jnp.wh...]
    slice x1 -> x0, local copies, waits for them, and re-layouts: 0.78 us -> none  [gathered_body(): inner_all = both_all[:clip_count]]
  transfers between devices with their start and end apart: 3 -> 3, of which waited for: 0 -> 0; matrix products, arithmetic and copies ran while one was open for 4% -> 3% of each run, Pallas kernels for 10% -> 10%
where the time goes in v9:
time: 50.3 us; the launch traced here: 50 us
  blocking collectives  21.3 us (42%)
  Pallas kernels  10.3 us (20%)
  starting transfers between devices  6.73 us (13%)
  other arithmetic  5.74 us (11%)
  local copies, waits for them, and re-layouts  3.32 us (7%)
  matrix products  2.24 us (4%)
    all_gather x1, blocking collectives, gathered_body(): both_all = lax.all_gather(both, 'rows', axis=2, tiled=True)  21.3 us
    pallas_call x2, Pallas kernels, conv_part(): pl.pallas_call(functools.partial(conv_part_kernel, plan, first_tap), in_s...  10.3 us
    ppermute x1, starting transfers between devices, gathered_body(): before = lax.ppermute(last, 'tm', [(i, i + 2) for i in range(sections - 2)])  3.29 us
    ppermute x1, starting transfers between devices, gathered_body(): prev = lax.ppermute(own, 'tm', ahead)  2.04 us
    unnamed x16, local copies, waits for them, and re-layouts  1.68 us
    ppermute x1, starting transfers between devices, gathered_body(): prev_counts = lax.ppermute(counts, 'tm', ahead)  1.39 us
    another operation x2, other arithmetic, gathered_body(): jnp.stack([jnp.where(prev_wide, prev[:, frame_count - 2], before), jnp.wh...  1.23 us
    select_n x1, other arithmetic, gathered_body(): jnp.where(prev_wide, prev[:, frame_count - 1], prev[:, 0])  1.15 us
  transfers between devices with their start and end apart: 3, of which 0 were waited for; matrix products, arithmetic and copies ran while one was open for 3% of the time, Pallas kernels for 10%

profile of v9, /device:TPU:0, one launch (start us, length us, event | category | flops | bytes accessed | tf_op | source)
XLA Modules:
  0.0 50.0 jit_solution(18420007424420758049)
XLA Ops:
  0.0 0.0 copy-start
  0.0 0.0 copy-start.3
  0.0 0.0 copy-start.7
  0.0 1.0 %pad_maximum_fusion.2 = bf16[4,2,1,32,384]{4,3,2,1,0:T(8,128)(2,1)S(1)} fusion(bf16[2,2,1,32,384]{4,3,2,1,0:T(8,128)(2,1)} %param.11, bf16[2,2,1,32,384]{4,3,2,1,0:T(8,128)(2,1)} %param.12), kind=kLoop, calls=%fused_computation.49 | loop fusion | flops 98304 | bytes 393216 | tf_op jit(solution)/shard_map/concatenate | solution.py:311
  1.0 21.3 %all_gather.3 = bf16[4,2,4,32,384]{4,3,2,0,1:T(8,128)(2,1)S(1)} all-gather(bf16[4,2,1,32,384]{4,3,2,0,1:T(8,128)(2,1)S(1)} %copy.31), channel_id=1, replica_groups=mesh['clips'=2,'tm'=4,'rows'=4] {'rows'}, dimensions={2}, use_global_device_ids=true | all-gather | bytes 983040 | tf_op jit(solution)/shard_map/all_gather | solution.py:312
  22.3 0.2 fusion.9
  22.5 0.0 copy-done.3
  22.5 0.3 fusion.16
  22.8 2.0 %collective-permute-start = (bf16[2,2,4,32,384]{4,3,2,0,1:T(8,128)(2,1)S(1)}, bf16[2,2,4,32,384]{4,3,2,0,1:T(8,128)(2,1)}, u32[]{:S(2)}, u32[]{:S(2)}) collective-permute-start(bf16[2,2,4,32,384]{4,3,2,0,1:T(8,128)(2,1)S(1)} %fusion.16), channel_id=1, source_target_pairs={{0,4},{4,8},{8,12},{1,5},{5,9},{9,13},{2,6},{6,10},{10,14},{3,7},{... | collective-permute-start | bytes 1179656 | tf_op jit(solution)/shard_map/ppermute | solution.py:318
  24.9 0.0 copy-done.7
  24.9 0.8 %fusion.26 = bf16[2,4,32,384]{3,2,1,0:T(8,128)(2,1)} fusion(bf16[2,2,4,32,384]{4,3,2,0,1:T(8,128)(2,1)S(1)} %fusion.16, pred[2]{0:T(512)(128)(4,1)S(1)} %broadcast_compare_fusion.1), kind=kLoop, calls=%fused_computation.47 | loop fusion | flops 98304 | bytes 589826 | tf_op jit(solution)/shard_map/jit(_where)/select_n | solution.py:317
  25.7 3.3 %collective-permute-start.1 = (bf16[2,4,32,384]{3,2,1,0:T(8,128)(2,1)}, bf16[2,4,32,384]{3,2,1,0:T(8,128)(2,1)S(1)}, u32[]{:S(2)}, u32[]{:S(2)}) collective-permute-start(bf16[2,4,32,384]{3,2,1,0:T(8,128)(2,1)} %fusion.26), channel_id=1, source_target_pairs={{0,8},{4,12},{1,9},{5,13},{2,10},{6,14},{3,11},{7,15},{16,24},{20,... | collective-permute-start | bytes 589832 | tf_op jit(solution)/shard_map/ppermute | solution.py:319
  29.0 1.4 %collective-permute-start.2 = (s32[2]{0:T(128)S(1)}, s32[2]{0:T(128)S(1)}, u32[]{:S(2)}, u32[]{:S(2)}) collective-permute-start(s32[2]{0:T(128)S(1)} %bitcast.43), channel_id=1, source_target_pairs={{0,4},{4,8},{8,12},{1,5},{5,9},{9,13},{2,6},{6,10},{10,14},{3,7},{... | collective-permute-start | bytes 32 | tf_op jit(solution)/shard_map/ppermute | solution.py:310
  30.4 0.3 pad_slice_fusion.2
  30.7 0.0 copy-start.2
  30.7 0.2 pad_maximum_fusion
  30.9 0.5 copy-done.2
  31.4 0.1 copy.22.x_ref
  31.6 5.1 %shard_map.109 = f32[2,2,128,384]{3,2,1,0:T(8,128)S(1)} custom-call(bf16[2,2,6,32,1152]{4,3,2,1,0:T(8,128)(2,1)S(1)} %copy.22.x_ref, bf16[3,3,3,384,384]{4,3,2,1,0:T(8,128)(2,1)} %w_hbm.3), custom_call_target="tpu_custom_call" | custom-call | flops 2038431744 | bytes 7864320 | tf_op jit(solution)/shard_map/pallas_call | solution.py:229
  36.7 0.0 collective-permute-done.2
  36.7 0.0 collective-permute-done.1
  36.7 0.0 collective-permute-done
  36.7 1.2 %bitcast_select_fusion = bf16[2,1,4,32,384]{4,3,2,1,0:T(8,128)(2,1)S(1)} fusion(bf16[2,2,4,32,384]{4,3,2,0,1:T(8,128)(2,1)} %collective-permute-done, pred[2]{0:T(512)(128)(4,1)S(1)} %broadcast_compare_fusion), kind=kLoop, calls=%fused_computation.50 | loop fusion | flops 98304 | bytes 589826 | tf_op jit(solution)/shard_map/jit(_where)/select_n | solution.py:328
  37.9 1.1 %fusion.27 = bf16[2,1,4,32,384]{4,3,2,1,0:T(8,128)(2,1)S(1)} fusion(bf16[2,4,32,384]{3,2,1,0:T(8,128)(2,1)S(1)} %collective-permute-done.1, pred[2]{0:T(512)(128)(4,1)S(1)} %broadcast_compare_fusion, bf16[2,2,4,32,384]{4,3,2,0,1:T(8,128)(2,1)} %collective-permute-done), kind=kLoop, calls=%fused_computation.52 | loop fusion | flops 98304 | bytes 589826 | tf_op jit(solution)/shard_map/stack | solution.py:325
  38.9 0.2 fusion.22
  39.1 0.4 fusion.32
  39.5 0.2 pad_maximum_fusion.1.x_ref
  39.7 5.2 %shard_map.110 = f32[2,2,128,384]{3,2,1,0:T(8,128)S(1)} custom-call(bf16[2,2,6,32,1152]{4,3,2,1,0:T(8,128)(2,1)S(1)} %pad_maximum_fusion.1.x_ref, bf16[3,3,3,384,384]{4,3,2,1,0:T(8,128)(2,1)} %w_hbm.3), custom_call_target="tpu_custom_call" | custom-call | flops 2038431744 | bytes 7864320 | tf_op jit(solution)/shard_map/pallas_call | solution.py:229
  44.9 0.0 copy-start.4
  44.9 0.1 add.71
  45.0 0.0 copy-start.5
  45.0 0.1 copy.26
  45.1 0.5 %copy-done.4 = f32[384]{0:T(512)S(1)} copy-done((f32[384]{0:T(512)S(1)}, f32[384]{0:T(512)}, u32[]{:S(2)}) %copy-start.4) | copy-done | bytes 1560
  45.6 0.0 copy-start.1
  45.6 0.2 fusion.17
  45.8 0.0 copy-done.5
  45.8 0.2 fusion.19
  46.0 0.0 slice-start
  46.1 0.6 %copy-done.1 = bf16[384,1152]{1,0:T(8,128)(2,1)S(1)} copy-done((bf16[384,1152]{1,0:T(8,128)(2,1)S(1)}, bf16[384,1152]{1,0:T(8,128)(2,1)}, u32[]{:S(2)}) %copy-start.1) | copy-done | bytes 884760
  46.7 0.6 %convolution_add_fusion = f32[512,768]{1,0:T(8,128)S(1)} fusion(bf16[512,384]{1,0:T(8,128)(2,1)S(1)} %bitcast.38, f32[768]{0:T(1024)S(1)} %slice.71, bf16[384,1152]{1,0:T(8,128)(2,1)S(1)} %copy-done.1), kind=kOutput, calls=%fused_computation.7 | convolution fusion | flops 302383104 | bytes 2560000 | tf_op jit(solution)/shard_map/dot_general | solution.py:342
  47.3 0.0 copy-start.6
  47.3 0.0 slice-done
  47.3 0.2 convolution_add_fusion.2
  47.5 0.9 %convolution_multiply_fusion = f32[4,32,128]{2,1,0:T(8,128)S(1)} fusion(f32[4,32,384]{2,1,0:T(8,128)S(1)} %bitcast.39, f32[4,128,768]{2,1,0:T(8,128)S(1)} %bitcast.35), kind=kOutput, calls=%fused_computation.17 | convolution fusion | flops 75513856 | bytes 1048576 | tf_op jit(solution)/shard_map/nqc,nkc->nqk/dot_general | solution.py:356
  48.5 0.2 fusion.33
  48.7 0.3 convolution_convert_fusion
  49.0 0.0 copy-done
  49.0 0.0 copy-done.6
  49.0 0.2 fusion.4
  49.2 0.1 fusion.29
  49.3 0.7 %copy.30 = bf16[2,2,1,32,384]{4,3,2,1,0:T(8,128)(2,1)} copy(bf16[2,2,1,32,384]{4,3,2,0,1:T(8,128)(2,1)S(1)} %fusion.29) | data formatting | bytes 196608 | tf_op jit(solution)/shard_map/convert_element_type | solution.py:375
  (10 shorter events, 0.1 us)
Async XLA Ops:
  0.0 49.0 %copy-start = (bf16[384,384]{1,0:T(8,128)(2,1)S(1)}, bf16[384,384]{1,0:T(8,128)(2,1)}, u32[]{:S(2)}) copy-start(bf16[384,384]{1,0:T(8,128)(2,1)} %param.20) | copy-start | bytes 884740
  0.0 22.5 %copy-start.3 = (f32[384]{0:T(512)S(1)}, f32[384]{0:T(512)}, u32[]{:S(2)}) copy-start(f32[384]{0:T(512)} %param.14) | copy-start | bytes 4612
  0.0 24.9 %copy-start.7 = (s32[2,1]{0,1:T(1,128)S(1)}, s32[2,1]{0,1:T(1,128)}, u32[]{:S(2)}) copy-start(s32[2,1]{0,1:T(1,128)} %param.13) | copy-start | bytes 28
  22.8 13.9 %collective-permute-start = (bf16[2,2,4,32,384]{4,3,2,0,1:T(8,128)(2,1)S(1)}, bf16[2,2,4,32,384]{4,3,2,0,1:T(8,128)(2,1)}, u32[]{:S(2)}, u32[]{:S(2)}) collective-permute-start(bf16[2,2,4,32,384]{4,3,2,0,1:T(8,128)(2,1)S(1)} %fusion.16), channel_id=1, source_target_pairs={{0,4},{4,8},{8,12},{1,5},{5,9},{9,13},{2,6},{6,10},{10,14},{3,7},{... | collective-permute-start | bytes 1179656 | tf_op jit(solution)/shard_map/ppermute | solution.py:318
  25.7 11.0 %collective-permute-start.1 = (bf16[2,4,32,384]{3,2,1,0:T(8,128)(2,1)}, bf16[2,4,32,384]{3,2,1,0:T(8,128)(2,1)S(1)}, u32[]{:S(2)}, u32[]{:S(2)}) collective-permute-start(bf16[2,4,32,384]{3,2,1,0:T(8,128)(2,1)} %fusion.26), channel_id=1, source_target_pairs={{0,8},{4,12},{1,9},{5,13},{2,10},{6,14},{3,11},{7,15},{16,24},{20,... | collective-permute-start | bytes 589832 | tf_op jit(solution)/shard_map/ppermute | solution.py:319
  29.0 7.7 %collective-permute-start.2 = (s32[2]{0:T(128)S(1)}, s32[2]{0:T(128)S(1)}, u32[]{:S(2)}, u32[]{:S(2)}) collective-permute-start(s32[2]{0:T(128)S(1)} %bitcast.43), channel_id=1, source_target_pairs={{0,4},{4,8},{8,12},{1,5},{5,9},{9,13},{2,6},{6,10},{10,14},{3,7},{... | collective-permute-start | bytes 32 | tf_op jit(solution)/shard_map/ppermute | solution.py:310
  30.7 0.7 %copy-start.2 = (f32[1152]{0:T(1024)S(1)}, f32[1152]{0:T(1024)}, u32[]{:S(2)}) copy-start(f32[1152]{0:T(1024)} %param.19) | copy-start | bytes 13828
  44.9 0.7 %copy-start.4 = (f32[384]{0:T(512)S(1)}, f32[384]{0:T(512)}, u32[]{:S(2)}) copy-start(f32[384]{0:T(512)} %param.16) | copy-start | bytes 4612
  45.0 0.8 %copy-start.5 = (f32[384]{0:T(512)S(1)}, f32[384]{0:T(512)}, u32[]{:S(2)}) copy-start(f32[384]{0:T(512)} %param.17) | copy-start | bytes 4612
  45.6 1.2 %copy-start.1 = (bf16[384,1152]{1,0:T(8,128)(2,1)S(1)}, bf16[384,1152]{1,0:T(8,128)(2,1)}, u32[]{:S(2)}) copy-start(bf16[384,1152]{1,0:T(8,128)(2,1)} %param.18) | copy-start | bytes 2654212
  46.0 1.3 %slice-start = ((f32[1152]{0:T(1024)}), f32[384]{0:T(512)S(1)}, s32[]{:S(2)}) async-start(f32[1152]{0:T(1024)} %param.19), calls=%async_computation | async-start | bytes 4096 | tf_op jit(solution)/shard_map/slice | solution.py:354
  47.3 1.7 %copy-start.6 = (f32[384]{0:T(512)S(1)}, f32[384]{0:T(512)}, u32[]{:S(2)}) copy-start(f32[384]{0:T(512)} %param.21) | copy-start | bytes 4612

commit v10 on v6

--- a/solution.py
+++ b/solution.py
@@ -238,7 +238,7 @@
             pltpu.VMEM((blocks, 3, channels, channels), causal_weight.dtype),
             pltpu.SemaphoreType.DMA((blocks,)),
         ],
-        compiler_params=pltpu.CompilerParams(vmem_limit_bytes=48 * 1024 * 1024),
+        compiler_params=pltpu.CompilerParams(vmem_limit_bytes=12 * 1024 * 1024),
         cost_estimate=pl.CostEstimate(
             flops=2 * clips * places * dots * 3 * channels * channels,
             transcendentals=0,

time: 49.8 us -> 53.3 us (1.070)
  local copies, waits for them, and re-layouts: 4.11 us -> 7.63 us
    unnamed x16 -> x22, local copies, waits for them, and re-layouts: 1.68 us -> 5.2 us
where the time goes in v10:
time: 53.3 us; the launch traced here: 53 us
  blocking collectives  21.3 us (40%)
  Pallas kernels  10.2 us (19%)
  local copies, waits for them, and re-layouts  7.63 us (14%)
  starting transfers between devices  6.7 us (13%)
  other arithmetic  4.51 us (8%)
  matrix products  2.24 us (4%)
    all_gather x1, blocking collectives, gathered_body(): both_all = lax.all_gather(both, 'rows', axis=2, tiled=True)  21.3 us
    pallas_call x2, Pallas kernels, conv_part(): pl.pallas_call(functools.partial(conv_part_kernel, plan, first_tap), in_s...  10.2 us
    unnamed x22, local copies, waits for them, and re-layouts  5.2 us
    ppermute x1, starting transfers between devices, gathered_body(): lax.ppermute(last_raw, 'tm', [(i, i + 2) for i in range(sections - 2)])  4 us
    ppermute x1, starting transfers between devices, gathered_body(): prev_counts = lax.ppermute(counts, 'tm', ahead)  1.39 us
    ppermute x1, starting transfers between devices, gathered_body(): prev_raw = lax.ppermute(inner_all, 'tm', ahead)  1.3 us
  transfers between devices with their start and end apart: 3, of which 0 were waited for; matrix products, arithmetic and copies ran while one was open for 4% of the time, Pallas kernels for 10%

profile of v10, /device:TPU:0, one launch (start us, length us, event | category | flops | bytes accessed | tf_op | source)
XLA Modules:
  0.0 53.0 jit_solution(5694110922770280400)
XLA Ops:
  0.0 0.0 copy-start
  0.0 0.0 copy-start.8
  0.0 0.0 copy-start.3
  0.0 1.0 %pad_maximum_fusion.2 = bf16[4,2,1,32,384]{4,3,2,1,0:T(8,128)(2,1)S(1)} fusion(bf16[2,2,1,32,384]{4,3,2,1,0:T(8,128)(2,1)} %param.11, bf16[2,2,1,32,384]{4,3,2,1,0:T(8,128)(2,1)} %param.12), kind=kLoop, calls=%fused_computation.72 | loop fusion | flops 98304 | bytes 393216 | tf_op jit(solution)/shard_map/concatenate | solution.py:311
  1.0 21.3 %all_gather.3 = bf16[4,2,4,32,384]{4,3,2,0,1:T(8,128)(2,1)S(1)} all-gather(bf16[4,2,1,32,384]{4,3,2,0,1:T(8,128)(2,1)S(1)} %copy.31), channel_id=1, replica_groups=mesh['clips'=2,'tm'=4,'rows'=4] {'rows'}, dimensions={2}, use_global_device_ids=true | all-gather | bytes 983040 | tf_op jit(solution)/shard_map/all_gather | solution.py:312
  22.3 0.8 %slice.77 = bf16[2,2,4,32,384]{4,3,2,0,1:T(8,128)(2,1)} slice(bf16[4,2,4,32,384]{4,3,2,0,1:T(8,128)(2,1)S(1)} %all_gather.3), slice={[0:2], [0:2], [0:4], [0:32], [0:384]} | slice | bytes 786432 | tf_op jit(solution)/shard_map/slice | solution.py:313
  23.1 1.3 %collective-permute-start = (bf16[2,2,4,32,384]{4,3,2,0,1:T(8,128)(2,1)}, bf16[2,2,4,32,384]{4,3,2,0,1:T(8,128)(2,1)S(1)}, u32[]{:S(2)}, u32[]{:S(2)}) collective-permute-start(bf16[2,2,4,32,384]{4,3,2,0,1:T(8,128)(2,1)} %slice.77), channel_id=1, source_target_pairs={{0,4},{4,8},{8,12},{1,5},{5,9},{9,13},{2,6},{6,10},{10,14},{3,7},{... | collective-permute-start | bytes 1179656 | tf_op jit(solution)/shard_map/ppermute | solution.py:317
  24.4 0.0 copy-done.8
  24.5 0.8 %fusion.44 = bf16[2,4,32,384]{3,2,1,0:T(8,128)(2,1)} fusion(bf16[4,2,4,32,384]{4,3,2,0,1:T(8,128)(2,1)S(1)} %all_gather.3, pred[2]{0:T(512)(128)(4,1)S(1)} %broadcast_compare_fusion.1), kind=kLoop, calls=%fused_computation.70 | loop fusion | flops 98304 | bytes 589826 | tf_op jit(solution)/shard_map/jit(_where)/select_n | solution.py:316
  25.2 4.0 %collective-permute-start.1 = (bf16[2,4,32,384]{3,2,1,0:T(8,128)(2,1)}, bf16[2,4,32,384]{3,2,1,0:T(8,128)(2,1)S(1)}, u32[]{:S(2)}, u32[]{:S(2)}) collective-permute-start(bf16[2,4,32,384]{3,2,1,0:T(8,128)(2,1)} %fusion.44), channel_id=1, source_target_pairs={{0,8},{4,12},{1,9},{5,13},{2,10},{6,14},{3,11},{7,15},{16,24},{20,... | collective-permute-start | bytes 589832 | tf_op jit(solution)/shard_map/ppermute | solution.py:318
  29.2 1.4 %collective-permute-start.2 = (s32[2]{0:T(128)S(1)}, s32[2]{0:T(128)S(1)}, u32[]{:S(2)}, u32[]{:S(2)}) collective-permute-start(s32[2]{0:T(128)S(1)} %bitcast.50), channel_id=1, source_target_pairs={{0,4},{4,8},{8,12},{1,5},{5,9},{9,13},{2,6},{6,10},{10,14},{3,7},{... | collective-permute-start | bytes 32 | tf_op jit(solution)/shard_map/ppermute | solution.py:310
  30.6 0.2 fusion.9
  30.8 0.0 copy-done.3
  30.8 0.3 fusion.16
  31.1 0.3 pad_slice_fusion.2
  31.5 0.0 copy-start.4
  31.5 0.2 pad_maximum_fusion
  31.7 0.5 copy-done.4
  32.2 0.1 copy.22.x_ref
  32.3 0.0 copy-start.1
  32.3 3.3 %copy-done.1 = bf16[3,3,3,384,384]{4,3,2,1,0:T(8,128)(2,1)S(1)} copy-done((bf16[3,3,3,384,384]{4,3,2,1,0:T(8,128)(2,1)S(1)}, bf16[3,3,3,384,384]{4,3,2,1,0:T(8,128)(2,1)}, u32[]{:S(2)}) %copy-start.1) | copy-done | bytes 7962648
  35.6 0.0 slice-start
  35.6 5.0 %shard_map.109 = f32[2,2,128,384]{3,2,1,0:T(8,128)S(1)} custom-call(bf16[2,2,6,32,1152]{4,3,2,1,0:T(8,128)(2,1)S(1)} %copy.22.x_ref, bf16[3,3,3,384,384]{4,3,2,1,0:T(8,128)(2,1)S(1)} %copy-done.1), custom_call_target="tpu_custom_call" | custom-call | flops 2038431744 | bytes 7864320 | tf_op jit(solution)/shard_map/pallas_call | solution.py:229
  40.6 0.0 slice-start.1
  40.7 0.0 collective-permute-done.2
  40.7 0.0 collective-permute-done.1
  40.7 0.0 collective-permute-done
  40.7 0.2 fusion.17
  40.9 0.3 fusion.24
  41.2 0.1 fusion.33
  41.3 0.1 fusion.43
  41.4 0.2 fusion.47
  41.7 0.2 fusion.30
  41.8 0.4 fusion.50
  42.2 0.2 pad_maximum_fusion.1.x_ref
  42.4 0.0 slice-done
  42.4 0.3 slice-done.1
  42.7 5.2 %shard_map.110 = f32[2,2,128,384]{3,2,1,0:T(8,128)S(1)} custom-call(bf16[2,2,6,32,1152]{4,3,2,1,0:T(8,128)(2,1)S(1)} %pad_maximum_fusion.1.x_ref, bf16[3,3,3,384,384]{4,3,2,1,0:T(8,128)(2,1)S(1)} %bitcast.41), custom_call_target="tpu_custom_call" | custom-call | flops 2038431744 | bytes 7864320 | tf_op jit(solution)/shard_map/pallas_call | solution.py:229
  47.9 0.0 copy-start.5
  47.9 0.1 add.102
  48.0 0.0 copy-start.6
  48.0 0.1 copy.26
  48.1 0.5 copy-done.5
  48.6 0.0 copy-start.2
  48.6 0.2 fusion.25
  48.8 0.0 copy-done.6
  48.8 0.2 fusion.27
  49.0 0.0 slice-start.2
  49.1 0.6 %copy-done.2 = bf16[384,1152]{1,0:T(8,128)(2,1)S(1)} copy-done((bf16[384,1152]{1,0:T(8,128)(2,1)S(1)}, bf16[384,1152]{1,0:T(8,128)(2,1)}, u32[]{:S(2)}) %copy-start.2) | copy-done | bytes 884760
  49.7 0.6 %convolution_add_fusion = f32[512,768]{1,0:T(8,128)S(1)} fusion(bf16[512,384]{1,0:T(8,128)(2,1)S(1)} %bitcast.45, f32[768]{0:T(1024)S(1)} %slice.73, bf16[384,1152]{1,0:T(8,128)(2,1)S(1)} %copy-done.2), kind=kOutput, calls=%fused_computation.7 | convolution fusion | flops 302383104 | bytes 2560000 | tf_op jit(solution)/shard_map/dot_general | solution.py:344
  50.3 0.0 copy-start.7
  50.3 0.0 slice-done.2
  50.3 0.2 convolution_add_fusion.2
  50.5 0.9 %convolution_multiply_fusion = f32[4,32,128]{2,1,0:T(8,128)S(1)} fusion(f32[4,32,384]{2,1,0:T(8,128)S(1)} %bitcast.46, f32[4,128,768]{2,1,0:T(8,128)S(1)} %bitcast.42), kind=kOutput, calls=%fused_computation.17 | convolution fusion | flops 75513856 | bytes 1048576 | tf_op jit(solution)/shard_map/nqc,nkc->nqk/dot_general | solution.py:358
  51.5 0.2 fusion.51
  51.7 0.3 convolution_convert_fusion
  52.0 0.0 copy-done
  52.0 0.0 copy-done.7
  52.0 0.2 fusion.4
  52.2 0.1 fusion.46
  52.3 0.7 %copy.30 = bf16[2,2,1,32,384]{4,3,2,1,0:T(8,128)(2,1)} copy(bf16[2,2,1,32,384]{4,3,2,0,1:T(8,128)(2,1)S(1)} %fusion.46) | data formatting | bytes 196608 | tf_op jit(solution)/shard_map/convert_element_type | solution.py:377
  (13 shorter events, 0.2 us)
Async XLA Ops:
  0.0 52.0 %copy-start = (bf16[384,384]{1,0:T(8,128)(2,1)S(1)}, bf16[384,384]{1,0:T(8,128)(2,1)}, u32[]{:S(2)}) copy-start(bf16[384,384]{1,0:T(8,128)(2,1)} %param.20) | copy-start | bytes 884740
  0.0 24.4 %copy-start.8 = (s32[2,1]{0,1:T(1,128)S(1)}, s32[2,1]{0,1:T(1,128)}, u32[]{:S(2)}) copy-start(s32[2,1]{0,1:T(1,128)} %param.13) | copy-start | bytes 28
  0.0 30.8 %copy-start.3 = (f32[384]{0:T(512)S(1)}, f32[384]{0:T(512)}, u32[]{:S(2)}) copy-start(f32[384]{0:T(512)} %param.14) | copy-start | bytes 4612
  23.1 17.6 %collective-permute-start = (bf16[2,2,4,32,384]{4,3,2,0,1:T(8,128)(2,1)}, bf16[2,2,4,32,384]{4,3,2,0,1:T(8,128)(2,1)S(1)}, u32[]{:S(2)}, u32[]{:S(2)}) collective-permute-start(bf16[2,2,4,32,384]{4,3,2,0,1:T(8,128)(2,1)} %slice.77), channel_id=1, source_target_pairs={{0,4},{4,8},{8,12},{1,5},{5,9},{9,13},{2,6},{6,10},{10,14},{3,7},{... | collective-permute-start | bytes 1179656 | tf_op jit(solution)/shard_map/ppermute | solution.py:317
  25.2 15.4 %collective-permute-start.1 = (bf16[2,4,32,384]{3,2,1,0:T(8,128)(2,1)}, bf16[2,4,32,384]{3,2,1,0:T(8,128)(2,1)S(1)}, u32[]{:S(2)}, u32[]{:S(2)}) collective-permute-start(bf16[2,4,32,384]{3,2,1,0:T(8,128)(2,1)} %fusion.44), channel_id=1, source_target_pairs={{0,8},{4,12},{1,9},{5,13},{2,10},{6,14},{3,11},{7,15},{16,24},{20,... | collective-permute-start | bytes 589832 | tf_op jit(solution)/shard_map/ppermute | solution.py:318
  29.2 11.4 %collective-permute-start.2 = (s32[2]{0:T(128)S(1)}, s32[2]{0:T(128)S(1)}, u32[]{:S(2)}, u32[]{:S(2)}) collective-permute-start(s32[2]{0:T(128)S(1)} %bitcast.50), channel_id=1, source_target_pairs={{0,4},{4,8},{8,12},{1,5},{5,9},{9,13},{2,6},{6,10},{10,14},{3,7},{... | collective-permute-start | bytes 32 | tf_op jit(solution)/shard_map/ppermute | solution.py:310
  31.5 0.7 %copy-start.4 = (f32[1152]{0:T(1024)S(1)}, f32[1152]{0:T(1024)}, u32[]{:S(2)}) copy-start(f32[1152]{0:T(1024)} %param.19) | copy-start | bytes 13828
  32.3 3.3 %copy-start.1 = (bf16[3,3,3,384,384]{4,3,2,1,0:T(8,128)(2,1)S(1)}, bf16[3,3,3,384,384]{4,3,2,1,0:T(8,128)(2,1)}, u32[]{:S(2)}) copy-start(bf16[3,3,3,384,384]{4,3,2,1,0:T(8,128)(2,1)} %w_hbm.3) | copy-start | bytes 23887876
  35.6 6.8 %slice-start = ((s8[7962624]{0:T(1024)(128)(4,1)}), s8[4194304]{0:T(1024)(128)(4,1)S(1)}, s32[]{:S(2)}) async-start(s8[7962624]{0:T(1024)(128)(4,1)} %bitcast.40), calls=%async_computation | async-start | bytes 8388608
  40.6 2.1 %slice-start.1 = ((s8[7962624]{0:T(1024)(128)(4,1)}), s8[3768320]{0:T(1024)(128)(4,1)S(1)}, s32[]{:S(2)}) async-start(s8[7962624]{0:T(1024)(128)(4,1)} %bitcast.40), calls=%async_computation.1 | async-start | bytes 7536640
  47.9 0.7 %copy-start.5 = (f32[384]{0:T(512)S(1)}, f32[384]{0:T(512)}, u32[]{:S(2)}) copy-start(f32[384]{0:T(512)} %param.16) | copy-start | bytes 4612
  48.0 0.8 %copy-start.6 = (f32[384]{0:T(512)S(1)}, f32[384]{0:T(512)}, u32[]{:S(2)}) copy-start(f32[384]{0:T(512)} %param.17) | copy-start | bytes 4612
  48.6 1.2 %copy-start.2 = (bf16[384,1152]{1,0:T(8,128)(2,1)S(1)}, bf16[384,1152]{1,0:T(8,128)(2,1)}, u32[]{:S(2)}) copy-start(bf16[384,1152]{1,0:T(8,128)(2,1)} %param.18) | copy-start | bytes 2654212
  49.0 1.3 %slice-start.2 = ((f32[1152]{0:T(1024)}), f32[384]{0:T(512)S(1)}, s32[]{:S(2)}) async-start(f32[1152]{0:T(1024)} %param.19), calls=%async_computation.2 | async-start | bytes 4096 | tf_op jit(solution)/shard_map/slice | solution.py:356
  50.3 1.7 %copy-start.7 = (f32[384]{0:T(512)S(1)}, f32[384]{0:T(512)}, u32[]{:S(2)}) copy-start(f32[384]{0:T(512)} %param.21) | copy-start | bytes 4612

commit v11 on v6

--- a/solution.py
+++ b/solution.py
@@ -309,6 +309,7 @@
     ahead = [(i, i + 1) for i in range(sections - 1)]
     prev_counts = lax.ppermute(counts, "tm", ahead)
     both = jnp.concatenate([inner_input, segment_input], axis=0)
+    prev_counts, both = lax.optimization_barrier((prev_counts, both))
     both_all = lax.all_gather(both, "rows", axis=2, tiled=True)
     inner_all = both_all[:clip_count]
     segment_all = both_all[clip_count:]

time: 49.8 us -> 51.6 us (1.036)
  the two profiles are of different devices: /device:TPU:0 before, /device:TPU:1 now
where the time goes in v11:
time: 51.6 us; the launch traced here: 51.3 us
  blocking collectives  17.9 us (35%)
  Pallas kernels  10.3 us (20%)
  starting transfers between devices  9.85 us (19%)
  other arithmetic  5.06 us (10%)
  local copies, waits for them, and re-layouts  3.59 us (7%)
  matrix products  2.24 us (4%)
  waiting for transfers between devices  2.01 us (4%)
    all_gather x1, blocking collectives, gathered_body(): both_all = lax.all_gather(both, 'rows', axis=2, tiled=True)  17.9 us
    pallas_call x2, Pallas kernels, conv_part(): pl.pallas_call(functools.partial(conv_part_kernel, plan, first_tap), in_s...  10.3 us
    ppermute x1, starting transfers between devices, gathered_body(): prev_counts = lax.ppermute(counts, 'tm', ahead)  4.63 us
    ppermute x1, starting transfers between devices, gathered_body(): prev_raw = lax.ppermute(inner_all, 'tm', ahead)  3.92 us
    ppermute x1, waiting for transfers between devices, gathered_body(): lax.ppermute(last_raw, 'tm', [(i, i + 2) for i in range(sections - 2)])  2.01 us
    ppermute x1, starting transfers between devices, gathered_body(): lax.ppermute(last_raw, 'tm', [(i, i + 2) for i in range(sections - 2)])  1.3 us
    unnamed x12, local copies, waits for them, and re-layouts  1.18 us
  transfers between devices with their start and end apart: 3, of which 1 were waited for; matrix products, arithmetic and copies ran while one was open for 7% of the time, Pallas kernels for 10%

profile of v11, /device:TPU:1, one launch (start us, length us, event | category | flops | bytes accessed | tf_op | source)
XLA Modules:
  0.0 51.3 jit_solution(1626307561088654257)
XLA Ops:
  0.0 0.0 copy-start
  0.0 0.0 copy-start.2
  0.0 4.6 %collective-permute-start = (s32[2]{0:T(128)}, s32[2]{0:T(128)S(1)}, u32[]{:S(2)}, u32[]{:S(2)}) collective-permute-start(s32[2]{0:T(128)} %bitcast.48), channel_id=1, source_target_pairs={{0,4},{4,8},{8,12},{1,5},{5,9},{9,13},{2,6},{6,10},{10,14},{3,7},{... | collective-permute-start | bytes 32 | tf_op jit(solution)/shard_map/ppermute | solution.py:310
  4.6 0.7 %broadcast_compare_fusion.1 = pred[2]{0:T(512)(128)(4,1)S(1)} fusion(s32[2,1]{0,1:T(1,128)} %param.13), kind=kLoop, calls=%fused_computation.87 | loop fusion | flops 2 | bytes 10 | tf_op jit(solution)/shard_map/gt | solution.py:316
  5.3 0.7 %slice.73 = f32[768]{0:T(1024)S(1)} slice(f32[1152]{0:T(1024)} %param.19), slice={[384:1152]} | slice | bytes 6144 | tf_op jit(solution)/shard_map/slice | solution.py:346
  6.0 0.7 %compare_convert_fusion = f32[2,2]{0,1:T(2,128)S(1)} fusion(s32[2]{0:T(128)} %bitcast.49), kind=kLoop, calls=%fused_computation.83 | loop fusion | flops 8 | bytes 24 | tf_op jit(solution)/shard_map/convert_element_type | solution.py:374
  6.7 1.0 %pad_maximum_fusion.2 = bf16[4,2,1,32,384]{4,3,2,1,0:T(8,128)(2,1)S(1)} fusion(bf16[2,2,1,32,384]{4,3,2,1,0:T(8,128)(2,1)} %param.11, bf16[2,2,1,32,384]{4,3,2,1,0:T(8,128)(2,1)} %param.12), kind=kLoop, calls=%fused_computation.72 | loop fusion | flops 98304 | bytes 393216 | tf_op jit(solution)/shard_map/concatenate | solution.py:311
  7.7 0.0 collective-permute-done
  7.7 17.9 %all_gather.3 = bf16[4,2,4,32,384]{4,3,2,0,1:T(8,128)(2,1)S(1)} all-gather(bf16[4,2,1,32,384]{4,3,2,0,1:T(8,128)(2,1)S(1)} %copy.31), channel_id=1, replica_groups=mesh['clips'=2,'tm'=4,'rows'=4] {'rows'}, dimensions={2}, use_global_device_ids=true | all-gather | bytes 983040 | tf_op jit(solution)/shard_map/all_gather | solution.py:313
  25.6 0.2 fusion.9
  25.8 0.0 copy-done.2
  25.8 0.3 fusion.16
  26.1 0.3 pad_slice_fusion.2
  26.5 3.9 %collective-permute-start.1 = (bf16[2,2,4,32,384]{4,3,2,0,1:T(8,128)(2,1)S(1)}, bf16[2,2,4,32,384]{4,3,2,0,1:T(8,128)(2,1)S(1)}, u32[]{:S(2)}, u32[]{:S(2)}) collective-permute-start(bf16[2,2,4,32,384]{4,3,2,0,1:T(8,128)(2,1)S(1)} %slice.77), channel_id=1, source_target_pairs={{0,4},{4,8},{8,12},{1,5},{5,9},{9,13},{2,6},{6,10},{10,14},{3,7},{... | collective-permute-start | bytes 1179656 | tf_op jit(solution)/shard_map/ppermute | solution.py:318
  30.4 0.1 fusion.44
  30.5 1.3 %collective-permute-start.2 = (bf16[2,4,32,384]{3,2,1,0:T(8,128)(2,1)S(1)}, bf16[2,4,32,384]{3,2,1,0:T(8,128)(2,1)S(1)}, u32[]{:S(2)}, u32[]{:S(2)}) collective-permute-start(bf16[2,4,32,384]{3,2,1,0:T(8,128)(2,1)S(1)} %fusion.44), channel_id=1, source_target_pairs={{0,8},{4,12},{1,9},{5,13},{2,10},{6,14},{3,11},{7,15},{16,24},{20,... | collective-permute-start | bytes 589832 | tf_op jit(solution)/shard_map/ppermute | solution.py:319
  31.8 0.2 pad_maximum_fusion
  32.0 0.2 copy.22.x_ref
  32.2 5.1 %shard_map.109 = f32[2,2,128,384]{3,2,1,0:T(8,128)S(1)} custom-call(bf16[2,2,6,32,1152]{4,3,2,1,0:T(8,128)(2,1)S(1)} %copy.22.x_ref, bf16[3,3,3,384,384]{4,3,2,1,0:T(8,128)(2,1)} %w_hbm.3), custom_call_target="tpu_custom_call" | custom-call | flops 2038431744 | bytes 7864320 | tf_op jit(solution)/shard_map/pallas_call | solution.py:229
  37.3 2.0 %collective-permute-done.2 = bf16[2,4,32,384]{3,2,1,0:T(8,128)(2,1)S(1)} collective-permute-done((bf16[2,4,32,384]{3,2,1,0:T(8,128)(2,1)S(1)}, bf16[2,4,32,384]{3,2,1,0:T(8,128)(2,1)S(1)}, u32[]{:S(2)}, u32[]{:S(2)}) %collective-permute-start.2) | collective-permute-done | bytes 196640 | tf_op jit(solution)/shard_map/ppermute | solution.py:319
  39.3 0.0 collective-permute-done.1
  39.3 0.2 fusion.17
  39.5 0.3 fusion.24
  39.8 0.1 fusion.33
  40.0 0.1 fusion.43
  40.0 0.2 fusion.47
  40.3 0.2 fusion.30
  40.5 0.4 fusion.50
  40.8 0.2 pad_maximum_fusion.1.x_ref
  41.0 5.2 %shard_map.110 = f32[2,2,128,384]{3,2,1,0:T(8,128)S(1)} custom-call(bf16[2,2,6,32,1152]{4,3,2,1,0:T(8,128)(2,1)S(1)} %pad_maximum_fusion.1.x_ref, bf16[3,3,3,384,384]{4,3,2,1,0:T(8,128)(2,1)} %w_hbm.3), custom_call_target="tpu_custom_call" | custom-call | flops 2038431744 | bytes 7864320 | tf_op jit(solution)/shard_map/pallas_call | solution.py:229
  46.2 0.0 copy-start.3
  46.2 0.1 add.102
  46.3 0.0 copy-start.4
  46.3 0.1 copy.26
  46.4 0.5 copy-done.3
  46.9 0.0 copy-start.1
  46.9 0.2 fusion.25
  47.2 0.0 copy-done.4
  47.2 0.2 fusion.27
  47.3 0.0 slice-start
  47.5 0.6 %copy-done.1 = bf16[384,1152]{1,0:T(8,128)(2,1)S(1)} copy-done((bf16[384,1152]{1,0:T(8,128)(2,1)S(1)}, bf16[384,1152]{1,0:T(8,128)(2,1)}, u32[]{:S(2)}) %copy-start.1) | copy-done | bytes 884760
  48.1 0.6 %convolution_add_fusion = f32[512,768]{1,0:T(8,128)S(1)} fusion(bf16[512,384]{1,0:T(8,128)(2,1)S(1)} %bitcast.43, f32[768]{0:T(1024)S(1)} %slice.73, bf16[384,1152]{1,0:T(8,128)(2,1)S(1)} %copy-done.1), kind=kOutput, calls=%fused_computation.7 | convolution fusion | flops 302383104 | bytes 2560000 | tf_op jit(solution)/shard_map/dot_general | solution.py:345
  48.7 0.0 copy-start.5
  48.7 0.0 slice-done
  48.7 0.2 convolution_add_fusion.2
  48.9 0.9 %convolution_multiply_fusion = f32[4,32,128]{2,1,0:T(8,128)S(1)} fusion(f32[4,32,384]{2,1,0:T(8,128)S(1)} %bitcast.44, f32[4,128,768]{2,1,0:T(8,128)S(1)} %bitcast.40), kind=kOutput, calls=%fused_computation.17 | convolution fusion | flops 75513856 | bytes 1048576 | tf_op jit(solution)/shard_map/nqc,nkc->nqk/dot_general | solution.py:359
  49.9 0.2 fusion.51
  50.0 0.3 convolution_convert_fusion
  50.3 0.0 copy-done
  50.4 0.0 copy-done.5
  50.4 0.2 fusion.4
  50.6 0.1 fusion.46
  50.7 0.7 %copy.30 = bf16[2,2,1,32,384]{4,3,2,1,0:T(8,128)(2,1)} copy(bf16[2,2,1,32,384]{4,3,2,0,1:T(8,128)(2,1)S(1)} %fusion.46) | data formatting | bytes 196608 | tf_op jit(solution)/shard_map/convert_element_type | solution.py:378
  (10 shorter events, 0.2 us)
Async XLA Ops:
  0.0 50.4 %copy-start = (bf16[384,384]{1,0:T(8,128)(2,1)S(1)}, bf16[384,384]{1,0:T(8,128)(2,1)}, u32[]{:S(2)}) copy-start(bf16[384,384]{1,0:T(8,128)(2,1)} %param.20) | copy-start | bytes 884740
  0.0 25.8 %copy-start.2 = (f32[384]{0:T(512)S(1)}, f32[384]{0:T(512)}, u32[]{:S(2)}) copy-start(f32[384]{0:T(512)} %param.14) | copy-start | bytes 4612
  0.0 7.7 %collective-permute-start = (s32[2]{0:T(128)}, s32[2]{0:T(128)S(1)}, u32[]{:S(2)}, u32[]{:S(2)}) collective-permute-start(s32[2]{0:T(128)} %bitcast.48), channel_id=1, source_target_pairs={{0,4},{4,8},{8,12},{1,5},{5,9},{9,13},{2,6},{6,10},{10,14},{3,7},{... | collective-permute-start | bytes 32 | tf_op jit(solution)/shard_map/ppermute | solution.py:310
  26.5 12.8 %collective-permute-start.1 = (bf16[2,2,4,32,384]{4,3,2,0,1:T(8,128)(2,1)S(1)}, bf16[2,2,4,32,384]{4,3,2,0,1:T(8,128)(2,1)S(1)}, u32[]{:S(2)}, u32[]{:S(2)}) collective-permute-start(bf16[2,2,4,32,384]{4,3,2,0,1:T(8,128)(2,1)S(1)} %slice.77), channel_id=1, source_target_pairs={{0,4},{4,8},{8,12},{1,5},{5,9},{9,13},{2,6},{6,10},{10,14},{3,7},{... | collective-permute-start | bytes 1179656 | tf_op jit(solution)/shard_map/ppermute | solution.py:318
  30.5 8.8 %collective-permute-start.2 = (bf16[2,4,32,384]{3,2,1,0:T(8,128)(2,1)S(1)}, bf16[2,4,32,384]{3,2,1,0:T(8,128)(2,1)S(1)}, u32[]{:S(2)}, u32[]{:S(2)}) collective-permute-start(bf16[2,4,32,384]{3,2,1,0:T(8,128)(2,1)S(1)} %fusion.44), channel_id=1, source_target_pairs={{0,8},{4,12},{1,9},{5,13},{2,10},{6,14},{3,11},{7,15},{16,24},{20,... | collective-permute-start | bytes 589832 | tf_op jit(solution)/shard_map/ppermute | solution.py:319
  46.2 0.7 %copy-start.3 = (f32[384]{0:T(512)S(1)}, f32[384]{0:T(512)}, u32[]{:S(2)}) copy-start(f32[384]{0:T(512)} %param.16) | copy-start | bytes 4612
  46.3 0.8 %copy-start.4 = (f32[384]{0:T(512)S(1)}, f32[384]{0:T(512)}, u32[]{:S(2)}) copy-start(f32[384]{0:T(512)} %param.17) | copy-start | bytes 4612
  46.9 1.2 %copy-start.1 = (bf16[384,1152]{1,0:T(8,128)(2,1)S(1)}, bf16[384,1152]{1,0:T(8,128)(2,1)}, u32[]{:S(2)}) copy-start(bf16[384,1152]{1,0:T(8,128)(2,1)} %param.18) | copy-start | bytes 2654212
  47.3 1.3 %slice-start = ((f32[1152]{0:T(1024)}), f32[384]{0:T(512)S(1)}, s32[]{:S(2)}) async-start(f32[1152]{0:T(1024)} %param.19), calls=%async_computation | async-start | bytes 4096 | tf_op jit(solution)/shard_map/slice | solution.py:357
  48.7 1.7 %copy-start.5 = (f32[384]{0:T(512)S(1)}, f32[384]{0:T(512)}, u32[]{:S(2)}) copy-start(f32[384]{0:T(512)} %param.21) | copy-start | bytes 4612

commit v12 on v6

--- a/solution.py
+++ b/solution.py
@@ -315,9 +315,10 @@
     wide = (counts > 1)[:, None, None, None]
     last_raw = jnp.where(wide, inner_all[:, frame_count - 1], inner_all[:, 0])
     prev_raw = lax.ppermute(inner_all, "tm", ahead)
-    before_raw = lax.ppermute(last_raw, "tm", [(i, i + 2) for i in range(sections - 2)])
     own = activate(inner_all, inner_gain)
     own_sum = own_conv(own, causal_weight)
+    own_sum, last_raw = lax.optimization_barrier((own_sum, last_raw))
+    before_raw = lax.ppermute(last_raw, "tm", [(i, i + 2) for i in range(sections - 2)])
     own_sum, prev_raw, before_raw, prev_counts = lax.optimization_barrier(
         (own_sum, prev_raw, before_raw, prev_counts)
     )

time: 49.8 us -> 51 us (1.024)
  waiting for transfers between devices: 0.01 us -> 2.63 us
  local copies, waits for them, and re-layouts: 4.11 us -> 3.38 us
  other arithmetic: 4.45 us -> 3.8 us
    ppermute x1, waiting for transfers between devices: 0.01 us -> 1.87 us  [gathered_body(): lax.ppermute(last_raw, 'tm', [(i, i + 2) for i in range(sections - 2)])]
    ppermute x1, waiting for transfers between devices: 0.01 us -> 0.76 us  [gathered_body(): prev_counts = lax.ppermute(counts, 'tm', ahead)]
    slice x1, local copies, waits for them, and re-layouts: 0.78 us -> 0.04 us  [gathered_body(): inner_all = both_all[:clip_count]]
    select_n x1, other arithmetic: 0.76 us -> 0.1 us  [gathered_body(): last_raw = jnp.where(wide, inner_all[:, frame_count - 1], inner_all[:, 0])]
  transfers between devices with their start and end apart: 3 -> 3, of which waited for: 0 -> 2; matrix products, arithmetic and copies ran while one was open for 4% -> 2% of each run, Pallas kernels for 10% -> 10%
where the time goes in v12:
time: 51 us; the launch traced here: 50.8 us
  blocking collectives  21.3 us (42%)
  Pallas kernels  10.3 us (20%)
  starting transfers between devices  6.72 us (13%)
  other arithmetic  3.8 us (7%)
  local copies, waits for them, and re-layouts  3.38 us (7%)
  waiting for transfers between devices  2.63 us (5%)
  matrix products  2.24 us (4%)
    all_gather x1, blocking collectives, gathered_body(): both_all = lax.all_gather(both, 'rows', axis=2, tiled=True)  21.3 us
    pallas_call x2, Pallas kernels, conv_part(): pl.pallas_call(functools.partial(conv_part_kernel, plan, first_tap), in_s...  10.3 us
    ppermute x1, starting transfers between devices, gathered_body(): lax.ppermute(last_raw, 'tm', [(i, i + 2) for i in range(sections - 2)])  4.01 us
    ppermute x1, waiting for transfers between devices, gathered_body(): lax.ppermute(last_raw, 'tm', [(i, i + 2) for i in range(sections - 2)])  1.87 us
    unnamed x16, local copies, waits for them, and re-layouts  1.65 us
    ppermute x1, starting transfers between devices, gathered_body(): prev_counts = lax.ppermute(counts, 'tm', ahead)  1.39 us
    ppermute x1, starting transfers between devices, gathered_body(): prev_raw = lax.ppermute(inner_all, 'tm', ahead)  1.31 us
    concatenate x1, other arithmetic, gathered_body(): both = jnp.concatenate([inner_input, segment_input], axis=0)  1.02 us
  transfers between devices with their start and end apart: 3, of which 2 were waited for; matrix products, arithmetic and copies ran while one was open for 2% of the time, Pallas kernels for 10%

profile of v12, /device:TPU:0, one launch (start us, length us, event | category | flops | bytes accessed | tf_op | source)
XLA Modules:
  0.0 50.8 jit_solution(1061017866759799917)
XLA Ops:
  0.0 0.0 copy-start
  0.0 0.0 copy-start.2
  0.0 1.0 %pad_maximum_fusion.2 = bf16[4,2,1,32,384]{4,3,2,1,0:T(8,128)(2,1)S(1)} fusion(bf16[2,2,1,32,384]{4,3,2,1,0:T(8,128)(2,1)} %param.11, bf16[2,2,1,32,384]{4,3,2,1,0:T(8,128)(2,1)} %param.12), kind=kLoop, calls=%fused_computation.72 | loop fusion | flops 98304 | bytes 393216 | tf_op jit(solution)/shard_map/concatenate | solution.py:311
  1.1 21.3 %all_gather.3 = bf16[4,2,4,32,384]{4,3,2,0,1:T(8,128)(2,1)S(1)} all-gather(bf16[4,2,1,32,384]{4,3,2,0,1:T(8,128)(2,1)S(1)} %copy.31), channel_id=1, replica_groups=mesh['clips'=2,'tm'=4,'rows'=4] {'rows'}, dimensions={2}, use_global_device_ids=true | all-gather | bytes 983040 | tf_op jit(solution)/shard_map/all_gather | solution.py:312
  22.4 1.3 %collective-permute-start = (bf16[2,2,4,32,384]{4,3,2,0,1:T(8,128)(2,1)S(1)}, bf16[2,2,4,32,384]{4,3,2,0,1:T(8,128)(2,1)S(1)}, u32[]{:S(2)}, u32[]{:S(2)}) collective-permute-start(bf16[2,2,4,32,384]{4,3,2,0,1:T(8,128)(2,1)S(1)} %slice.77), channel_id=1, source_target_pairs={{0,4},{4,8},{8,12},{1,5},{5,9},{9,13},{2,6},{6,10},{10,14},{3,7},{... | collective-permute-start | bytes 1179656 | tf_op jit(solution)/shard_map/ppermute | solution.py:317
  23.7 0.2 fusion.9
  23.9 0.0 copy-done.2
  23.9 0.3 fusion.16
  24.2 0.3 pad_slice_fusion.2
  24.5 0.2 pad_maximum_fusion
  24.7 0.0 copy-start.7
  24.7 0.2 copy.22.x_ref
  24.9 0.5 copy-done.7
  25.4 0.1 fusion.44
  25.5 0.0 copy-start.3
  25.5 5.1 %shard_map.109 = f32[2,2,128,384]{3,2,1,0:T(8,128)S(1)} custom-call(bf16[2,2,6,32,1152]{4,3,2,1,0:T(8,128)(2,1)S(1)} %copy.22.x_ref, bf16[3,3,3,384,384]{4,3,2,1,0:T(8,128)(2,1)} %w_hbm.3), custom_call_target="tpu_custom_call" | custom-call | flops 2038431744 | bytes 7864320 | tf_op jit(solution)/shard_map/pallas_call | solution.py:229
  30.6 4.0 %collective-permute-start.1 = (bf16[2,4,32,384]{3,2,1,0:T(8,128)(2,1)S(1)}, bf16[2,4,32,384]{3,2,1,0:T(8,128)(2,1)S(1)}, u32[]{:S(2)}, u32[]{:S(2)}) collective-permute-start(bf16[2,4,32,384]{3,2,1,0:T(8,128)(2,1)S(1)} %fusion.44), channel_id=1, source_target_pairs={{0,8},{4,12},{1,9},{5,13},{2,10},{6,14},{3,11},{7,15},{16,24},{20,... | collective-permute-start | bytes 589832 | tf_op jit(solution)/shard_map/ppermute | solution.py:321
  34.7 1.4 %collective-permute-start.2 = (s32[2]{0:T(128)S(1)}, s32[2]{0:T(128)S(1)}, u32[]{:S(2)}, u32[]{:S(2)}) collective-permute-start(s32[2]{0:T(128)S(1)} %bitcast.48), channel_id=1, source_target_pairs={{0,4},{4,8},{8,12},{1,5},{5,9},{9,13},{2,6},{6,10},{10,14},{3,7},{... | collective-permute-start | bytes 32 | tf_op jit(solution)/shard_map/ppermute | solution.py:310
  36.1 0.0 copy-done.3
  36.1 0.8 %collective-permute-done.2 = s32[2]{0:T(128)S(1)} collective-permute-done((s32[2]{0:T(128)S(1)}, s32[2]{0:T(128)S(1)}, u32[]{:S(2)}, u32[]{:S(2)}) %collective-permute-start.2) | collective-permute-done | bytes 40 | tf_op jit(solution)/shard_map/ppermute | solution.py:310
  36.9 1.9 %collective-permute-done.1 = bf16[2,4,32,384]{3,2,1,0:T(8,128)(2,1)S(1)} collective-permute-done((bf16[2,4,32,384]{3,2,1,0:T(8,128)(2,1)S(1)}, bf16[2,4,32,384]{3,2,1,0:T(8,128)(2,1)S(1)}, u32[]{:S(2)}, u32[]{:S(2)}) %collective-permute-start.1) | collective-permute-done | bytes 196640 | tf_op jit(solution)/shard_map/ppermute | solution.py:321
  38.7 0.0 collective-permute-done
  38.7 0.2 fusion.17
  38.9 0.3 fusion.24
  39.2 0.1 fusion.33
  39.4 0.1 fusion.43
  39.5 0.2 fusion.47
  39.7 0.2 fusion.30
  39.9 0.4 fusion.50
  40.3 0.2 pad_maximum_fusion.1.x_ref
  40.4 5.2 %shard_map.110 = f32[2,2,128,384]{3,2,1,0:T(8,128)S(1)} custom-call(bf16[2,2,6,32,1152]{4,3,2,1,0:T(8,128)(2,1)S(1)} %pad_maximum_fusion.1.x_ref, bf16[3,3,3,384,384]{4,3,2,1,0:T(8,128)(2,1)} %w_hbm.3), custom_call_target="tpu_custom_call" | custom-call | flops 2038431744 | bytes 7864320 | tf_op jit(solution)/shard_map/pallas_call | solution.py:229
  45.7 0.0 copy-start.4
  45.7 0.1 add.102
  45.8 0.0 copy-start.5
  45.8 0.1 copy.26
  45.8 0.5 %copy-done.4 = f32[384]{0:T(512)S(1)} copy-done((f32[384]{0:T(512)S(1)}, f32[384]{0:T(512)}, u32[]{:S(2)}) %copy-start.4) | copy-done | bytes 1560
  46.3 0.0 copy-start.1
  46.3 0.2 fusion.25
  46.6 0.0 copy-done.5
  46.6 0.2 fusion.27
  46.8 0.0 slice-start
  46.9 0.6 %copy-done.1 = bf16[384,1152]{1,0:T(8,128)(2,1)S(1)} copy-done((bf16[384,1152]{1,0:T(8,128)(2,1)S(1)}, bf16[384,1152]{1,0:T(8,128)(2,1)}, u32[]{:S(2)}) %copy-start.1) | copy-done | bytes 884760
  47.5 0.6 %convolution_add_fusion = f32[512,768]{1,0:T(8,128)S(1)} fusion(bf16[512,384]{1,0:T(8,128)(2,1)S(1)} %bitcast.43, f32[768]{0:T(1024)S(1)} %slice.73, bf16[384,1152]{1,0:T(8,128)(2,1)S(1)} %copy-done.1), kind=kOutput, calls=%fused_computation.7 | convolution fusion | flops 302383104 | bytes 2560000 | tf_op jit(solution)/shard_map/dot_general | solution.py:345
  48.1 0.0 copy-start.6
  48.1 0.0 slice-done
  48.1 0.2 convolution_add_fusion.2
  48.3 1.0 %convolution_multiply_fusion = f32[4,32,128]{2,1,0:T(8,128)S(1)} fusion(f32[4,32,384]{2,1,0:T(8,128)S(1)} %bitcast.44, f32[4,128,768]{2,1,0:T(8,128)S(1)} %bitcast.40), kind=kOutput, calls=%fused_computation.17 | convolution fusion | flops 75513856 | bytes 1048576 | tf_op jit(solution)/shard_map/nqc,nkc->nqk/dot_general | solution.py:359
  49.3 0.2 fusion.51
  49.5 0.3 convolution_convert_fusion
  49.8 0.0 copy-done
  49.8 0.0 copy-done.6
  49.8 0.2 fusion.4
  50.0 0.1 fusion.46
  50.1 0.7 %copy.30 = bf16[2,2,1,32,384]{4,3,2,1,0:T(8,128)(2,1)} copy(bf16[2,2,1,32,384]{4,3,2,0,1:T(8,128)(2,1)S(1)} %fusion.46) | data formatting | bytes 196608 | tf_op jit(solution)/shard_map/convert_element_type | solution.py:378
  (13 shorter events, 0.2 us)
Async XLA Ops:
  0.0 49.8 %copy-start = (bf16[384,384]{1,0:T(8,128)(2,1)S(1)}, bf16[384,384]{1,0:T(8,128)(2,1)}, u32[]{:S(2)}) copy-start(bf16[384,384]{1,0:T(8,128)(2,1)} %param.20) | copy-start | bytes 884740
  0.0 23.9 %copy-start.2 = (f32[384]{0:T(512)S(1)}, f32[384]{0:T(512)}, u32[]{:S(2)}) copy-start(f32[384]{0:T(512)} %param.14) | copy-start | bytes 4612
  22.4 16.3 %collective-permute-start = (bf16[2,2,4,32,384]{4,3,2,0,1:T(8,128)(2,1)S(1)}, bf16[2,2,4,32,384]{4,3,2,0,1:T(8,128)(2,1)S(1)}, u32[]{:S(2)}, u32[]{:S(2)}) collective-permute-start(bf16[2,2,4,32,384]{4,3,2,0,1:T(8,128)(2,1)S(1)} %slice.77), channel_id=1, source_target_pairs={{0,4},{4,8},{8,12},{1,5},{5,9},{9,13},{2,6},{6,10},{10,14},{3,7},{... | collective-permute-start | bytes 1179656 | tf_op jit(solution)/shard_map/ppermute | solution.py:317
  24.7 0.7 %copy-start.7 = (s32[2,1]{0,1:T(1,128)S(1)}, s32[2,1]{0,1:T(1,128)}, u32[]{:S(2)}) copy-start(s32[2,1]{0,1:T(1,128)} %param.13) | copy-start | bytes 28
  25.5 10.6 %copy-start.3 = (f32[1152]{0:T(1024)S(1)}, f32[1152]{0:T(1024)}, u32[]{:S(2)}) copy-start(f32[1152]{0:T(1024)} %param.19) | copy-start | bytes 13828
  30.6 8.1 %collective-permute-start.1 = (bf16[2,4,32,384]{3,2,1,0:T(8,128)(2,1)S(1)}, bf16[2,4,32,384]{3,2,1,0:T(8,128)(2,1)S(1)}, u32[]{:S(2)}, u32[]{:S(2)}) collective-permute-start(bf16[2,4,32,384]{3,2,1,0:T(8,128)(2,1)S(1)} %fusion.44), channel_id=1, source_target_pairs={{0,8},{4,12},{1,9},{5,13},{2,10},{6,14},{3,11},{7,15},{16,24},{20,... | collective-permute-start | bytes 589832 | tf_op jit(solution)/shard_map/ppermute | solution.py:321
  34.7 2.2 %collective-permute-start.2 = (s32[2]{0:T(128)S(1)}, s32[2]{0:T(128)S(1)}, u32[]{:S(2)}, u32[]{:S(2)}) collective-permute-start(s32[2]{0:T(128)S(1)} %bitcast.48), channel_id=1, source_target_pairs={{0,4},{4,8},{8,12},{1,5},{5,9},{9,13},{2,6},{6,10},{10,14},{3,7},{... | collective-permute-start | bytes 32 | tf_op jit(solution)/shard_map/ppermute | solution.py:310
  45.7 0.7 %copy-start.4 = (f32[384]{0:T(512)S(1)}, f32[384]{0:T(512)}, u32[]{:S(2)}) copy-start(f32[384]{0:T(512)} %param.16) | copy-start | bytes 4612
  45.8 0.8 %copy-start.5 = (f32[384]{0:T(512)S(1)}, f32[384]{0:T(512)}, u32[]{:S(2)}) copy-start(f32[384]{0:T(512)} %param.17) | copy-start | bytes 4612
  46.3 1.2 %copy-start.1 = (bf16[384,1152]{1,0:T(8,128)(2,1)S(1)}, bf16[384,1152]{1,0:T(8,128)(2,1)}, u32[]{:S(2)}) copy-start(bf16[384,1152]{1,0:T(8,128)(2,1)} %param.18) | copy-start | bytes 2654212
  46.8 1.3 %slice-start = ((f32[1152]{0:T(1024)}), f32[384]{0:T(512)S(1)}, s32[]{:S(2)}) async-start(f32[1152]{0:T(1024)} %param.19), calls=%async_computation | async-start | bytes 4096 | tf_op jit(solution)/shard_map/slice | solution.py:357
  48.1 1.7 %copy-start.6 = (f32[384]{0:T(512)S(1)}, f32[384]{0:T(512)}, u32[]{:S(2)}) copy-start(f32[384]{0:T(512)} %param.21) | copy-start | bytes 4612

commit v13 on v6

--- a/solution.py
+++ b/solution.py
@@ -309,7 +309,8 @@
     ahead = [(i, i + 1) for i in range(sections - 1)]
     prev_counts = lax.ppermute(counts, "tm", ahead)
     both = jnp.concatenate([inner_input, segment_input], axis=0)
-    both_all = lax.all_gather(both, "rows", axis=2, tiled=True)
+    both_all = lax.all_gather(both, "rows", axis=3, tiled=True)
+    both_all = both_all.reshape(2 * clip_count, frame_count, -1, column_count, channels)
     inner_all = both_all[:clip_count]
     segment_all = both_all[clip_count:]
     wide = (counts > 1)[:, None, None, None]

time: 49.8 us -> 51.1 us (1.026)
  other arithmetic: 4.45 us -> 7.31 us
  local copies, waits for them, and re-layouts: 4.11 us -> 2.4 us
    reduce_sum x4, other arithmetic: 0.65 us -> 1.65 us  [normalize(): jnp.mean(widened * widened, axis=-1, keepdims=True) + EPSILON]
    convert_element_type x2, other arithmetic: 0.61 us -> 1.61 us  [activate(): return jax.nn.silu(normalize(field, gain)).astype(jnp.bfloat16)]
    slice x1, local copies, waits for them, and re-layouts: 0.78 us -> 0.04 us  [gathered_body(): inner_all = both_all[:clip_count]]
    ppermute x1, starting transfers between devices: 1.3 us -> 2.04 us  [gathered_body(): prev_raw = lax.ppermute(inner_all, 'tm', ahead)]
    ppermute x1, starting transfers between devices: 4 us -> 3.29 us  [gathered_body(): lax.ppermute(last_raw, 'tm', [(i, i + 2) for i in range(sections - 2)])]
    convert_element_type x2 -> x0, local copies, waits for them, and re-layouts: 0.69 us -> none  [the longest x1 0.65 us: gathered_body(): return (summed * live_mask[:, :, None, None, None]).astype(jnp.bfloat16)]
    convert_element_type x1, other arithmetic: 0.09 us -> 0.73 us  [gathered_body(): return (summed * live_mask[:, :, None, None, None]).astype(jnp.bfloat16)]
    unnamed x16 -> x20, local copies, waits for them, and re-layouts: 1.68 us -> 1.33 us
where the time goes in v13:
time: 51.1 us; the launch traced here: 50.7 us
  blocking collectives  21.3 us (42%)
  Pallas kernels  10.4 us (20%)
  other arithmetic  7.31 us (14%)
  starting transfers between devices  6.73 us (13%)
  local copies, waits for them, and re-layouts  2.4 us (5%)
  matrix products  2.27 us (4%)
    all_gather x1, blocking collectives, gathered_body(): both_all = lax.all_gather(both, 'rows', axis=3, tiled=True)  21.3 us
    pallas_call x2, Pallas kernels, conv_part(): pl.pallas_call(functools.partial(conv_part_kernel, plan, first_tap), in_s...  10.4 us
    ppermute x1, starting transfers between devices, gathered_body(): lax.ppermute(last_raw, 'tm', [(i, i + 2) for i in range(sections - 2)])  3.29 us
    ppermute x1, starting transfers between devices, gathered_body(): prev_raw = lax.ppermute(inner_all, 'tm', ahead)  2.04 us
    reduce_sum x4, other arithmetic, normalize(): jnp.mean(widened * widened, axis=-1, keepdims=True) + EPSILON  1.65 us
    convert_element_type x2, other arithmetic, activate(): return jax.nn.silu(normalize(field, gain)).astype(jnp.bfloat16)  1.61 us
    ppermute x1, starting transfers between devices, gathered_body(): prev_counts = lax.ppermute(counts, 'tm', ahead)  1.39 us
    unnamed x20, local copies, waits for them, and re-layouts  1.33 us
  transfers between devices with their start and end apart: 3, of which 0 were waited for; matrix products, arithmetic and copies ran while one was open for 4% of the time, Pallas kernels for 10%

profile of v13, /device:TPU:0, one launch (start us, length us, event | category | flops | bytes accessed | tf_op | source)
XLA Modules:
  0.0 50.7 jit_solution(2025996483700834732)
XLA Ops:
  0.0 0.0 copy-start
  0.0 1.0 %pad_maximum_fusion.2 = bf16[4,2,1,32,384]{4,3,1,0,2:T(8,128)(2,1)S(1)} fusion(bf16[2,2,1,32,384]{4,3,1,0,2:T(8,128)(2,1)} %bitcast.71, bf16[2,2,1,32,384]{4,3,1,0,2:T(8,128)(2,1)} %bitcast.72), kind=kLoop, calls=%fused_computation.75 | loop fusion | flops 98304 | bytes 393216 | tf_op jit(solution)/shard_map/concatenate | solution.py:311
  1.0 0.0 copy-start.9
  1.0 21.3 %all_gather.3 = bf16[4,2,1,128,384]{4,3,1,0,2:T(8,128)(2,1)S(1)} all-gather(bf16[4,2,1,32,384]{4,3,1,0,2:T(8,128)(2,1)S(1)} %pad_maximum_fusion.2), channel_id=1, replica_groups=mesh['clips'=2,'tm'=4,'rows'=4] {'rows'}, dimensions={3}, use_global_device_ids=true | all-gather | bytes 983040 | tf_op jit(solution)/shard_map/all_gather | solution.py:312
  22.3 0.0 copy-start.1
  22.3 0.0 copy-start.4
  22.3 0.1 slice_convert_fusion.2
  22.5 2.0 %collective-permute-start = (bf16[2,2,4,32,384]{4,3,2,0,1:T(8,128)(2,1)S(1)}, bf16[2,2,4,32,384]{4,3,2,0,1:T(8,128)(2,1)}, u32[]{:S(2)}, u32[]{:S(2)}) collective-permute-start(bf16[2,2,4,32,384]{4,3,2,0,1:T(8,128)(2,1)S(1)} %bitcast.64), channel_id=1, source_target_pairs={{0,4},{4,8},{8,12},{1,5},{5,9},{9,13},{2,6},{6,10},{10,14},{3,7},{... | collective-permute-start | bytes 1179656 | tf_op jit(solution)/shard_map/ppermute | solution.py:318
  24.5 0.0 copy-done.9
  24.5 0.8 %fusion.42 = bf16[2,4,32,384]{3,2,1,0:T(8,128)(2,1)} fusion(bf16[2,2,4,32,384]{4,3,2,0,1:T(8,128)(2,1)S(1)} %bitcast.65, pred[2]{0:T(512)(128)(4,1)S(1)} %broadcast_compare_fusion.1), kind=kLoop, calls=%fused_computation.73 | loop fusion | flops 98304 | bytes 589826 | tf_op jit(solution)/shard_map/jit(_where)/select_n | solution.py:317
  25.3 3.3 %collective-permute-start.1 = (bf16[2,4,32,384]{3,2,1,0:T(8,128)(2,1)}, bf16[2,4,32,384]{3,2,1,0:T(8,128)(2,1)S(1)}, u32[]{:S(2)}, u32[]{:S(2)}) collective-permute-start(bf16[2,4,32,384]{3,2,1,0:T(8,128)(2,1)} %fusion.42), channel_id=1, source_target_pairs={{0,8},{4,12},{1,9},{5,13},{2,10},{6,14},{3,11},{7,15},{16,24},{20,... | collective-permute-start | bytes 589832 | tf_op jit(solution)/shard_map/ppermute | solution.py:319
  28.6 1.4 %collective-permute-start.2 = (s32[2]{0:T(128)S(1)}, s32[2]{0:T(128)S(1)}, u32[]{:S(2)}, u32[]{:S(2)}) collective-permute-start(s32[2]{0:T(128)S(1)} %bitcast.74), channel_id=1, source_target_pairs={{0,4},{4,8},{8,12},{1,5},{5,9},{9,13},{2,6},{6,10},{10,14},{3,7},{... | collective-permute-start | bytes 32 | tf_op jit(solution)/shard_map/ppermute | solution.py:310
  30.0 0.2 multiply_reduce_fusion.1
  30.1 0.0 copy-done.1
  30.2 0.1 rsqrt.43
  30.3 0.0 copy-done.4
  30.3 0.3 multiply_convert_fusion.1
  30.6 0.3 pad_slice_fusion.2
  30.9 0.0 copy-start.7
  30.9 0.2 pad_maximum_fusion
  31.1 0.1 compare_convert_fusion
  31.2 0.4 copy-done.7
  31.6 0.1 copy.25.x_ref
  31.8 5.1 %shard_map.109 = f32[2,2,128,384]{3,2,1,0:T(8,128)S(1)} custom-call(bf16[2,2,6,32,1152]{4,3,2,1,0:T(8,128)(2,1)S(1)} %copy.25.x_ref, bf16[3,3,3,384,384]{4,3,2,1,0:T(8,128)(2,1)} %w_hbm.3), custom_call_target="tpu_custom_call" | custom-call | flops 2038431744 | bytes 7864320 | tf_op jit(solution)/shard_map/pallas_call | solution.py:229
  36.9 0.0 collective-permute-done.2
  36.9 0.0 collective-permute-done.1
  36.9 0.0 collective-permute-done
  36.9 1.1 %fusion.9 = f32[2,2,4,32]{3,2,0,1:T(4,128)S(1)} fusion(bf16[2,2,4,32,384]{4,3,2,0,1:T(8,128)(2,1)} %collective-permute-done), kind=kLoop, calls=%fused_computation.25 | loop fusion | flops 589312 | bytes 395264 | tf_op jit(solution)/shard_map/reduce_sum | solution.py:54
  38.1 1.3 %fusion.16 = bf16[2,2,4,32,384]{4,3,2,0,1:T(8,128)(2,1)S(1)} fusion(bf16[2,2,4,32,384]{4,3,2,0,1:T(8,128)(2,1)} %collective-permute-done, f32[2,2,4,32]{3,2,0,1:T(4,128)S(1)} %add_rsqrt_fusion, f32[384]{0:T(512)S(1)} %copy-done.4), kind=kLoop, calls=%fused_computation.32 | loop fusion | flops 1572864 | bytes 790016 | tf_op jit(solution)/shard_map/convert_element_type | solution.py:184
  39.4 0.1 fusion.25
  39.6 0.1 fusion.41
  39.7 0.2 fusion.43
  39.9 0.2 fusion.22
  40.1 0.4 fusion.46
  40.5 0.2 pad_maximum_fusion.1.x_ref
  40.6 0.0 copy-start.2
  40.6 0.0 copy-start.5
  40.7 5.3 %shard_map.110 = f32[2,2,128,384]{3,2,1,0:T(8,128)S(1)} custom-call(bf16[2,2,6,32,1152]{4,3,2,1,0:T(8,128)(2,1)S(1)} %pad_maximum_fusion.1.x_ref, bf16[3,3,3,384,384]{4,3,2,1,0:T(8,128)(2,1)} %w_hbm.3), custom_call_target="tpu_custom_call" | custom-call | flops 2038431744 | bytes 7864320 | tf_op jit(solution)/shard_map/pallas_call | solution.py:229
  45.9 0.0 copy-done.2
  45.9 0.0 copy-done.5
  46.0 0.2 multiply_reduce_fusion
  46.2 0.1 rsqrt.47
  46.3 0.0 copy-start.6
  46.3 0.0 copy-start.3
  46.3 0.0 slice-start
  46.3 0.1 fusion.19
  46.4 0.1 add_convert_fusion
  46.5 0.4 copy-done.6
  47.0 0.1 fusion.40
  47.1 0.4 copy-done.3
  47.5 0.0 slice-done
  47.5 0.2 convolution_add_fusion.2
  47.7 0.0 copy-start.8
  47.7 0.6 %convolution_add_fusion = f32[512,768]{1,0:T(8,128)S(1)} fusion(f32[768]{0:T(1024)S(1)} %slice.76, bf16[384,1152]{1,0:T(8,128)(2,1)S(1)} %copy-done.3, bf16[512,384]{1,0:T(8,128)(2,1)S(1)} %fusion.19, f32[384]{0:T(512)S(1)} %copy-done.6, f32[512]{0:T(512)S(1)} %bitcast.73), kind=kOutput, calls=%fused_computation.7 | convolution fusion | flops 303169536 | bytes 2564096 | tf_op jit(solution)/shard_map/dot_general | solution.py:345
  48.3 0.9 %convolution_multiply_fusion = f32[4,32,128]{2,1,0:T(8,128)S(1)} fusion(f32[4,32,384]{2,1,0:T(8,128)S(1)} %bitcast.67, f32[4,128,768]{2,1,0:T(8,128)S(1)} %bitcast.62), kind=kOutput, calls=%fused_computation.17 | convolution fusion | flops 75513856 | bytes 1048576 | tf_op jit(solution)/shard_map/nqc,nkc->nqk/dot_general | solution.py:359
  49.3 0.2 fusion.47
  49.5 0.3 convolution_convert_fusion
  49.8 0.0 copy-done
  49.8 0.0 copy-done.8
  49.8 0.2 fusion.4
  50.0 0.7 %fusion.38 = bf16[2,2,1,32,384]{4,3,2,1,0:T(8,128)(2,1)} fusion(bf16[2,2,1,32,384]{4,3,2,1,0:T(8,128)(2,1)S(1)} %bitcast.70, f32[2,2]{1,0:T(2,128)S(1)} %compare_convert_fusion, bf16[2,2,4,32,384]{4,3,2,1,0:T(8,128)(2,1)S(1)} %add_convert_fusion, s32[]{:T(128)S(6)} %select_n.18), kind=kLoop, calls=%fused_computation.67 | loop fusion | flops 245760 | bytes 294932 | tf_op jit(solution)/shard_map/convert_element_type | solution.py:378
  (9 shorter events, 0.1 us)
Async XLA Ops:
  0.0 49.8 %copy-start = (bf16[384,384]{1,0:T(8,128)(2,1)S(1)}, bf16[384,384]{1,0:T(8,128)(2,1)}, u32[]{:S(2)}) copy-start(bf16[384,384]{1,0:T(8,128)(2,1)} %param.20) | copy-start | bytes 884740
  1.0 23.5 %copy-start.9 = (s32[2,1]{0,1:T(1,128)S(1)}, s32[2,1]{0,1:T(1,128)}, u32[]{:S(2)}) copy-start(s32[2,1]{0,1:T(1,128)} %param.13) | copy-start | bytes 28
  22.3 7.8 %copy-start.1 = (bf16[4,2,1,128,384]{4,3,1,0,2:T(8,128)(2,1)}, bf16[4,2,1,128,384]{4,3,1,0,2:T(8,128)(2,1)S(1)}, u32[]{:S(2)}) copy-start(bf16[4,2,1,128,384]{4,3,1,0,2:T(8,128)(2,1)S(1)} %all_gather.3) | copy-start | bytes 2359300
  22.3 7.9 %copy-start.4 = (f32[384]{0:T(512)S(1)}, f32[384]{0:T(512)}, u32[]{:S(2)}) copy-start(f32[384]{0:T(512)} %param.14) | copy-start | bytes 4612
  22.5 14.5 %collective-permute-start = (bf16[2,2,4,32,384]{4,3,2,0,1:T(8,128)(2,1)S(1)}, bf16[2,2,4,32,384]{4,3,2,0,1:T(8,128)(2,1)}, u32[]{:S(2)}, u32[]{:S(2)}) collective-permute-start(bf16[2,2,4,32,384]{4,3,2,0,1:T(8,128)(2,1)S(1)} %bitcast.64), channel_id=1, source_target_pairs={{0,4},{4,8},{8,12},{1,5},{5,9},{9,13},{2,6},{6,10},{10,14},{3,7},{... | collective-permute-start | bytes 1179656 | tf_op jit(solution)/shard_map/ppermute | solution.py:318
  25.3 11.6 %collective-permute-start.1 = (bf16[2,4,32,384]{3,2,1,0:T(8,128)(2,1)}, bf16[2,4,32,384]{3,2,1,0:T(8,128)(2,1)S(1)}, u32[]{:S(2)}, u32[]{:S(2)}) collective-permute-start(bf16[2,4,32,384]{3,2,1,0:T(8,128)(2,1)} %fusion.42), channel_id=1, source_target_pairs={{0,8},{4,12},{1,9},{5,13},{2,10},{6,14},{3,11},{7,15},{16,24},{20,... | collective-permute-start | bytes 589832 | tf_op jit(solution)/shard_map/ppermute | solution.py:319
  28.6 8.3 %collective-permute-start.2 = (s32[2]{0:T(128)S(1)}, s32[2]{0:T(128)S(1)}, u32[]{:S(2)}, u32[]{:S(2)}) collective-permute-start(s32[2]{0:T(128)S(1)} %bitcast.74), channel_id=1, source_target_pairs={{0,4},{4,8},{8,12},{1,5},{5,9},{9,13},{2,6},{6,10},{10,14},{3,7},{... | collective-permute-start | bytes 32 | tf_op jit(solution)/shard_map/ppermute | solution.py:310
  30.9 0.7 %copy-start.7 = (f32[1152]{0:T(1024)S(1)}, f32[1152]{0:T(1024)}, u32[]{:S(2)}) copy-start(f32[1152]{0:T(1024)} %param.19) | copy-start | bytes 13828
  40.6 5.3 %copy-start.2 = (bf16[4,2,1,128,384]{4,3,1,0,2:T(8,128)(2,1)S(1)}, bf16[4,2,1,128,384]{4,3,1,0,2:T(8,128)(2,1)}, u32[]{:S(2)}) copy-start(bf16[4,2,1,128,384]{4,3,1,0,2:T(8,128)(2,1)} %copy-done.1) | copy-start | bytes 2359300
  40.6 5.3 %copy-start.5 = (f32[384]{0:T(512)S(1)}, f32[384]{0:T(512)}, u32[]{:S(2)}) copy-start(f32[384]{0:T(512)} %param.16) | copy-start | bytes 4612
  46.3 0.7 %copy-start.6 = (f32[384]{0:T(512)S(1)}, f32[384]{0:T(512)}, u32[]{:S(2)}) copy-start(f32[384]{0:T(512)} %param.17) | copy-start | bytes 4612
  46.3 1.2 %copy-start.3 = (bf16[384,1152]{1,0:T(8,128)(2,1)S(1)}, bf16[384,1152]{1,0:T(8,128)(2,1)}, u32[]{:S(2)}) copy-start(bf16[384,1152]{1,0:T(8,128)(2,1)} %param.18) | copy-start | bytes 2654212
  46.3 1.2 %slice-start = ((f32[1152]{0:T(1024)}), f32[384]{0:T(512)S(1)}, s32[]{:S(2)}) async-start(f32[1152]{0:T(1024)} %param.19), calls=%async_computation | async-start | bytes 4096 | tf_op jit(solution)/shard_map/slice | solution.py:357
  47.7 2.1 %copy-start.8 = (f32[384]{0:T(512)S(1)}, f32[384]{0:T(512)}, u32[]{:S(2)}) copy-start(f32[384]{0:T(512)} %param.21) | copy-start | bytes 4612

commit v14 on v6

--- a/solution.py
+++ b/solution.py
@@ -290,6 +290,72 @@
     return total.reshape(clips, slots, height, columns, channels)
 
 
+def attend_kernel(res_ref, mine_ref, mask_ref, gain_ref, wkv_ref, bkv_ref, wq_ref, bq_ref,
+                  wo_ref, bo_ref, o_ref):
+    frames, places, channels = res_ref.shape
+    gain = gain_ref[...]
+    for n in range(frames):
+        wide = res_ref[n].astype(jnp.float32)
+        scale = lax.rsqrt(jnp.mean(wide * wide, axis=-1, keepdims=True) + EPSILON)
+        normed = (wide * scale * gain).astype(jnp.bfloat16)
+        packed = (
+            jnp.dot(normed, wkv_ref[...], preferred_element_type=jnp.float32) + bkv_ref[...]
+        )
+        key_vectors = packed[:, :channels]
+        values = packed[:, channels:].astype(jnp.bfloat16)
+        own = mine_ref[n].astype(jnp.float32)
+        own_scale = lax.rsqrt(jnp.mean(own * own, axis=-1, keepdims=True) + EPSILON)
+        own_normed = (own * own_scale * gain).astype(jnp.bfloat16)
+        queries = (
+            jnp.dot(own_normed, wq_ref[...], preferred_element_type=jnp.float32) + bq_ref[...]
+        )
+        scores = lax.dot_general(
+            queries, key_vectors, (((1,), (1,)), ((), ())),
+            precision=lax.Precision.HIGHEST, preferred_element_type=jnp.float32,
+        ) / math.sqrt(channels)
+        row_max = jnp.max(scores, axis=-1, keepdims=True)
+        exponent = jnp.exp(scores - row_max)
+        weights = (exponent / jnp.sum(exponent, axis=-1, keepdims=True)).astype(jnp.bfloat16)
+        attended = jnp.dot(weights, values, preferred_element_type=jnp.float32).astype(
+            jnp.bfloat16
+        )
+        projected = (
+            jnp.dot(attended, wo_ref[...], preferred_element_type=jnp.float32) + bo_ref[...]
+        ).astype(jnp.bfloat16)
+        summed = own + projected.astype(jnp.float32)
+        o_ref[n] = (summed * mask_ref[n]).astype(o_ref.dtype)
+
+
+def attend_local(residual, mine, mask, attention_gain, triple_weight, triple_bias,
+                 output_weight, output_bias):
+    frames, places, channels = residual.shape
+    own_places = mine.shape[1]
+    vmem = pl.BlockSpec(memory_space=pltpu.VMEM)
+    return pl.pallas_call(
+        attend_kernel,
+        in_specs=[vmem] * 10,
+        out_specs=vmem,
+        out_shape=jax.ShapeDtypeStruct((frames, own_places, channels), jnp.bfloat16),
+        cost_estimate=pl.CostEstimate(
+            flops=2 * frames * (places * channels * 2 * channels + 4 * own_places * channels * channels
+                                + 8 * own_places * places * channels),
+            transcendentals=frames * own_places * places,
+            bytes_accessed=triple_weight.size * 2 + output_weight.size * 2 + residual.size * 2,
+        ),
+    )(
+        residual,
+        mine,
+        mask,
+        attention_gain.reshape(1, channels),
+        triple_weight[:, channels:],
+        triple_bias[channels:].reshape(1, 2 * channels),
+        triple_weight[:, :channels],
+        triple_bias[:channels].reshape(1, channels),
+        output_weight,
+        output_bias.reshape(1, channels),
+    )
+
+
 def gathered_body(
     segment_input,
     inner_input,
@@ -335,46 +401,24 @@
     height = inner_all.shape[2]
     convolved = frame_major(own_sum + carried_sum, clip_count, height, column_count) + causal_bias
     residual = (segment_all.astype(jnp.float32) + convolved).astype(jnp.bfloat16)
-    normed = normalize(residual, attention_gain).astype(jnp.bfloat16)
-    height = normed.shape[2]
+    height = residual.shape[2]
     frames = clip_count * frame_count
-    places = height * column_count
-    flat = normed.reshape(frames * places, channels)
-    packed = (
-        jnp.dot(flat, triple_weight[:, channels:], preferred_element_type=jnp.float32)
-        + triple_bias[channels:]
-    ).reshape(frames, places, 2 * channels)
-    key_vectors = packed[:, :, :channels]
-    values = packed[:, :, channels:].astype(jnp.bfloat16)
     start = lax.axis_index("rows") * row_count
-    mine = lax.dynamic_slice_in_dim(normed, start, row_count, axis=2)
-    queries = (
-        jnp.dot(
-            mine.reshape(-1, channels), triple_weight[:, :channels],
-            preferred_element_type=jnp.float32,
-        )
-        + triple_bias[:channels]
-    ).reshape(frames, row_count * column_count, channels)
-    scores = jnp.einsum(
-        "nqc,nkc->nqk", queries, key_vectors, precision=lax.Precision.HIGHEST
-    ) / math.sqrt(channels)
-    row_max = jnp.max(scores, axis=-1, keepdims=True)
-    exponent = jnp.exp(scores - row_max)
-    weights = (exponent / jnp.sum(exponent, axis=-1, keepdims=True)).astype(jnp.bfloat16)
-    attended = jnp.einsum(
-        "nqk,nkc->nqc", weights, values, preferred_element_type=jnp.float32
-    ).astype(jnp.bfloat16)
-    projected = (
-        jnp.dot(attended.reshape(-1, channels), output_weight, preferred_element_type=jnp.float32)
-        + output_bias
-    ).astype(jnp.bfloat16)
-    projected = projected.reshape(clip_count, frame_count, row_count, column_count, channels)
-    residual_mine = lax.dynamic_slice_in_dim(residual, start, row_count, axis=2)
+    mine = lax.dynamic_slice_in_dim(residual, start, row_count, axis=2)
     live_mask = (jnp.arange(frame_count, dtype=jnp.int32)[None, :] < counts[:, None]).astype(
         jnp.float32
     )
-    summed = residual_mine.astype(jnp.float32) + projected.astype(jnp.float32)
-    return (summed * live_mask[:, :, None, None, None]).astype(jnp.bfloat16)
+    result = attend_local(
+        residual.reshape(frames, height * column_count, channels),
+        mine.reshape(frames, row_count * column_count, channels),
+        live_mask.reshape(frames, 1, 1),
+        attention_gain,
+        triple_weight,
+        triple_bias,
+        output_weight,
+        output_bias,
+    )
+    return result.reshape(clip_count, frame_count, row_count, column_count, channels)
 
 
 GATHER_LIMIT = 1 << 22

time: 49.8 us -> 60.8 us (1.22)
  Pallas kernels: 10.3 us -> 16.1 us
  local copies, waits for them, and re-layouts: 4.11 us -> 8.91 us
  matrix products: 2.24 us -> 0 us
  other arithmetic: 4.45 us -> 6.55 us
    pallas_call x0 -> x1, Pallas kernels: none -> 5.83 us  [attend_local(): pl.pallas_call(attend_kernel, in_specs=[vmem] * 10, out_specs=vmem, out_s...]
    reshape x0 -> x4, local copies, waits for them, and re-layouts: none -> 2.98 us  [the longest x1 1.25 us: attend_local(): output_bias.reshape(1, channels)]
    dot_general x5 -> x0, matrix products: 2.24 us -> none  [the longest x1 0.95 us: gathered_body(): jnp.einsum('nqc,nkc->nqk', queries, key_vectors, precision=lax.Precision....]
    slice x3 -> x5, local copies, waits for them, and re-layouts: 0.01 us -> 1.63 us  [the longest x1 0.86 us: attend_local(): triple_weight[:, channels:]]
    convert_element_type x2, local copies, waits for them, and re-layouts: 0.69 us -> 2.14 us  [the longest x1 1.34 us: gathered_body(): (jnp.arange(frame_count, dtype=jnp.int32)[None, :] < counts[:, None]).ast...]
    convert_element_type x1, other arithmetic: 0.01 us -> 1.36 us  [gathered_body(): (jnp.arange(frame_count, dtype=jnp.int32)[None, :] < counts[:, None]).ast...]
    unnamed x16 -> x10, local copies, waits for them, and re-layouts: 1.68 us -> 0.55 us
    slice x1, local copies, waits for them, and re-layouts: 0.78 us -> 0.04 us  [gathered_body(): inner_all = both_all[:clip_count]]
  transfers between devices with their start and end apart: 3 -> 3, of which waited for: 0 -> 0; matrix products, arithmetic and copies ran while one was open for 4% -> 16% of each run, Pallas kernels for 10% -> 8%
where the time goes in v14:
time: 60.8 us; the launch traced here: 60.4 us
  blocking collectives  21.3 us (35%)
  Pallas kernels  16.1 us (26%)
  local copies, waits for them, and re-layouts  8.91 us (15%)
  starting transfers between devices  7.29 us (12%)
  other arithmetic  6.55 us (11%)
    all_gather x1, blocking collectives, gathered_body(): both_all = lax.all_gather(both, 'rows', axis=2, tiled=True)  21.3 us
    pallas_call x2, Pallas kernels, conv_part(): pl.pallas_call(functools.partial(conv_part_kernel, plan, first_tap), in_s...  10.3 us
    pallas_call x1, Pallas kernels, attend_local(): pl.pallas_call(attend_kernel, in_specs=[vmem] * 10, out_specs=vmem, out_s...  5.83 us
    ppermute x1, starting transfers between devices, gathered_body(): lax.ppermute(last_raw, 'tm', [(i, i + 2) for i in range(sections - 2)])  4 us
    ppermute x1, starting transfers between devices, gathered_body(): prev_counts = lax.ppermute(counts, 'tm', ahead)  1.97 us
    convert_element_type x1, other arithmetic, gathered_body(): (jnp.arange(frame_count, dtype=jnp.int32)[None, :] < counts[:, None]).ast...  1.36 us
    convert_element_type x1, local copies, waits for them, and re-layouts, gathered_body(): (jnp.arange(frame_count, dtype=jnp.int32)[None, :] < counts[:, None]).ast...  1.34 us
    ppermute x1, starting transfers between devices, gathered_body(): prev_raw = lax.ppermute(inner_all, 'tm', ahead)  1.31 us
  transfers between devices with their start and end apart: 3, of which 0 were waited for; matrix products, arithmetic and copies ran while one was open for 16% of the time, Pallas kernels for 8%

profile of v14, /device:TPU:0, one launch (start us, length us, event | category | flops | bytes accessed | tf_op | source)
XLA Modules:
  0.0 60.4 jit_solution(860781221074990188)
XLA Ops:
  0.0 0.0 copy-start.1
  0.0 1.0 %pad_maximum_fusion.2 = bf16[4,2,1,32,384]{4,3,2,1,0:T(8,128)(2,1)S(1)} fusion(bf16[2,2,1,32,384]{4,3,2,1,0:T(8,128)(2,1)} %param.11, bf16[2,2,1,32,384]{4,3,2,1,0:T(8,128)(2,1)} %param.12), kind=kLoop, calls=%fused_computation.54 | loop fusion | flops 98304 | bytes 393216 | tf_op jit(solution)/shard_map/concatenate | solution.py:377
  1.0 21.3 %all_gather.3 = bf16[4,2,4,32,384]{4,3,2,0,1:T(8,128)(2,1)S(1)} all-gather(bf16[4,2,1,32,384]{4,3,2,0,1:T(8,128)(2,1)S(1)} %copy.23), channel_id=1, replica_groups=mesh['clips'=2,'tm'=4,'rows'=4] {'rows'}, dimensions={2}, use_global_device_ids=true | all-gather | bytes 983040 | tf_op jit(solution)/shard_map/all_gather | solution.py:378
  22.4 1.3 %collective-permute-start = (bf16[2,2,4,32,384]{4,3,2,0,1:T(8,128)(2,1)S(1)}, bf16[2,2,4,32,384]{4,3,2,0,1:T(8,128)(2,1)S(1)}, u32[]{:S(2)}, u32[]{:S(2)}) collective-permute-start(bf16[2,2,4,32,384]{4,3,2,0,1:T(8,128)(2,1)S(1)} %slice.68), channel_id=1, source_target_pairs={{0,4},{4,8},{8,12},{1,5},{5,9},{9,13},{2,6},{6,10},{10,14},{3,7},{... | collective-permute-start | bytes 1179656 | tf_op jit(solution)/shard_map/ppermute | solution.py:383
  23.7 0.7 %broadcast_compare_fusion.1 = pred[2]{0:T(512)(128)(4,1)S(1)} fusion(s32[2,1]{0,1:T(1,128)} %param.13), kind=kLoop, calls=%fused_computation.62 | loop fusion | flops 2 | bytes 10 | tf_op jit(solution)/shard_map/gt | solution.py:381
  24.3 0.8 %fusion.34 = bf16[2,4,32,384]{3,2,1,0:T(8,128)(2,1)} fusion(bf16[4,2,4,32,384]{4,3,2,0,1:T(8,128)(2,1)S(1)} %all_gather.3, pred[2]{0:T(512)(128)(4,1)S(1)} %broadcast_compare_fusion.1), kind=kLoop, calls=%fused_computation.52 | loop fusion | flops 98304 | bytes 589826 | tf_op jit(solution)/shard_map/jit(_where)/select_n | solution.py:382
  25.1 4.0 %collective-permute-start.1 = (bf16[2,4,32,384]{3,2,1,0:T(8,128)(2,1)}, bf16[2,4,32,384]{3,2,1,0:T(8,128)(2,1)S(1)}, u32[]{:S(2)}, u32[]{:S(2)}) collective-permute-start(bf16[2,4,32,384]{3,2,1,0:T(8,128)(2,1)} %fusion.34), channel_id=1, source_target_pairs={{0,8},{4,12},{1,9},{5,13},{2,10},{6,14},{3,11},{7,15},{16,24},{20,... | collective-permute-start | bytes 589832 | tf_op jit(solution)/shard_map/ppermute | solution.py:384
  29.1 2.0 %collective-permute-start.2 = (s32[2]{0:T(128)}, s32[2]{0:T(128)}, u32[]{:S(2)}, u32[]{:S(2)}) collective-permute-start(s32[2]{0:T(128)} %bitcast), channel_id=1, source_target_pairs={{0,4},{4,8},{8,12},{1,5},{5,9},{9,13},{2,6},{6,10},{10,14},{3,7},{... | collective-permute-start | bytes 32 | tf_op jit(solution)/shard_map/ppermute | solution.py:376
  31.1 0.2 fusion.5
  31.3 0.0 copy-done.1
  31.3 0.3 fusion.12
  31.6 0.3 pad_slice_fusion.2
  31.9 0.0 copy-start
  31.9 0.2 pad_maximum_fusion
  32.1 0.0 copy-start.2
  32.1 1.4 %compare_convert_fusion = f32[2,2]{1,0:T(2,128)} fusion(s32[2]{0:T(128)} %bitcast), kind=kLoop, calls=%fused_computation.59 | loop fusion | flops 8 | bytes 24 | tf_op jit(solution)/shard_map/convert_element_type | solution.py:408
  33.5 0.0 copy-done
  33.5 0.9 %slice.63.wkv_ref = bf16[384,768]{1,0:T(8,128)(2,1)} slice(bf16[384,1152]{1,0:T(8,128)(2,1)S(1)} %copy-done), slice={[0:384], [384:1152]} | slice | bytes 1179648 | tf_op jit(solution)/shard_map/slice | solution.py:350
  34.3 0.8 %slice.65.wq_ref = bf16[384,384]{1,0:T(8,128)(2,1)} slice(bf16[384,1152]{1,0:T(8,128)(2,1)S(1)} %copy-done), slice={[0:384], [0:384]} | slice | bytes 589824 | tf_op jit(solution)/shard_map/slice | solution.py:352
  35.1 0.0 copy-done.2
  35.1 0.0 copy-start.4
  35.1 0.0 slice-start
  35.1 0.1 copy.14.x_ref
  35.3 1.3 %reshape.94.mask_ref = f32[4,1,1]{2,1,0:T(1,128)} reshape(f32[2,2]{1,0:T(2,128)} %compare_convert_fusion) | data formatting | bytes 32 | tf_op jit(solution)/shard_map/convert_element_type | solution.py:408
  36.6 0.0 copy-done.4
  36.6 0.6 reshape.88.gain_ref
  37.2 0.6 reshape.89.bkv_ref
  37.8 0.0 slice-done
  37.8 0.6 reshape.90.bq_ref
  38.4 1.3 %reshape.91.bo_ref = f32[1,384]{1,0:T(1,128)} reshape(f32[384]{0:T(512)} %param.21) | data formatting | bytes 3072 | tf_op jit(solution)/shard_map/reshape | solution.py:355
  39.6 5.1 %shard_map.109 = f32[2,2,128,384]{3,2,1,0:T(8,128)S(1)} custom-call(bf16[2,2,6,32,1152]{4,3,2,1,0:T(8,128)(2,1)S(1)} %copy.14.x_ref, bf16[3,3,3,384,384]{4,3,2,1,0:T(8,128)(2,1)} %w_hbm.3), custom_call_target="tpu_custom_call" | custom-call | flops 2038431744 | bytes 7864320 | tf_op jit(solution)/shard_map/pallas_call | solution.py:229
  44.7 0.0 collective-permute-done.2
  44.7 0.0 collective-permute-done.1
  44.8 0.0 collective-permute-done
  44.8 0.2 fusion.13
  44.9 0.3 fusion.20
  45.3 0.7 %broadcast_compare_fusion = pred[2]{0:T(512)(128)(4,1)S(1)} fusion(s32[2]{0:T(128)} %collective-permute-done.2), kind=kLoop, calls=%fused_computation.61 | loop fusion | flops 2 | bytes 10 | tf_op jit(solution)/shard_map/gt | solution.py:392
  45.9 0.1 fusion.24
  46.1 0.1 fusion.33
  46.2 0.2 fusion.35
  46.4 0.2 fusion.22
  46.6 0.4 fusion.36
  47.0 0.2 pad_maximum_fusion.1.x_ref
  47.1 5.2 %shard_map.110 = f32[2,2,128,384]{3,2,1,0:T(8,128)S(1)} custom-call(bf16[2,2,6,32,1152]{4,3,2,1,0:T(8,128)(2,1)S(1)} %pad_maximum_fusion.1.x_ref, bf16[3,3,3,384,384]{4,3,2,1,0:T(8,128)(2,1)} %w_hbm.3), custom_call_target="tpu_custom_call" | custom-call | flops 2038431744 | bytes 7864320 | tf_op jit(solution)/shard_map/pallas_call | solution.py:229
  52.3 0.0 copy-start.3
  52.4 0.1 add.66
  52.5 0.1 copy.18
  52.5 0.5 copy-done.3
  53.0 0.1 add_convert_fusion
  53.1 0.8 %copy.19 = bf16[2,2,4,32,384]{4,3,2,1,0:T(8,128)(2,1)} copy(bf16[2,2,4,32,384]{4,3,2,0,1:T(8,128)(2,1)S(1)} %add_convert_fusion) | data formatting | bytes 786432 | tf_op jit(solution)/shard_map/convert_element_type | solution.py:403
  54.0 0.6 %copy.20 = bf16[2,2,1,32,384]{4,3,1,0,2:T(8,128)(2,1)} copy(bf16[2,2,1,32,384]{4,3,2,0,1:T(8,128)(2,1)S(1)} %constant_dynamic-slice_fusion) | data formatting | bytes 196608 | tf_op jit(solution)/shard_map/dynamic_slice | solution.py:407
  54.6 5.8 %shard_map.111 = bf16[4,32,384]{2,1,0:T(8,128)(2,1)} custom-call(bf16[4,128,384]{2,1,0:T(8,128)(2,1)} %bitcast.32, bf16[4,32,384]{2,1,0:T(8,128)(2,1)} %bitcast.33, f32[4,1,1]{2,1,0:T(1,128)} %reshape.94.mask_ref, f32[1,384]{1,0:T(1,128)} %reshape.88.gain_ref, bf16[384,768]{1,0:T(8,128)(2,1)} %slice.63.wkv_ref, f32[1,768]{1,0:T(1,128)} %reshape.89.bkv_ref, ...), custom_call_target="tpu_custom_call" | custom-call | flops 553648128 | bytes 1572864 | tf_op jit(solution)/shard_map/pallas_call | solution.py:334
  (7 shorter events, 0.1 us)
Async XLA Ops:
  0.0 31.3 %copy-start.1 = (f32[384]{0:T(512)S(1)}, f32[384]{0:T(512)}, u32[]{:S(2)}) copy-start(f32[384]{0:T(512)} %param.14) | copy-start | bytes 4612
  22.4 22.4 %collective-permute-start = (bf16[2,2,4,32,384]{4,3,2,0,1:T(8,128)(2,1)S(1)}, bf16[2,2,4,32,384]{4,3,2,0,1:T(8,128)(2,1)S(1)}, u32[]{:S(2)}, u32[]{:S(2)}) collective-permute-start(bf16[2,2,4,32,384]{4,3,2,0,1:T(8,128)(2,1)S(1)} %slice.68), channel_id=1, source_target_pairs={{0,4},{4,8},{8,12},{1,5},{5,9},{9,13},{2,6},{6,10},{10,14},{3,7},{... | collective-permute-start | bytes 1179656 | tf_op jit(solution)/shard_map/ppermute | solution.py:383
  25.1 19.6 %collective-permute-start.1 = (bf16[2,4,32,384]{3,2,1,0:T(8,128)(2,1)}, bf16[2,4,32,384]{3,2,1,0:T(8,128)(2,1)S(1)}, u32[]{:S(2)}, u32[]{:S(2)}) collective-permute-start(bf16[2,4,32,384]{3,2,1,0:T(8,128)(2,1)} %fusion.34), channel_id=1, source_target_pairs={{0,8},{4,12},{1,9},{5,13},{2,10},{6,14},{3,11},{7,15},{16,24},{20,... | collective-permute-start | bytes 589832 | tf_op jit(solution)/shard_map/ppermute | solution.py:384
  29.1 15.6 %collective-permute-start.2 = (s32[2]{0:T(128)}, s32[2]{0:T(128)}, u32[]{:S(2)}, u32[]{:S(2)}) collective-permute-start(s32[2]{0:T(128)} %bitcast), channel_id=1, source_target_pairs={{0,4},{4,8},{8,12},{1,5},{5,9},{9,13},{2,6},{6,10},{10,14},{3,7},{... | collective-permute-start | bytes 32 | tf_op jit(solution)/shard_map/ppermute | solution.py:376
  31.9 1.6 %copy-start = (bf16[384,1152]{1,0:T(8,128)(2,1)S(1)}, bf16[384,1152]{1,0:T(8,128)(2,1)}, u32[]{:S(2)}) copy-start(bf16[384,1152]{1,0:T(8,128)(2,1)} %param.18) | copy-start | bytes 2654212
  32.1 3.0 %copy-start.2 = (f32[1152]{0:T(1024)S(1)}, f32[1152]{0:T(1024)}, u32[]{:S(2)}) copy-start(f32[1152]{0:T(1024)} %param.19) | copy-start | bytes 13828
  35.1 1.5 %copy-start.4 = (f32[384]{0:T(512)S(1)}, f32[384]{0:T(512)}, u32[]{:S(2)}) copy-start(f32[384]{0:T(512)} %param.17) | copy-start | bytes 4612
  35.1 2.7 %slice-start = ((f32[1152]{0:T(1024)}), f32[384]{0:T(512)S(1)}, s32[]{:S(2)}) async-start(f32[1152]{0:T(1024)} %param.19), calls=%async_computation | async-start | bytes 4096 | tf_op jit(solution)/shard_map/slice | solution.py:353
  52.3 0.7 %copy-start.3 = (f32[384]{0:T(512)S(1)}, f32[384]{0:T(512)}, u32[]{:S(2)}) copy-start(f32[384]{0:T(512)} %param.16) | copy-start | bytes 4612

commit v15 on v6

--- a/solution.py
+++ b/solution.py
@@ -200,18 +200,23 @@
             copies.append(copy)
     written = set()
     for index, (frame, slot, count) in enumerate(plan):
-        for kh in range(3):
+        for kh in (1, 0, 2):
             slot_index = index * 3 + kh
             copies[slot_index].wait()
+            low = 1 if kh == 0 else 0
+            high = height - 1 if kh == 2 else height
+            if high <= low:
+                continue
             weight = w_vmem[slot_index].reshape(width, channels)
-            lhs = x_ref[:, frame : frame + count, kh : kh + height, :, :]
-            lhs = lhs.reshape(clips * count * places, width)
+            lhs = x_ref[:, frame : frame + count, low + kh : high + kh, :, :]
+            lhs = lhs.reshape(clips * count * (high - low) * columns, width)
             term = jnp.dot(lhs, weight, preferred_element_type=jnp.float32)
-            term = term.reshape(clips, count, places, channels)
+            term = term.reshape(clips, count, (high - low) * columns, channels)
+            rows_here = slice(low * columns, high * columns)
             for part in range(count):
                 target = slot + part
                 if target in written:
-                    o_ref[:, target] += term[:, part]
+                    o_ref[:, target, rows_here] += term[:, part]
                 else:
                     o_ref[:, target] = term[:, part]
                     written.add(target)

time: 49.8 us -> 49.4 us (level)
  no operation moved by 1% of the time
where the time goes in v15:
time: 49.4 us; the launch traced here: 49.1 us
  blocking collectives  21.3 us (43%)
  Pallas kernels  9.91 us (20%)
  starting transfers between devices  6.7 us (14%)
  other arithmetic  4.45 us (9%)
  local copies, waits for them, and re-layouts  4.11 us (8%)
  matrix products  2.24 us (5%)
    all_gather x1, blocking collectives, gathered_body(): both_all = lax.all_gather(both, 'rows', axis=2, tiled=True)  21.3 us
    pallas_call x2, Pallas kernels, conv_part(): pl.pallas_call(functools.partial(conv_part_kernel, plan, first_tap), in_s...  9.91 us
    ppermute x1, starting transfers between devices, gathered_body(): lax.ppermute(last_raw, 'tm', [(i, i + 2) for i in range(sections - 2)])  4 us
    unnamed x16, local copies, waits for them, and re-layouts  1.68 us
    ppermute x1, starting transfers between devices, gathered_body(): prev_counts = lax.ppermute(counts, 'tm', ahead)  1.39 us
    ppermute x1, starting transfers between devices, gathered_body(): prev_raw = lax.ppermute(inner_all, 'tm', ahead)  1.3 us
    concatenate x1, other arithmetic, gathered_body(): both = jnp.concatenate([inner_input, segment_input], axis=0)  1.01 us
  transfers between devices with their start and end apart: 3, of which 0 were waited for; matrix products, arithmetic and copies ran while one was open for 4% of the time, Pallas kernels for 10%

profile of v15, /device:TPU:0, one launch (start us, length us, event | category | flops | bytes accessed | tf_op | source)
XLA Modules:
  0.0 49.1 jit_solution(7886356384463473494)
XLA Ops:
  0.0 0.0 copy-start
  0.0 0.0 copy-start.7
  0.0 0.0 copy-start.2
  0.0 1.0 %pad_maximum_fusion.2 = bf16[4,2,1,32,384]{4,3,2,1,0:T(8,128)(2,1)S(1)} fusion(bf16[2,2,1,32,384]{4,3,2,1,0:T(8,128)(2,1)} %param.11, bf16[2,2,1,32,384]{4,3,2,1,0:T(8,128)(2,1)} %param.12), kind=kLoop, calls=%fused_computation.72 | loop fusion | flops 98304 | bytes 393216 | tf_op jit(solution)/shard_map/concatenate | solution.py:316
  1.0 21.3 %all_gather.3 = bf16[4,2,4,32,384]{4,3,2,0,1:T(8,128)(2,1)S(1)} all-gather(bf16[4,2,1,32,384]{4,3,2,0,1:T(8,128)(2,1)S(1)} %copy.31), channel_id=1, replica_groups=mesh['clips'=2,'tm'=4,'rows'=4] {'rows'}, dimensions={2}, use_global_device_ids=true | all-gather | bytes 983040 | tf_op jit(solution)/shard_map/all_gather | solution.py:317
  22.3 0.8 %slice.77 = bf16[2,2,4,32,384]{4,3,2,0,1:T(8,128)(2,1)} slice(bf16[4,2,4,32,384]{4,3,2,0,1:T(8,128)(2,1)S(1)} %all_gather.3), slice={[0:2], [0:2], [0:4], [0:32], [0:384]} | slice | bytes 786432 | tf_op jit(solution)/shard_map/slice | solution.py:318
  23.1 1.3 %collective-permute-start = (bf16[2,2,4,32,384]{4,3,2,0,1:T(8,128)(2,1)}, bf16[2,2,4,32,384]{4,3,2,0,1:T(8,128)(2,1)S(1)}, u32[]{:S(2)}, u32[]{:S(2)}) collective-permute-start(bf16[2,2,4,32,384]{4,3,2,0,1:T(8,128)(2,1)} %slice.77), channel_id=1, source_target_pairs={{0,4},{4,8},{8,12},{1,5},{5,9},{9,13},{2,6},{6,10},{10,14},{3,7},{... | collective-permute-start | bytes 1179656 | tf_op jit(solution)/shard_map/ppermute | solution.py:322
  24.4 0.0 copy-done.7
  24.5 0.8 %fusion.44 = bf16[2,4,32,384]{3,2,1,0:T(8,128)(2,1)} fusion(bf16[4,2,4,32,384]{4,3,2,0,1:T(8,128)(2,1)S(1)} %all_gather.3, pred[2]{0:T(512)(128)(4,1)S(1)} %broadcast_compare_fusion.1), kind=kLoop, calls=%fused_computation.70 | loop fusion | flops 98304 | bytes 589826 | tf_op jit(solution)/shard_map/jit(_where)/select_n | solution.py:321
  25.2 4.0 %collective-permute-start.1 = (bf16[2,4,32,384]{3,2,1,0:T(8,128)(2,1)}, bf16[2,4,32,384]{3,2,1,0:T(8,128)(2,1)S(1)}, u32[]{:S(2)}, u32[]{:S(2)}) collective-permute-start(bf16[2,4,32,384]{3,2,1,0:T(8,128)(2,1)} %fusion.44), channel_id=1, source_target_pairs={{0,8},{4,12},{1,9},{5,13},{2,10},{6,14},{3,11},{7,15},{16,24},{20,... | collective-permute-start | bytes 589832 | tf_op jit(solution)/shard_map/ppermute | solution.py:323
  29.2 1.4 %collective-permute-start.2 = (s32[2]{0:T(128)S(1)}, s32[2]{0:T(128)S(1)}, u32[]{:S(2)}, u32[]{:S(2)}) collective-permute-start(s32[2]{0:T(128)S(1)} %bitcast.48), channel_id=1, source_target_pairs={{0,4},{4,8},{8,12},{1,5},{5,9},{9,13},{2,6},{6,10},{10,14},{3,7},{... | collective-permute-start | bytes 32 | tf_op jit(solution)/shard_map/ppermute | solution.py:315
  30.6 0.2 fusion.9
  30.8 0.0 copy-done.2
  30.8 0.3 fusion.16
  31.1 0.3 pad_slice_fusion.2
  31.5 0.0 copy-start.3
  31.5 0.2 pad_maximum_fusion
  31.7 0.5 %copy-done.3 = f32[1152]{0:T(1024)S(1)} copy-done((f32[1152]{0:T(1024)S(1)}, f32[1152]{0:T(1024)}, u32[]{:S(2)}) %copy-start.3) | copy-done | bytes 4632
  32.2 0.1 copy.22.x_ref
  32.3 4.9 %shard_map.109 = f32[2,2,128,384]{3,2,1,0:T(8,128)S(1)} custom-call(bf16[2,2,6,32,1152]{4,3,2,1,0:T(8,128)(2,1)S(1)} %copy.22.x_ref, bf16[3,3,3,384,384]{4,3,2,1,0:T(8,128)(2,1)} %w_hbm.3), custom_call_target="tpu_custom_call" | custom-call | flops 2038431744 | bytes 7864320 | tf_op jit(solution)/shard_map/pallas_call | solution.py:234
  37.2 0.0 collective-permute-done.2
  37.2 0.0 collective-permute-done.1
  37.2 0.0 collective-permute-done
  37.2 0.2 fusion.17
  37.4 0.3 fusion.24
  37.7 0.1 fusion.33
  37.9 0.1 fusion.43
  38.0 0.2 fusion.47
  38.2 0.2 fusion.30
  38.4 0.4 fusion.50
  38.8 0.2 pad_maximum_fusion.1.x_ref
  39.0 5.0 %shard_map.110 = f32[2,2,128,384]{3,2,1,0:T(8,128)S(1)} custom-call(bf16[2,2,6,32,1152]{4,3,2,1,0:T(8,128)(2,1)S(1)} %pad_maximum_fusion.1.x_ref, bf16[3,3,3,384,384]{4,3,2,1,0:T(8,128)(2,1)} %w_hbm.3), custom_call_target="tpu_custom_call" | custom-call | flops 2038431744 | bytes 7864320 | tf_op jit(solution)/shard_map/pallas_call | solution.py:234
  44.0 0.0 copy-start.4
  44.0 0.1 add.102
  44.1 0.0 copy-start.5
  44.1 0.1 copy.26
  44.2 0.5 %copy-done.4 = f32[384]{0:T(512)S(1)} copy-done((f32[384]{0:T(512)S(1)}, f32[384]{0:T(512)}, u32[]{:S(2)}) %copy-start.4) | copy-done | bytes 1560
  44.7 0.0 copy-start.1
  44.7 0.2 fusion.25
  44.9 0.0 copy-done.5
  44.9 0.2 fusion.27
  45.1 0.0 slice-start
  45.2 0.6 %copy-done.1 = bf16[384,1152]{1,0:T(8,128)(2,1)S(1)} copy-done((bf16[384,1152]{1,0:T(8,128)(2,1)S(1)}, bf16[384,1152]{1,0:T(8,128)(2,1)}, u32[]{:S(2)}) %copy-start.1) | copy-done | bytes 884760
  45.8 0.6 %convolution_add_fusion = f32[512,768]{1,0:T(8,128)S(1)} fusion(bf16[512,384]{1,0:T(8,128)(2,1)S(1)} %bitcast.43, f32[768]{0:T(1024)S(1)} %slice.73, bf16[384,1152]{1,0:T(8,128)(2,1)S(1)} %copy-done.1), kind=kOutput, calls=%fused_computation.7 | convolution fusion | flops 302383104 | bytes 2560000 | tf_op jit(solution)/shard_map/dot_general | solution.py:349
  46.4 0.0 copy-start.6
  46.4 0.0 slice-done
  46.4 0.2 convolution_add_fusion.2
  46.7 0.9 %convolution_multiply_fusion = f32[4,32,128]{2,1,0:T(8,128)S(1)} fusion(f32[4,32,384]{2,1,0:T(8,128)S(1)} %bitcast.44, f32[4,128,768]{2,1,0:T(8,128)S(1)} %bitcast.40), kind=kOutput, calls=%fused_computation.17 | convolution fusion | flops 75513856 | bytes 1048576 | tf_op jit(solution)/shard_map/nqc,nkc->nqk/dot_general | solution.py:363
  47.6 0.2 fusion.51
  47.8 0.3 convolution_convert_fusion
  48.1 0.0 copy-done
  48.1 0.0 copy-done.6
  48.1 0.2 fusion.4
  48.3 0.1 fusion.46
  48.4 0.7 %copy.30 = bf16[2,2,1,32,384]{4,3,2,1,0:T(8,128)(2,1)} copy(bf16[2,2,1,32,384]{4,3,2,0,1:T(8,128)(2,1)S(1)} %fusion.46) | data formatting | bytes 196608 | tf_op jit(solution)/shard_map/convert_element_type | solution.py:382
  (12 shorter events, 0.2 us)
Async XLA Ops:
  0.0 48.1 %copy-start = (bf16[384,384]{1,0:T(8,128)(2,1)S(1)}, bf16[384,384]{1,0:T(8,128)(2,1)}, u32[]{:S(2)}) copy-start(bf16[384,384]{1,0:T(8,128)(2,1)} %param.20) | copy-start | bytes 884740
  0.0 24.4 %copy-start.7 = (s32[2,1]{0,1:T(1,128)S(1)}, s32[2,1]{0,1:T(1,128)}, u32[]{:S(2)}) copy-start(s32[2,1]{0,1:T(1,128)} %param.13) | copy-start | bytes 28
  0.0 30.8 %copy-start.2 = (f32[384]{0:T(512)S(1)}, f32[384]{0:T(512)}, u32[]{:S(2)}) copy-start(f32[384]{0:T(512)} %param.14) | copy-start | bytes 4612
  23.1 14.1 %collective-permute-start = (bf16[2,2,4,32,384]{4,3,2,0,1:T(8,128)(2,1)}, bf16[2,2,4,32,384]{4,3,2,0,1:T(8,128)(2,1)S(1)}, u32[]{:S(2)}, u32[]{:S(2)}) collective-permute-start(bf16[2,2,4,32,384]{4,3,2,0,1:T(8,128)(2,1)} %slice.77), channel_id=1, source_target_pairs={{0,4},{4,8},{8,12},{1,5},{5,9},{9,13},{2,6},{6,10},{10,14},{3,7},{... | collective-permute-start | bytes 1179656 | tf_op jit(solution)/shard_map/ppermute | solution.py:322
  25.2 12.0 %collective-permute-start.1 = (bf16[2,4,32,384]{3,2,1,0:T(8,128)(2,1)}, bf16[2,4,32,384]{3,2,1,0:T(8,128)(2,1)S(1)}, u32[]{:S(2)}, u32[]{:S(2)}) collective-permute-start(bf16[2,4,32,384]{3,2,1,0:T(8,128)(2,1)} %fusion.44), channel_id=1, source_target_pairs={{0,8},{4,12},{1,9},{5,13},{2,10},{6,14},{3,11},{7,15},{16,24},{20,... | collective-permute-start | bytes 589832 | tf_op jit(solution)/shard_map/ppermute | solution.py:323
  29.2 8.0 %collective-permute-start.2 = (s32[2]{0:T(128)S(1)}, s32[2]{0:T(128)S(1)}, u32[]{:S(2)}, u32[]{:S(2)}) collective-permute-start(s32[2]{0:T(128)S(1)} %bitcast.48), channel_id=1, source_target_pairs={{0,4},{4,8},{8,12},{1,5},{5,9},{9,13},{2,6},{6,10},{10,14},{3,7},{... | collective-permute-start | bytes 32 | tf_op jit(solution)/shard_map/ppermute | solution.py:315
  31.5 0.7 %copy-start.3 = (f32[1152]{0:T(1024)S(1)}, f32[1152]{0:T(1024)}, u32[]{:S(2)}) copy-start(f32[1152]{0:T(1024)} %param.19) | copy-start | bytes 13828
  44.0 0.7 %copy-start.4 = (f32[384]{0:T(512)S(1)}, f32[384]{0:T(512)}, u32[]{:S(2)}) copy-start(f32[384]{0:T(512)} %param.16) | copy-start | bytes 4612
  44.1 0.8 %copy-start.5 = (f32[384]{0:T(512)S(1)}, f32[384]{0:T(512)}, u32[]{:S(2)}) copy-start(f32[384]{0:T(512)} %param.17) | copy-start | bytes 4612
  44.7 1.2 %copy-start.1 = (bf16[384,1152]{1,0:T(8,128)(2,1)S(1)}, bf16[384,1152]{1,0:T(8,128)(2,1)}, u32[]{:S(2)}) copy-start(bf16[384,1152]{1,0:T(8,128)(2,1)} %param.18) | copy-start | bytes 2654212
  45.1 1.3 %slice-start = ((f32[1152]{0:T(1024)}), f32[384]{0:T(512)S(1)}, s32[]{:S(2)}) async-start(f32[1152]{0:T(1024)} %param.19), calls=%async_computation | async-start | bytes 4096 | tf_op jit(solution)/shard_map/slice | solution.py:361
  46.4 1.7 %copy-start.6 = (f32[384]{0:T(512)S(1)}, f32[384]{0:T(512)}, u32[]{:S(2)}) copy-start(f32[384]{0:T(512)} %param.21) | copy-start | bytes 4612

commit v16 on v15

--- a/solution.py
+++ b/solution.py
@@ -9,6 +9,7 @@
 from jax.experimental.pallas import tpu as pltpu
 
 EPSILON = 1e-06
+UNUSED_MARK = -100.0
 
 
 def prefix(part, axis, combine, identity):
@@ -312,23 +313,27 @@
     sections = lax.axis_size("tm")
     counts = lengths[:, 0]
     ahead = [(i, i + 1) for i in range(sections - 1)]
-    prev_counts = lax.ppermute(counts, "tm", ahead)
     both = jnp.concatenate([inner_input, segment_input], axis=0)
     both_all = lax.all_gather(both, "rows", axis=2, tiled=True)
     inner_all = both_all[:clip_count]
     segment_all = both_all[clip_count:]
     wide = (counts > 1)[:, None, None, None]
     last_raw = jnp.where(wide, inner_all[:, frame_count - 1], inner_all[:, 0])
-    prev_raw = lax.ppermute(inner_all, "tm", ahead)
+    marked = jnp.concatenate(
+        [
+            inner_all[:, : frame_count - 1],
+            jnp.where(wide, inner_all[:, frame_count - 1], UNUSED_MARK)[:, None],
+        ],
+        axis=1,
+    )
+    prev_raw = lax.ppermute(marked, "tm", ahead)
     before_raw = lax.ppermute(last_raw, "tm", [(i, i + 2) for i in range(sections - 2)])
     own = activate(inner_all, inner_gain)
     own_sum = own_conv(own, causal_weight)
-    own_sum, prev_raw, before_raw, prev_counts = lax.optimization_barrier(
-        (own_sum, prev_raw, before_raw, prev_counts)
-    )
+    own_sum, prev_raw, before_raw = lax.optimization_barrier((own_sum, prev_raw, before_raw))
     prev = activate(prev_raw, inner_gain)
     before = activate(before_raw, inner_gain)
-    prev_wide = (prev_counts > 1)[:, None, None, None]
+    prev_wide = (prev_raw[:, frame_count - 1, 0, 0, 0] > UNUSED_MARK / 2)[:, None, None, None]
     carried = jnp.stack(
         [
             jnp.where(prev_wide, prev[:, frame_count - 2], before),

time: 49.4 us -> 48.8 us (0.988)
  other arithmetic: 4.45 us -> 6.12 us
  starting transfers between devices: 6.7 us -> 5.3 us
  local copies, waits for them, and re-layouts: 4.11 us -> 3.34 us
    ppermute x2 -> x1, starting transfers between devices: 2.69 us -> 1.3 us  [gathered_body(): prev_raw = lax.ppermute(marked, 'tm', ahead)]
    concatenate x0 -> x1, other arithmetic: none -> 0.78 us  [gathered_body(): jnp.concatenate([inner_all[:, :frame_count - 1], jnp.where(wide, inner_al...]
    slice x1 -> x0, local copies, waits for them, and re-layouts: 0.78 us -> none  [gathered_body(): inner_all = both_all[:clip_count]]
    gt x1, other arithmetic: 0.01 us -> 0.66 us  [gathered_body(): wide = (counts > 1)[:, None, None, None]]
  transfers between devices with their start and end apart: 3 -> 2, of which waited for: 0 -> 0; matrix products, arithmetic and copies ran while one was open for 4% -> 4% of each run, Pallas kernels for 10% -> 10%
where the time goes in v16:
time: 48.8 us; the launch traced here: 48.6 us
  blocking collectives  21.3 us (44%)
  Pallas kernels  9.91 us (20%)
  other arithmetic  6.12 us (13%)
  starting transfers between devices  5.3 us (11%)
  local copies, waits for them, and re-layouts  3.34 us (7%)
  matrix products  2.24 us (5%)
    all_gather x1, blocking collectives, gathered_body(): both_all = lax.all_gather(both, 'rows', axis=2, tiled=True)  21.3 us
    pallas_call x2, Pallas kernels, conv_part(): pl.pallas_call(functools.partial(conv_part_kernel, plan, first_tap), in_s...  9.91 us
    ppermute x1, starting transfers between devices, gathered_body(): lax.ppermute(last_raw, 'tm', [(i, i + 2) for i in range(sections - 2)])  4 us
    unnamed x16, local copies, waits for them, and re-layouts  1.7 us
    ppermute x1, starting transfers between devices, gathered_body(): prev_raw = lax.ppermute(marked, 'tm', ahead)  1.3 us
    concatenate x1, other arithmetic, gathered_body(): both = jnp.concatenate([inner_input, segment_input], axis=0)  1.01 us
  transfers between devices with their start and end apart: 2, of which 0 were waited for; matrix products, arithmetic and copies ran while one was open for 4% of the time, Pallas kernels for 10%

profile of v16, /device:TPU:0, one launch (start us, length us, event | category | flops | bytes accessed | tf_op | source)
XLA Modules:
  0.0 48.6 jit_solution(15745303161658573217)
XLA Ops:
  0.0 0.0 copy-start
  0.0 1.0 %pad_maximum_fusion.3 = bf16[4,2,1,32,384]{4,3,2,1,0:T(8,128)(2,1)S(1)} fusion(bf16[2,2,1,32,384]{4,3,2,1,0:T(8,128)(2,1)} %param.11, bf16[2,2,1,32,384]{4,3,2,1,0:T(8,128)(2,1)} %param.12), kind=kLoop, calls=%fused_computation.70 | loop fusion | flops 98304 | bytes 393216 | tf_op jit(solution)/shard_map/concatenate | solution.py:316
  1.0 0.0 copy-start.2
  1.1 21.3 %all_gather.3 = bf16[4,2,4,32,384]{4,3,2,0,1:T(8,128)(2,1)S(1)} all-gather(bf16[4,2,1,32,384]{4,3,2,0,1:T(8,128)(2,1)S(1)} %copy.31), channel_id=1, replica_groups=mesh['clips'=2,'tm'=4,'rows'=4] {'rows'}, dimensions={2}, use_global_device_ids=true | all-gather | bytes 983040 | tf_op jit(solution)/shard_map/all_gather | solution.py:317
  22.4 0.7 %broadcast_compare_fusion = pred[2]{0:T(512)(128)(4,1)S(1)} fusion(s32[2,1]{0,1:T(1,128)} %param.13), kind=kLoop, calls=%fused_computation.87 | loop fusion | flops 2 | bytes 10 | tf_op jit(solution)/shard_map/gt | solution.py:320
  23.0 0.1 fusion.49
  23.1 0.8 %pad_maximum_fusion.2 = bf16[2,2,4,32,384]{4,3,2,0,1:T(8,128)(2,1)} fusion(bf16[2,1,4,32,384]{4,3,2,0,1:T(8,128)(2,1)S(1)} %get-tuple-element.14, bf16[2,1,4,32,384]{4,3,2,0,1:T(8,128)(2,1)S(1)} %get-tuple-element.13), kind=kLoop, calls=%fused_computation.65 | loop fusion | flops 196608 | bytes 786432 | tf_op jit(solution)/shard_map/concatenate | solution.py:322
  23.9 1.3 %collective-permute-start = (bf16[2,2,4,32,384]{4,3,2,0,1:T(8,128)(2,1)}, bf16[2,2,4,32,384]{4,3,2,0,1:T(8,128)(2,1)S(1)}, u32[]{:S(2)}, u32[]{:S(2)}) collective-permute-start(bf16[2,2,4,32,384]{4,3,2,0,1:T(8,128)(2,1)} %pad_maximum_fusion.2), channel_id=1, source_target_pairs={{0,4},{4,8},{8,12},{1,5},{5,9},{9,13},{2,6},{6,10},{10,14},{3,7},{... | collective-permute-start | bytes 1179656 | tf_op jit(solution)/shard_map/ppermute | solution.py:329
  25.2 0.8 %bitcast_select_fusion = bf16[2,4,32,384]{3,2,1,0:T(8,128)(2,1)} fusion(pred[2]{0:T(512)(128)(4,1)S(1)} %broadcast_compare_fusion, bf16[4,2,4,32,384]{4,3,2,0,1:T(8,128)(2,1)S(1)} %all_gather.3), kind=kLoop, calls=%fused_computation.71 | loop fusion | flops 98304 | bytes 589826 | tf_op jit(solution)/shard_map/jit(_where)/select_n | solution.py:321
  26.0 4.0 %collective-permute-start.1 = (bf16[2,4,32,384]{3,2,1,0:T(8,128)(2,1)}, bf16[2,4,32,384]{3,2,1,0:T(8,128)(2,1)S(1)}, u32[]{:S(2)}, u32[]{:S(2)}) collective-permute-start(bf16[2,4,32,384]{3,2,1,0:T(8,128)(2,1)} %bitcast_select_fusion), channel_id=1, source_target_pairs={{0,8},{4,12},{1,9},{5,13},{2,10},{6,14},{3,11},{7,15},{16,24},{20,... | collective-permute-start | bytes 589832 | tf_op jit(solution)/shard_map/ppermute | solution.py:330
  30.0 0.2 fusion.9
  30.1 0.0 copy-done.2
  30.2 0.3 fusion.16
  30.5 0.3 pad_slice_fusion.2
  30.8 0.0 copy-start.7
  30.8 0.0 copy-start.3
  30.8 0.2 pad_maximum_fusion
  31.0 0.5 copy-done.7
  31.5 0.1 copy-done.3
  31.5 0.1 copy.22.x_ref
  31.7 4.9 %shard_map.109 = f32[2,2,128,384]{3,2,1,0:T(8,128)S(1)} custom-call(bf16[2,2,6,32,1152]{4,3,2,1,0:T(8,128)(2,1)S(1)} %copy.22.x_ref, bf16[3,3,3,384,384]{4,3,2,1,0:T(8,128)(2,1)} %w_hbm.3), custom_call_target="tpu_custom_call" | custom-call | flops 2038431744 | bytes 7864320 | tf_op jit(solution)/shard_map/pallas_call | solution.py:235
  36.6 0.0 collective-permute-done.1
  36.6 0.0 collective-permute-done
  36.6 0.2 fusion.17
  36.8 0.1 compare_reduce_fusion
  36.9 0.3 fusion.24
  37.2 0.1 fusion.33
  37.4 0.1 fusion.43
  37.5 0.2 fusion.46
  37.7 0.2 fusion.30
  37.9 0.4 fusion.50
  38.3 0.2 pad_maximum_fusion.1.x_ref
  38.4 5.0 %shard_map.110 = f32[2,2,128,384]{3,2,1,0:T(8,128)S(1)} custom-call(bf16[2,2,6,32,1152]{4,3,2,1,0:T(8,128)(2,1)S(1)} %pad_maximum_fusion.1.x_ref, bf16[3,3,3,384,384]{4,3,2,1,0:T(8,128)(2,1)} %w_hbm.3), custom_call_target="tpu_custom_call" | custom-call | flops 2038431744 | bytes 7864320 | tf_op jit(solution)/shard_map/pallas_call | solution.py:235
  43.5 0.0 copy-start.4
  43.5 0.1 add.102
  43.6 0.0 copy-start.5
  43.6 0.1 copy.26
  43.6 0.5 %copy-done.4 = f32[384]{0:T(512)S(1)} copy-done((f32[384]{0:T(512)S(1)}, f32[384]{0:T(512)}, u32[]{:S(2)}) %copy-start.4) | copy-done | bytes 1560
  44.2 0.0 copy-start.1
  44.2 0.2 fusion.25
  44.4 0.0 copy-done.5
  44.4 0.2 fusion.27
  44.6 0.0 slice-start
  44.7 0.6 %copy-done.1 = bf16[384,1152]{1,0:T(8,128)(2,1)S(1)} copy-done((bf16[384,1152]{1,0:T(8,128)(2,1)S(1)}, bf16[384,1152]{1,0:T(8,128)(2,1)}, u32[]{:S(2)}) %copy-start.1) | copy-done | bytes 884760
  45.3 0.6 %convolution_add_fusion = f32[512,768]{1,0:T(8,128)S(1)} fusion(bf16[512,384]{1,0:T(8,128)(2,1)S(1)} %bitcast.39, f32[768]{0:T(1024)S(1)} %slice.79, bf16[384,1152]{1,0:T(8,128)(2,1)S(1)} %copy-done.1), kind=kOutput, calls=%fused_computation.7 | convolution fusion | flops 302383104 | bytes 2560000 | tf_op jit(solution)/shard_map/dot_general | solution.py:354
  45.9 0.0 copy-start.6
  45.9 0.0 slice-done
  45.9 0.2 convolution_add_fusion.2
  46.1 0.9 %convolution_multiply_fusion = f32[4,32,128]{2,1,0:T(8,128)S(1)} fusion(f32[4,32,384]{2,1,0:T(8,128)S(1)} %bitcast.40, f32[4,128,768]{2,1,0:T(8,128)S(1)} %bitcast.36), kind=kOutput, calls=%fused_computation.17 | convolution fusion | flops 75513856 | bytes 1048576 | tf_op jit(solution)/shard_map/nqc,nkc->nqk/dot_general | solution.py:368
  47.1 0.2 fusion.51
  47.3 0.3 convolution_convert_fusion
  47.6 0.0 copy-done
  47.6 0.0 copy-done.6
  47.6 0.2 fusion.4
  47.8 0.1 fusion.45
  47.9 0.7 %copy.30 = bf16[2,2,1,32,384]{4,3,2,1,0:T(8,128)(2,1)} copy(bf16[2,2,1,32,384]{4,3,2,0,1:T(8,128)(2,1)S(1)} %fusion.45) | data formatting | bytes 196608 | tf_op jit(solution)/shard_map/convert_element_type | solution.py:387
  (10 shorter events, 0.1 us)
Async XLA Ops:
  0.0 47.6 %copy-start = (bf16[384,384]{1,0:T(8,128)(2,1)S(1)}, bf16[384,384]{1,0:T(8,128)(2,1)}, u32[]{:S(2)}) copy-start(bf16[384,384]{1,0:T(8,128)(2,1)} %param.20) | copy-start | bytes 884740
  1.0 29.1 %copy-start.2 = (f32[384]{0:T(512)S(1)}, f32[384]{0:T(512)}, u32[]{:S(2)}) copy-start(f32[384]{0:T(512)} %param.14) | copy-start | bytes 4612
  23.9 12.7 %collective-permute-start = (bf16[2,2,4,32,384]{4,3,2,0,1:T(8,128)(2,1)}, bf16[2,2,4,32,384]{4,3,2,0,1:T(8,128)(2,1)S(1)}, u32[]{:S(2)}, u32[]{:S(2)}) collective-permute-start(bf16[2,2,4,32,384]{4,3,2,0,1:T(8,128)(2,1)} %pad_maximum_fusion.2), channel_id=1, source_target_pairs={{0,4},{4,8},{8,12},{1,5},{5,9},{9,13},{2,6},{6,10},{10,14},{3,7},{... | collective-permute-start | bytes 1179656 | tf_op jit(solution)/shard_map/ppermute | solution.py:329
  26.0 10.6 %collective-permute-start.1 = (bf16[2,4,32,384]{3,2,1,0:T(8,128)(2,1)}, bf16[2,4,32,384]{3,2,1,0:T(8,128)(2,1)S(1)}, u32[]{:S(2)}, u32[]{:S(2)}) collective-permute-start(bf16[2,4,32,384]{3,2,1,0:T(8,128)(2,1)} %bitcast_select_fusion), channel_id=1, source_target_pairs={{0,8},{4,12},{1,9},{5,13},{2,10},{6,14},{3,11},{7,15},{16,24},{20,... | collective-permute-start | bytes 589832 | tf_op jit(solution)/shard_map/ppermute | solution.py:330
  30.8 0.7 %copy-start.7 = (s32[2,1]{0,1:T(1,128)S(1)}, s32[2,1]{0,1:T(1,128)}, u32[]{:S(2)}) copy-start(s32[2,1]{0,1:T(1,128)} %param.13) | copy-start | bytes 28
  30.8 0.7 %copy-start.3 = (f32[1152]{0:T(1024)S(1)}, f32[1152]{0:T(1024)}, u32[]{:S(2)}) copy-start(f32[1152]{0:T(1024)} %param.19) | copy-start | bytes 13828
  43.5 0.7 %copy-start.4 = (f32[384]{0:T(512)S(1)}, f32[384]{0:T(512)}, u32[]{:S(2)}) copy-start(f32[384]{0:T(512)} %param.16) | copy-start | bytes 4612
  43.6 0.8 %copy-start.5 = (f32[384]{0:T(512)S(1)}, f32[384]{0:T(512)}, u32[]{:S(2)}) copy-start(f32[384]{0:T(512)} %param.17) | copy-start | bytes 4612
  44.2 1.2 %copy-start.1 = (bf16[384,1152]{1,0:T(8,128)(2,1)S(1)}, bf16[384,1152]{1,0:T(8,128)(2,1)}, u32[]{:S(2)}) copy-start(bf16[384,1152]{1,0:T(8,128)(2,1)} %param.18) | copy-start | bytes 2654212
  44.6 1.3 %slice-start = ((f32[1152]{0:T(1024)}), f32[384]{0:T(512)S(1)}, s32[]{:S(2)}) async-start(f32[1152]{0:T(1024)} %param.19), calls=%async_computation | async-start | bytes 4096 | tf_op jit(solution)/shard_map/slice | solution.py:366
  45.9 1.7 %copy-start.6 = (f32[384]{0:T(512)S(1)}, f32[384]{0:T(512)}, u32[]{:S(2)}) copy-start(f32[384]{0:T(512)} %param.21) | copy-start | bytes 4612

commit v17 on v16

--- a/solution.py
+++ b/solution.py
@@ -318,7 +318,6 @@
     inner_all = both_all[:clip_count]
     segment_all = both_all[clip_count:]
     wide = (counts > 1)[:, None, None, None]
-    last_raw = jnp.where(wide, inner_all[:, frame_count - 1], inner_all[:, 0])
     marked = jnp.concatenate(
         [
             inner_all[:, : frame_count - 1],
@@ -327,10 +326,12 @@
         axis=1,
     )
     prev_raw = lax.ppermute(marked, "tm", ahead)
-    before_raw = lax.ppermute(last_raw, "tm", [(i, i + 2) for i in range(sections - 2)])
+    before_all = lax.ppermute(marked, "tm", [(i, i + 2) for i in range(sections - 2)])
     own = activate(inner_all, inner_gain)
     own_sum = own_conv(own, causal_weight)
-    own_sum, prev_raw, before_raw = lax.optimization_barrier((own_sum, prev_raw, before_raw))
+    own_sum, prev_raw, before_all = lax.optimization_barrier((own_sum, prev_raw, before_all))
+    before_wide = (before_all[:, frame_count - 1, 0, 0, 0] > UNUSED_MARK / 2)[:, None, None, None]
+    before_raw = jnp.where(before_wide, before_all[:, frame_count - 1], before_all[:, 0])
     prev = activate(prev_raw, inner_gain)
     before = activate(before_raw, inner_gain)
     prev_wide = (prev_raw[:, frame_count - 1, 0, 0, 0] > UNUSED_MARK / 2)[:, None, None, None]

time: 48.8 us -> 55.6 us (1.14)
  the two profiles are of different devices: /device:TPU:0 before, /device:TPU:1 now
where the time goes in v17:
time: 55.6 us; the launch traced here: 55.3 us
  blocking collectives  18 us (32%)
  Pallas kernels  9.92 us (18%)
  starting transfers between devices  8.36 us (15%)
  other arithmetic  8.28 us (15%)
  waiting for transfers between devices  5.26 us (9%)
  local copies, waits for them, and re-layouts  2.84 us (5%)
  matrix products  2.24 us (4%)
    all_gather x1, blocking collectives, gathered_body(): both_all = lax.all_gather(both, 'rows', axis=2, tiled=True)  18 us
    pallas_call x2, Pallas kernels, conv_part(): pl.pallas_call(functools.partial(conv_part_kernel, plan, first_tap), in_s...  9.92 us
    ppermute x1, starting transfers between devices, gathered_body(): prev_raw = lax.ppermute(marked, 'tm', ahead)  6.31 us
    ppermute x1, waiting for transfers between devices, gathered_body(): lax.ppermute(marked, 'tm', [(i, i + 2) for i in range(sections - 2)])  5.26 us
    ppermute x1, starting transfers between devices, gathered_body(): lax.ppermute(marked, 'tm', [(i, i + 2) for i in range(sections - 2)])  2.05 us
    reduce_sum x4, other arithmetic, normalize(): jnp.mean(widened * widened, axis=-1, keepdims=True) + EPSILON  1.77 us
    select_n x1, other arithmetic, gathered_body(): jnp.where(prev_wide, prev[:, frame_count - 2], before)  1.42 us
    unnamed x16, local copies, waits for them, and re-layouts  1.2 us
  transfers between devices with their start and end apart: 2, of which 1 were waited for; matrix products, arithmetic and copies ran while one was open for 2% of the time, Pallas kernels for 9%

profile of v17, /device:TPU:1, one launch (start us, length us, event | category | flops | bytes accessed | tf_op | source)
XLA Modules:
  0.0 55.3 jit_solution(14567571761890491874)
XLA Ops:
  0.0 0.0 copy-start
  0.0 1.0 %pad_maximum_fusion.3 = bf16[4,2,1,32,384]{4,3,2,1,0:T(8,128)(2,1)S(1)} fusion(bf16[2,2,1,32,384]{4,3,2,1,0:T(8,128)(2,1)} %param.11, bf16[2,2,1,32,384]{4,3,2,1,0:T(8,128)(2,1)} %param.12), kind=kLoop, calls=%fused_computation.64 | loop fusion | flops 98304 | bytes 393216 | tf_op jit(solution)/shard_map/concatenate | solution.py:316
  1.0 0.0 copy-start.3
  1.0 0.0 copy-start.2
  1.1 18.0 %all_gather.3 = bf16[4,2,4,32,384]{4,3,2,0,1:T(8,128)(2,1)S(1)} all-gather(bf16[4,2,1,32,384]{4,3,2,0,1:T(8,128)(2,1)S(1)} %copy.33), channel_id=1, replica_groups=mesh['clips'=2,'tm'=4,'rows'=4] {'rows'}, dimensions={2}, use_global_device_ids=true | all-gather | bytes 983040 | tf_op jit(solution)/shard_map/all_gather | solution.py:317
  19.1 0.7 %broadcast_compare_fusion = pred[2]{0:T(512)(128)(4,1)S(1)} fusion(s32[2,1]{0,1:T(1,128)} %param.13), kind=kLoop, calls=%fused_computation.81 | loop fusion | flops 2 | bytes 10 | tf_op jit(solution)/shard_map/gt | solution.py:320
  19.8 0.1 fusion.40
  19.9 0.8 %pad_maximum_fusion.2 = bf16[2,2,4,32,384]{4,3,2,0,1:T(8,128)(2,1)} fusion(bf16[2,1,4,32,384]{4,3,2,0,1:T(8,128)(2,1)S(1)} %get-tuple-element.14, bf16[2,1,4,32,384]{4,3,2,0,1:T(8,128)(2,1)S(1)} %get-tuple-element.13), kind=kLoop, calls=%fused_computation.55 | loop fusion | flops 196608 | bytes 786432 | tf_op jit(solution)/shard_map/concatenate | solution.py:321
  20.6 6.3 %collective-permute-start = (bf16[2,2,4,32,384]{4,3,2,0,1:T(8,128)(2,1)}, bf16[2,2,4,32,384]{4,3,2,0,1:T(8,128)(2,1)S(1)}, u32[]{:S(2)}, u32[]{:S(2)}) collective-permute-start(bf16[2,2,4,32,384]{4,3,2,0,1:T(8,128)(2,1)} %pad_maximum_fusion.2), channel_id=1, source_target_pairs={{0,4},{4,8},{8,12},{1,5},{5,9},{9,13},{2,6},{6,10},{10,14},{3,7},{... | collective-permute-start | bytes 1179656 | tf_op jit(solution)/shard_map/ppermute | solution.py:328
  27.0 2.0 %collective-permute-start.1 = (bf16[2,2,4,32,384]{4,3,2,0,1:T(8,128)(2,1)}, bf16[2,2,4,32,384]{4,3,2,0,1:T(8,128)(2,1)}, u32[]{:S(2)}, u32[]{:S(2)}) collective-permute-start(bf16[2,2,4,32,384]{4,3,2,0,1:T(8,128)(2,1)} %pad_maximum_fusion.2), channel_id=1, source_target_pairs={{0,8},{4,12},{1,9},{5,13},{2,10},{6,14},{3,11},{7,15},{16,24},{20,... | collective-permute-start | bytes 1179656 | tf_op jit(solution)/shard_map/ppermute | solution.py:329
  29.0 0.2 fusion.9
  29.2 0.0 copy-done.3
  29.2 0.0 copy-done.2
  29.2 0.3 fusion.16
  29.5 0.3 pad_slice_fusion.2
  29.9 0.2 pad_maximum_fusion
  30.0 0.1 copy.23.x_ref
  30.2 0.0 copy-start.7
  30.2 4.9 %shard_map.109 = f32[2,2,128,384]{3,2,1,0:T(8,128)S(1)} custom-call(bf16[2,2,6,32,1152]{4,3,2,1,0:T(8,128)(2,1)S(1)} %copy.23.x_ref, bf16[3,3,3,384,384]{4,3,2,1,0:T(8,128)(2,1)} %w_hbm.3), custom_call_target="tpu_custom_call" | custom-call | flops 2038431744 | bytes 7864320 | tf_op jit(solution)/shard_map/pallas_call | solution.py:235
  35.1 0.0 copy-done.7
  35.1 0.0 collective-permute-done
  35.1 5.3 %collective-permute-done.1 = bf16[2,2,4,32,384]{4,3,2,0,1:T(8,128)(2,1)} collective-permute-done((bf16[2,2,4,32,384]{4,3,2,0,1:T(8,128)(2,1)}, bf16[2,2,4,32,384]{4,3,2,0,1:T(8,128)(2,1)}, u32[]{:S(2)}, u32[]{:S(2)}) %collective-permute-start.1) | collective-permute-done | bytes 393248 | tf_op jit(solution)/shard_map/ppermute | solution.py:329
  40.4 0.2 fusion.17
  40.6 0.9 %compare_reduce_fusion = (pred[2]{0:T(512)(128)(4,1)S(1)}, pred[2]{0:T(512)(128)(4,1)S(1)}) fusion(bf16[2,2,4,32,384]{4,3,2,0,1:T(8,128)(2,1)} %collective-permute-done.1, bf16[2,2,4,32,384]{4,3,2,0,1:T(8,128)(2,1)S(1)} %collective-permute-done), kind=kLoop, calls=%fused_computation.76 | loop fusion | flops 4 | bytes 12 | tf_op jit(solution)/shard_map/gt | solution.py:333
  41.4 1.2 %multiply_reduce_fusion = f32[2,4,32]{2,1,0:T(4,128)S(1)} fusion(pred[2]{0:T(512)(128)(4,1)S(1)} %get-tuple-element.23, bf16[2,2,4,32,384]{4,3,2,0,1:T(8,128)(2,1)} %collective-permute-done.1), kind=kLoop, calls=%fused_computation.57 | loop fusion | flops 392960 | bytes 394242 | tf_op jit(solution)/shard_map/reduce_sum | solution.py:55
  42.7 0.3 fusion.24
  43.0 1.4 %fusion.34 = (bf16[2,1,4,32,384]{4,3,2,1,0:T(8,128)(2,1)S(1)}, bf16[2,1,4,32,384]{4,3,2,1,0:T(8,128)(2,1)S(1)}) fusion(f32[384]{0:T(512)S(1)} %copy-done.2, f32[2,4,32]{2,1,0:T(4,128)S(1)} %add_rsqrt_fusion.3, pred[2]{0:T(512)(128)(4,1)S(1)} %get-tuple-element.23, pred[2]{0:T(512)(128)(4,1)S(1)} %get-tuple-element.24, ...), kind=kLoop, calls=%fused_computation.59 | loop fusion | flops 1081344 | bytes 1182212 | tf_op jit(solution)/shard_map/jit(_where)/select_n | solution.py:340
  44.4 0.2 fusion.30
  44.6 0.4 fusion.41
  45.0 0.2 pad_maximum_fusion.1.x_ref
  45.2 5.0 %shard_map.110 = f32[2,2,128,384]{3,2,1,0:T(8,128)S(1)} custom-call(bf16[2,2,6,32,1152]{4,3,2,1,0:T(8,128)(2,1)S(1)} %pad_maximum_fusion.1.x_ref, bf16[3,3,3,384,384]{4,3,2,1,0:T(8,128)(2,1)} %w_hbm.3), custom_call_target="tpu_custom_call" | custom-call | flops 2038431744 | bytes 7864320 | tf_op jit(solution)/shard_map/pallas_call | solution.py:235
  50.2 0.0 copy-start.4
  50.2 0.1 add.103
  50.3 0.0 copy-start.5
  50.3 0.1 copy.28
  50.4 0.5 copy-done.4
  50.9 0.0 copy-start.1
  50.9 0.2 fusion.25
  51.1 0.0 copy-done.5
  51.1 0.2 fusion.27
  51.3 0.0 slice-start
  51.4 0.6 %copy-done.1 = bf16[384,1152]{1,0:T(8,128)(2,1)S(1)} copy-done((bf16[384,1152]{1,0:T(8,128)(2,1)S(1)}, bf16[384,1152]{1,0:T(8,128)(2,1)}, u32[]{:S(2)}) %copy-start.1) | copy-done | bytes 884760
  52.1 0.6 %convolution_add_fusion = f32[512,768]{1,0:T(8,128)S(1)} fusion(bf16[512,384]{1,0:T(8,128)(2,1)S(1)} %bitcast.40, f32[768]{0:T(1024)S(1)} %slice.89, bf16[384,1152]{1,0:T(8,128)(2,1)S(1)} %copy-done.1), kind=kOutput, calls=%fused_computation.7 | convolution fusion | flops 302383104 | bytes 2560000 | tf_op jit(solution)/shard_map/dot_general | solution.py:355
  52.6 0.0 copy-start.6
  52.6 0.0 slice-done
  52.6 0.2 convolution_add_fusion.2
  52.9 0.9 %convolution_multiply_fusion = f32[4,32,128]{2,1,0:T(8,128)S(1)} fusion(f32[4,32,384]{2,1,0:T(8,128)S(1)} %bitcast.41, f32[4,128,768]{2,1,0:T(8,128)S(1)} %bitcast.37), kind=kOutput, calls=%fused_computation.17 | convolution fusion | flops 75513856 | bytes 1048576 | tf_op jit(solution)/shard_map/nqc,nkc->nqk/dot_general | solution.py:369
  53.8 0.2 fusion.42
  54.0 0.3 convolution_convert_fusion
  54.3 0.0 copy-done
  54.3 0.0 copy-done.6
  54.3 0.2 fusion.4
  54.5 0.1 fusion.37
  54.6 0.7 %copy.32 = bf16[2,2,1,32,384]{4,3,2,1,0:T(8,128)(2,1)} copy(bf16[2,2,1,32,384]{4,3,2,0,1:T(8,128)(2,1)S(1)} %fusion.37) | data formatting | bytes 196608 | tf_op jit(solution)/shard_map/convert_element_type | solution.py:388
  (10 shorter events, 0.1 us)
Async XLA Ops:
  0.0 54.3 %copy-start = (bf16[384,384]{1,0:T(8,128)(2,1)S(1)}, bf16[384,384]{1,0:T(8,128)(2,1)}, u32[]{:S(2)}) copy-start(bf16[384,384]{1,0:T(8,128)(2,1)} %param.20) | copy-start | bytes 884740
  1.0 28.2 %copy-start.3 = (f32[1152]{0:T(1024)S(1)}, f32[1152]{0:T(1024)}, u32[]{:S(2)}) copy-start(f32[1152]{0:T(1024)} %param.19) | copy-start | bytes 13828
  1.0 28.2 %copy-start.2 = (f32[384]{0:T(512)S(1)}, f32[384]{0:T(512)}, u32[]{:S(2)}) copy-start(f32[384]{0:T(512)} %param.14) | copy-start | bytes 4612
  20.6 14.5 %collective-permute-start = (bf16[2,2,4,32,384]{4,3,2,0,1:T(8,128)(2,1)}, bf16[2,2,4,32,384]{4,3,2,0,1:T(8,128)(2,1)S(1)}, u32[]{:S(2)}, u32[]{:S(2)}) collective-permute-start(bf16[2,2,4,32,384]{4,3,2,0,1:T(8,128)(2,1)} %pad_maximum_fusion.2), channel_id=1, source_target_pairs={{0,4},{4,8},{8,12},{1,5},{5,9},{9,13},{2,6},{6,10},{10,14},{3,7},{... | collective-permute-start | bytes 1179656 | tf_op jit(solution)/shard_map/ppermute | solution.py:328
  27.0 13.4 %collective-permute-start.1 = (bf16[2,2,4,32,384]{4,3,2,0,1:T(8,128)(2,1)}, bf16[2,2,4,32,384]{4,3,2,0,1:T(8,128)(2,1)}, u32[]{:S(2)}, u32[]{:S(2)}) collective-permute-start(bf16[2,2,4,32,384]{4,3,2,0,1:T(8,128)(2,1)} %pad_maximum_fusion.2), channel_id=1, source_target_pairs={{0,8},{4,12},{1,9},{5,13},{2,10},{6,14},{3,11},{7,15},{16,24},{20,... | collective-permute-start | bytes 1179656 | tf_op jit(solution)/shard_map/ppermute | solution.py:329
  30.2 4.9 %copy-start.7 = (s32[2,1]{0,1:T(1,128)S(1)}, s32[2,1]{0,1:T(1,128)}, u32[]{:S(2)}) copy-start(s32[2,1]{0,1:T(1,128)} %param.13) | copy-start | bytes 28
  50.2 0.7 %copy-start.4 = (f32[384]{0:T(512)S(1)}, f32[384]{0:T(512)}, u32[]{:S(2)}) copy-start(f32[384]{0:T(512)} %param.16) | copy-start | bytes 4612
  50.3 0.8 %copy-start.5 = (f32[384]{0:T(512)S(1)}, f32[384]{0:T(512)}, u32[]{:S(2)}) copy-start(f32[384]{0:T(512)} %param.17) | copy-start | bytes 4612
  50.9 1.2 %copy-start.1 = (bf16[384,1152]{1,0:T(8,128)(2,1)S(1)}, bf16[384,1152]{1,0:T(8,128)(2,1)}, u32[]{:S(2)}) copy-start(bf16[384,1152]{1,0:T(8,128)(2,1)} %param.18) | copy-start | bytes 2654212
  51.3 1.3 %slice-start = ((f32[1152]{0:T(1024)}), f32[384]{0:T(512)S(1)}, s32[]{:S(2)}) async-start(f32[1152]{0:T(1024)} %param.19), calls=%async_computation | async-start | bytes 4096 | tf_op jit(solution)/shard_map/slice | solution.py:367
  52.6 1.7 %copy-start.6 = (f32[384]{0:T(512)S(1)}, f32[384]{0:T(512)}, u32[]{:S(2)}) copy-start(f32[384]{0:T(512)} %param.21) | copy-start | bytes 4612

commit v18 on v16

--- a/solution.py
+++ b/solution.py
@@ -319,13 +319,8 @@
     segment_all = both_all[clip_count:]
     wide = (counts > 1)[:, None, None, None]
     last_raw = jnp.where(wide, inner_all[:, frame_count - 1], inner_all[:, 0])
-    marked = jnp.concatenate(
-        [
-            inner_all[:, : frame_count - 1],
-            jnp.where(wide, inner_all[:, frame_count - 1], UNUSED_MARK)[:, None],
-        ],
-        axis=1,
-    )
+    live = jnp.arange(frame_count, dtype=jnp.int32)[None, :] < counts[:, None]
+    marked = jnp.where(live[:, :, None, None, None], inner_all, UNUSED_MARK).astype(inner_all.dtype)
     prev_raw = lax.ppermute(marked, "tm", ahead)
     before_raw = lax.ppermute(last_raw, "tm", [(i, i + 2) for i in range(sections - 2)])
     own = activate(inner_all, inner_gain)

time: 48.8 us -> 48.9 us (level)
    select_n x0 -> x1, other arithmetic: none -> 0.85 us  [gathered_body(): jnp.where(live[:, :, None, None, None], inner_all, UNUSED_MARK)]
    concatenate x1 -> x0, other arithmetic: 0.78 us -> none  [gathered_body(): jnp.concatenate([inner_all[:, :frame_count - 1], jnp.where(wide, inner_al...]
    convert_element_type x1, other arithmetic: 0.01 us -> 0.73 us  [gathered_body(): (jnp.arange(frame_count, dtype=jnp.int32)[None, :] < counts[:, None]).ast...]
    gt x1, other arithmetic: 0.66 us -> 0.01 us  [gathered_body(): wide = (counts > 1)[:, None, None, None]]
where the time goes in v18:
time: 48.9 us; the launch traced here: 48.6 us
  blocking collectives  21.3 us (44%)
  Pallas kernels  9.91 us (20%)
  other arithmetic  6.13 us (13%)
  starting transfers between devices  5.3 us (11%)
  local copies, waits for them, and re-layouts  3.34 us (7%)
  matrix products  2.24 us (5%)
    all_gather x1, blocking collectives, gathered_body(): both_all = lax.all_gather(both, 'rows', axis=2, tiled=True)  21.3 us
    pallas_call x2, Pallas kernels, conv_part(): pl.pallas_call(functools.partial(conv_part_kernel, plan, first_tap), in_s...  9.91 us
    ppermute x1, starting transfers between devices, gathered_body(): lax.ppermute(last_raw, 'tm', [(i, i + 2) for i in range(sections - 2)])  4 us
    unnamed x16, local copies, waits for them, and re-layouts  1.69 us
    ppermute x1, starting transfers between devices, gathered_body(): prev_raw = lax.ppermute(marked, 'tm', ahead)  1.3 us
  transfers between devices with their start and end apart: 2, of which 0 were waited for; matrix products, arithmetic and copies ran while one was open for 4% of the time, Pallas kernels for 10%

profile of v18, /device:TPU:0, one launch (start us, length us, event | category | flops | bytes accessed | tf_op | source)
XLA Modules:
  0.0 48.6 jit_solution(9148566362657705046)
XLA Ops:
  0.0 0.0 copy-start
  0.0 0.0 copy-start.7
  0.0 0.7 %fusion.50 = (f32[2,2]{0,1:T(2,128)S(1)}, pred[2,2]{0,1:T(4,128)(4,1)S(1)}) fusion(s32[2]{0:T(128)} %bitcast.48), kind=kLoop, calls=%fused_computation.89 | loop fusion | flops 8 | bytes 28 | tf_op jit(solution)/shard_map/convert_element_type | solution.py:378
  0.7 0.0 copy-start.2
  0.7 1.0 %pad_maximum_fusion.2 = bf16[4,2,1,32,384]{4,3,2,1,0:T(8,128)(2,1)S(1)} fusion(bf16[2,2,1,32,384]{4,3,2,1,0:T(8,128)(2,1)} %param.11, bf16[2,2,1,32,384]{4,3,2,1,0:T(8,128)(2,1)} %param.12), kind=kLoop, calls=%fused_computation.73 | loop fusion | flops 98304 | bytes 393216 | tf_op jit(solution)/shard_map/concatenate | solution.py:316
  1.8 21.3 %all_gather.3 = bf16[4,2,4,32,384]{4,3,2,0,1:T(8,128)(2,1)S(1)} all-gather(bf16[4,2,1,32,384]{4,3,2,0,1:T(8,128)(2,1)S(1)} %copy.31), channel_id=1, replica_groups=mesh['clips'=2,'tm'=4,'rows'=4] {'rows'}, dimensions={2}, use_global_device_ids=true | all-gather | bytes 983040 | tf_op jit(solution)/shard_map/all_gather | solution.py:317
  23.0 0.9 %broadcast_select_fusion = bf16[2,2,4,32,384]{4,3,2,0,1:T(8,128)(2,1)} fusion(pred[2,2]{0,1:T(4,128)(4,1)S(1)} %get-tuple-element.20, bf16[4,2,4,32,384]{4,3,2,0,1:T(8,128)(2,1)S(1)} %all_gather.3), kind=kLoop, calls=%fused_computation.65 | loop fusion | flops 196608 | bytes 786436 | tf_op jit(solution)/shard_map/jit(_where)/select_n | solution.py:323
  23.9 1.3 %collective-permute-start = (bf16[2,2,4,32,384]{4,3,2,0,1:T(8,128)(2,1)}, bf16[2,2,4,32,384]{4,3,2,0,1:T(8,128)(2,1)S(1)}, u32[]{:S(2)}, u32[]{:S(2)}) collective-permute-start(bf16[2,2,4,32,384]{4,3,2,0,1:T(8,128)(2,1)} %broadcast_select_fusion), channel_id=1, source_target_pairs={{0,4},{4,8},{8,12},{1,5},{5,9},{9,13},{2,6},{6,10},{10,14},{3,7},{... | collective-permute-start | bytes 1179656 | tf_op jit(solution)/shard_map/ppermute | solution.py:324
  25.2 0.0 copy-done.7
  25.2 0.8 %fusion.44 = bf16[2,4,32,384]{3,2,1,0:T(8,128)(2,1)} fusion(bf16[4,2,4,32,384]{4,3,2,0,1:T(8,128)(2,1)S(1)} %all_gather.3, pred[2]{0:T(512)(128)(4,1)S(1)} %broadcast_compare_fusion), kind=kLoop, calls=%fused_computation.71 | loop fusion | flops 98304 | bytes 589826 | tf_op jit(solution)/shard_map/jit(_where)/select_n | solution.py:321
  26.0 4.0 %collective-permute-start.1 = (bf16[2,4,32,384]{3,2,1,0:T(8,128)(2,1)}, bf16[2,4,32,384]{3,2,1,0:T(8,128)(2,1)S(1)}, u32[]{:S(2)}, u32[]{:S(2)}) collective-permute-start(bf16[2,4,32,384]{3,2,1,0:T(8,128)(2,1)} %fusion.44), channel_id=1, source_target_pairs={{0,8},{4,12},{1,9},{5,13},{2,10},{6,14},{3,11},{7,15},{16,24},{20,... | collective-permute-start | bytes 589832 | tf_op jit(solution)/shard_map/ppermute | solution.py:325
  30.0 0.2 fusion.9
  30.2 0.0 copy-done.2
  30.2 0.3 fusion.16
  30.5 0.3 pad_slice_fusion.2
  30.8 0.0 copy-start.3
  30.8 0.2 pad_maximum_fusion
  31.0 0.5 %copy-done.3 = f32[1152]{0:T(1024)S(1)} copy-done((f32[1152]{0:T(1024)S(1)}, f32[1152]{0:T(1024)}, u32[]{:S(2)}) %copy-start.3) | copy-done | bytes 4632
  31.5 0.1 copy.22.x_ref
  31.7 4.9 %shard_map.112 = f32[2,2,128,384]{3,2,1,0:T(8,128)S(1)} custom-call(bf16[2,2,6,32,1152]{4,3,2,1,0:T(8,128)(2,1)S(1)} %copy.22.x_ref, bf16[3,3,3,384,384]{4,3,2,1,0:T(8,128)(2,1)} %w_hbm.3), custom_call_target="tpu_custom_call" | custom-call | flops 2038431744 | bytes 7864320 | tf_op jit(solution)/shard_map/pallas_call | solution.py:235
  36.6 0.0 collective-permute-done.1
  36.6 0.0 collective-permute-done
  36.6 0.2 fusion.17
  36.8 0.1 compare_reduce_fusion
  36.9 0.3 fusion.24
  37.2 0.1 fusion.33
  37.4 0.1 fusion.43
  37.5 0.2 fusion.47
  37.7 0.2 fusion.30
  37.9 0.4 fusion.51
  38.3 0.2 pad_maximum_fusion.1.x_ref
  38.4 5.0 %shard_map.113 = f32[2,2,128,384]{3,2,1,0:T(8,128)S(1)} custom-call(bf16[2,2,6,32,1152]{4,3,2,1,0:T(8,128)(2,1)S(1)} %pad_maximum_fusion.1.x_ref, bf16[3,3,3,384,384]{4,3,2,1,0:T(8,128)(2,1)} %w_hbm.3), custom_call_target="tpu_custom_call" | custom-call | flops 2038431744 | bytes 7864320 | tf_op jit(solution)/shard_map/pallas_call | solution.py:235
  43.5 0.0 copy-start.4
  43.5 0.1 add.102
  43.6 0.0 copy-start.5
  43.6 0.1 copy.26
  43.6 0.5 %copy-done.4 = f32[384]{0:T(512)S(1)} copy-done((f32[384]{0:T(512)S(1)}, f32[384]{0:T(512)}, u32[]{:S(2)}) %copy-start.4) | copy-done | bytes 1560
  44.2 0.0 copy-start.1
  44.2 0.2 fusion.25
  44.4 0.0 copy-done.5
  44.4 0.2 fusion.27
  44.6 0.0 slice-start
  44.7 0.6 %copy-done.1 = bf16[384,1152]{1,0:T(8,128)(2,1)S(1)} copy-done((bf16[384,1152]{1,0:T(8,128)(2,1)S(1)}, bf16[384,1152]{1,0:T(8,128)(2,1)}, u32[]{:S(2)}) %copy-start.1) | copy-done | bytes 884760
  45.3 0.6 %convolution_add_fusion = f32[512,768]{1,0:T(8,128)S(1)} fusion(bf16[512,384]{1,0:T(8,128)(2,1)S(1)} %bitcast.43, f32[768]{0:T(1024)S(1)} %slice.77, bf16[384,1152]{1,0:T(8,128)(2,1)S(1)} %copy-done.1), kind=kOutput, calls=%fused_computation.7 | convolution fusion | flops 302383104 | bytes 2560000 | tf_op jit(solution)/shard_map/dot_general | solution.py:349
  45.9 0.0 copy-start.6
  45.9 0.0 slice-done
  45.9 0.2 convolution_add_fusion.2
  46.1 0.9 %convolution_multiply_fusion = f32[4,32,128]{2,1,0:T(8,128)S(1)} fusion(f32[4,32,384]{2,1,0:T(8,128)S(1)} %bitcast.44, f32[4,128,768]{2,1,0:T(8,128)S(1)} %bitcast.40), kind=kOutput, calls=%fused_computation.17 | convolution fusion | flops 75513856 | bytes 1048576 | tf_op jit(solution)/shard_map/nqc,nkc->nqk/dot_general | solution.py:363
  47.1 0.2 fusion.52
  47.3 0.3 convolution_convert_fusion
  47.6 0.0 copy-done
  47.6 0.0 copy-done.6
  47.6 0.2 fusion.4
  47.8 0.1 fusion.46
  47.9 0.7 %copy.30 = bf16[2,2,1,32,384]{4,3,2,1,0:T(8,128)(2,1)} copy(bf16[2,2,1,32,384]{4,3,2,0,1:T(8,128)(2,1)S(1)} %fusion.46) | data formatting | bytes 196608 | tf_op jit(solution)/shard_map/convert_element_type | solution.py:382
  (10 shorter events, 0.1 us)
Async XLA Ops:
  0.0 47.6 %copy-start = (bf16[384,384]{1,0:T(8,128)(2,1)S(1)}, bf16[384,384]{1,0:T(8,128)(2,1)}, u32[]{:S(2)}) copy-start(bf16[384,384]{1,0:T(8,128)(2,1)} %param.20) | copy-start | bytes 884740
  0.0 25.2 %copy-start.7 = (s32[2,1]{0,1:T(1,128)S(1)}, s32[2,1]{0,1:T(1,128)}, u32[]{:S(2)}) copy-start(s32[2,1]{0,1:T(1,128)} %param.13) | copy-start | bytes 28
  0.7 29.4 %copy-start.2 = (f32[384]{0:T(512)S(1)}, f32[384]{0:T(512)}, u32[]{:S(2)}) copy-start(f32[384]{0:T(512)} %param.14) | copy-start | bytes 4612
  23.9 12.7 %collective-permute-start = (bf16[2,2,4,32,384]{4,3,2,0,1:T(8,128)(2,1)}, bf16[2,2,4,32,384]{4,3,2,0,1:T(8,128)(2,1)S(1)}, u32[]{:S(2)}, u32[]{:S(2)}) collective-permute-start(bf16[2,2,4,32,384]{4,3,2,0,1:T(8,128)(2,1)} %broadcast_select_fusion), channel_id=1, source_target_pairs={{0,4},{4,8},{8,12},{1,5},{5,9},{9,13},{2,6},{6,10},{10,14},{3,7},{... | collective-permute-start | bytes 1179656 | tf_op jit(solution)/shard_map/ppermute | solution.py:324
  26.0 10.6 %collective-permute-start.1 = (bf16[2,4,32,384]{3,2,1,0:T(8,128)(2,1)}, bf16[2,4,32,384]{3,2,1,0:T(8,128)(2,1)S(1)}, u32[]{:S(2)}, u32[]{:S(2)}) collective-permute-start(bf16[2,4,32,384]{3,2,1,0:T(8,128)(2,1)} %fusion.44), channel_id=1, source_target_pairs={{0,8},{4,12},{1,9},{5,13},{2,10},{6,14},{3,11},{7,15},{16,24},{20,... | collective-permute-start | bytes 589832 | tf_op jit(solution)/shard_map/ppermute | solution.py:325
  30.8 0.7 %copy-start.3 = (f32[1152]{0:T(1024)S(1)}, f32[1152]{0:T(1024)}, u32[]{:S(2)}) copy-start(f32[1152]{0:T(1024)} %param.19) | copy-start | bytes 13828
  43.5 0.7 %copy-start.4 = (f32[384]{0:T(512)S(1)}, f32[384]{0:T(512)}, u32[]{:S(2)}) copy-start(f32[384]{0:T(512)} %param.16) | copy-start | bytes 4612
  43.6 0.8 %copy-start.5 = (f32[384]{0:T(512)S(1)}, f32[384]{0:T(512)}, u32[]{:S(2)}) copy-start(f32[384]{0:T(512)} %param.17) | copy-start | bytes 4612
  44.2 1.2 %copy-start.1 = (bf16[384,1152]{1,0:T(8,128)(2,1)S(1)}, bf16[384,1152]{1,0:T(8,128)(2,1)}, u32[]{:S(2)}) copy-start(bf16[384,1152]{1,0:T(8,128)(2,1)} %param.18) | copy-start | bytes 2654212
  44.6 1.3 %slice-start = ((f32[1152]{0:T(1024)}), f32[384]{0:T(512)S(1)}, s32[]{:S(2)}) async-start(f32[1152]{0:T(1024)} %param.19), calls=%async_computation | async-start | bytes 4096 | tf_op jit(solution)/shard_map/slice | solution.py:361
  45.9 1.7 %copy-start.6 = (f32[384]{0:T(512)S(1)}, f32[384]{0:T(512)}, u32[]{:S(2)}) copy-start(f32[384]{0:T(512)} %param.21) | copy-start | bytes 4612

commit v19 on v16

--- a/solution.py
+++ b/solution.py
@@ -223,12 +223,18 @@
                     written.add(target)
 
 
-def conv_part(frames, causal_weight, plan, first_tap, slots):
+def column_taps(frames):
+    columns = frames.shape[3]
+    padded = jnp.pad(frames, ((0, 0), (0, 0), (1, 1), (1, 1), (0, 0)))
+    return jnp.concatenate(
+        [padded[:, :, :, kw : kw + columns] for kw in range(3)], axis=-1
+    )
+
+
+def conv_part(frames, causal_weight, plan, first_tap, slots, taps=None):
     clips, held, height, columns, channels = frames.shape
-    padded = jnp.pad(frames, ((0, 0), (0, 0), (1, 1), (1, 1), (0, 0)))
-    taps = jnp.concatenate(
-        [padded[:, :, :, kw : kw + columns] for kw in range(3)], axis=-1
-    )
+    if taps is None:
+        taps = column_taps(frames)
     places = height * columns
     dots = sum(count for _, _, count in plan) * 3
     blocks = len(plan) * 3
@@ -279,10 +285,10 @@
     return tuple(runs), taps[0]
 
 
-def own_conv(own_frames, causal_weight):
+def own_conv(own_frames, causal_weight, taps=None):
     own_table, _ = conv_plans(own_frames.shape[1])
     own_plan, own_first = plan_of(own_table)
-    return conv_part(own_frames, causal_weight, own_plan, own_first, own_frames.shape[1])
+    return conv_part(own_frames, causal_weight, own_plan, own_first, own_frames.shape[1], taps)
 
 
 def carried_conv(carried_frames, causal_weight, slots):
@@ -327,9 +333,11 @@
         axis=1,
     )
     prev_raw = lax.ppermute(marked, "tm", ahead)
+    own = activate(inner_all, inner_gain)
+    own_taps = column_taps(own)
+    own_taps, last_raw = lax.optimization_barrier((own_taps, last_raw))
     before_raw = lax.ppermute(last_raw, "tm", [(i, i + 2) for i in range(sections - 2)])
-    own = activate(inner_all, inner_gain)
-    own_sum = own_conv(own, causal_weight)
+    own_sum = own_conv(own, causal_weight, own_taps)
     own_sum, prev_raw, before_raw = lax.optimization_barrier((own_sum, prev_raw, before_raw))
     prev = activate(prev_raw, inner_gain)
     before = activate(before_raw, inner_gain)

time: 48.8 us -> 47.1 us (0.965)
  other arithmetic: 6.12 us -> 5.47 us
  starting transfers between devices: 5.3 us -> 4.71 us
  local copies, waits for them, and re-layouts: 3.34 us -> 2.84 us
    gt x1, other arithmetic: 0.66 us -> 0.01 us  [gathered_body(): wide = (counts > 1)[:, None, None, None]]
    ppermute x1, starting transfers between devices: 4 us -> 3.41 us  [gathered_body(): lax.ppermute(last_raw, 'tm', [(i, i + 2) for i in range(sections - 2)])]
    unnamed x16, local copies, waits for them, and re-layouts: 1.7 us -> 1.19 us
  transfers between devices with their start and end apart: 2 -> 2, of which waited for: 0 -> 0; matrix products, arithmetic and copies ran while one was open for 4% -> 2% of each run, Pallas kernels for 10% -> 10%
where the time goes in v19:
time: 47.1 us; the launch traced here: 46.8 us
  blocking collectives  21.3 us (45%)
  Pallas kernels  9.92 us (21%)
  other arithmetic  5.47 us (12%)
  starting transfers between devices  4.71 us (10%)
  local copies, waits for them, and re-layouts  2.84 us (6%)
  matrix products  2.24 us (5%)
    all_gather x1, blocking collectives, gathered_body(): both_all = lax.all_gather(both, 'rows', axis=2, tiled=True)  21.3 us
    pallas_call x2, Pallas kernels, conv_part(): pl.pallas_call(functools.partial(conv_part_kernel, plan, first_tap), in_s...  9.92 us
    ppermute x1, starting transfers between devices, gathered_body(): lax.ppermute(last_raw, 'tm', [(i, i + 2) for i in range(sections - 2)])  3.41 us
    ppermute x1, starting transfers between devices, gathered_body(): prev_raw = lax.ppermute(marked, 'tm', ahead)  1.3 us
    unnamed x16, local copies, waits for them, and re-layouts  1.19 us
    concatenate x1, other arithmetic, gathered_body(): both = jnp.concatenate([inner_input, segment_input], axis=0)  1.02 us
    dot_general x1, matrix products, gathered_body(): jnp.einsum('nqc,nkc->nqk', queries, key_vectors, precision=lax.Precision....  0.95 us
  transfers between devices with their start and end apart: 2, of which 0 were waited for; matrix products, arithmetic and copies ran while one was open for 2% of the time, Pallas kernels for 10%

profile of v19, /device:TPU:0, one launch (start us, length us, event | category | flops | bytes accessed | tf_op | source)
XLA Modules:
  0.0 46.8 jit_solution(131095761686238239)
XLA Ops:
  0.0 0.0 copy-start
  0.0 0.0 copy-start.2
  0.0 1.0 %pad_maximum_fusion.3 = bf16[4,2,1,32,384]{4,3,2,1,0:T(8,128)(2,1)S(1)} fusion(bf16[2,2,1,32,384]{4,3,2,1,0:T(8,128)(2,1)} %param.11, bf16[2,2,1,32,384]{4,3,2,1,0:T(8,128)(2,1)} %param.12), kind=kLoop, calls=%fused_computation.70 | loop fusion | flops 98304 | bytes 393216 | tf_op jit(solution)/shard_map/concatenate | solution.py:322
  1.1 21.3 %all_gather.3 = bf16[4,2,4,32,384]{4,3,2,0,1:T(8,128)(2,1)S(1)} all-gather(bf16[4,2,1,32,384]{4,3,2,0,1:T(8,128)(2,1)S(1)} %copy.31), channel_id=1, replica_groups=mesh['clips'=2,'tm'=4,'rows'=4] {'rows'}, dimensions={2}, use_global_device_ids=true | all-gather | bytes 983040 | tf_op jit(solution)/shard_map/all_gather | solution.py:323
  22.4 0.0 copy-start.7
  22.4 0.2 fusion.9
  22.5 0.0 copy-done.2
  22.5 0.3 fusion.16
  22.8 0.3 pad_slice_fusion.2
  23.2 0.0 copy-done.7
  23.2 0.8 %bitcast_select_fusion = bf16[2,4,32,384]{3,2,1,0:T(8,128)(2,1)} fusion(pred[2]{0:T(512)(128)(4,1)S(1)} %broadcast_compare_fusion, bf16[4,2,4,32,384]{4,3,2,0,1:T(8,128)(2,1)S(1)} %all_gather.3), kind=kLoop, calls=%fused_computation.71 | loop fusion | flops 98304 | bytes 589826 | tf_op jit(solution)/shard_map/jit(_where)/select_n | solution.py:327
  24.0 0.0 copy-start.3
  24.0 0.2 pad_maximum_fusion
  24.1 3.4 %collective-permute-start.1 = (bf16[2,4,32,384]{3,2,1,0:T(8,128)(2,1)}, bf16[2,4,32,384]{3,2,1,0:T(8,128)(2,1)S(1)}, u32[]{:S(2)}, u32[]{:S(2)}) collective-permute-start(bf16[2,4,32,384]{3,2,1,0:T(8,128)(2,1)} %bitcast_select_fusion), channel_id=1, source_target_pairs={{0,8},{4,12},{1,9},{5,13},{2,10},{6,14},{3,11},{7,15},{16,24},{20,... | collective-permute-start | bytes 589832 | tf_op jit(solution)/shard_map/ppermute | solution.py:339
  27.6 0.1 fusion.49
  27.7 0.8 %pad_maximum_fusion.2 = bf16[2,2,4,32,384]{4,3,2,0,1:T(8,128)(2,1)} fusion(bf16[2,1,4,32,384]{4,3,2,0,1:T(8,128)(2,1)S(1)} %get-tuple-element.18, bf16[2,1,4,32,384]{4,3,2,0,1:T(8,128)(2,1)S(1)} %get-tuple-element.17), kind=kLoop, calls=%fused_computation.65 | loop fusion | flops 196608 | bytes 786432 | tf_op jit(solution)/shard_map/concatenate | solution.py:328
  28.4 1.3 %collective-permute-start = (bf16[2,2,4,32,384]{4,3,2,0,1:T(8,128)(2,1)}, bf16[2,2,4,32,384]{4,3,2,0,1:T(8,128)(2,1)S(1)}, u32[]{:S(2)}, u32[]{:S(2)}) collective-permute-start(bf16[2,2,4,32,384]{4,3,2,0,1:T(8,128)(2,1)} %pad_maximum_fusion.2), channel_id=1, source_target_pairs={{0,4},{4,8},{8,12},{1,5},{5,9},{9,13},{2,6},{6,10},{10,14},{3,7},{... | collective-permute-start | bytes 1179656 | tf_op jit(solution)/shard_map/ppermute | solution.py:335
  29.8 0.0 copy-done.3
  29.8 0.1 copy.22.x_ref
  29.9 4.9 %shard_map.109 = f32[2,2,128,384]{3,2,1,0:T(8,128)S(1)} custom-call(bf16[2,2,6,32,1152]{4,3,2,1,0:T(8,128)(2,1)S(1)} %copy.22.x_ref, bf16[3,3,3,384,384]{4,3,2,1,0:T(8,128)(2,1)} %w_hbm.3), custom_call_target="tpu_custom_call" | custom-call | flops 2038431744 | bytes 7864320 | tf_op jit(solution)/shard_map/pallas_call | solution.py:241
  34.8 0.0 collective-permute-done.1
  34.9 0.0 collective-permute-done
  34.9 0.2 fusion.17
  35.0 0.1 compare_reduce_fusion
  35.2 0.3 fusion.24
  35.5 0.1 fusion.33
  35.6 0.1 fusion.43
  35.7 0.2 fusion.46
  36.0 0.2 fusion.30
  36.2 0.4 fusion.50
  36.5 0.2 pad_maximum_fusion.1.x_ref
  36.7 5.0 %shard_map.110 = f32[2,2,128,384]{3,2,1,0:T(8,128)S(1)} custom-call(bf16[2,2,6,32,1152]{4,3,2,1,0:T(8,128)(2,1)S(1)} %pad_maximum_fusion.1.x_ref, bf16[3,3,3,384,384]{4,3,2,1,0:T(8,128)(2,1)} %w_hbm.3), custom_call_target="tpu_custom_call" | custom-call | flops 2038431744 | bytes 7864320 | tf_op jit(solution)/shard_map/pallas_call | solution.py:241
  41.7 0.0 copy-start.4
  41.8 0.1 add.102
  41.8 0.0 copy-start.5
  41.9 0.1 copy.26
  41.9 0.5 %copy-done.4 = f32[384]{0:T(512)S(1)} copy-done((f32[384]{0:T(512)S(1)}, f32[384]{0:T(512)}, u32[]{:S(2)}) %copy-start.4) | copy-done | bytes 1560
  42.4 0.0 copy-start.1
  42.4 0.2 fusion.25
  42.7 0.0 copy-done.5
  42.7 0.2 fusion.27
  42.8 0.0 slice-start
  43.0 0.6 %copy-done.1 = bf16[384,1152]{1,0:T(8,128)(2,1)S(1)} copy-done((bf16[384,1152]{1,0:T(8,128)(2,1)S(1)}, bf16[384,1152]{1,0:T(8,128)(2,1)}, u32[]{:S(2)}) %copy-start.1) | copy-done | bytes 884760
  43.6 0.6 %convolution_add_fusion = f32[512,768]{1,0:T(8,128)S(1)} fusion(bf16[512,384]{1,0:T(8,128)(2,1)S(1)} %bitcast.39, f32[768]{0:T(1024)S(1)} %slice.79, bf16[384,1152]{1,0:T(8,128)(2,1)S(1)} %copy-done.1), kind=kOutput, calls=%fused_computation.7 | convolution fusion | flops 302383104 | bytes 2560000 | tf_op jit(solution)/shard_map/dot_general | solution.py:362
  44.2 0.0 copy-start.6
  44.2 0.0 slice-done
  44.2 0.2 convolution_add_fusion.2
  44.4 0.9 %convolution_multiply_fusion = f32[4,32,128]{2,1,0:T(8,128)S(1)} fusion(f32[4,32,384]{2,1,0:T(8,128)S(1)} %bitcast.40, f32[4,128,768]{2,1,0:T(8,128)S(1)} %bitcast.36), kind=kOutput, calls=%fused_computation.17 | convolution fusion | flops 75513856 | bytes 1048576 | tf_op jit(solution)/shard_map/nqc,nkc->nqk/dot_general | solution.py:376
  45.4 0.2 fusion.51
  45.5 0.3 convolution_convert_fusion
  45.8 0.0 copy-done
  45.9 0.0 copy-done.6
  45.9 0.2 fusion.4
  46.1 0.1 fusion.45
  46.2 0.7 %copy.30 = bf16[2,2,1,32,384]{4,3,2,1,0:T(8,128)(2,1)} copy(bf16[2,2,1,32,384]{4,3,2,0,1:T(8,128)(2,1)S(1)} %fusion.45) | data formatting | bytes 196608 | tf_op jit(solution)/shard_map/convert_element_type | solution.py:395
  (11 shorter events, 0.1 us)
Async XLA Ops:
  0.0 45.9 %copy-start = (bf16[384,384]{1,0:T(8,128)(2,1)S(1)}, bf16[384,384]{1,0:T(8,128)(2,1)}, u32[]{:S(2)}) copy-start(bf16[384,384]{1,0:T(8,128)(2,1)} %param.20) | copy-start | bytes 884740
  0.0 22.5 %copy-start.2 = (f32[384]{0:T(512)S(1)}, f32[384]{0:T(512)}, u32[]{:S(2)}) copy-start(f32[384]{0:T(512)} %param.14) | copy-start | bytes 4612
  22.4 0.8 %copy-start.7 = (s32[2,1]{0,1:T(1,128)S(1)}, s32[2,1]{0,1:T(1,128)}, u32[]{:S(2)}) copy-start(s32[2,1]{0,1:T(1,128)} %param.13) | copy-start | bytes 28
  24.0 5.8 %copy-start.3 = (f32[1152]{0:T(1024)S(1)}, f32[1152]{0:T(1024)}, u32[]{:S(2)}) copy-start(f32[1152]{0:T(1024)} %param.19) | copy-start | bytes 13828
  24.1 10.7 %collective-permute-start.1 = (bf16[2,4,32,384]{3,2,1,0:T(8,128)(2,1)}, bf16[2,4,32,384]{3,2,1,0:T(8,128)(2,1)S(1)}, u32[]{:S(2)}, u32[]{:S(2)}) collective-permute-start(bf16[2,4,32,384]{3,2,1,0:T(8,128)(2,1)} %bitcast_select_fusion), channel_id=1, source_target_pairs={{0,8},{4,12},{1,9},{5,13},{2,10},{6,14},{3,11},{7,15},{16,24},{20,... | collective-permute-start | bytes 589832 | tf_op jit(solution)/shard_map/ppermute | solution.py:339
  28.4 6.4 %collective-permute-start = (bf16[2,2,4,32,384]{4,3,2,0,1:T(8,128)(2,1)}, bf16[2,2,4,32,384]{4,3,2,0,1:T(8,128)(2,1)S(1)}, u32[]{:S(2)}, u32[]{:S(2)}) collective-permute-start(bf16[2,2,4,32,384]{4,3,2,0,1:T(8,128)(2,1)} %pad_maximum_fusion.2), channel_id=1, source_target_pairs={{0,4},{4,8},{8,12},{1,5},{5,9},{9,13},{2,6},{6,10},{10,14},{3,7},{... | collective-permute-start | bytes 1179656 | tf_op jit(solution)/shard_map/ppermute | solution.py:335
  41.7 0.7 %copy-start.4 = (f32[384]{0:T(512)S(1)}, f32[384]{0:T(512)}, u32[]{:S(2)}) copy-start(f32[384]{0:T(512)} %param.16) | copy-start | bytes 4612
  41.8 0.8 %copy-start.5 = (f32[384]{0:T(512)S(1)}, f32[384]{0:T(512)}, u32[]{:S(2)}) copy-start(f32[384]{0:T(512)} %param.17) | copy-start | bytes 4612
  42.4 1.2 %copy-start.1 = (bf16[384,1152]{1,0:T(8,128)(2,1)S(1)}, bf16[384,1152]{1,0:T(8,128)(2,1)}, u32[]{:S(2)}) copy-start(bf16[384,1152]{1,0:T(8,128)(2,1)} %param.18) | copy-start | bytes 2654212
  42.8 1.3 %slice-start = ((f32[1152]{0:T(1024)}), f32[384]{0:T(512)S(1)}, s32[]{:S(2)}) async-start(f32[1152]{0:T(1024)} %param.19), calls=%async_computation | async-start | bytes 4096 | tf_op jit(solution)/shard_map/slice | solution.py:374
  44.2 1.7 %copy-start.6 = (f32[384]{0:T(512)S(1)}, f32[384]{0:T(512)}, u32[]{:S(2)}) copy-start(f32[384]{0:T(512)} %param.21) | copy-start | bytes 4612

commit v20 on v19

--- a/solution.py
+++ b/solution.py
@@ -332,10 +332,10 @@
         ],
         axis=1,
     )
-    prev_raw = lax.ppermute(marked, "tm", ahead)
     own = activate(inner_all, inner_gain)
     own_taps = column_taps(own)
-    own_taps, last_raw = lax.optimization_barrier((own_taps, last_raw))
+    own_taps, last_raw, marked = lax.optimization_barrier((own_taps, last_raw, marked))
+    prev_raw = lax.ppermute(marked, "tm", ahead)
     before_raw = lax.ppermute(last_raw, "tm", [(i, i + 2) for i in range(sections - 2)])
     own_sum = own_conv(own, causal_weight, own_taps)
     own_sum, prev_raw, before_raw = lax.optimization_barrier((own_sum, prev_raw, before_raw))

time: 47.1 us -> 49.5 us (1.051)
  the two profiles are of different devices: /device:TPU:0 before, /device:TPU:1 now
where the time goes in v20:
time: 49.5 us; the launch traced here: 49.3 us
  blocking collectives  18 us (36%)
  Pallas kernels  9.91 us (20%)
  starting transfers between devices  7.63 us (15%)
  other arithmetic  5.46 us (11%)
  local copies, waits for them, and re-layouts  2.84 us (6%)
  waiting for transfers between devices  2.83 us (6%)
  matrix products  2.24 us (5%)
    all_gather x1, blocking collectives, gathered_body(): both_all = lax.all_gather(both, 'rows', axis=2, tiled=True)  18 us
    pallas_call x2, Pallas kernels, conv_part(): pl.pallas_call(functools.partial(conv_part_kernel, plan, first_tap), in_s...  9.91 us
    ppermute x1, starting transfers between devices, gathered_body(): prev_raw = lax.ppermute(marked, 'tm', ahead)  6.32 us
    ppermute x1, waiting for transfers between devices, gathered_body(): lax.ppermute(last_raw, 'tm', [(i, i + 2) for i in range(sections - 2)])  2.83 us
    ppermute x1, starting transfers between devices, gathered_body(): lax.ppermute(last_raw, 'tm', [(i, i + 2) for i in range(sections - 2)])  1.3 us
    unnamed x16, local copies, waits for them, and re-layouts  1.19 us
    concatenate x1, other arithmetic, gathered_body(): both = jnp.concatenate([inner_input, segment_input], axis=0)  1.01 us
  transfers between devices with their start and end apart: 2, of which 1 were waited for; matrix products, arithmetic and copies ran while one was open for 0% of the time, Pallas kernels for 10%

profile of v20, /device:TPU:1, one launch (start us, length us, event | category | flops | bytes accessed | tf_op | source)
XLA Modules:
  0.0 49.3 jit_solution(7434941842106059943)
XLA Ops:
  0.0 0.0 copy-start
  0.0 0.0 copy-start.7
  0.0 0.0 copy-start.2
  0.0 1.0 %pad_maximum_fusion.3 = bf16[4,2,1,32,384]{4,3,2,1,0:T(8,128)(2,1)S(1)} fusion(bf16[2,2,1,32,384]{4,3,2,1,0:T(8,128)(2,1)} %param.11, bf16[2,2,1,32,384]{4,3,2,1,0:T(8,128)(2,1)} %param.12), kind=kLoop, calls=%fused_computation.70 | loop fusion | flops 98304 | bytes 393216 | tf_op jit(solution)/shard_map/concatenate | solution.py:322
  1.1 18.0 %all_gather.3 = bf16[4,2,4,32,384]{4,3,2,0,1:T(8,128)(2,1)S(1)} all-gather(bf16[4,2,1,32,384]{4,3,2,0,1:T(8,128)(2,1)S(1)} %copy.31), channel_id=1, replica_groups=mesh['clips'=2,'tm'=4,'rows'=4] {'rows'}, dimensions={2}, use_global_device_ids=true | all-gather | bytes 983040 | tf_op jit(solution)/shard_map/all_gather | solution.py:323
  19.1 0.2 fusion.9
  19.2 0.0 copy-done.7
  19.3 0.1 fusion.49
  19.4 0.8 %bitcast_select_fusion = bf16[2,4,32,384]{3,2,1,0:T(8,128)(2,1)} fusion(pred[2]{0:T(512)(128)(4,1)S(1)} %broadcast_compare_fusion, bf16[4,2,4,32,384]{4,3,2,0,1:T(8,128)(2,1)S(1)} %all_gather.3), kind=kLoop, calls=%fused_computation.71 | loop fusion | flops 98304 | bytes 589826 | tf_op jit(solution)/shard_map/jit(_where)/select_n | solution.py:327
  20.1 0.0 copy-done.2
  20.1 0.3 fusion.16
  20.5 0.3 pad_slice_fusion.2
  20.8 0.8 %pad_maximum_fusion.2 = bf16[2,2,4,32,384]{4,3,2,0,1:T(8,128)(2,1)} fusion(bf16[2,1,4,32,384]{4,3,2,0,1:T(8,128)(2,1)S(1)} %get-tuple-element.20, bf16[2,1,4,32,384]{4,3,2,0,1:T(8,128)(2,1)S(1)} %get-tuple-element.19), kind=kLoop, calls=%fused_computation.65 | loop fusion | flops 196608 | bytes 786432 | tf_op jit(solution)/shard_map/concatenate | solution.py:328
  21.6 0.0 copy-start.3
  21.6 0.2 pad_maximum_fusion
  21.8 6.3 %collective-permute-start = (bf16[2,2,4,32,384]{4,3,2,0,1:T(8,128)(2,1)}, bf16[2,2,4,32,384]{4,3,2,0,1:T(8,128)(2,1)S(1)}, u32[]{:S(2)}, u32[]{:S(2)}) collective-permute-start(bf16[2,2,4,32,384]{4,3,2,0,1:T(8,128)(2,1)} %pad_maximum_fusion.2), channel_id=1, source_target_pairs={{0,4},{4,8},{8,12},{1,5},{5,9},{9,13},{2,6},{6,10},{10,14},{3,7},{... | collective-permute-start | bytes 1179656 | tf_op jit(solution)/shard_map/ppermute | solution.py:338
  28.1 1.3 %collective-permute-start.1 = (bf16[2,4,32,384]{3,2,1,0:T(8,128)(2,1)}, bf16[2,4,32,384]{3,2,1,0:T(8,128)(2,1)S(1)}, u32[]{:S(2)}, u32[]{:S(2)}) collective-permute-start(bf16[2,4,32,384]{3,2,1,0:T(8,128)(2,1)} %bitcast_select_fusion), channel_id=1, source_target_pairs={{0,8},{4,12},{1,9},{5,13},{2,10},{6,14},{3,11},{7,15},{16,24},{20,... | collective-permute-start | bytes 589832 | tf_op jit(solution)/shard_map/ppermute | solution.py:339
  29.4 0.0 copy-done.3
  29.4 0.1 copy.22.x_ref
  29.6 4.9 %shard_map.109 = f32[2,2,128,384]{3,2,1,0:T(8,128)S(1)} custom-call(bf16[2,2,6,32,1152]{4,3,2,1,0:T(8,128)(2,1)S(1)} %copy.22.x_ref, bf16[3,3,3,384,384]{4,3,2,1,0:T(8,128)(2,1)} %w_hbm.3), custom_call_target="tpu_custom_call" | custom-call | flops 2038431744 | bytes 7864320 | tf_op jit(solution)/shard_map/pallas_call | solution.py:241
  34.5 2.8 %collective-permute-done.1 = bf16[2,4,32,384]{3,2,1,0:T(8,128)(2,1)S(1)} collective-permute-done((bf16[2,4,32,384]{3,2,1,0:T(8,128)(2,1)}, bf16[2,4,32,384]{3,2,1,0:T(8,128)(2,1)S(1)}, u32[]{:S(2)}, u32[]{:S(2)}) %collective-permute-start.1) | collective-permute-done | bytes 196640 | tf_op jit(solution)/shard_map/ppermute | solution.py:339
  37.3 0.0 collective-permute-done
  37.3 0.2 fusion.17
  37.5 0.1 compare_reduce_fusion
  37.6 0.3 fusion.24
  37.9 0.1 fusion.33
  38.1 0.1 fusion.43
  38.2 0.2 fusion.46
  38.4 0.2 fusion.30
  38.6 0.4 fusion.50
  39.0 0.2 pad_maximum_fusion.1.x_ref
  39.2 5.0 %shard_map.110 = f32[2,2,128,384]{3,2,1,0:T(8,128)S(1)} custom-call(bf16[2,2,6,32,1152]{4,3,2,1,0:T(8,128)(2,1)S(1)} %pad_maximum_fusion.1.x_ref, bf16[3,3,3,384,384]{4,3,2,1,0:T(8,128)(2,1)} %w_hbm.3), custom_call_target="tpu_custom_call" | custom-call | flops 2038431744 | bytes 7864320 | tf_op jit(solution)/shard_map/pallas_call | solution.py:241
  44.2 0.0 copy-start.4
  44.2 0.1 add.102
  44.3 0.0 copy-start.5
  44.3 0.1 copy.26
  44.4 0.5 %copy-done.4 = f32[384]{0:T(512)S(1)} copy-done((f32[384]{0:T(512)S(1)}, f32[384]{0:T(512)}, u32[]{:S(2)}) %copy-start.4) | copy-done | bytes 1560
  44.9 0.0 copy-start.1
  44.9 0.2 fusion.25
  45.1 0.0 copy-done.5
  45.1 0.2 fusion.27
  45.3 0.0 slice-start
  45.4 0.6 %copy-done.1 = bf16[384,1152]{1,0:T(8,128)(2,1)S(1)} copy-done((bf16[384,1152]{1,0:T(8,128)(2,1)S(1)}, bf16[384,1152]{1,0:T(8,128)(2,1)}, u32[]{:S(2)}) %copy-start.1) | copy-done | bytes 884760
  46.0 0.6 %convolution_add_fusion = f32[512,768]{1,0:T(8,128)S(1)} fusion(bf16[512,384]{1,0:T(8,128)(2,1)S(1)} %bitcast.39, f32[768]{0:T(1024)S(1)} %slice.79, bf16[384,1152]{1,0:T(8,128)(2,1)S(1)} %copy-done.1), kind=kOutput, calls=%fused_computation.7 | convolution fusion | flops 302383104 | bytes 2560000 | tf_op jit(solution)/shard_map/dot_general | solution.py:362
  46.6 0.0 copy-start.6
  46.6 0.0 slice-done
  46.6 0.2 convolution_add_fusion.2
  46.8 0.9 %convolution_multiply_fusion = f32[4,32,128]{2,1,0:T(8,128)S(1)} fusion(f32[4,32,384]{2,1,0:T(8,128)S(1)} %bitcast.40, f32[4,128,768]{2,1,0:T(8,128)S(1)} %bitcast.36), kind=kOutput, calls=%fused_computation.17 | convolution fusion | flops 75513856 | bytes 1048576 | tf_op jit(solution)/shard_map/nqc,nkc->nqk/dot_general | solution.py:376
  47.8 0.2 fusion.51
  48.0 0.3 convolution_convert_fusion
  48.3 0.0 copy-done
  48.3 0.0 copy-done.6
  48.3 0.2 fusion.4
  48.5 0.1 fusion.45
  48.6 0.7 %copy.30 = bf16[2,2,1,32,384]{4,3,2,1,0:T(8,128)(2,1)} copy(bf16[2,2,1,32,384]{4,3,2,0,1:T(8,128)(2,1)S(1)} %fusion.45) | data formatting | bytes 196608 | tf_op jit(solution)/shard_map/convert_element_type | solution.py:395
  (11 shorter events, 0.1 us)
Async XLA Ops:
  0.0 48.3 %copy-start = (bf16[384,384]{1,0:T(8,128)(2,1)S(1)}, bf16[384,384]{1,0:T(8,128)(2,1)}, u32[]{:S(2)}) copy-start(bf16[384,384]{1,0:T(8,128)(2,1)} %param.20) | copy-start | bytes 884740
  0.0 19.2 %copy-start.7 = (s32[2,1]{0,1:T(1,128)S(1)}, s32[2,1]{0,1:T(1,128)}, u32[]{:S(2)}) copy-start(s32[2,1]{0,1:T(1,128)} %param.13) | copy-start | bytes 28
  0.0 20.1 %copy-start.2 = (f32[384]{0:T(512)S(1)}, f32[384]{0:T(512)}, u32[]{:S(2)}) copy-start(f32[384]{0:T(512)} %param.14) | copy-start | bytes 4612
  21.6 7.8 %copy-start.3 = (f32[1152]{0:T(1024)S(1)}, f32[1152]{0:T(1024)}, u32[]{:S(2)}) copy-start(f32[1152]{0:T(1024)} %param.19) | copy-start | bytes 13828
  21.8 15.6 %collective-permute-start = (bf16[2,2,4,32,384]{4,3,2,0,1:T(8,128)(2,1)}, bf16[2,2,4,32,384]{4,3,2,0,1:T(8,128)(2,1)S(1)}, u32[]{:S(2)}, u32[]{:S(2)}) collective-permute-start(bf16[2,2,4,32,384]{4,3,2,0,1:T(8,128)(2,1)} %pad_maximum_fusion.2), channel_id=1, source_target_pairs={{0,4},{4,8},{8,12},{1,5},{5,9},{9,13},{2,6},{6,10},{10,14},{3,7},{... | collective-permute-start | bytes 1179656 | tf_op jit(solution)/shard_map/ppermute | solution.py:338
  28.1 9.2 %collective-permute-start.1 = (bf16[2,4,32,384]{3,2,1,0:T(8,128)(2,1)}, bf16[2,4,32,384]{3,2,1,0:T(8,128)(2,1)S(1)}, u32[]{:S(2)}, u32[]{:S(2)}) collective-permute-start(bf16[2,4,32,384]{3,2,1,0:T(8,128)(2,1)} %bitcast_select_fusion), channel_id=1, source_target_pairs={{0,8},{4,12},{1,9},{5,13},{2,10},{6,14},{3,11},{7,15},{16,24},{20,... | collective-permute-start | bytes 589832 | tf_op jit(solution)/shard_map/ppermute | solution.py:339
  44.2 0.7 %copy-start.4 = (f32[384]{0:T(512)S(1)}, f32[384]{0:T(512)}, u32[]{:S(2)}) copy-start(f32[384]{0:T(512)} %param.16) | copy-start | bytes 4612
  44.3 0.8 %copy-start.5 = (f32[384]{0:T(512)S(1)}, f32[384]{0:T(512)}, u32[]{:S(2)}) copy-start(f32[384]{0:T(512)} %param.17) | copy-start | bytes 4612
  44.9 1.2 %copy-start.1 = (bf16[384,1152]{1,0:T(8,128)(2,1)S(1)}, bf16[384,1152]{1,0:T(8,128)(2,1)}, u32[]{:S(2)}) copy-start(bf16[384,1152]{1,0:T(8,128)(2,1)} %param.18) | copy-start | bytes 2654212
  45.3 1.3 %slice-start = ((f32[1152]{0:T(1024)}), f32[384]{0:T(512)S(1)}, s32[]{:S(2)}) async-start(f32[1152]{0:T(1024)} %param.19), calls=%async_computation | async-start | bytes 4096 | tf_op jit(solution)/shard_map/slice | solution.py:374
  46.6 1.7 %copy-start.6 = (f32[384]{0:T(512)S(1)}, f32[384]{0:T(512)}, u32[]{:S(2)}) copy-start(f32[384]{0:T(512)} %param.21) | copy-start | bytes 4612

commit v21 on v19

--- a/solution.py
+++ b/solution.py
@@ -335,7 +335,7 @@
     prev_raw = lax.ppermute(marked, "tm", ahead)
     own = activate(inner_all, inner_gain)
     own_taps = column_taps(own)
-    own_taps, last_raw = lax.optimization_barrier((own_taps, last_raw))
+    own_taps, last_raw, _ = lax.optimization_barrier((own_taps, last_raw, marked))
     before_raw = lax.ppermute(last_raw, "tm", [(i, i + 2) for i in range(sections - 2)])
     own_sum = own_conv(own, causal_weight, own_taps)
     own_sum, prev_raw, before_raw = lax.optimization_barrier((own_sum, prev_raw, before_raw))

time: 47.1 us -> 48.7 us (1.034)
  other arithmetic: 5.47 us -> 6.12 us
  starting transfers between devices: 4.71 us -> 5.31 us
    gt x1, other arithmetic: 0.01 us -> 0.66 us  [gathered_body(): wide = (counts > 1)[:, None, None, None]]
    ppermute x1, starting transfers between devices: 3.41 us -> 4.01 us  [gathered_body(): lax.ppermute(last_raw, 'tm', [(i, i + 2) for i in range(sections - 2)])]
  transfers between devices with their start and end apart: 2 -> 2, of which waited for: 0 -> 1; matrix products, arithmetic and copies ran while one was open for 2% -> 4% of each run, Pallas kernels for 10% -> 10%
where the time goes in v21:
time: 48.7 us; the launch traced here: 48.5 us
  blocking collectives  21.3 us (44%)
  Pallas kernels  9.91 us (20%)
  other arithmetic  6.12 us (13%)
  starting transfers between devices  5.31 us (11%)
  local copies, waits for them, and re-layouts  2.84 us (6%)
  matrix products  2.24 us (5%)
    all_gather x1, blocking collectives, gathered_body(): both_all = lax.all_gather(both, 'rows', axis=2, tiled=True)  21.3 us
    pallas_call x2, Pallas kernels, conv_part(): pl.pallas_call(functools.partial(conv_part_kernel, plan, first_tap), in_s...  9.91 us
    ppermute x1, starting transfers between devices, gathered_body(): lax.ppermute(last_raw, 'tm', [(i, i + 2) for i in range(sections - 2)])  4.01 us
    ppermute x1, starting transfers between devices, gathered_body(): prev_raw = lax.ppermute(marked, 'tm', ahead)  1.3 us
    unnamed x16, local copies, waits for them, and re-layouts  1.19 us
    concatenate x1, other arithmetic, gathered_body(): both = jnp.concatenate([inner_input, segment_input], axis=0)  1.01 us
  transfers between devices with their start and end apart: 2, of which 1 were waited for; matrix products, arithmetic and copies ran while one was open for 4% of the time, Pallas kernels for 10%

profile of v21, /device:TPU:0, one launch (start us, length us, event | category | flops | bytes accessed | tf_op | source)
XLA Modules:
  0.0 48.5 jit_solution(6281359539042175203)
XLA Ops:
  0.0 0.0 copy-start
  0.0 1.0 %pad_maximum_fusion.3 = bf16[4,2,1,32,384]{4,3,2,1,0:T(8,128)(2,1)S(1)} fusion(bf16[2,2,1,32,384]{4,3,2,1,0:T(8,128)(2,1)} %param.11, bf16[2,2,1,32,384]{4,3,2,1,0:T(8,128)(2,1)} %param.12), kind=kLoop, calls=%fused_computation.70 | loop fusion | flops 98304 | bytes 393216 | tf_op jit(solution)/shard_map/concatenate | solution.py:322
  1.0 0.0 copy-start.2
  1.1 21.3 %all_gather.3 = bf16[4,2,4,32,384]{4,3,2,0,1:T(8,128)(2,1)S(1)} all-gather(bf16[4,2,1,32,384]{4,3,2,0,1:T(8,128)(2,1)S(1)} %copy.31), channel_id=1, replica_groups=mesh['clips'=2,'tm'=4,'rows'=4] {'rows'}, dimensions={2}, use_global_device_ids=true | all-gather | bytes 983040 | tf_op jit(solution)/shard_map/all_gather | solution.py:323
  22.4 0.7 %broadcast_compare_fusion = pred[2]{0:T(512)(128)(4,1)S(1)} fusion(s32[2,1]{0,1:T(1,128)} %param.13), kind=kLoop, calls=%fused_computation.87 | loop fusion | flops 2 | bytes 10 | tf_op jit(solution)/shard_map/gt | solution.py:326
  23.0 0.1 fusion.49
  23.1 0.8 %pad_maximum_fusion.2 = bf16[2,2,4,32,384]{4,3,2,0,1:T(8,128)(2,1)} fusion(bf16[2,1,4,32,384]{4,3,2,0,1:T(8,128)(2,1)S(1)} %get-tuple-element.18, bf16[2,1,4,32,384]{4,3,2,0,1:T(8,128)(2,1)S(1)} %get-tuple-element.17), kind=kLoop, calls=%fused_computation.65 | loop fusion | flops 196608 | bytes 786432 | tf_op jit(solution)/shard_map/concatenate | solution.py:328
  23.9 1.3 %collective-permute-start = (bf16[2,2,4,32,384]{4,3,2,0,1:T(8,128)(2,1)}, bf16[2,2,4,32,384]{4,3,2,0,1:T(8,128)(2,1)S(1)}, u32[]{:S(2)}, u32[]{:S(2)}) collective-permute-start(bf16[2,2,4,32,384]{4,3,2,0,1:T(8,128)(2,1)} %pad_maximum_fusion.2), channel_id=1, source_target_pairs={{0,4},{4,8},{8,12},{1,5},{5,9},{9,13},{2,6},{6,10},{10,14},{3,7},{... | collective-permute-start | bytes 1179656 | tf_op jit(solution)/shard_map/ppermute | solution.py:335
  25.2 0.2 fusion.9
  25.4 0.8 %bitcast_select_fusion = bf16[2,4,32,384]{3,2,1,0:T(8,128)(2,1)} fusion(pred[2]{0:T(512)(128)(4,1)S(1)} %broadcast_compare_fusion, bf16[4,2,4,32,384]{4,3,2,0,1:T(8,128)(2,1)S(1)} %all_gather.3), kind=kLoop, calls=%fused_computation.71 | loop fusion | flops 98304 | bytes 589826 | tf_op jit(solution)/shard_map/jit(_where)/select_n | solution.py:327
  26.1 0.0 copy-done.2
  26.1 0.3 fusion.16
  26.5 0.3 pad_slice_fusion.2
  26.8 0.0 copy-start.7
  26.8 0.0 copy-start.3
  26.8 0.2 pad_maximum_fusion
  27.0 4.0 %collective-permute-start.1 = (bf16[2,4,32,384]{3,2,1,0:T(8,128)(2,1)}, bf16[2,4,32,384]{3,2,1,0:T(8,128)(2,1)S(1)}, u32[]{:S(2)}, u32[]{:S(2)}) collective-permute-start(bf16[2,4,32,384]{3,2,1,0:T(8,128)(2,1)} %bitcast_select_fusion), channel_id=1, source_target_pairs={{0,8},{4,12},{1,9},{5,13},{2,10},{6,14},{3,11},{7,15},{16,24},{20,... | collective-permute-start | bytes 589832 | tf_op jit(solution)/shard_map/ppermute | solution.py:339
  31.0 0.0 copy-done.7
  31.0 0.0 copy-done.3
  31.1 0.1 copy.22.x_ref
  31.2 4.9 %shard_map.109 = f32[2,2,128,384]{3,2,1,0:T(8,128)S(1)} custom-call(bf16[2,2,6,32,1152]{4,3,2,1,0:T(8,128)(2,1)S(1)} %copy.22.x_ref, bf16[3,3,3,384,384]{4,3,2,1,0:T(8,128)(2,1)} %w_hbm.3), custom_call_target="tpu_custom_call" | custom-call | flops 2038431744 | bytes 7864320 | tf_op jit(solution)/shard_map/pallas_call | solution.py:241
  36.1 0.4 collective-permute-done.1
  36.5 0.0 collective-permute-done
  36.5 0.2 fusion.17
  36.7 0.1 compare_reduce_fusion
  36.8 0.3 fusion.24
  37.1 0.1 fusion.33
  37.3 0.1 fusion.43
  37.4 0.2 fusion.46
  37.6 0.2 fusion.30
  37.8 0.4 fusion.50
  38.2 0.2 pad_maximum_fusion.1.x_ref
  38.4 5.0 %shard_map.110 = f32[2,2,128,384]{3,2,1,0:T(8,128)S(1)} custom-call(bf16[2,2,6,32,1152]{4,3,2,1,0:T(8,128)(2,1)S(1)} %pad_maximum_fusion.1.x_ref, bf16[3,3,3,384,384]{4,3,2,1,0:T(8,128)(2,1)} %w_hbm.3), custom_call_target="tpu_custom_call" | custom-call | flops 2038431744 | bytes 7864320 | tf_op jit(solution)/shard_map/pallas_call | solution.py:241
  43.4 0.0 copy-start.4
  43.4 0.1 add.102
  43.5 0.0 copy-start.5
  43.5 0.1 copy.26
  43.6 0.5 %copy-done.4 = f32[384]{0:T(512)S(1)} copy-done((f32[384]{0:T(512)S(1)}, f32[384]{0:T(512)}, u32[]{:S(2)}) %copy-start.4) | copy-done | bytes 1560
  44.1 0.0 copy-start.1
  44.1 0.2 fusion.25
  44.3 0.0 copy-done.5
  44.3 0.2 fusion.27
  44.5 0.0 slice-start
  44.6 0.6 %copy-done.1 = bf16[384,1152]{1,0:T(8,128)(2,1)S(1)} copy-done((bf16[384,1152]{1,0:T(8,128)(2,1)S(1)}, bf16[384,1152]{1,0:T(8,128)(2,1)}, u32[]{:S(2)}) %copy-start.1) | copy-done | bytes 884760
  45.2 0.6 %convolution_add_fusion = f32[512,768]{1,0:T(8,128)S(1)} fusion(bf16[512,384]{1,0:T(8,128)(2,1)S(1)} %bitcast.39, f32[768]{0:T(1024)S(1)} %slice.79, bf16[384,1152]{1,0:T(8,128)(2,1)S(1)} %copy-done.1), kind=kOutput, calls=%fused_computation.7 | convolution fusion | flops 302383104 | bytes 2560000 | tf_op jit(solution)/shard_map/dot_general | solution.py:362
  45.8 0.0 copy-start.6
  45.8 0.0 slice-done
  45.8 0.2 convolution_add_fusion.2
  46.1 0.9 %convolution_multiply_fusion = f32[4,32,128]{2,1,0:T(8,128)S(1)} fusion(f32[4,32,384]{2,1,0:T(8,128)S(1)} %bitcast.40, f32[4,128,768]{2,1,0:T(8,128)S(1)} %bitcast.36), kind=kOutput, calls=%fused_computation.17 | convolution fusion | flops 75513856 | bytes 1048576 | tf_op jit(solution)/shard_map/nqc,nkc->nqk/dot_general | solution.py:376
  47.0 0.2 fusion.51
  47.2 0.3 convolution_convert_fusion
  47.5 0.0 copy-done
  47.5 0.0 copy-done.6
  47.5 0.2 fusion.4
  47.7 0.1 fusion.45
  47.8 0.7 %copy.30 = bf16[2,2,1,32,384]{4,3,2,1,0:T(8,128)(2,1)} copy(bf16[2,2,1,32,384]{4,3,2,0,1:T(8,128)(2,1)S(1)} %fusion.45) | data formatting | bytes 196608 | tf_op jit(solution)/shard_map/convert_element_type | solution.py:395
  (10 shorter events, 0.1 us)
Async XLA Ops:
  0.0 47.5 %copy-start = (bf16[384,384]{1,0:T(8,128)(2,1)S(1)}, bf16[384,384]{1,0:T(8,128)(2,1)}, u32[]{:S(2)}) copy-start(bf16[384,384]{1,0:T(8,128)(2,1)} %param.20) | copy-start | bytes 884740
  1.0 25.1 %copy-start.2 = (f32[384]{0:T(512)S(1)}, f32[384]{0:T(512)}, u32[]{:S(2)}) copy-start(f32[384]{0:T(512)} %param.14) | copy-start | bytes 4612
  23.9 12.6 %collective-permute-start = (bf16[2,2,4,32,384]{4,3,2,0,1:T(8,128)(2,1)}, bf16[2,2,4,32,384]{4,3,2,0,1:T(8,128)(2,1)S(1)}, u32[]{:S(2)}, u32[]{:S(2)}) collective-permute-start(bf16[2,2,4,32,384]{4,3,2,0,1:T(8,128)(2,1)} %pad_maximum_fusion.2), channel_id=1, source_target_pairs={{0,4},{4,8},{8,12},{1,5},{5,9},{9,13},{2,6},{6,10},{10,14},{3,7},{... | collective-permute-start | bytes 1179656 | tf_op jit(solution)/shard_map/ppermute | solution.py:335
  26.8 4.2 %copy-start.7 = (s32[2,1]{0,1:T(1,128)S(1)}, s32[2,1]{0,1:T(1,128)}, u32[]{:S(2)}) copy-start(s32[2,1]{0,1:T(1,128)} %param.13) | copy-start | bytes 28
  26.8 4.2 %copy-start.3 = (f32[1152]{0:T(1024)S(1)}, f32[1152]{0:T(1024)}, u32[]{:S(2)}) copy-start(f32[1152]{0:T(1024)} %param.19) | copy-start | bytes 13828
  27.0 9.5 %collective-permute-start.1 = (bf16[2,4,32,384]{3,2,1,0:T(8,128)(2,1)}, bf16[2,4,32,384]{3,2,1,0:T(8,128)(2,1)S(1)}, u32[]{:S(2)}, u32[]{:S(2)}) collective-permute-start(bf16[2,4,32,384]{3,2,1,0:T(8,128)(2,1)} %bitcast_select_fusion), channel_id=1, source_target_pairs={{0,8},{4,12},{1,9},{5,13},{2,10},{6,14},{3,11},{7,15},{16,24},{20,... | collective-permute-start | bytes 589832 | tf_op jit(solution)/shard_map/ppermute | solution.py:339
  43.4 0.7 %copy-start.4 = (f32[384]{0:T(512)S(1)}, f32[384]{0:T(512)}, u32[]{:S(2)}) copy-start(f32[384]{0:T(512)} %param.16) | copy-start | bytes 4612
  43.5 0.8 %copy-start.5 = (f32[384]{0:T(512)S(1)}, f32[384]{0:T(512)}, u32[]{:S(2)}) copy-start(f32[384]{0:T(512)} %param.17) | copy-start | bytes 4612
  44.1 1.2 %copy-start.1 = (bf16[384,1152]{1,0:T(8,128)(2,1)S(1)}, bf16[384,1152]{1,0:T(8,128)(2,1)}, u32[]{:S(2)}) copy-start(bf16[384,1152]{1,0:T(8,128)(2,1)} %param.18) | copy-start | bytes 2654212
  44.5 1.3 %slice-start = ((f32[1152]{0:T(1024)}), f32[384]{0:T(512)S(1)}, s32[]{:S(2)}) async-start(f32[1152]{0:T(1024)} %param.19), calls=%async_computation | async-start | bytes 4096 | tf_op jit(solution)/shard_map/slice | solution.py:374
  45.8 1.7 %copy-start.6 = (f32[384]{0:T(512)S(1)}, f32[384]{0:T(512)}, u32[]{:S(2)}) copy-start(f32[384]{0:T(512)} %param.21) | copy-start | bytes 4612

commit v22 on v19

--- a/solution.py
+++ b/solution.py
@@ -185,11 +185,13 @@
     return jax.nn.silu(normalize(field, gain)).astype(jnp.bfloat16)
 
 
-def conv_part_kernel(plan, first_tap, x_ref, w_hbm, o_ref, w_vmem, sems):
+def conv_part_kernel(plan, first_tap, x_hbm, w_hbm, o_ref, x_ref, w_vmem, sems, x_sem):
     clips, held, rows, columns, width = x_ref.shape
     height = rows - 2
     places = height * columns
     channels = w_vmem.shape[-1]
+    x_copy = pltpu.make_async_copy(x_hbm, x_ref, x_sem)
+    x_copy.start()
     copies = []
     for index in range(len(plan)):
         for kh in range(3):
@@ -199,6 +201,7 @@
             )
             copy.start()
             copies.append(copy)
+    x_copy.wait()
     written = set()
     for index, (frame, slot, count) in enumerate(plan):
         for kh in (1, 0, 2):
@@ -241,14 +244,16 @@
     return pl.pallas_call(
         functools.partial(conv_part_kernel, plan, first_tap),
         in_specs=[
-            pl.BlockSpec(memory_space=pltpu.VMEM),
+            pl.BlockSpec(memory_space=pl.ANY),
             pl.BlockSpec(memory_space=pl.ANY),
         ],
         out_specs=pl.BlockSpec(memory_space=pltpu.VMEM),
         out_shape=jax.ShapeDtypeStruct((clips, slots, places, channels), jnp.float32),
         scratch_shapes=[
+            pltpu.VMEM(taps.shape, taps.dtype),
             pltpu.VMEM((blocks, 3, channels, channels), causal_weight.dtype),
             pltpu.SemaphoreType.DMA((blocks,)),
+            pltpu.SemaphoreType.DMA(()),
         ],
         compiler_params=pltpu.CompilerParams(vmem_limit_bytes=48 * 1024 * 1024),
         cost_estimate=pl.CostEstimate(

time: 47.1 us -> 47.8 us (1.015)
  Pallas kernels: 9.92 us -> 10.6 us
    pallas_call x2, Pallas kernels: 9.92 us -> 10.6 us  [conv_part(): pl.pallas_call(functools.partial(conv_part_kernel, plan, first_tap), in_s...]
  transfers between devices with their start and end apart: 2 -> 2, of which waited for: 0 -> 0; matrix products, arithmetic and copies ran while one was open for 2% -> 2% of each run, Pallas kernels for 10% -> 11%
where the time goes in v22:
time: 47.8 us; the launch traced here: 47.6 us
  blocking collectives  21.3 us (45%)
  Pallas kernels  10.6 us (22%)
  other arithmetic  5.47 us (11%)
  starting transfers between devices  4.71 us (10%)
  local copies, waits for them, and re-layouts  2.84 us (6%)
  matrix products  2.24 us (5%)
    all_gather x1, blocking collectives, gathered_body(): both_all = lax.all_gather(both, 'rows', axis=2, tiled=True)  21.3 us
    pallas_call x2, Pallas kernels, conv_part(): pl.pallas_call(functools.partial(conv_part_kernel, plan, first_tap), in_s...  10.6 us
    ppermute x1, starting transfers between devices, gathered_body(): lax.ppermute(last_raw, 'tm', [(i, i + 2) for i in range(sections - 2)])  3.41 us
    ppermute x1, starting transfers between devices, gathered_body(): prev_raw = lax.ppermute(marked, 'tm', ahead)  1.3 us
    unnamed x16, local copies, waits for them, and re-layouts  1.19 us
    concatenate x1, other arithmetic, gathered_body(): both = jnp.concatenate([inner_input, segment_input], axis=0)  1.02 us
  transfers between devices with their start and end apart: 2, of which 0 were waited for; matrix products, arithmetic and copies ran while one was open for 2% of the time, Pallas kernels for 11%

profile of v22, /device:TPU:0, one launch (start us, length us, event | category | flops | bytes accessed | tf_op | source)
XLA Modules:
  0.0 47.6 jit_solution(5793558615742349917)
XLA Ops:
  0.0 0.0 copy-start
  0.0 0.0 copy-start.2
  0.0 1.0 %pad_maximum_fusion.3 = bf16[4,2,1,32,384]{4,3,2,1,0:T(8,128)(2,1)S(1)} fusion(bf16[2,2,1,32,384]{4,3,2,1,0:T(8,128)(2,1)} %param.11, bf16[2,2,1,32,384]{4,3,2,1,0:T(8,128)(2,1)} %param.12), kind=kLoop, calls=%fused_computation.70 | loop fusion | flops 98304 | bytes 393216 | tf_op jit(solution)/shard_map/concatenate | solution.py:327
  1.1 21.3 %all_gather.3 = bf16[4,2,4,32,384]{4,3,2,0,1:T(8,128)(2,1)S(1)} all-gather(bf16[4,2,1,32,384]{4,3,2,0,1:T(8,128)(2,1)S(1)} %copy.31), channel_id=1, replica_groups=mesh['clips'=2,'tm'=4,'rows'=4] {'rows'}, dimensions={2}, use_global_device_ids=true | all-gather | bytes 983040 | tf_op jit(solution)/shard_map/all_gather | solution.py:328
  22.4 0.0 copy-start.7
  22.4 0.2 fusion.9
  22.5 0.0 copy-done.2
  22.5 0.3 fusion.16
  22.8 0.3 pad_slice_fusion.2
  23.2 0.0 copy-done.7
  23.2 0.8 %bitcast_select_fusion = bf16[2,4,32,384]{3,2,1,0:T(8,128)(2,1)} fusion(pred[2]{0:T(512)(128)(4,1)S(1)} %broadcast_compare_fusion, bf16[4,2,4,32,384]{4,3,2,0,1:T(8,128)(2,1)S(1)} %all_gather.3), kind=kLoop, calls=%fused_computation.71 | loop fusion | flops 98304 | bytes 589826 | tf_op jit(solution)/shard_map/jit(_where)/select_n | solution.py:332
  24.0 0.0 copy-start.3
  24.0 0.2 pad_maximum_fusion
  24.1 3.4 %collective-permute-start.1 = (bf16[2,4,32,384]{3,2,1,0:T(8,128)(2,1)}, bf16[2,4,32,384]{3,2,1,0:T(8,128)(2,1)S(1)}, u32[]{:S(2)}, u32[]{:S(2)}) collective-permute-start(bf16[2,4,32,384]{3,2,1,0:T(8,128)(2,1)} %bitcast_select_fusion), channel_id=1, source_target_pairs={{0,8},{4,12},{1,9},{5,13},{2,10},{6,14},{3,11},{7,15},{16,24},{20,... | collective-permute-start | bytes 589832 | tf_op jit(solution)/shard_map/ppermute | solution.py:344
  27.6 0.1 fusion.49
  27.7 0.8 %pad_maximum_fusion.2 = bf16[2,2,4,32,384]{4,3,2,0,1:T(8,128)(2,1)} fusion(bf16[2,1,4,32,384]{4,3,2,0,1:T(8,128)(2,1)S(1)} %get-tuple-element.18, bf16[2,1,4,32,384]{4,3,2,0,1:T(8,128)(2,1)S(1)} %get-tuple-element.17), kind=kLoop, calls=%fused_computation.65 | loop fusion | flops 196608 | bytes 786432 | tf_op jit(solution)/shard_map/concatenate | solution.py:333
  28.4 1.3 %collective-permute-start = (bf16[2,2,4,32,384]{4,3,2,0,1:T(8,128)(2,1)}, bf16[2,2,4,32,384]{4,3,2,0,1:T(8,128)(2,1)S(1)}, u32[]{:S(2)}, u32[]{:S(2)}) collective-permute-start(bf16[2,2,4,32,384]{4,3,2,0,1:T(8,128)(2,1)} %pad_maximum_fusion.2), channel_id=1, source_target_pairs={{0,4},{4,8},{8,12},{1,5},{5,9},{9,13},{2,6},{6,10},{10,14},{3,7},{... | collective-permute-start | bytes 1179656 | tf_op jit(solution)/shard_map/ppermute | solution.py:340
  29.8 0.0 copy-done.3
  29.8 0.1 copy.22.x_hbm
  29.9 5.3 %shard_map.109 = f32[2,2,128,384]{3,2,1,0:T(8,128)S(1)} custom-call(bf16[2,2,6,32,1152]{4,3,2,1,0:T(8,128)(2,1)S(1)} %copy.22.x_hbm, bf16[3,3,3,384,384]{4,3,2,1,0:T(8,128)(2,1)} %w_hbm.3), custom_call_target="tpu_custom_call" | custom-call | flops 2038431744 | bytes 7864320 | tf_op jit(solution)/shard_map/pallas_call | solution.py:244
  35.2 0.0 collective-permute-done.1
  35.2 0.0 collective-permute-done
  35.2 0.2 fusion.17
  35.4 0.1 compare_reduce_fusion
  35.5 0.3 fusion.24
  35.9 0.1 fusion.33
  36.0 0.1 fusion.43
  36.1 0.2 fusion.46
  36.3 0.2 fusion.30
  36.5 0.4 fusion.50
  36.9 0.2 pad_maximum_fusion.1.x_hbm
  37.1 5.4 %shard_map.110 = f32[2,2,128,384]{3,2,1,0:T(8,128)S(1)} custom-call(bf16[2,2,6,32,1152]{4,3,2,1,0:T(8,128)(2,1)S(1)} %pad_maximum_fusion.1.x_hbm, bf16[3,3,3,384,384]{4,3,2,1,0:T(8,128)(2,1)} %w_hbm.3), custom_call_target="tpu_custom_call" | custom-call | flops 2038431744 | bytes 7864320 | tf_op jit(solution)/shard_map/pallas_call | solution.py:244
  42.5 0.0 copy-start.4
  42.5 0.1 add.102
  42.6 0.0 copy-start.5
  42.6 0.1 copy.26
  42.6 0.5 %copy-done.4 = f32[384]{0:T(512)S(1)} copy-done((f32[384]{0:T(512)S(1)}, f32[384]{0:T(512)}, u32[]{:S(2)}) %copy-start.4) | copy-done | bytes 1560
  43.2 0.0 copy-start.1
  43.2 0.2 fusion.25
  43.4 0.0 copy-done.5
  43.4 0.2 fusion.27
  43.6 0.0 slice-start
  43.7 0.6 %copy-done.1 = bf16[384,1152]{1,0:T(8,128)(2,1)S(1)} copy-done((bf16[384,1152]{1,0:T(8,128)(2,1)S(1)}, bf16[384,1152]{1,0:T(8,128)(2,1)}, u32[]{:S(2)}) %copy-start.1) | copy-done | bytes 884760
  44.3 0.6 %convolution_add_fusion = f32[512,768]{1,0:T(8,128)S(1)} fusion(bf16[512,384]{1,0:T(8,128)(2,1)S(1)} %bitcast.39, f32[768]{0:T(1024)S(1)} %slice.79, bf16[384,1152]{1,0:T(8,128)(2,1)S(1)} %copy-done.1), kind=kOutput, calls=%fused_computation.7 | convolution fusion | flops 302383104 | bytes 2560000 | tf_op jit(solution)/shard_map/dot_general | solution.py:367
  44.9 0.0 copy-start.6
  44.9 0.0 slice-done
  44.9 0.2 convolution_add_fusion.2
  45.1 0.9 %convolution_multiply_fusion = f32[4,32,128]{2,1,0:T(8,128)S(1)} fusion(f32[4,32,384]{2,1,0:T(8,128)S(1)} %bitcast.40, f32[4,128,768]{2,1,0:T(8,128)S(1)} %bitcast.36), kind=kOutput, calls=%fused_computation.17 | convolution fusion | flops 75513856 | bytes 1048576 | tf_op jit(solution)/shard_map/nqc,nkc->nqk/dot_general | solution.py:381
  46.1 0.2 fusion.51
  46.3 0.3 convolution_convert_fusion
  46.6 0.0 copy-done
  46.6 0.0 copy-done.6
  46.6 0.2 fusion.4
  46.8 0.1 fusion.45
  46.9 0.7 %copy.30 = bf16[2,2,1,32,384]{4,3,2,1,0:T(8,128)(2,1)} copy(bf16[2,2,1,32,384]{4,3,2,0,1:T(8,128)(2,1)S(1)} %fusion.45) | data formatting | bytes 196608 | tf_op jit(solution)/shard_map/convert_element_type | solution.py:400
  (11 shorter events, 0.1 us)
Async XLA Ops:
  0.0 46.6 %copy-start = (bf16[384,384]{1,0:T(8,128)(2,1)S(1)}, bf16[384,384]{1,0:T(8,128)(2,1)}, u32[]{:S(2)}) copy-start(bf16[384,384]{1,0:T(8,128)(2,1)} %param.20) | copy-start | bytes 884740
  0.0 22.5 %copy-start.2 = (f32[384]{0:T(512)S(1)}, f32[384]{0:T(512)}, u32[]{:S(2)}) copy-start(f32[384]{0:T(512)} %param.14) | copy-start | bytes 4612
  22.4 0.8 %copy-start.7 = (s32[2,1]{0,1:T(1,128)S(1)}, s32[2,1]{0,1:T(1,128)}, u32[]{:S(2)}) copy-start(s32[2,1]{0,1:T(1,128)} %param.13) | copy-start | bytes 28
  24.0 5.8 %copy-start.3 = (f32[1152]{0:T(1024)S(1)}, f32[1152]{0:T(1024)}, u32[]{:S(2)}) copy-start(f32[1152]{0:T(1024)} %param.19) | copy-start | bytes 13828
  24.1 11.1 %collective-permute-start.1 = (bf16[2,4,32,384]{3,2,1,0:T(8,128)(2,1)}, bf16[2,4,32,384]{3,2,1,0:T(8,128)(2,1)S(1)}, u32[]{:S(2)}, u32[]{:S(2)}) collective-permute-start(bf16[2,4,32,384]{3,2,1,0:T(8,128)(2,1)} %bitcast_select_fusion), channel_id=1, source_target_pairs={{0,8},{4,12},{1,9},{5,13},{2,10},{6,14},{3,11},{7,15},{16,24},{20,... | collective-permute-start | bytes 589832 | tf_op jit(solution)/shard_map/ppermute | solution.py:344
  28.4 6.8 %collective-permute-start = (bf16[2,2,4,32,384]{4,3,2,0,1:T(8,128)(2,1)}, bf16[2,2,4,32,384]{4,3,2,0,1:T(8,128)(2,1)S(1)}, u32[]{:S(2)}, u32[]{:S(2)}) collective-permute-start(bf16[2,2,4,32,384]{4,3,2,0,1:T(8,128)(2,1)} %pad_maximum_fusion.2), channel_id=1, source_target_pairs={{0,4},{4,8},{8,12},{1,5},{5,9},{9,13},{2,6},{6,10},{10,14},{3,7},{... | collective-permute-start | bytes 1179656 | tf_op jit(solution)/shard_map/ppermute | solution.py:340
  42.5 0.7 %copy-start.4 = (f32[384]{0:T(512)S(1)}, f32[384]{0:T(512)}, u32[]{:S(2)}) copy-start(f32[384]{0:T(512)} %param.16) | copy-start | bytes 4612
  42.6 0.8 %copy-start.5 = (f32[384]{0:T(512)S(1)}, f32[384]{0:T(512)}, u32[]{:S(2)}) copy-start(f32[384]{0:T(512)} %param.17) | copy-start | bytes 4612
  43.2 1.2 %copy-start.1 = (bf16[384,1152]{1,0:T(8,128)(2,1)S(1)}, bf16[384,1152]{1,0:T(8,128)(2,1)}, u32[]{:S(2)}) copy-start(bf16[384,1152]{1,0:T(8,128)(2,1)} %param.18) | copy-start | bytes 2654212
  43.6 1.3 %slice-start = ((f32[1152]{0:T(1024)}), f32[384]{0:T(512)S(1)}, s32[]{:S(2)}) async-start(f32[1152]{0:T(1024)} %param.19), calls=%async_computation | async-start | bytes 4096 | tf_op jit(solution)/shard_map/slice | solution.py:379
  44.9 1.7 %copy-start.6 = (f32[384]{0:T(512)S(1)}, f32[384]{0:T(512)}, u32[]{:S(2)}) copy-start(f32[384]{0:T(512)} %param.21) | copy-start | bytes 4612
